TPU v7x, 32 devices: a whole 2x2x4 slice. The times are simulated.
32 devices in a mesh: section: 4 (over z), dp: 2 (over core), seq: 4 (over y, x).
Axes of the slice: x: 2, y: 2, z: 4, core: 2. Of those that a mesh axis runs over, the one named last changes fastest.
Arguments:
- qkv: bfloat16 [4, 4, 256, 6144], P('section', 'dp', 'seq'), may hold values from -5 to 5
- stream_lengths: int32 [4, 4], P('section'), may hold values from 1 to 192, 256 in all within a row
- doc_lengths: int32 [4, 4, 8], P('section'), may hold values from 1 to 128, 256 in all within a row
- hand_over: int32 [4, 2], P('section'), may hold values from 0 to 1
Outputs:
- handoff: bfloat16 [4, 4, 256, 4096], P('section', 'dp', 'seq')
Inputs may be any that keep to these rules, and one draw needn't show every extreme that they name: `stream_lengths`: each entry is the length of one row; the 4 entries of one section, taken together, sum to 256, and in each section one entry is exactly the most.
All inputs are finite; a program needn't handle non-finite values.
Results may differ from a plain program's by a relative error of at most 0.0013.
Values may be sent and summed in bfloat16 or wider, within the bound.
No kernel may reach another device: no remote copies, remote signals or barrier semaphores. Data moves between devices by JAX's collectives and lax.ppermute only.
A program may use at most 64 MiB of HBM per device.

v0:
```python
import jax
import jax.numpy as jnp
from jax import lax
from jax.sharding import PartitionSpec as P

H = 32
HD = 128
KV_HEADS = 8
D = 4096
RPR = 2


def swapped(block, axis, distance):
    count = lax.axis_size(axis)
    route = []
    for low in range(count):
        high = low | 1 << distance
        if high != low and high < count:
            route += [(low, high), (high, low)]
    return lax.ppermute(block, axis, route)


def passed_along(value, axis, steps):
    count = lax.axis_size(axis)
    pairs = [(source, (source + steps) % count) for source in range(count)]
    return lax.ppermute(value, axis, pairs)


def attend(row_data, row_ids, stream_lengths, doc_ends, seq_count):
    seg_len = row_data.shape[1]
    length = seg_len * seq_count
    heads_dev = H // seq_count
    group_size = H // KV_HEADS
    kv_dev = max(1, heads_dev // group_size)
    copies = max(1, group_size // heads_dev)
    group_local = heads_dev // kv_dev
    q_width = H * HD
    key_value_width = KV_HEADS * HD
    query_send = row_data[..., :q_width].reshape(RPR, seg_len, seq_count, heads_dev * HD)
    key_portion = row_data[..., q_width : q_width + key_value_width]
    value_part = row_data[..., q_width + key_value_width :]
    key_send = jnp.repeat(key_portion.reshape(RPR, seg_len, KV_HEADS, HD), copies, axis=2).reshape(
        RPR, seg_len, seq_count, kv_dev * HD
    )
    value_send = jnp.repeat(value_part.reshape(RPR, seg_len, KV_HEADS, HD), copies, axis=2).reshape(
        RPR, seg_len, seq_count, kv_dev * HD
    )
    query_heads, kv_heads = (
        lax.all_to_all(query_send, "seq", split_axis=2, concat_axis=1, tiled=True),
        lax.all_to_all(
            jnp.concatenate([key_send, value_send], axis=3),
            "seq",
            split_axis=2,
            concat_axis=1,
            tiled=True,
        ),
    )
    key_block = kv_heads[:, :, 0, : kv_dev * HD]
    value_block = kv_heads[:, :, 0, kv_dev * HD :]
    query_tile_rows = query_heads[:, :, 0, :]
    positions = jnp.arange(length, dtype=jnp.int32)
    row_match = (
        jnp.arange(doc_ends.shape[0], dtype=jnp.int32)[None, :] == row_ids[:, None]
    ).astype(jnp.int32)
    ends_rows = jnp.sum(row_match[:, :, None] * doc_ends[None, :, :], axis=1)
    lengths_rows = jnp.sum(row_match * stream_lengths[None, :], axis=1)
    doc_index = jnp.sum(
        (positions[None, :, None] >= ends_rows[:, None, :]).astype(jnp.int32), axis=2
    )
    causal = positions[:, None] >= positions[None, :]
    score_scale = HD ** (-0.5)
    results = []
    for slot_index in range(RPR):
        allowed = causal & (doc_index[slot_index][:, None] == doc_index[slot_index][None, :])
        query_row = query_tile_rows[slot_index].reshape(length, kv_dev, group_local, HD)
        key_row = key_block[slot_index].reshape(length, kv_dev, HD)
        value_row = value_block[slot_index].reshape(length, kv_dev, HD)
        scores = (
            jnp.einsum("qkgd,skd->kgqs", query_row, key_row, preferred_element_type=jnp.float32)
            * score_scale
        )
        row_top = jnp.max(jnp.where(allowed, scores, -jnp.inf), axis=-1, keepdims=True)
        weights = jnp.where(allowed, jnp.exp(scores - row_top), 0.0)
        row_total = jnp.sum(weights, axis=-1)
        rounded = weights.astype(jnp.bfloat16)
        summed = jnp.einsum(
            "kgqs,skd->qkgd", rounded, value_row, preferred_element_type=jnp.float32
        )
        result = summed / jnp.transpose(row_total, (2, 0, 1))[..., None]
        valid = (positions < lengths_rows[slot_index]).astype(jnp.float32)
        result = result * valid[:, None, None, None]
        results.append(result.reshape(length, heads_dev * HD).astype(jnp.bfloat16))
    return jnp.stack(results, axis=0)


def shards(qkv, stream_lengths, doc_lengths, hand_over):
    seq_count = lax.axis_size("seq")
    replica = lax.axis_index("dp")
    partner = jnp.bitwise_xor(replica, 1)
    handed = lax.dynamic_index_in_dim(hand_over[0], replica, 0, keepdims=False)
    partner_handed = lax.dynamic_index_in_dim(hand_over[0], partner, 0, keepdims=False)
    own_rows = qkv[0]
    seg_len = own_rows.shape[1]
    doc_ends = jnp.cumsum(doc_lengths[0], axis=1)
    lengths_all = stream_lengths[0]
    given = lax.dynamic_index_in_dim(own_rows, handed, 0, keepdims=True)
    kept = lax.dynamic_index_in_dim(own_rows, 1 - handed, 0, keepdims=True)
    received = swapped(given, "dp", 0)
    row_ids = jnp.stack([2 * replica + 1 - handed, 2 * partner + partner_handed])
    attention_output = attend(
        jnp.concatenate([kept, received], axis=0), row_ids, lengths_all, doc_ends, seq_count
    )
    grouped = attention_output.reshape(RPR, seq_count, seg_len, attention_output.shape[2])
    tokens = lax.all_to_all(grouped, "seq", split_axis=1, concat_axis=3, tiled=True)
    tokens = passed_along(tokens, "section", 1)
    return tokens.reshape(1, RPR, seg_len, D)


def solution(mesh):
    return jax.shard_map(
        shards,
        mesh=mesh,
        in_specs=(
            P("section", "dp", "seq", None),
            P("section", None),
            P("section", None, None),
            P("section", None),
        ),
        out_specs=P("section", "dp", "seq", None),
        check_vma=False,
    )
```

profile of v0, /device:TPU:0, one launch (start us, length us, event | category | flops | bytes accessed | tf_op | source)
XLA Modules:
  0.0 89.6 jit_solution(12574448168181887721)
XLA Ops:
  0.0 1.4 %constant_dynamic-slice_fusion = (s32[1,1]{1,0:T(1,128)}, s32[1,1]{1,0:T(1,128)}) fusion(s32[1,2]{1,0:T(1,128)} %param.7, s32[]{:T(128)S(6)} %select_n.30, s32[]{:T(128)S(6)} %select_n.27), kind=kLoop, calls=%fused_computation.53 | loop fusion | bytes 24 | tf_op jit(solution)/shard_map/jit(dynamic_index_in_dim)/dynamic_slice | solution.py:101
  4.9 1.5 %dynamic-slice_bitcast_fusion.1 = (bf16[1,64,6144]{2,1,0:T(8,128)(2,1)S(1)}, bf16[1,64,6144]{2,1,0:T(8,128)(2,1)S(1)}) fusion(bf16[1,2,64,6144]{3,2,1,0:T(8,128)(2,1)} %param.4, s32[]{:T(128)S(6)} %select_n.28, s32[]{:T(128)S(6)} %select_n.29), kind=kLoop, calls=%fused_computation.34 | loop fusion | bytes 3145736 | tf_op jit(solution)/shard_map/jit(dynamic_index_in_dim)/dynamic_slice | solution.py:107
  6.3 0.6 collective-permute-start
  7.6 0.2 reduce_window_sum.14
  8.4 0.1 pad_add_fusion
  8.5 0.2 select_reduce_fusion
  8.7 0.7 fusion.38
  9.4 0.6 compare_convert_fusion.1
  10.0 0.1 fusion.30
  10.1 0.1 multiply_reduce_fusion
  10.2 0.1 convert_reduce_fusion
  10.3 0.2 reshape_reshape_broadcast_in_dim_reshape.6
  10.5 0.2 reshape_reshape_broadcast_in_dim_reshape.7
  10.7 0.2 pad_maximum_fusion.2
  10.9 0.9 copy.54
  11.8 4.7 %all-to-all-start = ((bf16[2,64,4,512]{3,1,0,2:T(8,128)(2,1)}), bf16[2,64,4,512]{3,1,0,2:T(8,128)(2,1)S(1)}, u32[]{:S(2)}, u32[]{:S(2)}) async-start(bf16[2,64,4,512]{3,1,0,2:T(8,128)(2,1)} %copy.54), calls=%async_computation | async-start | bytes 1048576 | tf_op jit(solution)/shard_map/all_to_all | solution.py:50
  16.5 0.1 pad_maximum_fusion
  16.6 1.1 %copy.88 = bf16[2,8,4,8,1024]{4,3,1,0,2:T(8,128)(2,1)} copy(bf16[2,8,4,8,1024]{4,3,2,1,0:T(8,128)(2,1)S(1)} %bitcast.113) | data formatting | bytes 2097152 | tf_op jit(solution)/shard_map/reshape | solution.py:39
  17.7 7.5 %all-to-all-done = bf16[2,64,4,512]{3,1,0,2:T(8,128)(2,1)S(1)} async-done(((bf16[2,64,4,512]{3,1,0,2:T(8,128)(2,1)}), bf16[2,64,4,512]{3,1,0,2:T(8,128)(2,1)S(1)}, u32[]{:S(2)}, u32[]{:S(2)}) %all-to-all-start) | async-done | bytes 524320 | tf_op jit(solution)/shard_map/all_to_all | solution.py:50
  25.2 3.5 %all-to-all-start.1 = ((bf16[2,64,4,1024]{3,1,0,2:T(8,128)(2,1)}), bf16[2,64,4,1024]{3,1,0,2:T(8,128)(2,1)S(1)}, u32[]{:S(2)}, u32[]{:S(2)}) async-start(bf16[2,64,4,1024]{3,1,0,2:T(8,128)(2,1)} %bitcast.111), calls=%async_computation.1 | async-start | bytes 2097152 | tf_op jit(solution)/shard_map/all_to_all | solution.py:49
  28.7 0.7 compare_convert_fusion
  29.4 0.1 fusion.29
  29.6 0.1 fusion.28
  29.8 0.1 copy.57
  29.9 0.1 copy.56
  30.0 0.1 copy.64
  30.1 0.1 copy.63
  30.2 12.0 %all-to-all-done.1 = bf16[2,64,4,1024]{3,1,0,2:T(8,128)(2,1)S(1)} async-done(((bf16[2,64,4,1024]{3,1,0,2:T(8,128)(2,1)}), bf16[2,64,4,1024]{3,1,0,2:T(8,128)(2,1)S(1)}, u32[]{:S(2)}, u32[]{:S(2)}) %all-to-all-start.1) | async-done | bytes 1048608 | tf_op jit(solution)/shard_map/all_to_all | solution.py:49
  42.1 0.1 fusion.35
  42.2 0.4 reshape_squeeze.20
  42.6 0.5 fusion.26
  43.1 0.9 fusion.40
  44.0 0.3 fusion.14
  44.3 0.3 copy.62
  44.6 0.4 convert_element_type.63
  45.0 0.4 reshape_squeeze.23
  45.4 0.5 fusion.24
  45.8 0.9 fusion.39
  46.7 0.3 fusion.15
  47.1 0.3 copy.68
  47.4 0.4 convert_element_type.67
  47.8 0.1 pad_maximum_fusion.1
  47.9 0.1 copy.69
  47.9 16.1 %all_to_all.51 = bf16[2,4,64,1024]{3,2,0,1:T(8,128)(2,1)S(1)} all-to-all(bf16[2,4,64,1024]{3,2,0,1:T(8,128)(2,1)S(1)} %copy.69), channel_id=1, replica_groups=mesh['section'=4,'dp'=2,'seq'=4] {'seq'}, dimensions={1} | all-to-all | bytes 2097152 | tf_op jit(solution)/shard_map/all_to_all | solution.py:114
  64.0 0.1 copy.82
  64.1 1.6 %collective-permute-start.1 = (bf16[2,1,64,4096]{3,2,0,1:T(8,128)(2,1)S(1)}, bf16[2,1,64,4096]{3,2,0,1:T(8,128)(2,1)S(1)}, u32[]{:S(2)}, u32[]{:S(2)}) collective-permute-start(bf16[2,1,64,4096]{3,2,0,1:T(8,128)(2,1)S(1)} %bitcast.116), channel_id=1, source_target_pairs={{0,8},{8,16},{16,24},{24,0},{1,9},{9,17},{17,25},{25,1},{2,10},{10... | collective-permute-start | bytes 3145736 | tf_op jit(solution)/shard_map/ppermute | solution.py:26
  65.7 22.9 %collective-permute-done.1 = bf16[2,1,64,4096]{3,2,0,1:T(8,128)(2,1)S(1)} collective-permute-done((bf16[2,1,64,4096]{3,2,0,1:T(8,128)(2,1)S(1)}, bf16[2,1,64,4096]{3,2,0,1:T(8,128)(2,1)S(1)}, u32[]{:S(2)}, u32[]{:S(2)}) %collective-permute-start.1) | collective-permute-done | bytes 1048608 | tf_op jit(solution)/shard_map/ppermute | solution.py:26
  88.7 1.0 %copy.90 = bf16[1,2,64,4096]{3,2,1,0:T(8,128)(2,1)} copy(bf16[1,2,64,4096]{3,2,1,0:T(8,128)(2,1)S(1)} %bitcast.117) | data formatting | bytes 2097152
  (9 shorter events, 0.1 us)
Async XLA Ops:
  0.0 7.6 %copy-start = (s32[1,4,8]{2,1,0:T(4,128)S(1)}, s32[1,4,8]{2,1,0:T(4,128)}, u32[]{:S(2)}) copy-start(s32[1,4,8]{2,1,0:T(4,128)} %param.6) | copy-start | bytes 388
  0.0 8.5 %copy-start.1 = (s32[1,4]{1,0:T(1,128)S(1)}, s32[1,4]{1,0:T(1,128)}, u32[]{:S(2)}) copy-start(s32[1,4]{1,0:T(1,128)} %param.5) | copy-start | bytes 52
  6.3 3.9 %collective-permute-start = (bf16[1,64,6144]{2,1,0:T(8,128)(2,1)S(1)}, bf16[1,64,6144]{2,1,0:T(8,128)(2,1)S(1)}, u32[]{:S(2)}, u32[]{:S(2)}) collective-permute-start(bf16[1,64,6144]{2,1,0:T(8,128)(2,1)S(1)} %get-tuple-element.8), channel_id=1, source_target_pairs={{0,4},{4,0},{1,5},{5,1},{2,6},{6,2},{3,7},{7,3},{8,12},{12,8},{9,1... | collective-permute-start | bytes 2359304 | tf_op jit(solution)/shard_map/ppermute | solution.py:20
  11.8 13.4 %all-to-all-start = ((bf16[2,64,4,512]{3,1,0,2:T(8,128)(2,1)}), bf16[2,64,4,512]{3,1,0,2:T(8,128)(2,1)S(1)}, u32[]{:S(2)}, u32[]{:S(2)}) async-start(bf16[2,64,4,512]{3,1,0,2:T(8,128)(2,1)} %copy.54), calls=%async_computation | async-start | bytes 1048576 | tf_op jit(solution)/shard_map/all_to_all | solution.py:50
  25.2 16.9 %all-to-all-start.1 = ((bf16[2,64,4,1024]{3,1,0,2:T(8,128)(2,1)}), bf16[2,64,4,1024]{3,1,0,2:T(8,128)(2,1)S(1)}, u32[]{:S(2)}, u32[]{:S(2)}) async-start(bf16[2,64,4,1024]{3,1,0,2:T(8,128)(2,1)} %bitcast.111), calls=%async_computation.1 | async-start | bytes 2097152 | tf_op jit(solution)/shard_map/all_to_all | solution.py:49
  64.1 24.6 %collective-permute-start.1 = (bf16[2,1,64,4096]{3,2,0,1:T(8,128)(2,1)S(1)}, bf16[2,1,64,4096]{3,2,0,1:T(8,128)(2,1)S(1)}, u32[]{:S(2)}, u32[]{:S(2)}) collective-permute-start(bf16[2,1,64,4096]{3,2,0,1:T(8,128)(2,1)S(1)} %bitcast.116), channel_id=1, source_target_pairs={{0,8},{8,16},{16,24},{24,0},{1,9},{9,17},{17,25},{25,1},{2,10},{10... | collective-permute-start | bytes 3145736 | tf_op jit(solution)/shard_map/ppermute | solution.py:26
where the time goes:
time: 90 us; the launch traced here: 89.6 us
  waiting for transfers between devices  42.4 us (47%)
  blocking collectives  16.1 us (18%)
  starting transfers between devices  10.4 us (12%)
  local copies, waits for them, and re-layouts  9.62 us (11%)
  between operations  5.03 us (6%)
  other arithmetic  4.47 us (5%)
  matrix products  1.61 us (2%)
    ppermute x1, waiting for transfers between devices, passed_along(): return lax.ppermute(value, axis, pairs)  22.9 us
    all_to_all x1, blocking collectives, shards(): lax.all_to_all(grouped, 'seq', split_axis=1, concat_axis=3, tiled=True)  16.1 us
    all_to_all x1, waiting for transfers between devices, attend(): lax.all_to_all(query_send, 'seq', split_axis=2, concat_axis=1, tiled=True)  12 us
    all_to_all x1, waiting for transfers between devices, attend(): lax.all_to_all(jnp.concatenate([key_send, value_send], axis=3), 'seq', sp...  7.52 us
    all_to_all x1, starting transfers between devices, attend(): lax.all_to_all(jnp.concatenate([key_send, value_send], axis=3), 'seq', sp...  4.71 us
    all_to_all x1, starting transfers between devices, attend(): lax.all_to_all(query_send, 'seq', split_axis=2, concat_axis=1, tiled=True)  3.52 us
  transfers between devices with their start and end apart: 4, of which 3 were waited for; matrix products, arithmetic and copies ran while one was open for 5% of the time, Pallas kernels for 0%

commit v1 on v0

v1 whole, which is shorter than its diff:
```python
import jax
import jax.numpy as jnp
from jax import lax
from jax.sharding import PartitionSpec as P

H = 32
HD = 128
KV_HEADS = 8
D = 4096
RPR = 2


def swapped(block, axis, distance):
    count = lax.axis_size(axis)
    route = []
    for low in range(count):
        high = low | 1 << distance
        if high != low and high < count:
            route += [(low, high), (high, low)]
    return lax.ppermute(block, axis, route)


def passed_along(value, axis, steps):
    count = lax.axis_size(axis)
    pairs = [(source, (source + steps) % count) for source in range(count)]
    return lax.ppermute(value, axis, pairs)


def doc_of(positions, ends):
    return jnp.sum((positions[:, None] >= ends[None, :]).astype(jnp.int32), axis=1)


def attend_row(query_rows, key_rows, value_rows, query_pos, key_pos, ends, length):
    seg_len = query_rows.shape[0]
    key_len = key_rows.shape[0]
    group_size = H // KV_HEADS
    query_doc = doc_of(query_pos, ends)
    key_doc = doc_of(key_pos, ends)
    allowed = (key_pos[None, :] <= query_pos[:, None]) & (key_doc[None, :] == query_doc[:, None])
    queries = query_rows.reshape(seg_len, KV_HEADS, group_size, HD)
    keys = key_rows.reshape(key_len, KV_HEADS, HD)
    values = value_rows.reshape(key_len, KV_HEADS, HD)
    scores = (
        jnp.einsum("qkgd,skd->kgqs", queries, keys, preferred_element_type=jnp.float32)
        * HD ** (-0.5)
    )
    row_top = jnp.max(jnp.where(allowed, scores, -jnp.inf), axis=-1, keepdims=True)
    weights = jnp.where(allowed, jnp.exp(scores - row_top), 0.0)
    row_total = jnp.sum(weights, axis=-1)
    rounded = weights.astype(jnp.bfloat16)
    summed = jnp.einsum("kgqs,skd->qkgd", rounded, values, preferred_element_type=jnp.float32)
    result = summed / jnp.transpose(row_total, (2, 0, 1))[..., None]
    valid = (query_pos < length).astype(jnp.float32)
    result = result * valid[:, None, None, None]
    return result.reshape(seg_len, D).astype(jnp.bfloat16)


def shards(qkv, stream_lengths, doc_lengths, hand_over):
    seq_count = lax.axis_size("seq")
    seq_index = lax.axis_index("seq")
    replica = lax.axis_index("dp")
    partner = jnp.bitwise_xor(replica, 1)
    handed = lax.dynamic_index_in_dim(hand_over[0], replica, 0, keepdims=False)
    partner_handed = lax.dynamic_index_in_dim(hand_over[0], partner, 0, keepdims=False)
    own_rows = qkv[0]
    seg_len = own_rows.shape[1]
    doc_ends = jnp.cumsum(doc_lengths[0], axis=1)
    lengths_all = stream_lengths[0]
    given = lax.dynamic_index_in_dim(own_rows, handed, 0, keepdims=True)
    kept = lax.dynamic_index_in_dim(own_rows, 1 - handed, 0, keepdims=True)
    received = swapped(given, "dp", 0)
    rows = jnp.concatenate([kept, received], axis=0)
    row_ids = [2 * replica + 1 - handed, 2 * partner + partner_handed]

    kv_local = rows[..., D:]
    pieces = [kv_local]
    chunk_ids = [seq_index]
    for shift in range(1, seq_count):
        pieces.append(passed_along(kv_local, "seq", shift))
        chunk_ids.append((seq_index - shift) % seq_count)
    kv_all = jnp.concatenate(pieces, axis=1)
    local = jnp.arange(seg_len, dtype=jnp.int32)
    key_pos = jnp.concatenate([chunk * seg_len + local for chunk in chunk_ids])
    query_pos = seq_index * seg_len + local
    key_value_width = KV_HEADS * HD

    results = []
    for slot in range(RPR):
        ends = lax.dynamic_index_in_dim(doc_ends, row_ids[slot], 0, keepdims=False)
        length = lax.dynamic_index_in_dim(lengths_all, row_ids[slot], 0, keepdims=False)
        results.append(
            attend_row(
                rows[slot, :, :D],
                kv_all[slot, :, :key_value_width],
                kv_all[slot, :, key_value_width:],
                query_pos,
                key_pos,
                ends,
                length,
            )
        )
    out = jnp.stack(results, axis=0)
    out = passed_along(out, "section", 1)
    return out.reshape(1, RPR, seg_len, D)


def solution(mesh):
    return jax.shard_map(
        shards,
        mesh=mesh,
        in_specs=(
            P("section", "dp", "seq", None),
            P("section", None),
            P("section", None, None),
            P("section", None),
        ),
        out_specs=P("section", "dp", "seq", None),
        check_vma=False,
    )
```

time: 90 us -> 88.6 us (0.984)
  blocking collectives: 16.1 us -> 0 us
  local copies, waits for them, and re-layouts: 9.62 us -> 18.5 us
  waiting for transfers between devices: 42.4 us -> 47.2 us
  starting transfers between devices: 10.4 us -> 6.66 us
  matrix products: 1.61 us -> 4.83 us
  other arithmetic: 4.47 us -> 6.6 us
    ppermute x1 -> x4, waiting for transfers between devices: 22.9 us -> 47.2 us  [passed_along(): return lax.ppermute(value, axis, pairs)]
    all_to_all x2 -> x0, waiting for transfers between devices: 19.5 us -> none  [the longest x1 12 us: attend(): lax.all_to_all(query_send, 'seq', split_axis=2, concat_axis=1, tiled=True)]
    all_to_all x1 -> x0, blocking collectives: 16.1 us -> none  [shards(): lax.all_to_all(grouped, 'seq', split_axis=1, concat_axis=3, tiled=True)]
    all_to_all x2 -> x0, starting transfers between devices: 8.23 us -> none  [the longest x1 4.71 us: attend(): lax.all_to_all(jnp.concatenate([key_send, value_send], axis=3), 'seq', sp...]
    ppermute x0 -> x4, local copies, waits for them, and re-layouts: none -> 5.9 us  [the longest x3 4.35 us: passed_along(): return lax.ppermute(value, axis, pairs)]
    ppermute x1 -> x4, starting transfers between devices: 1.63 us -> 6.17 us  [passed_along(): return lax.ppermute(value, axis, pairs)]
    concatenate x2 -> x3, other arithmetic: 0.32 us -> 3.87 us  [the longest x1 2.55 us: shards(): kv_all = jnp.concatenate(pieces, axis=1)]
    sub x0 -> x1, matrix products: none -> 2.3 us  [attend_row(): weights = jnp.where(allowed, jnp.exp(scores - row_top), 0.0)]
  transfers between devices with their start and end apart: 4 -> 5, of which waited for: 3 -> 3; matrix products, arithmetic and copies ran while one was open for 5% -> 9% of each run, Pallas kernels for 0% -> 0%
where the time goes in v1:
time: 88.6 us; the launch traced here: 88.1 us
  waiting for transfers between devices  47.2 us (53%)
  local copies, waits for them, and re-layouts  18.5 us (21%)
  starting transfers between devices  6.66 us (8%)
  other arithmetic  6.6 us (7%)
  matrix products  4.83 us (5%)
  between operations  4.25 us (5%)
    ppermute x4, waiting for transfers between devices, passed_along(): return lax.ppermute(value, axis, pairs)  47.2 us
    ppermute x4, starting transfers between devices, passed_along(): return lax.ppermute(value, axis, pairs)  6.17 us
    ppermute x3, local copies, waits for them, and re-layouts, passed_along(): return lax.ppermute(value, axis, pairs)  4.35 us
    dynamic_slice x2, local copies, waits for them, and re-layouts, shards(): kept = lax.dynamic_index_in_dim(own_rows, 1 - handed, 0, keepdims=True)  3.22 us
    concatenate x1, other arithmetic, shards(): kv_all = jnp.concatenate(pieces, axis=1)  2.55 us
    sub x1, matrix products, attend_row(): weights = jnp.where(allowed, jnp.exp(scores - row_top), 0.0)  2.3 us
    unnamed x9, local copies, waits for them, and re-layouts  2.28 us
    dot_general x2, matrix products, attend_row(): jnp.einsum('kgqs,skd->qkgd', rounded, values, preferred_element_type=jnp....  2.11 us
  transfers between devices with their start and end apart: 5, of which 3 were waited for; matrix products, arithmetic and copies ran while one was open for 9% of the time, Pallas kernels for 0%

profile of v1, /device:TPU:0, one launch (start us, length us, event | category | flops | bytes accessed | tf_op | source)
XLA Modules:
  0.0 88.1 jit_solution(7191214093129321766)
XLA Ops:
  0.0 0.0 copy-start.3
  0.0 1.4 %constant_dynamic-slice_fusion.2 = (s32[1,1]{1,0:T(1,128)}, s32[1,1]{1,0:T(1,128)}) fusion(s32[1,2]{1,0:T(1,128)} %param.7, s32[]{:T(128)S(6)} %select_n.61, s32[]{:T(128)S(6)} %select_n.52), kind=kLoop, calls=%fused_computation.45 | loop fusion | bytes 24 | tf_op jit(solution)/shard_map/jit(dynamic_index_in_dim)/dynamic_slice | solution.py:64
  4.2 2.4 %constant_dynamic-slice_fusion.5 = (bf16[1,1,64,6144]{3,2,1,0:T(8,128)(2,1)S(1)}, bf16[1,64,6144]{2,1,0:T(8,128)(2,1)}) fusion(bf16[1,2,64,6144]{3,2,1,0:T(8,128)(2,1)} %param.4, s32[]{:T(128)S(6)} %select_n.53, s32[]{:T(128)S(6)} %select_n.54), kind=kLoop, calls=%fused_computation.48 | loop fusion | bytes 3145736 | tf_op jit(solution)/shard_map/jit(dynamic_index_in_dim)/dynamic_slice | solution.py:70
  6.6 0.5 collective-permute-start
  8.3 0.0 copy-done.3
  8.4 0.2 reduce_window_sum.11
  8.5 0.8 copy.34
  9.4 1.0 %slice.30 = bf16[1,64,4096]{1,2,0:T(8,128)(2,1)} slice(bf16[1,64,6144]{1,2,0:T(8,128)(2,1)S(1)} %bitcast.89), slice={[0:1], [0:64], [0:4096]} | slice | bytes 1048576 | tf_op jit(solution)/shard_map/slice | solution.py:93
  10.4 0.0 copy-done.2
  10.4 0.7 constant_dynamic-slice_fusion.3
  11.1 1.3 %compare_convert_fusion = (f32[64]{0:T(128)S(1)}, f32[64]{0:T(128)S(1)}) fusion(s32[]{:T(128)} %bitcast.23, s32[]{:T(128)S(6)} %mul.47, s32[]{:T(128)} %bitcast.13), kind=kLoop, calls=%fused_computation.50 | loop fusion | flops 320 | bytes 524 | tf_op jit(solution)/shard_map/convert_element_type | solution.py:53
  12.4 0.0 collective-permute-done
  12.4 1.6 %copy.35 = bf16[1,64,6144]{1,2,0:T(8,128)(2,1)} copy(bf16[1,64,6144]{2,1,0:T(8,128)(2,1)S(1)} %collective-permute-done) | data formatting | bytes 1572864 | tf_op jit(solution)/shard_map/ppermute | solution.py:20
  13.9 1.2 %pad_maximum_fusion.1 = bf16[2,64,2048]{1,2,0:T(8,128)(2,1)S(1)} fusion(bf16[1,64,6144]{1,2,0:T(8,128)(2,1)} %copy.35, bf16[1,64,6144]{1,2,0:T(8,128)(2,1)S(1)} %bitcast.90), kind=kLoop, calls=%fused_computation.23 | loop fusion | flops 1048576 | bytes 2097152 | tf_op jit(solution)/shard_map/concatenate | solution.py:72
  15.2 1.1 %copy.36 = bf16[2,64,2048]{2,1,0:T(8,128)(2,1)} copy(bf16[2,64,2048]{1,2,0:T(8,128)(2,1)S(1)} %pad_maximum_fusion.1) | data formatting | bytes 1048576 | tf_op jit(solution)/shard_map/slice | solution.py:75
  16.3 3.4 %collective-permute-start.3 = (bf16[2,64,2048]{2,1,0:T(8,128)(2,1)}, bf16[2,64,2048]{2,1,0:T(8,128)(2,1)S(1)}, u32[]{:S(2)}, u32[]{:S(2)}) collective-permute-start(bf16[2,64,2048]{2,1,0:T(8,128)(2,1)} %copy.36), channel_id=1, source_target_pairs={{0,3},{1,0},{2,1},{3,2},{4,7},{5,4},{6,5},{7,6},{8,11},{9,8},{10,9... | collective-permute-start | bytes 1572872 | tf_op jit(solution)/shard_map/ppermute | solution.py:26
  19.7 0.5 collective-permute-start.2
  20.3 0.6 collective-permute-start.1
  20.8 0.1 pad_add_fusion
  20.9 0.1 convert_reduce_fusion.3
  21.0 0.1 convert_reduce_fusion.1
  21.1 0.1 compare_and_fusion.1
  21.2 1.2 %reshape_squeeze.23 = bf16[64,8,4,128]{3,2,1,0:T(4,128)(2,1)} reshape(bf16[1,64,4096]{2,1,0:T(8,128)(2,1)S(1)} %slice.33) | data formatting | bytes 1048576 | tf_op jit(solution)/shard_map/reshape;squeeze | solution.py:40
  22.4 10.0 %collective-permute-done.3 = bf16[2,64,2048]{2,1,0:T(8,128)(2,1)S(1)} collective-permute-done((bf16[2,64,2048]{2,1,0:T(8,128)(2,1)}, bf16[2,64,2048]{2,1,0:T(8,128)(2,1)S(1)}, u32[]{:S(2)}, u32[]{:S(2)}) %collective-permute-start.3) | collective-permute-done | bytes 524320 | tf_op jit(solution)/shard_map/ppermute | solution.py:26
  32.4 0.5 copy.41
  32.9 12.4 %collective-permute-done.2 = bf16[2,64,2048]{2,1,0:T(8,128)(2,1)} collective-permute-done((bf16[2,64,2048]{2,1,0:T(8,128)(2,1)}, bf16[2,64,2048]{2,1,0:T(8,128)(2,1)}, u32[]{:S(2)}, u32[]{:S(2)}) %collective-permute-start.2) | collective-permute-done | bytes 524320 | tf_op jit(solution)/shard_map/ppermute | solution.py:26
  45.4 1.5 %copy.40 = bf16[2,64,2048]{1,2,0:T(8,128)(2,1)S(1)} copy(bf16[2,64,2048]{2,1,0:T(8,128)(2,1)} %collective-permute-done.2) | data formatting | bytes 1048576 | tf_op jit(solution)/shard_map/ppermute | solution.py:26
  46.9 0.0 collective-permute-done.1
  46.9 2.4 %copy.39 = bf16[2,64,2048]{1,2,0:T(8,128)(2,1)} copy(bf16[2,64,2048]{2,1,0:T(8,128)(2,1)} %collective-permute-done.1) | data formatting | bytes 1048576 | tf_op jit(solution)/shard_map/ppermute | solution.py:26
  49.2 2.6 %pad_maximum_fusion = bf16[2,256,2048]{1,2,0:T(8,128)(2,1)S(1)} fusion(bf16[2,64,2048]{1,2,0:T(8,128)(2,1)S(1)} %copy.41, bf16[2,64,2048]{1,2,0:T(8,128)(2,1)S(1)} %copy.40, bf16[2,64,2048]{1,2,0:T(8,128)(2,1)} %copy.39, bf16[2,64,2048]{1,2,0:T(8,128)(2,1)S(1)} %pad_maximum_fusion.1), kind=kLoop, calls=%fused_computation.2 | loop fusion | flops 8388608 | bytes 4194304 | tf_op jit(solution)/shard_map/concatenate | solution.py:81
  51.8 0.0 copy-start.1
  51.8 0.1 fusion.34
  52.0 1.1 %copy-done.1 = bf16[1,64,4096]{1,2,0:T(8,128)(2,1)S(1)} copy-done((bf16[1,64,4096]{1,2,0:T(8,128)(2,1)S(1)}, bf16[1,64,4096]{1,2,0:T(8,128)(2,1)}, u32[]{:S(2)}) %copy-start.1) | copy-done | bytes 524312
  53.0 2.3 %fusion.36 = (f32[8,4,64]{2,1,0:T(4,128)S(1)}, bf16[8,4,64,256]{3,2,1,0:T(8,128)(2,1)}) fusion(pred[64,256]{1,0:T(8,128)(4,1)S(1)} %get-tuple-element.17, bf16[256,8,128,1]{0,2,3,1:T(8,128)(2,1)S(1)} %bitcast.96, bf16[64,8,4,128]{0,3,2,1:T(8,128)(2,1)S(1)} %bitcast.92), kind=kOutput, calls=%fused_computation.65 | convolution fusion | flops 272105728 | bytes 2121728 | tf_op jit(solution)/shard_map/sub | solution.py:48
  55.3 1.7 %fusion.14 = bf16[64,8,4,128]{3,0,2,1:T(8,128)(2,1)S(1)} fusion(bf16[256,8,128,1]{0,2,3,1:T(8,128)(2,1)S(1)} %bitcast.95, bf16[8,4,64,256]{3,2,1,0:T(8,128)(2,1)} %get-tuple-element.26, f32[64]{0:T(128)S(1)} %get-tuple-element.28, f32[64,8,4]{0,2,1:T(4,128)S(1)} %bitcast.99), kind=kOutput, calls=%fused_computation.21 | convolution fusion | flops 135004160 | bytes 2105600 | tf_op jit(solution)/shard_map/kgqs,skd->qkgd/dot_general | solution.py:51
  57.0 0.0 copy-start
  57.0 0.4 copy.46
  57.4 0.4 convert_element_type.63
  57.8 0.2 copy-done
  58.0 0.4 fusion.24
  58.5 0.9 %fusion.35 = (f32[8,4,64]{2,1,0:T(4,128)S(1)}, bf16[8,4,64,256]{3,2,1,0:T(8,128)(2,1)S(1)}) fusion(f32[8,256,64,4]{1,2,3,0:T(8,128)S(1)} %fusion.24, pred[64,256]{1,0:T(8,128)(4,1)S(1)} %get-tuple-element.18), kind=kOutput, calls=%fused_computation.64 | output fusion | flops 3670271 | bytes 3170304 | tf_op jit(solution)/shard_map/sub | solution.py:48
  59.4 0.5 fusion.15
  59.8 0.4 copy.50
  60.2 0.4 convert_element_type.69
  60.6 0.1 pad_maximum_fusion.2
  60.7 1.6 %collective-permute-start.4 = (bf16[2,64,4096]{2,1,0:T(8,128)(2,1)S(1)}, bf16[2,64,4096]{2,1,0:T(8,128)(2,1)S(1)}, u32[]{:S(2)}, u32[]{:S(2)}) collective-permute-start(bf16[2,64,4096]{2,1,0:T(8,128)(2,1)S(1)} %pad_maximum_fusion.2), channel_id=1, source_target_pairs={{0,8},{8,16},{16,24},{24,0},{1,9},{9,17},{17,25},{25,1},{2,10},{10... | collective-permute-start | bytes 3145736 | tf_op jit(solution)/shard_map/ppermute | solution.py:26
  62.4 24.7 %collective-permute-done.4 = bf16[2,64,4096]{2,1,0:T(8,128)(2,1)S(1)} collective-permute-done((bf16[2,64,4096]{2,1,0:T(8,128)(2,1)S(1)}, bf16[2,64,4096]{2,1,0:T(8,128)(2,1)S(1)}, u32[]{:S(2)}, u32[]{:S(2)}) %collective-permute-start.4) | collective-permute-done | bytes 1048608 | tf_op jit(solution)/shard_map/ppermute | solution.py:26
  87.1 1.0 %copy.68 = bf16[1,2,64,4096]{3,2,1,0:T(8,128)(2,1)} copy(bf16[1,2,64,4096]{3,2,1,0:T(8,128)(2,1)S(1)} %bitcast.93) | data formatting | bytes 2097152
  (5 shorter events, 0.1 us)
Async XLA Ops:
  0.0 8.3 %copy-start.3 = (s32[1,4,8]{2,1,0:T(4,128)S(1)}, s32[1,4,8]{2,1,0:T(4,128)}, u32[]{:S(2)}) copy-start(s32[1,4,8]{2,1,0:T(4,128)} %param.6) | copy-start | bytes 388
  6.6 5.8 %collective-permute-start = (bf16[1,64,6144]{2,1,0:T(8,128)(2,1)}, bf16[1,64,6144]{2,1,0:T(8,128)(2,1)S(1)}, u32[]{:S(2)}, u32[]{:S(2)}) collective-permute-start(bf16[1,64,6144]{2,1,0:T(8,128)(2,1)} %get-tuple-element.14), channel_id=1, source_target_pairs={{0,4},{4,0},{1,5},{5,1},{2,6},{6,2},{3,7},{7,3},{8,12},{12,8},{9,1... | collective-permute-start | bytes 2359304 | tf_op jit(solution)/shard_map/ppermute | solution.py:20
  8.5 1.9 %copy-start.2 = (s32[1,4]{1,0:T(1,128)S(1)}, s32[1,4]{1,0:T(1,128)}, u32[]{:S(2)}) copy-start(s32[1,4]{1,0:T(1,128)} %param.5) | copy-start | bytes 52
  16.3 16.1 %collective-permute-start.3 = (bf16[2,64,2048]{2,1,0:T(8,128)(2,1)}, bf16[2,64,2048]{2,1,0:T(8,128)(2,1)S(1)}, u32[]{:S(2)}, u32[]{:S(2)}) collective-permute-start(bf16[2,64,2048]{2,1,0:T(8,128)(2,1)} %copy.36), channel_id=1, source_target_pairs={{0,3},{1,0},{2,1},{3,2},{4,7},{5,4},{6,5},{7,6},{8,11},{9,8},{10,9... | collective-permute-start | bytes 1572872 | tf_op jit(solution)/shard_map/ppermute | solution.py:26
  19.7 25.6 %collective-permute-start.2 = (bf16[2,64,2048]{2,1,0:T(8,128)(2,1)}, bf16[2,64,2048]{2,1,0:T(8,128)(2,1)}, u32[]{:S(2)}, u32[]{:S(2)}) collective-permute-start(bf16[2,64,2048]{2,1,0:T(8,128)(2,1)} %copy.36), channel_id=1, source_target_pairs={{0,2},{1,3},{2,0},{3,1},{4,6},{5,7},{6,4},{7,5},{8,10},{9,11},{10,... | collective-permute-start | bytes 1572872 | tf_op jit(solution)/shard_map/ppermute | solution.py:26
  20.3 26.6 %collective-permute-start.1 = (bf16[2,64,2048]{2,1,0:T(8,128)(2,1)}, bf16[2,64,2048]{2,1,0:T(8,128)(2,1)}, u32[]{:S(2)}, u32[]{:S(2)}) collective-permute-start(bf16[2,64,2048]{2,1,0:T(8,128)(2,1)} %copy.36), channel_id=1, source_target_pairs={{0,1},{1,2},{2,3},{3,0},{4,5},{5,6},{6,7},{7,4},{8,9},{9,10},{10,1... | collective-permute-start | bytes 1572872 | tf_op jit(solution)/shard_map/ppermute | solution.py:26
  51.8 1.2 %copy-start.1 = (bf16[1,64,4096]{1,2,0:T(8,128)(2,1)S(1)}, bf16[1,64,4096]{1,2,0:T(8,128)(2,1)}, u32[]{:S(2)}) copy-start(bf16[1,64,4096]{1,2,0:T(8,128)(2,1)} %slice.30) | copy-start | bytes 1572868
  57.0 1.0 %copy-start = (bf16[64,8,4,128]{3,2,1,0:T(4,128)(2,1)S(1)}, bf16[64,8,4,128]{3,2,1,0:T(4,128)(2,1)}, u32[]{:S(2)}) copy-start(bf16[64,8,4,128]{3,2,1,0:T(4,128)(2,1)} %reshape_squeeze.23) | copy-start | bytes 1572868
  60.7 26.3 %collective-permute-start.4 = (bf16[2,64,4096]{2,1,0:T(8,128)(2,1)S(1)}, bf16[2,64,4096]{2,1,0:T(8,128)(2,1)S(1)}, u32[]{:S(2)}, u32[]{:S(2)}) collective-permute-start(bf16[2,64,4096]{2,1,0:T(8,128)(2,1)S(1)} %pad_maximum_fusion.2), channel_id=1, source_target_pairs={{0,8},{8,16},{16,24},{24,0},{1,9},{9,17},{17,25},{25,1},{2,10},{10... | collective-permute-start | bytes 3145736 | tf_op jit(solution)/shard_map/ppermute | solution.py:26

commit v2 on v1

--- a/solution.py
+++ b/solution.py
@@ -64,43 +64,44 @@
     partner_handed = lax.dynamic_index_in_dim(hand_over[0], partner, 0, keepdims=False)
     own_rows = qkv[0]
     seg_len = own_rows.shape[1]
+    length_all = seg_len * seq_count
     doc_ends = jnp.cumsum(doc_lengths[0], axis=1)
     lengths_all = stream_lengths[0]
-    given = lax.dynamic_index_in_dim(own_rows, handed, 0, keepdims=True)
-    kept = lax.dynamic_index_in_dim(own_rows, 1 - handed, 0, keepdims=True)
+    given = lax.dynamic_index_in_dim(own_rows, handed, 0, keepdims=False)
+    kept = lax.dynamic_index_in_dim(own_rows, 1 - handed, 0, keepdims=False)
     received = swapped(given, "dp", 0)
-    rows = jnp.concatenate([kept, received], axis=0)
     row_ids = [2 * replica + 1 - handed, 2 * partner + partner_handed]
-
-    kv_local = rows[..., D:]
-    pieces = [kv_local]
-    chunk_ids = [seq_index]
-    for shift in range(1, seq_count):
-        pieces.append(passed_along(kv_local, "seq", shift))
-        chunk_ids.append((seq_index - shift) % seq_count)
-    kv_all = jnp.concatenate(pieces, axis=1)
+    reach = min(seq_count - 1, -(-(length_all // 2 - 1) // seg_len))
     local = jnp.arange(seg_len, dtype=jnp.int32)
-    key_pos = jnp.concatenate([chunk * seg_len + local for chunk in chunk_ids])
     query_pos = seq_index * seg_len + local
     key_value_width = KV_HEADS * HD
+    far = jnp.int32(4 * length_all)
 
-    results = []
-    for slot in range(RPR):
+    outs = []
+    for slot, row in enumerate([kept, received]):
+        kv_local = row[:, D:]
+        pieces = [kv_local]
+        key_pos = [query_pos]
+        for shift in range(1, reach + 1):
+            pairs = [(source, source + shift) for source in range(seq_count - shift)]
+            pieces.append(lax.ppermute(kv_local, "seq", pairs))
+            chunk = seq_index - shift
+            key_pos.append(jnp.where(chunk >= 0, chunk * seg_len + local, far))
+        kv_all = jnp.concatenate(pieces, axis=0)
+        key_pos = jnp.concatenate(key_pos)
         ends = lax.dynamic_index_in_dim(doc_ends, row_ids[slot], 0, keepdims=False)
         length = lax.dynamic_index_in_dim(lengths_all, row_ids[slot], 0, keepdims=False)
-        results.append(
-            attend_row(
-                rows[slot, :, :D],
-                kv_all[slot, :, :key_value_width],
-                kv_all[slot, :, key_value_width:],
-                query_pos,
-                key_pos,
-                ends,
-                length,
-            )
+        result = attend_row(
+            row[:, :D],
+            kv_all[:, :key_value_width],
+            kv_all[:, key_value_width:],
+            query_pos,
+            key_pos,
+            ends,
+            length,
         )
-    out = jnp.stack(results, axis=0)
-    out = passed_along(out, "section", 1)
+        outs.append(passed_along(result, "section", 1))
+    out = jnp.stack(outs, axis=0)
     return out.reshape(1, RPR, seg_len, D)
 
 

time: 88.6 us -> 63.5 us (0.72)
  waiting for transfers between devices: 47.2 us -> 24.2 us
  starting transfers between devices: 6.66 us -> 19.4 us
  local copies, waits for them, and re-layouts: 18.5 us -> 6.32 us
  matrix products: 4.83 us -> 1.83 us
    ppermute x4 -> x2, waiting for transfers between devices: 47.2 us -> 14.1 us  [passed_along(): return lax.ppermute(value, axis, pairs)]
    ppermute x0 -> x4, starting transfers between devices: none -> 16.1 us  [shards(): pieces.append(lax.ppermute(kv_local, 'seq', pairs))]
    ppermute x0 -> x4, waiting for transfers between devices: none -> 10 us  [shards(): pieces.append(lax.ppermute(kv_local, 'seq', pairs))]
    ppermute x4 -> x0, local copies, waits for them, and re-layouts: 5.9 us -> none  [the longest x3 4.35 us: passed_along(): return lax.ppermute(value, axis, pairs)]
    dynamic_slice x2 -> x0, local copies, waits for them, and re-layouts: 3.22 us -> none  [shards(): kept = lax.dynamic_index_in_dim(own_rows, 1 - handed, 0, keepdims=True)]
    ppermute x4 -> x2, starting transfers between devices: 6.17 us -> 3.25 us  [passed_along(): return lax.ppermute(value, axis, pairs)]
    sub x1 -> x0, matrix products: 2.3 us -> none  [attend_row(): weights = jnp.where(allowed, jnp.exp(scores - row_top), 0.0)]
    slice x4, local copies, waits for them, and re-layouts: 2.33 us -> 0.11 us  [the longest x2 0.07 us: shards(): row[:, :D]]
  transfers between devices with their start and end apart: 5 -> 7, of which waited for: 3 -> 4; matrix products, arithmetic and copies ran while one was open for 9% -> 17% of each run, Pallas kernels for 0% -> 0%
where the time goes in v2:
time: 63.5 us; the launch traced here: 63.2 us
  waiting for transfers between devices  24.2 us (38%)
  starting transfers between devices  19.4 us (31%)
  other arithmetic  6.82 us (11%)
  local copies, waits for them, and re-layouts  6.32 us (10%)
  between operations  4.64 us (7%)
  matrix products  1.83 us (3%)
    ppermute x4, starting transfers between devices, shards(): pieces.append(lax.ppermute(kv_local, 'seq', pairs))  16.1 us
    ppermute x2, waiting for transfers between devices, passed_along(): return lax.ppermute(value, axis, pairs)  14.1 us
    ppermute x4, waiting for transfers between devices, shards(): pieces.append(lax.ppermute(kv_local, 'seq', pairs))  10 us
    ppermute x2, starting transfers between devices, passed_along(): return lax.ppermute(value, axis, pairs)  3.25 us
    concatenate x2, other arithmetic, shards(): kv_all = jnp.concatenate(pieces, axis=0)  2.01 us
    sub x2, other arithmetic, attend_row(): weights = jnp.where(allowed, jnp.exp(scores - row_top), 0.0)  1.94 us
    convert_element_type x4, local copies, waits for them, and re-layouts, attend_row(): return result.reshape(seg_len, D).astype(jnp.bfloat16)  1.59 us
    squeeze x1, local copies, waits for them, and re-layouts, shards(): kept = lax.dynamic_index_in_dim(own_rows, 1 - handed, 0, keepdims=False)  1.48 us
  transfers between devices with their start and end apart: 7, of which 4 were waited for; matrix products, arithmetic and copies ran while one was open for 17% of the time, Pallas kernels for 0%

profile of v2, /device:TPU:0, one launch (start us, length us, event | category | flops | bytes accessed | tf_op | source)
XLA Modules:
  0.0 63.2 jit_solution(8459928517542411959)
XLA Ops:
  0.0 0.0 copy-start.1
  0.0 0.0 copy-start
  0.0 1.4 %constant_dynamic-slice_fusion.2 = (s32[1,1]{1,0:T(1,128)}, s32[1,1]{1,0:T(1,128)}) fusion(s32[1,2]{1,0:T(1,128)} %param.7, s32[]{:T(128)S(6)} %select_n.65, s32[]{:T(128)S(6)} %select_n.55), kind=kLoop, calls=%fused_computation.55 | loop fusion | bytes 24 | tf_op jit(solution)/shard_map/jit(dynamic_index_in_dim)/dynamic_slice | solution.py:64
  4.5 1.5 %dynamic-slice_bitcast_fusion.1 = (bf16[64,6144]{1,0:T(8,128)(2,1)S(1)}, bf16[64,6144]{1,0:T(8,128)(2,1)S(1)}) fusion(bf16[1,2,64,6144]{3,2,1,0:T(8,128)(2,1)} %param.4, s32[]{:T(128)S(6)} %select_n.56, s32[]{:T(128)S(6)} %select_n.64), kind=kLoop, calls=%fused_computation.34 | loop fusion | bytes 3145736 | tf_op jit(solution)/shard_map/jit(dynamic_index_in_dim)/squeeze | solution.py:71
  6.0 4.9 %collective-permute-start = (bf16[64,2048]{1,0:T(8,128)(2,1)S(1)}, bf16[64,2048]{1,0:T(8,128)(2,1)S(1)}, u32[]{:S(2)}, u32[]{:S(2)}) collective-permute-start(bf16[64,2048]{1,0:T(8,128)(2,1)S(1)} %slice.32), channel_id=1, source_target_pairs={{0,1},{1,2},{2,3},{4,5},{5,6},{6,7},{8,9},{9,10},{10,11},{12,13},{... | collective-permute-start | bytes 786440 | tf_op jit(solution)/shard_map/ppermute | solution.py:87
  10.9 4.1 %collective-permute-start.1 = (bf16[64,2048]{1,0:T(8,128)(2,1)S(1)}, bf16[64,2048]{1,0:T(8,128)(2,1)}, u32[]{:S(2)}, u32[]{:S(2)}) collective-permute-start(bf16[64,2048]{1,0:T(8,128)(2,1)S(1)} %slice.32), channel_id=1, source_target_pairs={{0,2},{1,3},{4,6},{5,7},{8,10},{9,11},{12,14},{13,15},{16,18},{17,... | collective-permute-start | bytes 786440 | tf_op jit(solution)/shard_map/ppermute | solution.py:87
  15.0 0.0 collective-permute-start.3
  16.3 0.0 copy-done.1
  16.3 0.2 reduce_window_sum.11
  16.5 0.1 pad_add_fusion
  16.6 0.1 convert_reduce_fusion.3
  16.7 0.1 convert_reduce_fusion.1
  16.8 0.0 copy-done
  16.8 0.7 %constant_dynamic-slice_fusion.3 = (s32[1,1]{1,0:T(1,128)}, s32[1,1]{1,0:T(1,128)}) fusion(s32[1,4]{1,0:T(1,128)S(1)} %copy-done, s32[]{:T(128)S(6)} %select_n.61, s32[]{:T(128)S(6)} %select_n.66), kind=kLoop, calls=%fused_computation.56 | loop fusion | bytes 24 | tf_op jit(solution)/shard_map/jit(dynamic_index_in_dim)/dynamic_slice | solution.py:93
  17.4 1.3 %compare_convert_fusion = (f32[64]{0:T(128)S(1)}, f32[64]{0:T(128)S(1)}) fusion(s32[]{:T(128)} %bitcast.19, s32[]{:T(128)S(6)} %mul.45, s32[]{:T(128)} %bitcast.9), kind=kLoop, calls=%fused_computation.59 | loop fusion | flops 320 | bytes 524 | tf_op jit(solution)/shard_map/convert_element_type | solution.py:53
  18.8 0.4 reshape.63
  19.1 0.1 compare_and_fusion.1
  19.2 0.0 collective-permute-done
  19.2 3.7 %collective-permute-done.1 = bf16[64,2048]{1,0:T(8,128)(2,1)} collective-permute-done((bf16[64,2048]{1,0:T(8,128)(2,1)S(1)}, bf16[64,2048]{1,0:T(8,128)(2,1)}, u32[]{:S(2)}, u32[]{:S(2)}) %collective-permute-start.1) | collective-permute-done | bytes 262176 | tf_op jit(solution)/shard_map/ppermute | solution.py:87
  23.0 1.0 %pad_maximum_fusion = bf16[192,2048]{1,0:T(8,128)(2,1)S(1)} fusion(bf16[64,2048]{1,0:T(8,128)(2,1)} %collective-permute-done.1, bf16[64,2048]{1,0:T(8,128)(2,1)S(1)} %collective-permute-done, bf16[64,2048]{1,0:T(8,128)(2,1)S(1)} %slice.32), kind=kLoop, calls=%fused_computation.31 | loop fusion | flops 2359296 | bytes 1572864 | tf_op jit(solution)/shard_map/concatenate | solution.py:90
  24.0 0.1 slice_bitcast_fusion.3
  24.0 0.1 copy.34
  24.1 0.1 copy.33
  24.2 0.5 fusion.26
  24.7 1.0 %fusion.39 = (f32[8,4,64]{2,1,0:T(4,128)S(1)}, bf16[8,4,64,192]{3,2,1,0:T(8,128)(2,1)S(1)}) fusion(f32[8,192,64,4]{1,2,3,0:T(8,128)S(1)} %fusion.26, pred[64,192]{1,0:T(8,128)(4,1)S(1)} %get-tuple-element.17), kind=kOutput, calls=%fused_computation.72 | output fusion | flops 2752703 | bytes 2379776 | tf_op jit(solution)/shard_map/sub | solution.py:48
  25.6 0.0 collective-permute-done.3
  25.7 1.3 %collective-permute-start.4 = (bf16[64,2048]{1,0:T(8,128)(2,1)S(1)}, bf16[64,2048]{1,0:T(8,128)(2,1)S(1)}, u32[]{:S(2)}, u32[]{:S(2)}) collective-permute-start(bf16[64,2048]{1,0:T(8,128)(2,1)S(1)} %slice.36), channel_id=1, source_target_pairs={{0,1},{1,2},{2,3},{4,5},{5,6},{6,7},{8,9},{9,10},{10,11},{12,13},{... | collective-permute-start | bytes 786440 | tf_op jit(solution)/shard_map/ppermute | solution.py:87
  27.0 5.8 %collective-permute-start.5 = (bf16[64,2048]{1,0:T(8,128)(2,1)S(1)}, bf16[64,2048]{1,0:T(8,128)(2,1)}, u32[]{:S(2)}, u32[]{:S(2)}) collective-permute-start(bf16[64,2048]{1,0:T(8,128)(2,1)S(1)} %slice.36), channel_id=1, source_target_pairs={{0,2},{1,3},{4,6},{5,7},{8,10},{9,11},{12,14},{13,15},{16,18},{17,... | collective-permute-start | bytes 786440 | tf_op jit(solution)/shard_map/ppermute | solution.py:87
  32.8 0.5 fusion.14
  33.2 0.4 copy.16
  33.7 0.4 convert_element_type.49
  34.1 1.6 %collective-permute-start.2 = (bf16[64,4096]{1,0:T(8,128)(2,1)S(1)}, bf16[64,4096]{1,0:T(8,128)(2,1)S(1)}, u32[]{:S(2)}, u32[]{:S(2)}) collective-permute-start(bf16[64,4096]{1,0:T(8,128)(2,1)S(1)} %convert_element_type.49), channel_id=1, source_target_pairs={{0,8},{8,16},{16,24},{24,0},{1,9},{9,17},{17,25},{25,1},{2,10},{10... | collective-permute-start | bytes 1572872 | tf_op jit(solution)/shard_map/ppermute | solution.py:26
  35.7 0.4 reshape.66
  36.1 0.0 collective-permute-done.4
  36.1 6.3 %collective-permute-done.5 = bf16[64,2048]{1,0:T(8,128)(2,1)} collective-permute-done((bf16[64,2048]{1,0:T(8,128)(2,1)S(1)}, bf16[64,2048]{1,0:T(8,128)(2,1)}, u32[]{:S(2)}, u32[]{:S(2)}) %collective-permute-start.5) | collective-permute-done | bytes 262176 | tf_op jit(solution)/shard_map/ppermute | solution.py:87
  42.4 1.0 %pad_maximum_fusion.1 = bf16[192,2048]{1,0:T(8,128)(2,1)S(1)} fusion(bf16[64,2048]{1,0:T(8,128)(2,1)} %collective-permute-done.5, bf16[64,2048]{1,0:T(8,128)(2,1)S(1)} %collective-permute-done.4, bf16[64,2048]{1,0:T(8,128)(2,1)S(1)} %slice.36), kind=kLoop, calls=%fused_computation.32 | loop fusion | flops 2359296 | bytes 1572864 | tf_op jit(solution)/shard_map/concatenate | solution.py:90
  43.4 0.1 slice_bitcast_fusion.1
  43.5 0.1 copy.36
  43.6 0.1 copy.35
  43.6 0.5 fusion.24
  44.1 1.0 %fusion.38 = (f32[8,4,64]{2,1,0:T(4,128)S(1)}, bf16[8,4,64,192]{3,2,1,0:T(8,128)(2,1)S(1)}) fusion(f32[8,192,64,4]{1,2,3,0:T(8,128)S(1)} %fusion.24, pred[64,192]{1,0:T(8,128)(4,1)S(1)} %get-tuple-element.18), kind=kOutput, calls=%fused_computation.71 | output fusion | flops 2752703 | bytes 2379776 | tf_op jit(solution)/shard_map/sub | solution.py:48
  45.1 0.5 fusion.15
  45.5 0.4 copy.20
  45.9 0.4 convert_element_type.55
  46.3 1.6 %collective-permute-start.6 = (bf16[64,4096]{1,0:T(8,128)(2,1)S(1)}, bf16[64,4096]{1,0:T(8,128)(2,1)S(1)}, u32[]{:S(2)}, u32[]{:S(2)}) collective-permute-start(bf16[64,4096]{1,0:T(8,128)(2,1)S(1)} %convert_element_type.55), channel_id=1, source_target_pairs={{0,8},{8,16},{16,24},{24,0},{1,9},{9,17},{17,25},{25,1},{2,10},{10... | collective-permute-start | bytes 1572872 | tf_op jit(solution)/shard_map/ppermute | solution.py:26
  48.0 1.6 %collective-permute-done.2 = bf16[64,4096]{1,0:T(8,128)(2,1)S(1)} collective-permute-done((bf16[64,4096]{1,0:T(8,128)(2,1)S(1)}, bf16[64,4096]{1,0:T(8,128)(2,1)S(1)}, u32[]{:S(2)}, u32[]{:S(2)}) %collective-permute-start.2) | collective-permute-done | bytes 524320 | tf_op jit(solution)/shard_map/ppermute | solution.py:26
  49.5 12.6 %collective-permute-done.6 = bf16[64,4096]{1,0:T(8,128)(2,1)S(1)} collective-permute-done((bf16[64,4096]{1,0:T(8,128)(2,1)S(1)}, bf16[64,4096]{1,0:T(8,128)(2,1)S(1)}, u32[]{:S(2)}, u32[]{:S(2)}) %collective-permute-start.6) | collective-permute-done | bytes 524320 | tf_op jit(solution)/shard_map/ppermute | solution.py:26
  62.1 1.1 %maximum_bitcast_fusion = bf16[1,2,64,4096]{3,2,1,0:T(8,128)(2,1)} fusion(bf16[1,64,4096]{2,1,0:T(8,128)(2,1)S(1)} %bitcast.88, bf16[1,64,4096]{2,1,0:T(8,128)(2,1)S(1)} %bitcast.87), kind=kLoop, calls=%fused_computation.22 | loop fusion | flops 524288 | bytes 2097152 | tf_op jit(solution)/shard_map/reshape | solution.py:105
  (7 shorter events, 0.1 us)
Async XLA Ops:
  0.0 16.3 %copy-start.1 = (s32[1,4,8]{2,1,0:T(4,128)S(1)}, s32[1,4,8]{2,1,0:T(4,128)}, u32[]{:S(2)}) copy-start(s32[1,4,8]{2,1,0:T(4,128)} %param.6) | copy-start | bytes 388
  0.0 16.8 %copy-start = (s32[1,4]{1,0:T(1,128)S(1)}, s32[1,4]{1,0:T(1,128)}, u32[]{:S(2)}) copy-start(s32[1,4]{1,0:T(1,128)} %param.5) | copy-start | bytes 52
  6.0 13.2 %collective-permute-start = (bf16[64,2048]{1,0:T(8,128)(2,1)S(1)}, bf16[64,2048]{1,0:T(8,128)(2,1)S(1)}, u32[]{:S(2)}, u32[]{:S(2)}) collective-permute-start(bf16[64,2048]{1,0:T(8,128)(2,1)S(1)} %slice.32), channel_id=1, source_target_pairs={{0,1},{1,2},{2,3},{4,5},{5,6},{6,7},{8,9},{9,10},{10,11},{12,13},{... | collective-permute-start | bytes 786440 | tf_op jit(solution)/shard_map/ppermute | solution.py:87
  10.9 12.1 %collective-permute-start.1 = (bf16[64,2048]{1,0:T(8,128)(2,1)S(1)}, bf16[64,2048]{1,0:T(8,128)(2,1)}, u32[]{:S(2)}, u32[]{:S(2)}) collective-permute-start(bf16[64,2048]{1,0:T(8,128)(2,1)S(1)} %slice.32), channel_id=1, source_target_pairs={{0,2},{1,3},{4,6},{5,7},{8,10},{9,11},{12,14},{13,15},{16,18},{17,... | collective-permute-start | bytes 786440 | tf_op jit(solution)/shard_map/ppermute | solution.py:87
  15.0 10.6 %collective-permute-start.3 = (bf16[64,6144]{1,0:T(8,128)(2,1)S(1)}, bf16[64,6144]{1,0:T(8,128)(2,1)S(1)}, u32[]{:S(2)}, u32[]{:S(2)}) collective-permute-start(bf16[64,6144]{1,0:T(8,128)(2,1)S(1)} %get-tuple-element.10), channel_id=1, source_target_pairs={{0,4},{4,0},{1,5},{5,1},{2,6},{6,2},{3,7},{7,3},{8,12},{12,8},{9,1... | collective-permute-start | bytes 2359304 | tf_op jit(solution)/shard_map/ppermute | solution.py:20
  25.7 10.4 %collective-permute-start.4 = (bf16[64,2048]{1,0:T(8,128)(2,1)S(1)}, bf16[64,2048]{1,0:T(8,128)(2,1)S(1)}, u32[]{:S(2)}, u32[]{:S(2)}) collective-permute-start(bf16[64,2048]{1,0:T(8,128)(2,1)S(1)} %slice.36), channel_id=1, source_target_pairs={{0,1},{1,2},{2,3},{4,5},{5,6},{6,7},{8,9},{9,10},{10,11},{12,13},{... | collective-permute-start | bytes 786440 | tf_op jit(solution)/shard_map/ppermute | solution.py:87
  27.0 15.4 %collective-permute-start.5 = (bf16[64,2048]{1,0:T(8,128)(2,1)S(1)}, bf16[64,2048]{1,0:T(8,128)(2,1)}, u32[]{:S(2)}, u32[]{:S(2)}) collective-permute-start(bf16[64,2048]{1,0:T(8,128)(2,1)S(1)} %slice.36), channel_id=1, source_target_pairs={{0,2},{1,3},{4,6},{5,7},{8,10},{9,11},{12,14},{13,15},{16,18},{17,... | collective-permute-start | bytes 786440 | tf_op jit(solution)/shard_map/ppermute | solution.py:87
  34.1 15.5 %collective-permute-start.2 = (bf16[64,4096]{1,0:T(8,128)(2,1)S(1)}, bf16[64,4096]{1,0:T(8,128)(2,1)S(1)}, u32[]{:S(2)}, u32[]{:S(2)}) collective-permute-start(bf16[64,4096]{1,0:T(8,128)(2,1)S(1)} %convert_element_type.49), channel_id=1, source_target_pairs={{0,8},{8,16},{16,24},{24,0},{1,9},{9,17},{17,25},{25,1},{2,10},{10... | collective-permute-start | bytes 1572872 | tf_op jit(solution)/shard_map/ppermute | solution.py:26
  46.3 15.8 %collective-permute-start.6 = (bf16[64,4096]{1,0:T(8,128)(2,1)S(1)}, bf16[64,4096]{1,0:T(8,128)(2,1)S(1)}, u32[]{:S(2)}, u32[]{:S(2)}) collective-permute-start(bf16[64,4096]{1,0:T(8,128)(2,1)S(1)} %convert_element_type.55), channel_id=1, source_target_pairs={{0,8},{8,16},{16,24},{24,0},{1,9},{9,17},{17,25},{25,1},{2,10},{10... | collective-permute-start | bytes 1572872 | tf_op jit(solution)/shard_map/ppermute | solution.py:26

commit v3 on v2

--- a/solution.py
+++ b/solution.py
@@ -55,22 +55,35 @@
     return result.reshape(seg_len, D).astype(jnp.bfloat16)
 
 
+def gathered(block, seq_index, seq_count, reach):
+    if seq_count == 4 and reach == 2:
+        over_x = lax.ppermute(block, "seq", [(0, 1), (2, 3)])
+        over_y = lax.ppermute(block, "seq", [(0, 2), (1, 3)])
+        relayed = lax.ppermute(over_y, "seq", [(3, 2)])
+        odd = seq_index % 2 == 1
+        return [
+            (over_x, jnp.where(odd, seq_index - 1, -1)),
+            (over_y, seq_index - 2),
+            (relayed, jnp.where(seq_index == 2, 1, -1)),
+        ]
+    pieces = []
+    for shift in range(1, reach + 1):
+        pairs = [(source, source + shift) for source in range(seq_count - shift)]
+        pieces.append((lax.ppermute(block, "seq", pairs), seq_index - shift))
+    return pieces
+
+
 def shards(qkv, stream_lengths, doc_lengths, hand_over):
     seq_count = lax.axis_size("seq")
     seq_index = lax.axis_index("seq")
     replica = lax.axis_index("dp")
     partner = jnp.bitwise_xor(replica, 1)
     handed = lax.dynamic_index_in_dim(hand_over[0], replica, 0, keepdims=False)
-    partner_handed = lax.dynamic_index_in_dim(hand_over[0], partner, 0, keepdims=False)
     own_rows = qkv[0]
     seg_len = own_rows.shape[1]
     length_all = seg_len * seq_count
     doc_ends = jnp.cumsum(doc_lengths[0], axis=1)
     lengths_all = stream_lengths[0]
-    given = lax.dynamic_index_in_dim(own_rows, handed, 0, keepdims=False)
-    kept = lax.dynamic_index_in_dim(own_rows, 1 - handed, 0, keepdims=False)
-    received = swapped(given, "dp", 0)
-    row_ids = [2 * replica + 1 - handed, 2 * partner + partner_handed]
     reach = min(seq_count - 1, -(-(length_all // 2 - 1) // seg_len))
     local = jnp.arange(seg_len, dtype=jnp.int32)
     query_pos = seq_index * seg_len + local
@@ -78,30 +91,35 @@
     far = jnp.int32(4 * length_all)
 
     outs = []
-    for slot, row in enumerate([kept, received]):
+    for own_index in [1 - handed, handed]:
+        row = lax.dynamic_index_in_dim(own_rows, own_index, 0, keepdims=False)
         kv_local = row[:, D:]
         pieces = [kv_local]
         key_pos = [query_pos]
-        for shift in range(1, reach + 1):
-            pairs = [(source, source + shift) for source in range(seq_count - shift)]
-            pieces.append(lax.ppermute(kv_local, "seq", pairs))
-            chunk = seq_index - shift
+        for piece, chunk in gathered(kv_local, seq_index, seq_count, reach):
+            pieces.append(piece)
             key_pos.append(jnp.where(chunk >= 0, chunk * seg_len + local, far))
         kv_all = jnp.concatenate(pieces, axis=0)
         key_pos = jnp.concatenate(key_pos)
-        ends = lax.dynamic_index_in_dim(doc_ends, row_ids[slot], 0, keepdims=False)
-        length = lax.dynamic_index_in_dim(lengths_all, row_ids[slot], 0, keepdims=False)
-        result = attend_row(
-            row[:, :D],
-            kv_all[:, :key_value_width],
-            kv_all[:, key_value_width:],
-            query_pos,
-            key_pos,
-            ends,
-            length,
+        row_id = 2 * replica + own_index
+        ends = lax.dynamic_index_in_dim(doc_ends, row_id, 0, keepdims=False)
+        length = lax.dynamic_index_in_dim(lengths_all, row_id, 0, keepdims=False)
+        outs.append(
+            attend_row(
+                row[:, :D],
+                kv_all[:, :key_value_width],
+                kv_all[:, key_value_width:],
+                query_pos,
+                key_pos,
+                ends,
+                length,
+            )
         )
-        outs.append(passed_along(result, "section", 1))
-    out = jnp.stack(outs, axis=0)
+    kept_out, given_out = outs
+    sent = [passed_along(kept_out, "section", 1)]
+    received = swapped(given_out, "dp", 0)
+    sent.append(passed_along(received, "section", 1))
+    out = jnp.stack(sent, axis=0)
     return out.reshape(1, RPR, seg_len, D)
 
 

time: 63.5 us -> 92.7 us (1.46)
  the two profiles are of different devices: /device:TPU:0 before, /device:TPU:4 now
where the time goes in v3:
time: 92.7 us; the launch traced here: 92.2 us
  waiting for transfers between devices  44.5 us (48%)
  starting transfers between devices  14.7 us (16%)
  local copies, waits for them, and re-layouts  14.1 us (15%)
  matrix products  7.96 us (9%)
  other arithmetic  6.95 us (7%)
  between operations  4.02 us (4%)
    ppermute x2, waiting for transfers between devices, passed_along(): return lax.ppermute(value, axis, pairs)  23.9 us
    ppermute x2, waiting for transfers between devices, gathered(): relayed = lax.ppermute(over_y, 'seq', [(3, 2)])  11.5 us
    ppermute x2, waiting for transfers between devices, gathered(): over_y = lax.ppermute(block, 'seq', [(0, 2), (1, 3)])  9.06 us
    ppermute x2, starting transfers between devices, gathered(): over_x = lax.ppermute(block, 'seq', [(0, 1), (2, 3)])  6.29 us
    dynamic_slice x3, local copies, waits for them, and re-layouts, shards(): row = lax.dynamic_index_in_dim(own_rows, own_index, 0, keepdims=False)  5.04 us
    sub x2, matrix products, attend_row(): weights = jnp.where(allowed, jnp.exp(scores - row_top), 0.0)  4.63 us
    concatenate x2, other arithmetic, shards(): kv_all = jnp.concatenate(pieces, axis=0)  4.06 us
    dot_general x2, matrix products, attend_row(): jnp.einsum('kgqs,skd->qkgd', rounded, values, preferred_element_type=jnp....  3.33 us
  transfers between devices with their start and end apart: 9, of which 6 were waited for; matrix products, arithmetic and copies ran while one was open for 15% of the time, Pallas kernels for 0%

profile of v3, /device:TPU:4, one launch (start us, length us, event | category | flops | bytes accessed | tf_op | source)
XLA Modules:
  0.0 92.2 jit_solution(13841095561729033619)
XLA Ops:
  0.0 0.7 copy-done
  0.7 0.6 constant_dynamic-slice_fusion.6
  4.4 2.4 %constant_dynamic-slice_fusion.5 = (bf16[1,1,64,6144]{3,2,1,0:T(8,128)(2,1)S(1)}, bf16[1,1,64,6144]{3,2,1,0:T(8,128)(2,1)}) fusion(bf16[1,2,64,6144]{3,2,1,0:T(8,128)(2,1)} %param.4, s32[]{:T(128)S(6)} %select_n.82, s32[]{:T(128)S(6)} %select_n.95), kind=kLoop, calls=%fused_computation.48 | loop fusion | bytes 3145736 | tf_op jit(solution)/shard_map/jit(dynamic_index_in_dim)/dynamic_slice | solution.py:95
  6.8 0.8 copy.17
  7.7 0.8 slice.32
  8.5 1.3 %collective-permute-start.1 = (bf16[64,2048]{0,1:T(8,128)(2,1)}, bf16[64,2048]{0,1:T(8,128)(2,1)}, u32[]{:S(2)}, u32[]{:S(2)}) collective-permute-start(bf16[64,2048]{0,1:T(8,128)(2,1)} %slice.32), channel_id=1, source_target_pairs={{0,2},{1,3},{4,6},{5,7},{8,10},{9,11},{12,14},{13,15},{16,18},{17,... | collective-permute-start | bytes 786440 | tf_op jit(solution)/shard_map/ppermute | solution.py:61
  9.8 4.2 %collective-permute-start = (bf16[64,2048]{0,1:T(8,128)(2,1)}, bf16[64,2048]{0,1:T(8,128)(2,1)}, u32[]{:S(2)}, u32[]{:S(2)}) collective-permute-start(bf16[64,2048]{0,1:T(8,128)(2,1)} %slice.32), channel_id=1, source_target_pairs={{0,1},{2,3},{4,5},{6,7},{8,9},{10,11},{12,13},{14,15},{16,17},{18,... | collective-permute-start | bytes 786440 | tf_op jit(solution)/shard_map/ppermute | solution.py:60
  14.0 1.8 %copy.23 = bf16[1,1,64,6144]{2,3,1,0:T(8,128)(2,1)S(1)} copy(bf16[1,1,64,6144]{3,2,1,0:T(8,128)(2,1)} %get-tuple-element.10) | data formatting | bytes 1572864 | tf_op jit(solution)/shard_map/jit(dynamic_index_in_dim)/dynamic_slice | solution.py:95
  15.8 0.8 slice.36
  16.7 1.3 %collective-permute-start.5 = (bf16[64,2048]{0,1:T(8,128)(2,1)}, bf16[64,2048]{0,1:T(8,128)(2,1)}, u32[]{:S(2)}, u32[]{:S(2)}) collective-permute-start(bf16[64,2048]{0,1:T(8,128)(2,1)} %slice.36), channel_id=1, source_target_pairs={{0,2},{1,3},{4,6},{5,7},{8,10},{9,11},{12,14},{13,15},{16,18},{17,... | collective-permute-start | bytes 786440 | tf_op jit(solution)/shard_map/ppermute | solution.py:61
  18.0 2.1 %collective-permute-start.4 = (bf16[64,2048]{0,1:T(8,128)(2,1)}, bf16[64,2048]{0,1:T(8,128)(2,1)}, u32[]{:S(2)}, u32[]{:S(2)}) collective-permute-start(bf16[64,2048]{0,1:T(8,128)(2,1)} %slice.36), channel_id=1, source_target_pairs={{0,1},{2,3},{4,5},{6,7},{8,9},{10,11},{12,13},{14,15},{16,17},{18,... | collective-permute-start | bytes 786440 | tf_op jit(solution)/shard_map/ppermute | solution.py:60
  20.7 0.2 reduce_window_sum.11
  20.9 0.1 pad_add_fusion
  21.0 0.6 constant_dynamic-slice_fusion.3
  21.6 0.1 convert_reduce_fusion.3
  21.7 0.1 convert_reduce_fusion.1
  21.8 3.7 %collective-permute-done.1 = bf16[64,2048]{0,1:T(8,128)(2,1)} collective-permute-done((bf16[64,2048]{0,1:T(8,128)(2,1)}, bf16[64,2048]{0,1:T(8,128)(2,1)}, u32[]{:S(2)}, u32[]{:S(2)}) %collective-permute-start.1) | collective-permute-done | bytes 262176 | tf_op jit(solution)/shard_map/ppermute | solution.py:61
  25.5 1.3 %collective-permute-start.2 = (bf16[64,2048]{0,1:T(8,128)(2,1)}, bf16[64,2048]{0,1:T(8,128)(2,1)S(1)}, u32[]{:S(2)}, u32[]{:S(2)}) collective-permute-start(bf16[64,2048]{0,1:T(8,128)(2,1)} %collective-permute-done.1), channel_id=1, source_target_pairs={{3,2},{7,6},{11,10},{15,14},{19,18},{23,22},{27,26},{31,30}} | collective-permute-start | bytes 786440 | tf_op jit(solution)/shard_map/ppermute | solution.py:62
  26.8 1.3 %compare_convert_fusion = (f32[64]{0:T(128)S(1)}, f32[64]{0:T(128)S(1)}) fusion(s32[]{:T(128)} %bitcast.24, s32[]{:T(128)S(6)} %mul.47, s32[]{:T(128)} %bitcast.12), kind=kLoop, calls=%fused_computation.41 | loop fusion | flops 320 | bytes 524 | tf_op jit(solution)/shard_map/convert_element_type | solution.py:53
  28.1 1.0 %slice.35 = bf16[64,4096]{0,1:T(8,128)(2,1)} slice(bf16[64,6144]{0,1:T(8,128)(2,1)S(1)} %bitcast.95), slice={[0:64], [0:4096]} | slice | bytes 1048576 | tf_op jit(solution)/shard_map/slice | solution.py:109
  29.2 1.0 %slice.39 = bf16[64,4096]{0,1:T(8,128)(2,1)} slice(bf16[64,6144]{0,1:T(8,128)(2,1)S(1)} %bitcast.97), slice={[0:64], [0:4096]} | slice | bytes 1048576 | tf_op jit(solution)/shard_map/slice | solution.py:109
  30.2 0.1 compare_and_fusion.1
  30.3 5.3 %collective-permute-done.5 = bf16[64,2048]{0,1:T(8,128)(2,1)} collective-permute-done((bf16[64,2048]{0,1:T(8,128)(2,1)}, bf16[64,2048]{0,1:T(8,128)(2,1)}, u32[]{:S(2)}, u32[]{:S(2)}) %collective-permute-start.5) | collective-permute-done | bytes 262176 | tf_op jit(solution)/shard_map/ppermute | solution.py:61
  35.6 1.3 %collective-permute-start.6 = (bf16[64,2048]{0,1:T(8,128)(2,1)}, bf16[64,2048]{0,1:T(8,128)(2,1)S(1)}, u32[]{:S(2)}, u32[]{:S(2)}) collective-permute-start(bf16[64,2048]{0,1:T(8,128)(2,1)} %collective-permute-done.5), channel_id=1, source_target_pairs={{3,2},{7,6},{11,10},{15,14},{19,18},{23,22},{27,26},{31,30}} | collective-permute-start | bytes 786440 | tf_op jit(solution)/shard_map/ppermute | solution.py:62
  36.9 2.4 %collective-permute-done.2 = bf16[64,2048]{0,1:T(8,128)(2,1)S(1)} collective-permute-done((bf16[64,2048]{0,1:T(8,128)(2,1)}, bf16[64,2048]{0,1:T(8,128)(2,1)S(1)}, u32[]{:S(2)}, u32[]{:S(2)}) %collective-permute-start.2) | collective-permute-done | bytes 262176 | tf_op jit(solution)/shard_map/ppermute | solution.py:62
  39.3 2.0 %pad_maximum_fusion = bf16[256,2048]{0,1:T(8,128)(2,1)S(1)} fusion(bf16[64,2048]{0,1:T(8,128)(2,1)S(1)} %collective-permute-done.2, bf16[64,2048]{0,1:T(8,128)(2,1)} %collective-permute-done.1, bf16[64,2048]{0,1:T(8,128)(2,1)} %collective-permute-done, bf16[64,2048]{0,1:T(8,128)(2,1)} %slice.32), kind=kLoop, calls=%fused_computation.22 | loop fusion | flops 4194304 | bytes 2097152 | tf_op jit(solution)/shard_map/concatenate | solution.py:102
  41.3 0.1 fusion.34
  41.4 0.0 collective-permute-done.4
  41.4 9.1 %collective-permute-done.6 = bf16[64,2048]{0,1:T(8,128)(2,1)S(1)} collective-permute-done((bf16[64,2048]{0,1:T(8,128)(2,1)}, bf16[64,2048]{0,1:T(8,128)(2,1)S(1)}, u32[]{:S(2)}, u32[]{:S(2)}) %collective-permute-start.6) | collective-permute-done | bytes 262176 | tf_op jit(solution)/shard_map/ppermute | solution.py:62
  50.5 2.0 %pad_maximum_fusion.1 = bf16[256,2048]{0,1:T(8,128)(2,1)S(1)} fusion(bf16[64,2048]{0,1:T(8,128)(2,1)S(1)} %collective-permute-done.6, bf16[64,2048]{0,1:T(8,128)(2,1)} %collective-permute-done.5, bf16[64,2048]{0,1:T(8,128)(2,1)} %collective-permute-done.4, bf16[64,2048]{0,1:T(8,128)(2,1)} %slice.36), kind=kLoop, calls=%fused_computation.23 | loop fusion | flops 4194304 | bytes 2097152 | tf_op jit(solution)/shard_map/concatenate | solution.py:102
  52.6 0.0 copy-start.2
  52.6 0.9 fusion.35
  53.5 0.5 copy-done.2
  54.0 2.3 %fusion.36 = (f32[8,4,64]{2,1,0:T(4,128)S(1)}, bf16[8,4,64,256]{3,2,1,0:T(8,128)(2,1)}) fusion(pred[64,256]{1,0:T(8,128)(4,1)S(1)} %get-tuple-element.18, bf16[256,8,128,1]{0,2,3,1:T(8,128)(2,1)S(1)} %bitcast.105, bf16[64,8,4,128]{0,3,2,1:T(8,128)(2,1)S(1)} %bitcast.99), kind=kOutput, calls=%fused_computation.63 | convolution fusion | flops 272105728 | bytes 2121728 | tf_op jit(solution)/shard_map/sub | solution.py:48
  56.3 1.7 %fusion.15 = bf16[64,8,4,128]{3,0,2,1:T(8,128)(2,1)S(1)} fusion(bf16[256,8,128,1]{0,2,3,1:T(8,128)(2,1)S(1)} %bitcast.103, bf16[8,4,64,256]{3,2,1,0:T(8,128)(2,1)} %get-tuple-element.22, f32[64]{0:T(128)S(1)} %get-tuple-element.25, f32[64,8,4]{0,2,1:T(4,128)S(1)} %bitcast.108), kind=kOutput, calls=%fused_computation.21 | convolution fusion | flops 135004160 | bytes 2105600 | tf_op jit(solution)/shard_map/kgqs,skd->qkgd/dot_general | solution.py:51
  58.0 0.4 copy.28
  58.4 0.4 convert_element_type.55
  58.8 0.1 collective-permute-start.7
  58.9 0.3 copy-done.1
  59.2 2.3 %fusion.37 = (f32[8,4,64]{2,1,0:T(4,128)S(1)}, bf16[8,4,64,256]{3,2,1,0:T(8,128)(2,1)}) fusion(pred[64,256]{1,0:T(8,128)(4,1)S(1)} %get-tuple-element.17, bf16[256,8,128,1]{0,2,3,1:T(8,128)(2,1)S(1)} %bitcast.101, bf16[64,8,4,128]{0,3,2,1:T(8,128)(2,1)S(1)} %bitcast.98), kind=kOutput, calls=%fused_computation.64 | convolution fusion | flops 272105728 | bytes 2121728 | tf_op jit(solution)/shard_map/sub | solution.py:48
  61.5 1.7 %fusion.14 = bf16[64,8,4,128]{3,0,2,1:T(8,128)(2,1)S(1)} fusion(bf16[256,8,128,1]{0,2,3,1:T(8,128)(2,1)S(1)} %bitcast.100, bf16[8,4,64,256]{3,2,1,0:T(8,128)(2,1)} %get-tuple-element.24, f32[64]{0:T(128)S(1)} %get-tuple-element.26, f32[64,8,4]{0,2,1:T(4,128)S(1)} %bitcast.107), kind=kOutput, calls=%fused_computation.20 | convolution fusion | flops 135004160 | bytes 2105600 | tf_op jit(solution)/shard_map/kgqs,skd->qkgd/dot_general | solution.py:51
  63.2 0.4 copy.22
  63.6 0.4 convert_element_type.49
  64.0 1.6 %collective-permute-start.3 = (bf16[64,4096]{1,0:T(8,128)(2,1)S(1)}, bf16[64,4096]{1,0:T(8,128)(2,1)S(1)}, u32[]{:S(2)}, u32[]{:S(2)}) collective-permute-start(bf16[64,4096]{1,0:T(8,128)(2,1)S(1)} %convert_element_type.49), channel_id=1, source_target_pairs={{0,8},{8,16},{16,24},{24,0},{1,9},{9,17},{17,25},{25,1},{2,10},{10... | collective-permute-start | bytes 1572872 | tf_op jit(solution)/shard_map/ppermute | solution.py:26
  65.6 1.6 %collective-permute-start.8 = (bf16[64,4096]{1,0:T(8,128)(2,1)S(1)}, bf16[64,4096]{1,0:T(8,128)(2,1)S(1)}, u32[]{:S(2)}, u32[]{:S(2)}) collective-permute-start(bf16[64,4096]{1,0:T(8,128)(2,1)S(1)} %collective-permute-done.7), channel_id=1, source_target_pairs={{0,8},{8,16},{16,24},{24,0},{1,9},{9,17},{17,25},{25,1},{2,10},{10... | collective-permute-start | bytes 1572872 | tf_op jit(solution)/shard_map/ppermute | solution.py:26
  67.2 13.4 %collective-permute-done.3 = bf16[64,4096]{1,0:T(8,128)(2,1)S(1)} collective-permute-done((bf16[64,4096]{1,0:T(8,128)(2,1)S(1)}, bf16[64,4096]{1,0:T(8,128)(2,1)S(1)}, u32[]{:S(2)}, u32[]{:S(2)}) %collective-permute-start.3) | collective-permute-done | bytes 524320 | tf_op jit(solution)/shard_map/ppermute | solution.py:26
  80.6 10.5 %collective-permute-done.8 = bf16[64,4096]{1,0:T(8,128)(2,1)S(1)} collective-permute-done((bf16[64,4096]{1,0:T(8,128)(2,1)S(1)}, bf16[64,4096]{1,0:T(8,128)(2,1)S(1)}, u32[]{:S(2)}, u32[]{:S(2)}) %collective-permute-start.8) | collective-permute-done | bytes 524320 | tf_op jit(solution)/shard_map/ppermute | solution.py:26
  91.1 1.1 %maximum_bitcast_fusion = bf16[1,2,64,4096]{3,2,1,0:T(8,128)(2,1)} fusion(bf16[1,64,4096]{2,1,0:T(8,128)(2,1)S(1)} %bitcast.104, bf16[1,64,4096]{2,1,0:T(8,128)(2,1)S(1)} %bitcast.102), kind=kLoop, calls=%fused_computation.24 | loop fusion | flops 524288 | bytes 2097152 | tf_op jit(solution)/shard_map/reshape | solution.py:123
  (13 shorter events, 0.0 us)
Async XLA Ops:
  0.0 0.7 copy-start
  8.5 17.0 %collective-permute-start.1 = (bf16[64,2048]{0,1:T(8,128)(2,1)}, bf16[64,2048]{0,1:T(8,128)(2,1)}, u32[]{:S(2)}, u32[]{:S(2)}) collective-permute-start(bf16[64,2048]{0,1:T(8,128)(2,1)} %slice.32), channel_id=1, source_target_pairs={{0,2},{1,3},{4,6},{5,7},{8,10},{9,11},{12,14},{13,15},{16,18},{17,... | collective-permute-start | bytes 786440 | tf_op jit(solution)/shard_map/ppermute | solution.py:61
  9.8 27.1 %collective-permute-start = (bf16[64,2048]{0,1:T(8,128)(2,1)}, bf16[64,2048]{0,1:T(8,128)(2,1)}, u32[]{:S(2)}, u32[]{:S(2)}) collective-permute-start(bf16[64,2048]{0,1:T(8,128)(2,1)} %slice.32), channel_id=1, source_target_pairs={{0,1},{2,3},{4,5},{6,7},{8,9},{10,11},{12,13},{14,15},{16,17},{18,... | collective-permute-start | bytes 786440 | tf_op jit(solution)/shard_map/ppermute | solution.py:60
  14.0 6.7 %copy-start.5 = (s32[1,4,8]{2,1,0:T(4,128)S(1)}, s32[1,4,8]{2,1,0:T(4,128)}, u32[]{:S(2)}) copy-start(s32[1,4,8]{2,1,0:T(4,128)} %param.6) | copy-start | bytes 388
  14.0 7.0 %copy-start.4 = (s32[1,4]{1,0:T(1,128)S(1)}, s32[1,4]{1,0:T(1,128)}, u32[]{:S(2)}) copy-start(s32[1,4]{1,0:T(1,128)} %param.5) | copy-start | bytes 52
  16.7 18.9 %collective-permute-start.5 = (bf16[64,2048]{0,1:T(8,128)(2,1)}, bf16[64,2048]{0,1:T(8,128)(2,1)}, u32[]{:S(2)}, u32[]{:S(2)}) collective-permute-start(bf16[64,2048]{0,1:T(8,128)(2,1)} %slice.36), channel_id=1, source_target_pairs={{0,2},{1,3},{4,6},{5,7},{8,10},{9,11},{12,14},{13,15},{16,18},{17,... | collective-permute-start | bytes 786440 | tf_op jit(solution)/shard_map/ppermute | solution.py:61
  18.0 23.4 %collective-permute-start.4 = (bf16[64,2048]{0,1:T(8,128)(2,1)}, bf16[64,2048]{0,1:T(8,128)(2,1)}, u32[]{:S(2)}, u32[]{:S(2)}) collective-permute-start(bf16[64,2048]{0,1:T(8,128)(2,1)} %slice.36), channel_id=1, source_target_pairs={{0,1},{2,3},{4,5},{6,7},{8,9},{10,11},{12,13},{14,15},{16,17},{18,... | collective-permute-start | bytes 786440 | tf_op jit(solution)/shard_map/ppermute | solution.py:60
  25.5 13.8 %collective-permute-start.2 = (bf16[64,2048]{0,1:T(8,128)(2,1)}, bf16[64,2048]{0,1:T(8,128)(2,1)S(1)}, u32[]{:S(2)}, u32[]{:S(2)}) collective-permute-start(bf16[64,2048]{0,1:T(8,128)(2,1)} %collective-permute-done.1), channel_id=1, source_target_pairs={{3,2},{7,6},{11,10},{15,14},{19,18},{23,22},{27,26},{31,30}} | collective-permute-start | bytes 786440 | tf_op jit(solution)/shard_map/ppermute | solution.py:62
  35.6 14.9 %collective-permute-start.6 = (bf16[64,2048]{0,1:T(8,128)(2,1)}, bf16[64,2048]{0,1:T(8,128)(2,1)S(1)}, u32[]{:S(2)}, u32[]{:S(2)}) collective-permute-start(bf16[64,2048]{0,1:T(8,128)(2,1)} %collective-permute-done.5), channel_id=1, source_target_pairs={{3,2},{7,6},{11,10},{15,14},{19,18},{23,22},{27,26},{31,30}} | collective-permute-start | bytes 786440 | tf_op jit(solution)/shard_map/ppermute | solution.py:62
  52.6 1.4 %copy-start.2 = (bf16[64,4096]{0,1:T(8,128)(2,1)S(1)}, bf16[64,4096]{0,1:T(8,128)(2,1)}, u32[]{:S(2)}) copy-start(bf16[64,4096]{0,1:T(8,128)(2,1)} %slice.39) | copy-start | bytes 1572868
  54.0 2.3 %copy-start.3 = (bf16[256,1024]{0,1:T(8,128)(2,1)S(1)}, bf16[256,1024]{0,1:T(8,128)(2,1)}, u32[]{:S(2)}) copy-start(bf16[256,1024]{0,1:T(8,128)(2,1)} %get-tuple-element.14) | copy-start | bytes 1572868
  58.0 1.2 %copy-start.1 = (bf16[64,4096]{0,1:T(8,128)(2,1)S(1)}, bf16[64,4096]{0,1:T(8,128)(2,1)}, u32[]{:S(2)}) copy-start(bf16[64,4096]{0,1:T(8,128)(2,1)} %slice.35) | copy-start | bytes 1572868
  58.8 6.8 %collective-permute-start.7 = (bf16[64,4096]{1,0:T(8,128)(2,1)S(1)}, bf16[64,4096]{1,0:T(8,128)(2,1)S(1)}, u32[]{:S(2)}, u32[]{:S(2)}) collective-permute-start(bf16[64,4096]{1,0:T(8,128)(2,1)S(1)} %convert_element_type.55), channel_id=1, source_target_pairs={{0,4},{4,0},{1,5},{5,1},{2,6},{6,2},{3,7},{7,3},{8,12},{12,8},{9,1... | collective-permute-start | bytes 1572872 | tf_op jit(solution)/shard_map/ppermute | solution.py:20
  64.0 16.6 %collective-permute-start.3 = (bf16[64,4096]{1,0:T(8,128)(2,1)S(1)}, bf16[64,4096]{1,0:T(8,128)(2,1)S(1)}, u32[]{:S(2)}, u32[]{:S(2)}) collective-permute-start(bf16[64,4096]{1,0:T(8,128)(2,1)S(1)} %convert_element_type.49), channel_id=1, source_target_pairs={{0,8},{8,16},{16,24},{24,0},{1,9},{9,17},{17,25},{25,1},{2,10},{10... | collective-permute-start | bytes 1572872 | tf_op jit(solution)/shard_map/ppermute | solution.py:26
  65.6 25.5 %collective-permute-start.8 = (bf16[64,4096]{1,0:T(8,128)(2,1)S(1)}, bf16[64,4096]{1,0:T(8,128)(2,1)S(1)}, u32[]{:S(2)}, u32[]{:S(2)}) collective-permute-start(bf16[64,4096]{1,0:T(8,128)(2,1)S(1)} %collective-permute-done.7), channel_id=1, source_target_pairs={{0,8},{8,16},{16,24},{24,0},{1,9},{9,17},{17,25},{25,1},{2,10},{10... | collective-permute-start | bytes 1572872 | tf_op jit(solution)/shard_map/ppermute | solution.py:26

commit v4 on v3

--- a/solution.py
+++ b/solution.py
@@ -90,13 +90,15 @@
     key_value_width = KV_HEADS * HD
     far = jnp.int32(4 * length_all)
 
-    outs = []
-    for own_index in [1 - handed, handed]:
+    def prepare(own_index):
         row = lax.dynamic_index_in_dim(own_rows, own_index, 0, keepdims=False)
         kv_local = row[:, D:]
+        return row, kv_local
+
+    def attend_own(row, kv_local, pieces_and_chunks, own_index):
         pieces = [kv_local]
         key_pos = [query_pos]
-        for piece, chunk in gathered(kv_local, seq_index, seq_count, reach):
+        for piece, chunk in pieces_and_chunks:
             pieces.append(piece)
             key_pos.append(jnp.where(chunk >= 0, chunk * seg_len + local, far))
         kv_all = jnp.concatenate(pieces, axis=0)
@@ -104,21 +106,34 @@
         row_id = 2 * replica + own_index
         ends = lax.dynamic_index_in_dim(doc_ends, row_id, 0, keepdims=False)
         length = lax.dynamic_index_in_dim(lengths_all, row_id, 0, keepdims=False)
-        outs.append(
-            attend_row(
-                row[:, :D],
-                kv_all[:, :key_value_width],
-                kv_all[:, key_value_width:],
-                query_pos,
-                key_pos,
-                ends,
-                length,
+        return attend_row(
+            row[:, :D],
+            kv_all[:, :key_value_width],
+            kv_all[:, key_value_width:],
+            query_pos,
+            key_pos,
+            ends,
+            length,
+        )
+
+    kept_row, kept_kv = prepare(1 - handed)
+    given_row, given_kv = prepare(handed)
+    kept_pieces = gathered(kept_kv, seq_index, seq_count, reach)
+    given_kv = lax.optimization_barrier((given_kv, kept_pieces[0][0], kept_pieces[1][0]))[0]
+    given_pieces = gathered(given_kv, seq_index, seq_count, reach)
+    kept_out = attend_own(kept_row, kept_kv, kept_pieces, 1 - handed)
+    sent = [passed_along(kept_out, "section", 1)]
+    given_row = lax.optimization_barrier((given_row, kept_out))[0]
+    given_out = attend_own(given_row, given_kv, given_pieces, handed)
+    sections = lax.axis_size("section")
+    replicas = lax.axis_size("dp")
+    pairs = []
+    for section in range(sections):
+        for rep in range(replicas):
+            pairs.append(
+                (section * replicas + rep, (section + 1) % sections * replicas + (rep ^ 1))
             )
-        )
-    kept_out, given_out = outs
-    sent = [passed_along(kept_out, "section", 1)]
-    received = swapped(given_out, "dp", 0)
-    sent.append(passed_along(received, "section", 1))
+    sent.append(lax.ppermute(given_out, ("section", "dp"), pairs))
     out = jnp.stack(sent, axis=0)
     return out.reshape(1, RPR, seg_len, D)
 

time: 92.7 us -> 84.6 us (0.913)
  the two profiles are of different devices: /device:TPU:4 before, /device:TPU:5 now
where the time goes in v4:
time: 84.6 us; the launch traced here: 84 us
  waiting for transfers between devices  31.6 us (37%)
  starting transfers between devices  20.4 us (24%)
  local copies, waits for them, and re-layouts  10.4 us (12%)
  matrix products  9.35 us (11%)
  other arithmetic  8.07 us (10%)
  between operations  4.1 us (5%)
    ppermute x1, waiting for transfers between devices, shards(): sent.append(lax.ppermute(given_out, ('section', 'dp'), pairs))  14.1 us
    ppermute x2, waiting for transfers between devices, gathered(): relayed = lax.ppermute(over_y, 'seq', [(3, 2)])  9.69 us
    ppermute x2, starting transfers between devices, gathered(): over_x = lax.ppermute(block, 'seq', [(0, 1), (2, 3)])  9.53 us
    ppermute x2, waiting for transfers between devices, gathered(): over_y = lax.ppermute(block, 'seq', [(0, 2), (1, 3)])  7.77 us
    sub x2, matrix products, attend_row(): weights = jnp.where(allowed, jnp.exp(scores - row_top), 0.0)  5.84 us
    ppermute x1, starting transfers between devices, shards(): sent.append(lax.ppermute(given_out, ('section', 'dp'), pairs))  4.47 us
    concatenate x2, other arithmetic, attend_own(): kv_all = jnp.concatenate(pieces, axis=0)  4.08 us
    dot_general x2, matrix products, attend_row(): jnp.einsum('kgqs,skd->qkgd', rounded, values, preferred_element_type=jnp....  3.51 us
  transfers between devices with their start and end apart: 8, of which 4 were waited for; matrix products, arithmetic and copies ran while one was open for 26% of the time, Pallas kernels for 0%

profile of v4, /device:TPU:5, one launch (start us, length us, event | category | flops | bytes accessed | tf_op | source)
XLA Modules:
  0.0 84.0 jit_solution(1106752407541594286)
XLA Ops:
  0.0 0.0 copy-start
  0.0 0.7 copy-done
  0.7 0.6 constant_dynamic-slice_fusion.6
  4.5 1.5 %constant_dynamic-slice_fusion.5 = (bf16[1,1,64,6144]{3,2,1,0:T(8,128)(2,1)S(1)}, bf16[1,1,64,6144]{3,2,1,0:T(8,128)(2,1)S(1)}) fusion(bf16[1,2,64,6144]{3,2,1,0:T(8,128)(2,1)} %param.4, s32[]{:T(128)S(6)} %select_n.82, s32[]{:T(128)S(6)} %select_n.95), kind=kLoop, calls=%fused_computation.48 | loop fusion | bytes 3145736 | tf_op jit(solution)/shard_map/jit(dynamic_index_in_dim)/dynamic_slice | solution.py:94
  6.0 0.0 copy-start.3
  6.0 0.0 copy-start.2
  6.0 0.9 %copy.17 = bf16[1,1,64,6144]{2,3,1,0:T(8,128)(2,1)S(1)} copy(bf16[1,1,64,6144]{3,2,1,0:T(8,128)(2,1)S(1)} %get-tuple-element.13) | data formatting | bytes 1572864 | tf_op jit(solution)/shard_map/jit(dynamic_index_in_dim)/dynamic_slice | solution.py:94
  6.9 1.3 %collective-permute-start.1 = (bf16[64,2048]{0,1:T(8,128)(2,1)S(1)}, bf16[64,2048]{0,1:T(8,128)(2,1)}, u32[]{:S(2)}, u32[]{:S(2)}) collective-permute-start(bf16[64,2048]{0,1:T(8,128)(2,1)S(1)} %slice.32), channel_id=1, source_target_pairs={{0,2},{1,3},{4,6},{5,7},{8,10},{9,11},{12,14},{13,15},{16,18},{17,... | collective-permute-start | bytes 786440 | tf_op jit(solution)/shard_map/ppermute | solution.py:61
  8.2 3.9 %collective-permute-start = (bf16[64,2048]{0,1:T(8,128)(2,1)S(1)}, bf16[64,2048]{0,1:T(8,128)(2,1)}, u32[]{:S(2)}, u32[]{:S(2)}) collective-permute-start(bf16[64,2048]{0,1:T(8,128)(2,1)S(1)} %slice.32), channel_id=1, source_target_pairs={{0,1},{2,3},{4,5},{6,7},{8,9},{10,11},{12,13},{14,15},{16,17},{18,... | collective-permute-start | bytes 786440 | tf_op jit(solution)/shard_map/ppermute | solution.py:60
  12.8 0.2 reduce_window_sum.11
  13.1 0.1 pad_add_fusion
  13.1 0.7 constant_dynamic-slice_fusion
  13.8 0.1 convert_reduce_fusion.3
  13.9 0.1 convert_reduce_fusion.1
  14.0 7.8 %collective-permute-done.1 = bf16[64,2048]{0,1:T(8,128)(2,1)} collective-permute-done((bf16[64,2048]{0,1:T(8,128)(2,1)S(1)}, bf16[64,2048]{0,1:T(8,128)(2,1)}, u32[]{:S(2)}, u32[]{:S(2)}) %collective-permute-start.1) | collective-permute-done | bytes 262176 | tf_op jit(solution)/shard_map/ppermute | solution.py:61
  21.7 1.3 %collective-permute-start.2 = (bf16[64,2048]{0,1:T(8,128)(2,1)}, bf16[64,2048]{0,1:T(8,128)(2,1)}, u32[]{:S(2)}, u32[]{:S(2)}) collective-permute-start(bf16[64,2048]{0,1:T(8,128)(2,1)} %collective-permute-done.1), channel_id=1, source_target_pairs={{3,2},{7,6},{11,10},{15,14},{19,18},{23,22},{27,26},{31,30}} | collective-permute-start | bytes 786440 | tf_op jit(solution)/shard_map/ppermute | solution.py:62
  23.0 1.3 %compare_convert_fusion = (f32[64]{0:T(128)S(1)}, f32[64]{0:T(128)S(1)}) fusion(s32[]{:T(128)} %bitcast.24, s32[]{:T(128)S(6)} %mul.47, s32[]{:T(128)} %bitcast.12), kind=kLoop, calls=%fused_computation.41 | loop fusion | flops 320 | bytes 524 | tf_op jit(solution)/shard_map/convert_element_type | solution.py:53
  24.4 1.0 %slice.35 = bf16[64,4096]{0,1:T(8,128)(2,1)} slice(bf16[64,6144]{0,1:T(8,128)(2,1)S(1)} %bitcast.95), slice={[0:64], [0:4096]} | slice | bytes 1048576 | tf_op jit(solution)/shard_map/slice | solution.py:110
  25.4 0.9 %copy.23 = bf16[1,1,64,6144]{2,3,1,0:T(8,128)(2,1)S(1)} copy(bf16[1,1,64,6144]{3,2,1,0:T(8,128)(2,1)S(1)} %get-tuple-element.14) | data formatting | bytes 1572864 | tf_op jit(solution)/shard_map/jit(dynamic_index_in_dim)/dynamic_slice | solution.py:94
  26.4 0.1 compare_and_fusion.1
  26.5 0.0 collective-permute-done
  26.5 1.3 %collective-permute-start.5 = (bf16[64,2048]{0,1:T(8,128)(2,1)S(1)}, bf16[64,2048]{0,1:T(8,128)(2,1)}, u32[]{:S(2)}, u32[]{:S(2)}) collective-permute-start(bf16[64,2048]{0,1:T(8,128)(2,1)S(1)} %slice.36), channel_id=1, source_target_pairs={{0,2},{1,3},{4,6},{5,7},{8,10},{9,11},{12,14},{13,15},{16,18},{17,... | collective-permute-start | bytes 786440 | tf_op jit(solution)/shard_map/ppermute | solution.py:61
  27.8 5.6 %collective-permute-start.4 = (bf16[64,2048]{0,1:T(8,128)(2,1)S(1)}, bf16[64,2048]{0,1:T(8,128)(2,1)}, u32[]{:S(2)}, u32[]{:S(2)}) collective-permute-start(bf16[64,2048]{0,1:T(8,128)(2,1)S(1)} %slice.36), channel_id=1, source_target_pairs={{0,1},{2,3},{4,5},{6,7},{8,9},{10,11},{12,13},{14,15},{16,17},{18,... | collective-permute-start | bytes 786440 | tf_op jit(solution)/shard_map/ppermute | solution.py:60
  33.4 2.5 %collective-permute-done.2 = bf16[64,2048]{0,1:T(8,128)(2,1)} collective-permute-done((bf16[64,2048]{0,1:T(8,128)(2,1)}, bf16[64,2048]{0,1:T(8,128)(2,1)}, u32[]{:S(2)}, u32[]{:S(2)}) %collective-permute-start.2) | collective-permute-done | bytes 262176 | tf_op jit(solution)/shard_map/ppermute | solution.py:62
  35.9 2.0 %pad_maximum_fusion = bf16[256,2048]{0,1:T(8,128)(2,1)S(1)} fusion(bf16[64,2048]{0,1:T(8,128)(2,1)} %collective-permute-done.2, bf16[64,2048]{0,1:T(8,128)(2,1)} %collective-permute-done.1, bf16[64,2048]{0,1:T(8,128)(2,1)} %collective-permute-done, bf16[64,2048]{0,1:T(8,128)(2,1)S(1)} %slice.32), kind=kLoop, calls=%fused_computation.22 | loop fusion | flops 4194304 | bytes 2097152 | tf_op jit(solution)/shard_map/concatenate | solution.py:104
  37.9 0.0 copy-start.1
  37.9 1.1 %fusion.34 = (bf16[256,1024]{0,1:T(8,128)(2,1)}, bf16[256,1024]{0,1:T(8,128)(2,1)}) fusion(bf16[256,2048]{0,1:T(8,128)(2,1)S(1)} %pad_maximum_fusion), kind=kLoop, calls=%fused_computation.61 | loop fusion | bytes 2097152 | tf_op jit(solution)/shard_map/slice | solution.py:111
  39.1 0.5 copy-done.1
  39.5 3.5 %fusion.36 = (f32[8,4,64]{2,1,0:T(4,128)S(1)}, bf16[8,4,64,256]{3,2,1,0:T(8,128)(2,1)}) fusion(pred[64,256]{1,0:T(8,128)(4,1)S(1)} %get-tuple-element.21, bf16[256,8,128,1]{0,2,3,1:T(8,128)(2,1)} %bitcast.104, bf16[64,8,4,128]{0,3,2,1:T(8,128)(2,1)S(1)} %bitcast.98), kind=kOutput, calls=%fused_computation.63 | convolution fusion | flops 272105728 | bytes 2121728 | tf_op jit(solution)/shard_map/sub | solution.py:48
  43.1 0.0 collective-permute-done.5
  43.1 1.3 %collective-permute-start.6 = (bf16[64,2048]{0,1:T(8,128)(2,1)}, bf16[64,2048]{0,1:T(8,128)(2,1)}, u32[]{:S(2)}, u32[]{:S(2)}) collective-permute-start(bf16[64,2048]{0,1:T(8,128)(2,1)} %collective-permute-done.5), channel_id=1, source_target_pairs={{3,2},{7,6},{11,10},{15,14},{19,18},{23,22},{27,26},{31,30}} | collective-permute-start | bytes 786440 | tf_op jit(solution)/shard_map/ppermute | solution.py:62
  44.4 1.8 %fusion.14 = bf16[64,8,4,128]{3,0,2,1:T(8,128)(2,1)S(1)} fusion(bf16[256,8,128,1]{0,2,3,1:T(8,128)(2,1)} %bitcast.100, bf16[8,4,64,256]{3,2,1,0:T(8,128)(2,1)} %get-tuple-element.26, f32[64]{0:T(128)S(1)} %get-tuple-element.30, f32[64,8,4]{0,2,1:T(4,128)S(1)} %bitcast.106), kind=kOutput, calls=%fused_computation.20 | convolution fusion | flops 135004160 | bytes 2105600 | tf_op jit(solution)/shard_map/kgqs,skd->qkgd/dot_general | solution.py:51
  46.2 0.4 copy.22
  46.6 1.2 %convert_element_type.49 = bf16[64,4096]{1,0:T(8,128)(2,1)} reshape(bf16[64,8,4,128]{3,2,1,0:T(4,128)(2,1)S(1)} %copy.22) | data formatting | bytes 1048576 | tf_op jit(solution)/shard_map/convert_element_type | solution.py:55
  47.8 1.3 %collective-permute-start.3 = (bf16[64,4096]{1,0:T(8,128)(2,1)}, bf16[64,4096]{1,0:T(8,128)(2,1)}, u32[]{:S(2)}, u32[]{:S(2)}) collective-permute-start(bf16[64,4096]{1,0:T(8,128)(2,1)} %convert_element_type.49), channel_id=1, source_target_pairs={{0,8},{8,16},{16,24},{24,0},{1,9},{9,17},{17,25},{25,1},{2,10},{10... | collective-permute-start | bytes 1572872 | tf_op jit(solution)/shard_map/ppermute | solution.py:26
  49.1 0.1 slice.31
  49.2 0.0 collective-permute-done.4
  49.2 7.2 %collective-permute-done.6 = bf16[64,2048]{0,1:T(8,128)(2,1)} collective-permute-done((bf16[64,2048]{0,1:T(8,128)(2,1)}, bf16[64,2048]{0,1:T(8,128)(2,1)}, u32[]{:S(2)}, u32[]{:S(2)}) %collective-permute-start.6) | collective-permute-done | bytes 262176 | tf_op jit(solution)/shard_map/ppermute | solution.py:62
  56.4 2.0 %pad_maximum_fusion.1 = bf16[256,2048]{0,1:T(8,128)(2,1)S(1)} fusion(bf16[64,2048]{0,1:T(8,128)(2,1)} %collective-permute-done.6, bf16[64,2048]{0,1:T(8,128)(2,1)} %collective-permute-done.5, bf16[64,2048]{0,1:T(8,128)(2,1)} %collective-permute-done.4, bf16[64,2048]{0,1:T(8,128)(2,1)S(1)} %slice.36), kind=kLoop, calls=%fused_computation.23 | loop fusion | flops 4194304 | bytes 2097152 | tf_op jit(solution)/shard_map/concatenate | solution.py:104
  58.4 0.1 fusion.35
  58.5 2.3 %fusion.37 = (f32[8,4,64]{2,1,0:T(4,128)S(1)}, bf16[8,4,64,256]{3,2,1,0:T(8,128)(2,1)}) fusion(pred[64,256]{1,0:T(8,128)(4,1)S(1)} %get-tuple-element.22, bf16[256,8,128,1]{0,2,3,1:T(8,128)(2,1)S(1)} %bitcast.103, bf16[64,8,4,128]{0,3,2,1:T(8,128)(2,1)S(1)} %bitcast.99), kind=kOutput, calls=%fused_computation.64 | convolution fusion | flops 272105728 | bytes 2121728 | tf_op jit(solution)/shard_map/sub | solution.py:48
  60.8 1.7 %fusion.15 = bf16[64,8,4,128]{3,0,2,1:T(8,128)(2,1)S(1)} fusion(bf16[256,8,128,1]{0,2,3,1:T(8,128)(2,1)S(1)} %bitcast.101, bf16[8,4,64,256]{3,2,1,0:T(8,128)(2,1)} %get-tuple-element.28, f32[64]{0:T(128)S(1)} %get-tuple-element.29, f32[64,8,4]{0,2,1:T(4,128)S(1)} %bitcast.107), kind=kOutput, calls=%fused_computation.21 | convolution fusion | flops 135004160 | bytes 2105600 | tf_op jit(solution)/shard_map/kgqs,skd->qkgd/dot_general | solution.py:51
  62.5 0.4 copy.28
  62.9 0.4 convert_element_type.55
  63.3 4.5 %collective-permute-start.7 = (bf16[64,4096]{1,0:T(8,128)(2,1)S(1)}, bf16[64,4096]{1,0:T(8,128)(2,1)S(1)}, u32[]{:S(2)}, u32[]{:S(2)}) collective-permute-start(bf16[64,4096]{1,0:T(8,128)(2,1)S(1)} %convert_element_type.55), channel_id=1, source_target_pairs={{0,12},{4,8},{8,20},{12,16},{16,28},{20,24},{24,4},{28,0},{1,13},{... | collective-permute-start | bytes 1572872 | tf_op jit(solution)/shard_map/ppermute | solution.py:136
  67.8 0.0 collective-permute-done.3
  67.8 14.1 %collective-permute-done.7 = bf16[64,4096]{1,0:T(8,128)(2,1)S(1)} collective-permute-done((bf16[64,4096]{1,0:T(8,128)(2,1)S(1)}, bf16[64,4096]{1,0:T(8,128)(2,1)S(1)}, u32[]{:S(2)}, u32[]{:S(2)}) %collective-permute-start.7) | collective-permute-done | bytes 524320 | tf_op jit(solution)/shard_map/ppermute | solution.py:136
  81.9 2.1 %maximum_bitcast_fusion = bf16[1,2,64,4096]{3,2,1,0:T(8,128)(2,1)} fusion(bf16[1,64,4096]{2,1,0:T(8,128)(2,1)S(1)} %bitcast.102, bf16[1,64,4096]{2,1,0:T(8,128)(2,1)} %bitcast.13), kind=kLoop, calls=%fused_computation.24 | loop fusion | flops 524288 | bytes 2097152 | tf_op jit(solution)/shard_map/reshape | solution.py:138
  (7 shorter events, 0.1 us)
Async XLA Ops:
  0.0 0.7 copy-start
  6.0 6.9 %copy-start.3 = (s32[1,4,8]{2,1,0:T(4,128)S(1)}, s32[1,4,8]{2,1,0:T(4,128)}, u32[]{:S(2)}) copy-start(s32[1,4,8]{2,1,0:T(4,128)} %param.6) | copy-start | bytes 388
  6.0 7.2 %copy-start.2 = (s32[1,4]{1,0:T(1,128)S(1)}, s32[1,4]{1,0:T(1,128)}, u32[]{:S(2)}) copy-start(s32[1,4]{1,0:T(1,128)} %param.5) | copy-start | bytes 52
  6.9 14.8 %collective-permute-start.1 = (bf16[64,2048]{0,1:T(8,128)(2,1)S(1)}, bf16[64,2048]{0,1:T(8,128)(2,1)}, u32[]{:S(2)}, u32[]{:S(2)}) collective-permute-start(bf16[64,2048]{0,1:T(8,128)(2,1)S(1)} %slice.32), channel_id=1, source_target_pairs={{0,2},{1,3},{4,6},{5,7},{8,10},{9,11},{12,14},{13,15},{16,18},{17,... | collective-permute-start | bytes 786440 | tf_op jit(solution)/shard_map/ppermute | solution.py:61
  8.2 18.2 %collective-permute-start = (bf16[64,2048]{0,1:T(8,128)(2,1)S(1)}, bf16[64,2048]{0,1:T(8,128)(2,1)}, u32[]{:S(2)}, u32[]{:S(2)}) collective-permute-start(bf16[64,2048]{0,1:T(8,128)(2,1)S(1)} %slice.32), channel_id=1, source_target_pairs={{0,1},{2,3},{4,5},{6,7},{8,9},{10,11},{12,13},{14,15},{16,17},{18,... | collective-permute-start | bytes 786440 | tf_op jit(solution)/shard_map/ppermute | solution.py:60
  21.7 14.2 %collective-permute-start.2 = (bf16[64,2048]{0,1:T(8,128)(2,1)}, bf16[64,2048]{0,1:T(8,128)(2,1)}, u32[]{:S(2)}, u32[]{:S(2)}) collective-permute-start(bf16[64,2048]{0,1:T(8,128)(2,1)} %collective-permute-done.1), channel_id=1, source_target_pairs={{3,2},{7,6},{11,10},{15,14},{19,18},{23,22},{27,26},{31,30}} | collective-permute-start | bytes 786440 | tf_op jit(solution)/shard_map/ppermute | solution.py:62
  26.5 16.6 %collective-permute-start.5 = (bf16[64,2048]{0,1:T(8,128)(2,1)S(1)}, bf16[64,2048]{0,1:T(8,128)(2,1)}, u32[]{:S(2)}, u32[]{:S(2)}) collective-permute-start(bf16[64,2048]{0,1:T(8,128)(2,1)S(1)} %slice.36), channel_id=1, source_target_pairs={{0,2},{1,3},{4,6},{5,7},{8,10},{9,11},{12,14},{13,15},{16,18},{17,... | collective-permute-start | bytes 786440 | tf_op jit(solution)/shard_map/ppermute | solution.py:61
  27.8 21.4 %collective-permute-start.4 = (bf16[64,2048]{0,1:T(8,128)(2,1)S(1)}, bf16[64,2048]{0,1:T(8,128)(2,1)}, u32[]{:S(2)}, u32[]{:S(2)}) collective-permute-start(bf16[64,2048]{0,1:T(8,128)(2,1)S(1)} %slice.36), channel_id=1, source_target_pairs={{0,1},{2,3},{4,5},{6,7},{8,9},{10,11},{12,13},{14,15},{16,17},{18,... | collective-permute-start | bytes 786440 | tf_op jit(solution)/shard_map/ppermute | solution.py:60
  37.9 1.6 %copy-start.1 = (bf16[64,4096]{0,1:T(8,128)(2,1)S(1)}, bf16[64,4096]{0,1:T(8,128)(2,1)}, u32[]{:S(2)}) copy-start(bf16[64,4096]{0,1:T(8,128)(2,1)} %slice.35) | copy-start | bytes 1572868
  43.1 13.3 %collective-permute-start.6 = (bf16[64,2048]{0,1:T(8,128)(2,1)}, bf16[64,2048]{0,1:T(8,128)(2,1)}, u32[]{:S(2)}, u32[]{:S(2)}) collective-permute-start(bf16[64,2048]{0,1:T(8,128)(2,1)} %collective-permute-done.5), channel_id=1, source_target_pairs={{3,2},{7,6},{11,10},{15,14},{19,18},{23,22},{27,26},{31,30}} | collective-permute-start | bytes 786440 | tf_op jit(solution)/shard_map/ppermute | solution.py:62
  47.8 20.0 %collective-permute-start.3 = (bf16[64,4096]{1,0:T(8,128)(2,1)}, bf16[64,4096]{1,0:T(8,128)(2,1)}, u32[]{:S(2)}, u32[]{:S(2)}) collective-permute-start(bf16[64,4096]{1,0:T(8,128)(2,1)} %convert_element_type.49), channel_id=1, source_target_pairs={{0,8},{8,16},{16,24},{24,0},{1,9},{9,17},{17,25},{25,1},{2,10},{10... | collective-permute-start | bytes 1572872 | tf_op jit(solution)/shard_map/ppermute | solution.py:26
  63.3 18.6 %collective-permute-start.7 = (bf16[64,4096]{1,0:T(8,128)(2,1)S(1)}, bf16[64,4096]{1,0:T(8,128)(2,1)S(1)}, u32[]{:S(2)}, u32[]{:S(2)}) collective-permute-start(bf16[64,4096]{1,0:T(8,128)(2,1)S(1)} %convert_element_type.55), channel_id=1, source_target_pairs={{0,12},{4,8},{8,20},{12,16},{16,28},{20,24},{24,4},{28,0},{1,13},{... | collective-permute-start | bytes 1572872 | tf_op jit(solution)/shard_map/ppermute | solution.py:136

commit v5 on v4

--- a/solution.py
+++ b/solution.py
@@ -57,14 +57,13 @@
 
 def gathered(block, seq_index, seq_count, reach):
     if seq_count == 4 and reach == 2:
-        over_x = lax.ppermute(block, "seq", [(0, 1), (2, 3)])
-        over_y = lax.ppermute(block, "seq", [(0, 2), (1, 3)])
-        relayed = lax.ppermute(over_y, "seq", [(3, 2)])
+        over_y = lax.ppermute(block, "seq", [(j, j ^ 2) for j in range(4)])
         odd = seq_index % 2 == 1
+        onward = jnp.where(odd, over_y, block)
+        over_x = lax.ppermute(onward, "seq", [(j, j ^ 1) for j in range(4)])
         return [
-            (over_x, jnp.where(odd, seq_index - 1, -1)),
-            (over_y, seq_index - 2),
-            (relayed, jnp.where(seq_index == 2, 1, -1)),
+            (over_y, jnp.bitwise_xor(seq_index, 2)),
+            (over_x, jnp.where(odd, seq_index - 1, jnp.bitwise_xor(seq_index, 3))),
         ]
     pieces = []
     for shift in range(1, reach + 1):
@@ -119,7 +118,7 @@
     kept_row, kept_kv = prepare(1 - handed)
     given_row, given_kv = prepare(handed)
     kept_pieces = gathered(kept_kv, seq_index, seq_count, reach)
-    given_kv = lax.optimization_barrier((given_kv, kept_pieces[0][0], kept_pieces[1][0]))[0]
+    given_kv = lax.optimization_barrier((given_kv, kept_pieces[0][0]))[0]
     given_pieces = gathered(given_kv, seq_index, seq_count, reach)
     kept_out = attend_own(kept_row, kept_kv, kept_pieces, 1 - handed)
     sent = [passed_along(kept_out, "section", 1)]

time: 84.6 us -> 56.6 us (0.67)
  the two profiles are of different devices: /device:TPU:5 before, /device:TPU:1 now
where the time goes in v5:
time: 56.6 us; the launch traced here: 56.3 us
  waiting for transfers between devices  26.1 us (46%)
  starting transfers between devices  11.3 us (20%)
  other arithmetic  6.78 us (12%)
  local copies, waits for them, and re-layouts  6.22 us (11%)
  between operations  4.11 us (7%)
  matrix products  1.83 us (3%)
    ppermute x1, waiting for transfers between devices, shards(): sent.append(lax.ppermute(given_out, ('section', 'dp'), pairs))  14 us
    ppermute x2, waiting for transfers between devices, gathered(): over_y = lax.ppermute(block, 'seq', [(j, j ^ 2) for j in range(4)])  6.47 us
    ppermute x1, starting transfers between devices, shards(): sent.append(lax.ppermute(given_out, ('section', 'dp'), pairs))  5.05 us
    ppermute x2, starting transfers between devices, gathered(): over_y = lax.ppermute(block, 'seq', [(j, j ^ 2) for j in range(4)])  3.43 us
    ppermute x2, waiting for transfers between devices, gathered(): over_x = lax.ppermute(onward, 'seq', [(j, j ^ 1) for j in range(4)])  2.96 us
    ppermute x1, waiting for transfers between devices, passed_along(): return lax.ppermute(value, axis, pairs)  2.66 us
    reshape x1, other arithmetic, shards(): return out.reshape(1, RPR, seg_len, D)  2.11 us
    sub x2, other arithmetic, attend_row(): weights = jnp.where(allowed, jnp.exp(scores - row_top), 0.0)  1.94 us
  transfers between devices with their start and end apart: 6, of which 6 were waited for; matrix products, arithmetic and copies ran while one was open for 16% of the time, Pallas kernels for 0%

profile of v5, /device:TPU:1, one launch (start us, length us, event | category | flops | bytes accessed | tf_op | source)
XLA Modules:
  0.0 56.3 jit_solution(892322964075620931)
XLA Ops:
  0.0 0.0 copy-start
  0.0 0.0 copy-start.2
  0.0 0.0 copy-start.1
  0.0 0.6 %copy-done = s32[1,2]{1,0:T(1,128)S(1)} copy-done((s32[1,2]{1,0:T(1,128)S(1)}, s32[1,2]{1,0:T(1,128)}, u32[]{:S(2)}) %copy-start) | copy-done | bytes 32
  0.7 0.6 %constant_dynamic-slice_fusion.4 = s32[1,1]{1,0:T(1,128)} fusion(s32[1,2]{1,0:T(1,128)S(1)} %copy-done, s32[]{:T(128)S(6)} %select_n.77), kind=kLoop, calls=%fused_computation.63 | loop fusion | bytes 12 | tf_op jit(solution)/shard_map/jit(dynamic_index_in_dim)/dynamic_slice | solution.py:80
  4.5 1.5 %dynamic-slice_bitcast_fusion.1 = (bf16[64,6144]{1,0:T(8,128)(2,1)S(1)}, bf16[64,6144]{1,0:T(8,128)(2,1)S(1)}) fusion(bf16[1,2,64,6144]{3,2,1,0:T(8,128)(2,1)} %param.4, s32[]{:T(128)S(6)} %select_n.78, s32[]{:T(128)S(6)} %select_n.90), kind=kLoop, calls=%fused_computation.33 | loop fusion | bytes 3145736 | tf_op jit(solution)/shard_map/jit(dynamic_index_in_dim)/squeeze | solution.py:93
  6.0 2.1 %collective-permute-start = (bf16[64,2048]{1,0:T(8,128)(2,1)S(1)}, bf16[64,2048]{1,0:T(8,128)(2,1)S(1)}, u32[]{:S(2)}, u32[]{:S(2)}) collective-permute-start(bf16[64,2048]{1,0:T(8,128)(2,1)S(1)} %slice.32), channel_id=1, source_target_pairs={{0,2},{1,3},{2,0},{3,1},{4,6},{5,7},{6,4},{7,5},{8,10},{9,11},{10,... | collective-permute-start | bytes 786440 | tf_op jit(solution)/shard_map/ppermute | solution.py:60
  8.8 0.0 copy-done.2
  8.8 0.2 reduce_window_sum.11
  9.0 0.1 pad_add_fusion
  9.1 0.0 copy-done.1
  9.1 0.7 %constant_dynamic-slice_fusion = (s32[1,1]{1,0:T(1,128)}, s32[1,1]{1,0:T(1,128)}) fusion(s32[1,4]{1,0:T(1,128)S(1)} %copy-done.1, s32[]{:T(128)S(6)} %select_n.92, s32[]{:T(128)S(6)} %select_n.87), kind=kLoop, calls=%fused_computation.59 | loop fusion | bytes 24 | tf_op jit(solution)/shard_map/jit(dynamic_index_in_dim)/dynamic_slice | solution.py:107
  9.7 0.1 convert_reduce_fusion.2
  9.8 0.1 convert_reduce_fusion
  9.9 4.2 %collective-permute-done = bf16[64,2048]{1,0:T(8,128)(2,1)S(1)} collective-permute-done((bf16[64,2048]{1,0:T(8,128)(2,1)S(1)}, bf16[64,2048]{1,0:T(8,128)(2,1)S(1)}, u32[]{:S(2)}, u32[]{:S(2)}) %collective-permute-start) | collective-permute-done | bytes 262176 | tf_op jit(solution)/shard_map/ppermute | solution.py:60
  14.2 1.2 %collective-permute-start.1 = (bf16[64,2048]{1,0:T(8,128)(2,1)S(1)}, bf16[64,2048]{1,0:T(8,128)(2,1)S(1)}, u32[]{:S(2)}, u32[]{:S(2)}) collective-permute-start(bf16[64,2048]{1,0:T(8,128)(2,1)S(1)} %broadcast_select_fusion.1), channel_id=1, source_target_pairs={{0,1},{1,0},{2,3},{3,2},{4,5},{5,4},{6,7},{7,6},{8,9},{9,8},{10,11... | collective-permute-start | bytes 786440 | tf_op jit(solution)/shard_map/ppermute | solution.py:63
  15.4 1.3 %compare_convert_fusion = (f32[64]{0:T(128)S(1)}, f32[64]{0:T(128)S(1)}) fusion(s32[]{:T(128)} %bitcast.18, s32[]{:T(128)S(6)} %mul.43, s32[]{:T(128)} %bitcast.9), kind=kLoop, calls=%fused_computation.57 | loop fusion | flops 320 | bytes 524 | tf_op jit(solution)/shard_map/convert_element_type | solution.py:53
  16.8 0.4 reshape.61
  17.2 0.1 compare_and_fusion
  17.3 1.3 %collective-permute-start.3 = (bf16[64,2048]{1,0:T(8,128)(2,1)S(1)}, bf16[64,2048]{1,0:T(8,128)(2,1)S(1)}, u32[]{:S(2)}, u32[]{:S(2)}) collective-permute-start(bf16[64,2048]{1,0:T(8,128)(2,1)S(1)} %slice.36), channel_id=1, source_target_pairs={{0,2},{1,3},{2,0},{3,1},{4,6},{5,7},{6,4},{7,5},{8,10},{9,11},{10,... | collective-permute-start | bytes 786440 | tf_op jit(solution)/shard_map/ppermute | solution.py:60
  18.6 2.3 %collective-permute-done.1 = bf16[64,2048]{1,0:T(8,128)(2,1)S(1)} collective-permute-done((bf16[64,2048]{1,0:T(8,128)(2,1)S(1)}, bf16[64,2048]{1,0:T(8,128)(2,1)S(1)}, u32[]{:S(2)}, u32[]{:S(2)}) %collective-permute-start.1) | collective-permute-done | bytes 262176 | tf_op jit(solution)/shard_map/ppermute | solution.py:63
  20.8 0.1 pad_maximum_fusion
  20.9 0.1 slice_bitcast_fusion.3
  21.0 0.1 copy.34
  21.0 0.1 copy.33
  21.1 2.3 %collective-permute-done.3 = bf16[64,2048]{1,0:T(8,128)(2,1)S(1)} collective-permute-done((bf16[64,2048]{1,0:T(8,128)(2,1)S(1)}, bf16[64,2048]{1,0:T(8,128)(2,1)S(1)}, u32[]{:S(2)}, u32[]{:S(2)}) %collective-permute-start.3) | collective-permute-done | bytes 262176 | tf_op jit(solution)/shard_map/ppermute | solution.py:60
  23.4 0.8 %broadcast_select_fusion = (bf16[64,2048]{1,0:T(8,128)(2,1)}, bf16[192,2048]{1,0:T(8,128)(2,1)S(1)}) fusion(bf16[64,2048]{1,0:T(8,128)(2,1)S(1)} %collective-permute-done.3, bf16[64,2048]{1,0:T(8,128)(2,1)S(1)} %slice.36, pred[]{:T(512)S(6)} %eq.17), kind=kLoop, calls=%fused_computation.46 | loop fusion | flops 131071 | bytes 1048577 | tf_op jit(solution)/shard_map/jit(_where)/select_n | solution.py:62
  24.1 0.6 %collective-permute-start.4 = (bf16[64,2048]{1,0:T(8,128)(2,1)}, bf16[64,2048]{1,0:T(8,128)(2,1)S(1)}, u32[]{:S(2)}, u32[]{:S(2)}) collective-permute-start(bf16[64,2048]{1,0:T(8,128)(2,1)} %get-tuple-element.19), channel_id=1, source_target_pairs={{0,1},{1,0},{2,3},{3,2},{4,5},{5,4},{6,7},{7,6},{8,9},{9,8},{10,11... | collective-permute-start | bytes 786440 | tf_op jit(solution)/shard_map/ppermute | solution.py:63
  24.7 0.5 fusion.26
  25.2 1.0 %fusion.38 = (f32[8,4,64]{2,1,0:T(4,128)S(1)}, bf16[8,4,64,192]{3,2,1,0:T(8,128)(2,1)S(1)}) fusion(f32[8,192,64,4]{1,2,3,0:T(8,128)S(1)} %fusion.26, pred[64,192]{1,0:T(8,128)(4,1)S(1)} %get-tuple-element.24), kind=kOutput, calls=%fused_computation.74 | output fusion | flops 2752703 | bytes 2379776 | tf_op jit(solution)/shard_map/sub | solution.py:48
  26.2 0.5 fusion.14
  26.6 0.4 copy.16
  27.1 0.4 convert_element_type.49
  27.4 1.0 %collective-permute-start.2 = (bf16[64,4096]{1,0:T(8,128)(2,1)S(1)}, bf16[64,4096]{1,0:T(8,128)(2,1)}, u32[]{:S(2)}, u32[]{:S(2)}) collective-permute-start(bf16[64,4096]{1,0:T(8,128)(2,1)S(1)} %convert_element_type.49), channel_id=1, source_target_pairs={{0,8},{8,16},{16,24},{24,0},{1,9},{9,17},{17,25},{25,1},{2,10},{10... | collective-permute-start | bytes 1572872 | tf_op jit(solution)/shard_map/ppermute | solution.py:26
  28.5 0.4 reshape.64
  28.9 0.7 %collective-permute-done.4 = bf16[64,2048]{1,0:T(8,128)(2,1)S(1)} collective-permute-done((bf16[64,2048]{1,0:T(8,128)(2,1)}, bf16[64,2048]{1,0:T(8,128)(2,1)S(1)}, u32[]{:S(2)}, u32[]{:S(2)}) %collective-permute-start.4) | collective-permute-done | bytes 262176 | tf_op jit(solution)/shard_map/ppermute | solution.py:63
  29.6 0.1 slice_bitcast_fusion.1
  29.7 0.1 copy.36
  29.7 0.1 copy.35
  29.8 0.5 fusion.24
  30.3 1.0 %fusion.39 = (f32[8,4,64]{2,1,0:T(4,128)S(1)}, bf16[8,4,64,192]{3,2,1,0:T(8,128)(2,1)S(1)}) fusion(f32[8,192,64,4]{1,2,3,0:T(8,128)S(1)} %fusion.24, pred[64,192]{1,0:T(8,128)(4,1)S(1)} %get-tuple-element.23), kind=kOutput, calls=%fused_computation.75 | output fusion | flops 2752703 | bytes 2379776 | tf_op jit(solution)/shard_map/sub | solution.py:48
  31.2 0.5 fusion.15
  31.7 0.4 copy.20
  32.1 0.4 convert_element_type.55
  32.5 5.0 %collective-permute-start.5 = (bf16[64,4096]{1,0:T(8,128)(2,1)S(1)}, bf16[64,4096]{1,0:T(8,128)(2,1)S(1)}, u32[]{:S(2)}, u32[]{:S(2)}) collective-permute-start(bf16[64,4096]{1,0:T(8,128)(2,1)S(1)} %convert_element_type.55), channel_id=1, source_target_pairs={{0,12},{4,8},{8,20},{12,16},{16,28},{20,24},{24,4},{28,0},{1,13},{... | collective-permute-start | bytes 1572872 | tf_op jit(solution)/shard_map/ppermute | solution.py:135
  37.6 2.7 %collective-permute-done.2 = bf16[64,4096]{1,0:T(8,128)(2,1)} collective-permute-done((bf16[64,4096]{1,0:T(8,128)(2,1)S(1)}, bf16[64,4096]{1,0:T(8,128)(2,1)}, u32[]{:S(2)}, u32[]{:S(2)}) %collective-permute-start.2) | collective-permute-done | bytes 524320 | tf_op jit(solution)/shard_map/ppermute | solution.py:26
  40.2 14.0 %collective-permute-done.5 = bf16[64,4096]{1,0:T(8,128)(2,1)S(1)} collective-permute-done((bf16[64,4096]{1,0:T(8,128)(2,1)S(1)}, bf16[64,4096]{1,0:T(8,128)(2,1)S(1)}, u32[]{:S(2)}, u32[]{:S(2)}) %collective-permute-start.5) | collective-permute-done | bytes 524320 | tf_op jit(solution)/shard_map/ppermute | solution.py:135
  54.2 2.1 %maximum_bitcast_fusion = bf16[1,2,64,4096]{3,2,1,0:T(8,128)(2,1)} fusion(bf16[1,64,4096]{2,1,0:T(8,128)(2,1)S(1)} %bitcast.86, bf16[1,64,4096]{2,1,0:T(8,128)(2,1)} %bitcast.10), kind=kLoop, calls=%fused_computation.22 | loop fusion | flops 524288 | bytes 2097152 | tf_op jit(solution)/shard_map/reshape | solution.py:137
  (10 shorter events, 0.2 us)
Async XLA Ops:
  0.0 0.7 %copy-start = (s32[1,2]{1,0:T(1,128)S(1)}, s32[1,2]{1,0:T(1,128)}, u32[]{:S(2)}) copy-start(s32[1,2]{1,0:T(1,128)} %param.7) | copy-start | bytes 28
  0.0 8.8 %copy-start.2 = (s32[1,4,8]{2,1,0:T(4,128)S(1)}, s32[1,4,8]{2,1,0:T(4,128)}, u32[]{:S(2)}) copy-start(s32[1,4,8]{2,1,0:T(4,128)} %param.6) | copy-start | bytes 388
  0.0 9.1 %copy-start.1 = (s32[1,4]{1,0:T(1,128)S(1)}, s32[1,4]{1,0:T(1,128)}, u32[]{:S(2)}) copy-start(s32[1,4]{1,0:T(1,128)} %param.5) | copy-start | bytes 52
  6.0 8.1 %collective-permute-start = (bf16[64,2048]{1,0:T(8,128)(2,1)S(1)}, bf16[64,2048]{1,0:T(8,128)(2,1)S(1)}, u32[]{:S(2)}, u32[]{:S(2)}) collective-permute-start(bf16[64,2048]{1,0:T(8,128)(2,1)S(1)} %slice.32), channel_id=1, source_target_pairs={{0,2},{1,3},{2,0},{3,1},{4,6},{5,7},{6,4},{7,5},{8,10},{9,11},{10,... | collective-permute-start | bytes 786440 | tf_op jit(solution)/shard_map/ppermute | solution.py:60
  14.2 6.7 %collective-permute-start.1 = (bf16[64,2048]{1,0:T(8,128)(2,1)S(1)}, bf16[64,2048]{1,0:T(8,128)(2,1)S(1)}, u32[]{:S(2)}, u32[]{:S(2)}) collective-permute-start(bf16[64,2048]{1,0:T(8,128)(2,1)S(1)} %broadcast_select_fusion.1), channel_id=1, source_target_pairs={{0,1},{1,0},{2,3},{3,2},{4,5},{5,4},{6,7},{7,6},{8,9},{9,8},{10,11... | collective-permute-start | bytes 786440 | tf_op jit(solution)/shard_map/ppermute | solution.py:63
  17.3 6.1 %collective-permute-start.3 = (bf16[64,2048]{1,0:T(8,128)(2,1)S(1)}, bf16[64,2048]{1,0:T(8,128)(2,1)S(1)}, u32[]{:S(2)}, u32[]{:S(2)}) collective-permute-start(bf16[64,2048]{1,0:T(8,128)(2,1)S(1)} %slice.36), channel_id=1, source_target_pairs={{0,2},{1,3},{2,0},{3,1},{4,6},{5,7},{6,4},{7,5},{8,10},{9,11},{10,... | collective-permute-start | bytes 786440 | tf_op jit(solution)/shard_map/ppermute | solution.py:60
  24.1 5.4 %collective-permute-start.4 = (bf16[64,2048]{1,0:T(8,128)(2,1)}, bf16[64,2048]{1,0:T(8,128)(2,1)S(1)}, u32[]{:S(2)}, u32[]{:S(2)}) collective-permute-start(bf16[64,2048]{1,0:T(8,128)(2,1)} %get-tuple-element.19), channel_id=1, source_target_pairs={{0,1},{1,0},{2,3},{3,2},{4,5},{5,4},{6,7},{7,6},{8,9},{9,8},{10,11... | collective-permute-start | bytes 786440 | tf_op jit(solution)/shard_map/ppermute | solution.py:63
  27.4 12.8 %collective-permute-start.2 = (bf16[64,4096]{1,0:T(8,128)(2,1)S(1)}, bf16[64,4096]{1,0:T(8,128)(2,1)}, u32[]{:S(2)}, u32[]{:S(2)}) collective-permute-start(bf16[64,4096]{1,0:T(8,128)(2,1)S(1)} %convert_element_type.49), channel_id=1, source_target_pairs={{0,8},{8,16},{16,24},{24,0},{1,9},{9,17},{17,25},{25,1},{2,10},{10... | collective-permute-start | bytes 1572872 | tf_op jit(solution)/shard_map/ppermute | solution.py:26
  32.5 21.7 %collective-permute-start.5 = (bf16[64,4096]{1,0:T(8,128)(2,1)S(1)}, bf16[64,4096]{1,0:T(8,128)(2,1)S(1)}, u32[]{:S(2)}, u32[]{:S(2)}) collective-permute-start(bf16[64,4096]{1,0:T(8,128)(2,1)S(1)} %convert_element_type.55), channel_id=1, source_target_pairs={{0,12},{4,8},{8,20},{12,16},{16,28},{20,24},{24,4},{28,0},{1,13},{... | collective-permute-start | bytes 1572872 | tf_op jit(solution)/shard_map/ppermute | solution.py:135

commit v6 on v5

--- a/solution.py
+++ b/solution.py
@@ -77,7 +77,6 @@
     seq_index = lax.axis_index("seq")
     replica = lax.axis_index("dp")
     partner = jnp.bitwise_xor(replica, 1)
-    handed = lax.dynamic_index_in_dim(hand_over[0], replica, 0, keepdims=False)
     own_rows = qkv[0]
     seg_len = own_rows.shape[1]
     length_all = seg_len * seq_count
@@ -88,11 +87,6 @@
     query_pos = seq_index * seg_len + local
     key_value_width = KV_HEADS * HD
     far = jnp.int32(4 * length_all)
-
-    def prepare(own_index):
-        row = lax.dynamic_index_in_dim(own_rows, own_index, 0, keepdims=False)
-        kv_local = row[:, D:]
-        return row, kv_local
 
     def attend_own(row, kv_local, pieces_and_chunks, own_index):
         pieces = [kv_local]
@@ -115,24 +109,26 @@
             length,
         )
 
-    kept_row, kept_kv = prepare(1 - handed)
-    given_row, given_kv = prepare(handed)
-    kept_pieces = gathered(kept_kv, seq_index, seq_count, reach)
-    given_kv = lax.optimization_barrier((given_kv, kept_pieces[0][0]))[0]
-    given_pieces = gathered(given_kv, seq_index, seq_count, reach)
-    kept_out = attend_own(kept_row, kept_kv, kept_pieces, 1 - handed)
-    sent = [passed_along(kept_out, "section", 1)]
-    given_row = lax.optimization_barrier((given_row, kept_out))[0]
-    given_out = attend_own(given_row, given_kv, given_pieces, handed)
-    sections = lax.axis_size("section")
-    replicas = lax.axis_size("dp")
-    pairs = []
-    for section in range(sections):
-        for rep in range(replicas):
-            pairs.append(
-                (section * replicas + rep, (section + 1) % sections * replicas + (rep ^ 1))
-            )
-    sent.append(lax.ppermute(given_out, ("section", "dp"), pairs))
+    first_row, second_row = own_rows[0], own_rows[1]
+    first_kv = first_row[:, D:]
+    first_pieces = gathered(first_kv, seq_index, seq_count, reach)
+    second_kv = lax.optimization_barrier((second_row[:, D:], first_pieces[0][0]))[0]
+    second_pieces = gathered(second_kv, seq_index, seq_count, reach)
+    first_out = attend_own(first_row, first_kv, first_pieces, 0)
+    first_next = passed_along(first_out, "section", 1)
+    second_row = lax.optimization_barrier((second_row, first_out))[0]
+    second_out = attend_own(second_row, second_kv, second_pieces, 1)
+    second_next = passed_along(second_out, "section", 1)
+
+    previous_hand = passed_along(hand_over[0], "section", 1)
+    own_hand = lax.dynamic_index_in_dim(previous_hand, replica, 0, keepdims=False)
+    partner_hand = lax.dynamic_index_in_dim(previous_hand, partner, 0, keepdims=False)
+    partner_first = swapped(first_next, "dp", 0)
+    partner_second = swapped(second_next, "dp", 0)
+    sent = [
+        jnp.where(own_hand == 1, first_next, second_next),
+        jnp.where(partner_hand == 0, partner_first, partner_second),
+    ]
     out = jnp.stack(sent, axis=0)
     return out.reshape(1, RPR, seg_len, D)
 

time: 56.6 us -> 56.9 us (level)
  the two profiles are of different devices: /device:TPU:1 before, /device:TPU:0 now
where the time goes in v6:
time: 56.9 us; the launch traced here: 56.7 us
  waiting for transfers between devices  28.1 us (49%)
  starting transfers between devices  12.3 us (22%)
  local copies, waits for them, and re-layouts  6.58 us (12%)
  other arithmetic  6.46 us (11%)
  matrix products  1.84 us (3%)
  between operations  1.44 us (3%)
    ppermute x3, waiting for transfers between devices, passed_along(): return lax.ppermute(value, axis, pairs)  14.4 us
    ppermute x2, waiting for transfers between devices, gathered(): over_y = lax.ppermute(block, 'seq', [(j, j ^ 2) for j in range(4)])  7.7 us
    ppermute x3, starting transfers between devices, passed_along(): return lax.ppermute(value, axis, pairs)  4.77 us
    ppermute x2, starting transfers between devices, gathered(): over_y = lax.ppermute(block, 'seq', [(j, j ^ 2) for j in range(4)])  4.65 us
    ppermute x2, waiting for transfers between devices, gathered(): over_x = lax.ppermute(onward, 'seq', [(j, j ^ 1) for j in range(4)])  3.97 us
    ppermute x2, starting transfers between devices, gathered(): over_x = lax.ppermute(onward, 'seq', [(j, j ^ 1) for j in range(4)])  2.31 us
    ppermute x2, waiting for transfers between devices, swapped(): return lax.ppermute(block, axis, route)  2.09 us
    sub x2, other arithmetic, attend_row(): weights = jnp.where(allowed, jnp.exp(scores - row_top), 0.0)  1.94 us
  transfers between devices with their start and end apart: 9, of which 7 were waited for; matrix products, arithmetic and copies ran while one was open for 19% of the time, Pallas kernels for 0%

profile of v6, /device:TPU:0, one launch (start us, length us, event | category | flops | bytes accessed | tf_op | source)
XLA Modules:
  0.0 56.7 jit_solution(6156514971155660080)
XLA Ops:
  0.0 1.5 %slice_bitcast_fusion = (bf16[64,6144]{1,0:T(8,128)(2,1)S(1)}, bf16[64,6144]{1,0:T(8,128)(2,1)S(1)}) fusion(bf16[1,2,64,6144]{3,2,1,0:T(8,128)(2,1)} %param.4), kind=kLoop, calls=%fused_computation.32 | loop fusion | bytes 3145728 | tf_op jit(solution)/shard_map/squeeze | solution.py:112
  1.6 3.1 %collective-permute-start.1 = (bf16[64,2048]{1,0:T(8,128)(2,1)S(1)}, bf16[64,2048]{1,0:T(8,128)(2,1)S(1)}, u32[]{:S(2)}, u32[]{:S(2)}) collective-permute-start(bf16[64,2048]{1,0:T(8,128)(2,1)S(1)} %slice.42), channel_id=1, source_target_pairs={{0,2},{1,3},{2,0},{3,1},{4,6},{5,7},{6,4},{7,5},{8,10},{9,11},{10,... | collective-permute-start | bytes 786440 | tf_op jit(solution)/shard_map/ppermute | solution.py:60
  4.6 0.2 reduce_window_sum.11
  4.8 0.1 pad_add_fusion
  4.9 0.7 %constant_dynamic-slice_fusion = (s32[1,1]{1,0:T(1,128)}, s32[1,1]{1,0:T(1,128)}) fusion(s32[1,4]{1,0:T(1,128)S(1)} %copy-done, s32[]{:T(128)S(6)} %select_n.101, s32[]{:T(128)S(6)} %select_n.97), kind=kLoop, calls=%fused_computation.62 | loop fusion | bytes 24 | tf_op jit(solution)/shard_map/jit(dynamic_index_in_dim)/dynamic_slice | solution.py:101
  5.6 0.1 convert_reduce_fusion.2
  5.7 0.1 convert_reduce_fusion
  5.7 5.2 %collective-permute-done.1 = bf16[64,2048]{1,0:T(8,128)(2,1)S(1)} collective-permute-done((bf16[64,2048]{1,0:T(8,128)(2,1)S(1)}, bf16[64,2048]{1,0:T(8,128)(2,1)S(1)}, u32[]{:S(2)}, u32[]{:S(2)}) %collective-permute-start.1) | collective-permute-done | bytes 262176 | tf_op jit(solution)/shard_map/ppermute | solution.py:60
  10.9 0.7 %broadcast_select_fusion.1 = bf16[64,2048]{1,0:T(8,128)(2,1)} fusion(bf16[64,2048]{1,0:T(8,128)(2,1)S(1)} %collective-permute-done.1, pred[]{:T(512)S(6)} %eq.47, bf16[64,6144]{1,0:T(8,128)(2,1)S(1)} %get-tuple-element.14), kind=kLoop, calls=%fused_computation.49 | loop fusion | flops 131072 | bytes 786433 | tf_op jit(solution)/shard_map/jit(_where)/select_n | solution.py:62
  11.7 1.7 %collective-permute-start.2 = (bf16[64,2048]{1,0:T(8,128)(2,1)}, bf16[64,2048]{1,0:T(8,128)(2,1)S(1)}, u32[]{:S(2)}, u32[]{:S(2)}) collective-permute-start(bf16[64,2048]{1,0:T(8,128)(2,1)} %broadcast_select_fusion.1), channel_id=1, source_target_pairs={{0,1},{1,0},{2,3},{3,2},{4,5},{5,4},{6,7},{7,6},{8,9},{9,8},{10,11... | collective-permute-start | bytes 786440 | tf_op jit(solution)/shard_map/ppermute | solution.py:63
  13.4 1.2 %compare_convert_fusion = (f32[64]{0:T(128)S(1)}, f32[64]{0:T(128)S(1)}) fusion(s32[]{:T(128)} %bitcast.18, s32[]{:T(128)S(6)} %mul.43, s32[]{:T(128)} %bitcast.10), kind=kLoop, calls=%fused_computation.59 | loop fusion | flops 320 | bytes 524 | tf_op jit(solution)/shard_map/convert_element_type | solution.py:53
  14.7 0.4 reshape.63
  15.1 0.1 compare_and_fusion
  15.2 1.6 %collective-permute-start.4 = (bf16[64,2048]{1,0:T(8,128)(2,1)S(1)}, bf16[64,2048]{1,0:T(8,128)(2,1)S(1)}, u32[]{:S(2)}, u32[]{:S(2)}) collective-permute-start(bf16[64,2048]{1,0:T(8,128)(2,1)S(1)} %slice.46), channel_id=1, source_target_pairs={{0,2},{1,3},{2,0},{3,1},{4,6},{5,7},{6,4},{7,5},{8,10},{9,11},{10,... | collective-permute-start | bytes 786440 | tf_op jit(solution)/shard_map/ppermute | solution.py:60
  16.8 2.6 %collective-permute-done.2 = bf16[64,2048]{1,0:T(8,128)(2,1)S(1)} collective-permute-done((bf16[64,2048]{1,0:T(8,128)(2,1)}, bf16[64,2048]{1,0:T(8,128)(2,1)S(1)}, u32[]{:S(2)}, u32[]{:S(2)}) %collective-permute-start.2) | collective-permute-done | bytes 262176 | tf_op jit(solution)/shard_map/ppermute | solution.py:63
  19.3 0.1 pad_maximum_fusion
  19.4 0.1 slice_bitcast_fusion.5
  19.5 0.1 copy.34
  19.5 0.1 copy.33
  19.6 2.5 %collective-permute-done.4 = bf16[64,2048]{1,0:T(8,128)(2,1)S(1)} collective-permute-done((bf16[64,2048]{1,0:T(8,128)(2,1)S(1)}, bf16[64,2048]{1,0:T(8,128)(2,1)S(1)}, u32[]{:S(2)}, u32[]{:S(2)}) %collective-permute-start.4) | collective-permute-done | bytes 262176 | tf_op jit(solution)/shard_map/ppermute | solution.py:60
  22.1 0.8 %broadcast_select_fusion = (bf16[64,2048]{1,0:T(8,128)(2,1)}, bf16[192,2048]{1,0:T(8,128)(2,1)S(1)}) fusion(bf16[64,2048]{1,0:T(8,128)(2,1)S(1)} %collective-permute-done.4, bf16[64,2048]{1,0:T(8,128)(2,1)S(1)} %slice.46, pred[]{:T(512)S(6)} %eq.47), kind=kLoop, calls=%fused_computation.48 | loop fusion | flops 131071 | bytes 1048577 | tf_op jit(solution)/shard_map/jit(_where)/select_n | solution.py:62
  22.9 0.6 %collective-permute-start.5 = (bf16[64,2048]{1,0:T(8,128)(2,1)}, bf16[64,2048]{1,0:T(8,128)(2,1)}, u32[]{:S(2)}, u32[]{:S(2)}) collective-permute-start(bf16[64,2048]{1,0:T(8,128)(2,1)} %get-tuple-element.19), channel_id=1, source_target_pairs={{0,1},{1,0},{2,3},{3,2},{4,5},{5,4},{6,7},{7,6},{8,9},{9,8},{10,11... | collective-permute-start | bytes 786440 | tf_op jit(solution)/shard_map/ppermute | solution.py:63
  23.5 0.5 fusion.26
  24.0 1.0 %fusion.39 = (f32[8,4,64]{2,1,0:T(4,128)S(1)}, bf16[8,4,64,192]{3,2,1,0:T(8,128)(2,1)S(1)}) fusion(f32[8,192,64,4]{1,2,3,0:T(8,128)S(1)} %fusion.26, pred[64,192]{1,0:T(8,128)(4,1)S(1)} %get-tuple-element.24), kind=kOutput, calls=%fused_computation.76 | output fusion | flops 2752703 | bytes 2379776 | tf_op jit(solution)/shard_map/sub | solution.py:48
  24.9 0.5 fusion.14
  25.4 0.4 copy.16
  25.8 0.4 convert_element_type.49
  26.2 1.6 %collective-permute-start.3 = (bf16[64,4096]{1,0:T(8,128)(2,1)S(1)}, bf16[64,4096]{1,0:T(8,128)(2,1)S(1)}, u32[]{:S(2)}, u32[]{:S(2)}) collective-permute-start(bf16[64,4096]{1,0:T(8,128)(2,1)S(1)} %convert_element_type.49), channel_id=1, source_target_pairs={{0,8},{8,16},{16,24},{24,0},{1,9},{9,17},{17,25},{25,1},{2,10},{10... | collective-permute-start | bytes 1572872 | tf_op jit(solution)/shard_map/ppermute | solution.py:26
  27.8 0.4 reshape.66
  28.2 1.4 %collective-permute-done.5 = bf16[64,2048]{1,0:T(8,128)(2,1)} collective-permute-done((bf16[64,2048]{1,0:T(8,128)(2,1)}, bf16[64,2048]{1,0:T(8,128)(2,1)}, u32[]{:S(2)}, u32[]{:S(2)}) %collective-permute-start.5) | collective-permute-done | bytes 262176 | tf_op jit(solution)/shard_map/ppermute | solution.py:63
  29.6 1.0 %constant_dynamic-update-slice_fusion = bf16[192,2048]{1,0:T(8,128)(2,1)S(1)} fusion(bf16[192,2048]{1,0:T(8,128)(2,1)S(1)} %constant_dynamic-update-slice_fusion.1, bf16[64,2048]{1,0:T(8,128)(2,1)} %collective-permute-done.5), kind=kLoop, calls=%fused_computation.52 | loop fusion | bytes 524288 | tf_op jit(solution)/shard_map/concatenate | solution.py:97
  30.6 0.1 copy.36
  30.7 0.1 copy.35
  30.8 0.5 fusion.24
  31.2 1.0 %fusion.40 = (f32[8,4,64]{2,1,0:T(4,128)S(1)}, bf16[8,4,64,192]{3,2,1,0:T(8,128)(2,1)S(1)}) fusion(f32[8,192,64,4]{1,2,3,0:T(8,128)S(1)} %fusion.24, pred[64,192]{1,0:T(8,128)(4,1)S(1)} %get-tuple-element.23), kind=kOutput, calls=%fused_computation.77 | output fusion | flops 2752703 | bytes 2379776 | tf_op jit(solution)/shard_map/sub | solution.py:48
  32.2 0.5 fusion.15
  32.7 0.4 copy.20
  33.1 0.4 convert_element_type.55
  33.5 1.6 %collective-permute-start.6 = (bf16[64,4096]{1,0:T(8,128)(2,1)S(1)}, bf16[64,4096]{1,0:T(8,128)(2,1)S(1)}, u32[]{:S(2)}, u32[]{:S(2)}) collective-permute-start(bf16[64,4096]{1,0:T(8,128)(2,1)S(1)} %convert_element_type.55), channel_id=1, source_target_pairs={{0,8},{8,16},{16,24},{24,0},{1,9},{9,17},{17,25},{25,1},{2,10},{10... | collective-permute-start | bytes 1572872 | tf_op jit(solution)/shard_map/ppermute | solution.py:26
  35.1 1.6 %collective-permute-start = (s32[2]{0:T(128)S(1)}, s32[2]{0:T(128)S(1)}, u32[]{:S(2)}, u32[]{:S(2)}) collective-permute-start(s32[2]{0:T(128)S(1)} %bitcast.93), channel_id=1, source_target_pairs={{0,8},{8,16},{16,24},{24,0},{1,9},{9,17},{17,25},{25,1},{2,10},{10... | collective-permute-start | bytes 32 | tf_op jit(solution)/shard_map/ppermute | solution.py:26
  36.7 14.4 %collective-permute-done = s32[2]{0:T(128)S(1)} collective-permute-done((s32[2]{0:T(128)S(1)}, s32[2]{0:T(128)S(1)}, u32[]{:S(2)}, u32[]{:S(2)}) %collective-permute-start) | collective-permute-done | bytes 40 | tf_op jit(solution)/shard_map/ppermute | solution.py:26
  51.1 0.6 %fusion.38 = (s32[1]{0:T(128)}, s32[1]{0:T(128)}) fusion(s32[2]{0:T(128)S(1)} %collective-permute-done, s32[]{:T(128)S(6)} %select_n.87, s32[]{:T(128)S(6)} %select_n.105), kind=kLoop, calls=%fused_computation.75 | loop fusion | bytes 24 | tf_op jit(solution)/shard_map/jit(dynamic_index_in_dim)/dynamic_slice | solution.py:124
  52.9 0.1 collective-permute-start.7
  53.0 0.5 collective-permute-start.8
  53.5 0.1 select_bitcast_fusion.1
  53.5 1.3 %collective-permute-done.7 = bf16[64,4096]{1,0:T(8,128)(2,1)S(1)} collective-permute-done((bf16[64,4096]{1,0:T(8,128)(2,1)S(1)}, bf16[64,4096]{1,0:T(8,128)(2,1)S(1)}, u32[]{:S(2)}, u32[]{:S(2)}) %collective-permute-start.7) | collective-permute-done | bytes 524320 | tf_op jit(solution)/shard_map/ppermute | solution.py:20
  54.9 0.7 %collective-permute-done.8 = bf16[64,4096]{1,0:T(8,128)(2,1)S(1)} collective-permute-done((bf16[64,4096]{1,0:T(8,128)(2,1)S(1)}, bf16[64,4096]{1,0:T(8,128)(2,1)S(1)}, u32[]{:S(2)}, u32[]{:S(2)}) %collective-permute-start.8) | collective-permute-done | bytes 524320 | tf_op jit(solution)/shard_map/ppermute | solution.py:20
  55.7 1.1 %maximum_bitcast_fusion = bf16[1,2,64,4096]{3,2,1,0:T(8,128)(2,1)} fusion(bf16[1,64,4096]{2,1,0:T(8,128)(2,1)S(1)} %select_bitcast_fusion, bf16[1,64,4096]{2,1,0:T(8,128)(2,1)S(1)} %select_bitcast_fusion.1), kind=kLoop, calls=%fused_computation.22 | loop fusion | flops 524288 | bytes 2097152 | tf_op jit(solution)/shard_map/reshape | solution.py:133
  (18 shorter events, 0.3 us)
Async XLA Ops:
  0.0 4.6 %copy-start.1 = (s32[1,4,8]{2,1,0:T(4,128)S(1)}, s32[1,4,8]{2,1,0:T(4,128)}, u32[]{:S(2)}) copy-start(s32[1,4,8]{2,1,0:T(4,128)} %param.6) | copy-start | bytes 388
  0.0 4.9 %copy-start = (s32[1,4]{1,0:T(1,128)S(1)}, s32[1,4]{1,0:T(1,128)}, u32[]{:S(2)}) copy-start(s32[1,4]{1,0:T(1,128)} %param.5) | copy-start | bytes 52
  1.6 9.4 %collective-permute-start.1 = (bf16[64,2048]{1,0:T(8,128)(2,1)S(1)}, bf16[64,2048]{1,0:T(8,128)(2,1)S(1)}, u32[]{:S(2)}, u32[]{:S(2)}) collective-permute-start(bf16[64,2048]{1,0:T(8,128)(2,1)S(1)} %slice.42), channel_id=1, source_target_pairs={{0,2},{1,3},{2,0},{3,1},{4,6},{5,7},{6,4},{7,5},{8,10},{9,11},{10,... | collective-permute-start | bytes 786440 | tf_op jit(solution)/shard_map/ppermute | solution.py:60
  11.7 7.7 %collective-permute-start.2 = (bf16[64,2048]{1,0:T(8,128)(2,1)}, bf16[64,2048]{1,0:T(8,128)(2,1)S(1)}, u32[]{:S(2)}, u32[]{:S(2)}) collective-permute-start(bf16[64,2048]{1,0:T(8,128)(2,1)} %broadcast_select_fusion.1), channel_id=1, source_target_pairs={{0,1},{1,0},{2,3},{3,2},{4,5},{5,4},{6,7},{7,6},{8,9},{9,8},{10,11... | collective-permute-start | bytes 786440 | tf_op jit(solution)/shard_map/ppermute | solution.py:63
  15.2 7.0 %collective-permute-start.4 = (bf16[64,2048]{1,0:T(8,128)(2,1)S(1)}, bf16[64,2048]{1,0:T(8,128)(2,1)S(1)}, u32[]{:S(2)}, u32[]{:S(2)}) collective-permute-start(bf16[64,2048]{1,0:T(8,128)(2,1)S(1)} %slice.46), channel_id=1, source_target_pairs={{0,2},{1,3},{2,0},{3,1},{4,6},{5,7},{6,4},{7,5},{8,10},{9,11},{10,... | collective-permute-start | bytes 786440 | tf_op jit(solution)/shard_map/ppermute | solution.py:60
  22.9 6.7 %collective-permute-start.5 = (bf16[64,2048]{1,0:T(8,128)(2,1)}, bf16[64,2048]{1,0:T(8,128)(2,1)}, u32[]{:S(2)}, u32[]{:S(2)}) collective-permute-start(bf16[64,2048]{1,0:T(8,128)(2,1)} %get-tuple-element.19), channel_id=1, source_target_pairs={{0,1},{1,0},{2,3},{3,2},{4,5},{5,4},{6,7},{7,6},{8,9},{9,8},{10,11... | collective-permute-start | bytes 786440 | tf_op jit(solution)/shard_map/ppermute | solution.py:63
  26.2 26.7 %collective-permute-start.3 = (bf16[64,4096]{1,0:T(8,128)(2,1)S(1)}, bf16[64,4096]{1,0:T(8,128)(2,1)S(1)}, u32[]{:S(2)}, u32[]{:S(2)}) collective-permute-start(bf16[64,4096]{1,0:T(8,128)(2,1)S(1)} %convert_element_type.49), channel_id=1, source_target_pairs={{0,8},{8,16},{16,24},{24,0},{1,9},{9,17},{17,25},{25,1},{2,10},{10... | collective-permute-start | bytes 1572872 | tf_op jit(solution)/shard_map/ppermute | solution.py:26
  32.7 2.5 %copy-start.2 = (s32[1,2]{1,0:T(1,128)S(1)}, s32[1,2]{1,0:T(1,128)}, u32[]{:S(2)}) copy-start(s32[1,2]{1,0:T(1,128)} %param.7) | copy-start | bytes 28
  33.5 19.5 %collective-permute-start.6 = (bf16[64,4096]{1,0:T(8,128)(2,1)S(1)}, bf16[64,4096]{1,0:T(8,128)(2,1)S(1)}, u32[]{:S(2)}, u32[]{:S(2)}) collective-permute-start(bf16[64,4096]{1,0:T(8,128)(2,1)S(1)} %convert_element_type.55), channel_id=1, source_target_pairs={{0,8},{8,16},{16,24},{24,0},{1,9},{9,17},{17,25},{25,1},{2,10},{10... | collective-permute-start | bytes 1572872 | tf_op jit(solution)/shard_map/ppermute | solution.py:26
  35.1 15.9 %collective-permute-start = (s32[2]{0:T(128)S(1)}, s32[2]{0:T(128)S(1)}, u32[]{:S(2)}, u32[]{:S(2)}) collective-permute-start(s32[2]{0:T(128)S(1)} %bitcast.93), channel_id=1, source_target_pairs={{0,8},{8,16},{16,24},{24,0},{1,9},{9,17},{17,25},{25,1},{2,10},{10... | collective-permute-start | bytes 32 | tf_op jit(solution)/shard_map/ppermute | solution.py:26
  52.9 2.0 %collective-permute-start.7 = (bf16[64,4096]{1,0:T(8,128)(2,1)S(1)}, bf16[64,4096]{1,0:T(8,128)(2,1)S(1)}, u32[]{:S(2)}, u32[]{:S(2)}) collective-permute-start(bf16[64,4096]{1,0:T(8,128)(2,1)S(1)} %collective-permute-done.3), channel_id=1, source_target_pairs={{0,4},{4,0},{1,5},{5,1},{2,6},{6,2},{3,7},{7,3},{8,12},{12,8},{9,1... | collective-permute-start | bytes 1572872 | tf_op jit(solution)/shard_map/ppermute | solution.py:20
  53.0 2.6 %collective-permute-start.8 = (bf16[64,4096]{1,0:T(8,128)(2,1)S(1)}, bf16[64,4096]{1,0:T(8,128)(2,1)S(1)}, u32[]{:S(2)}, u32[]{:S(2)}) collective-permute-start(bf16[64,4096]{1,0:T(8,128)(2,1)S(1)} %collective-permute-done.6), channel_id=1, source_target_pairs={{0,4},{4,0},{1,5},{5,1},{2,6},{6,2},{3,7},{7,3},{8,12},{12,8},{9,1... | collective-permute-start | bytes 1572872 | tf_op jit(solution)/shard_map/ppermute | solution.py:20

commit v7 on v6

--- a/solution.py
+++ b/solution.py
@@ -116,11 +116,11 @@
     second_pieces = gathered(second_kv, seq_index, seq_count, reach)
     first_out = attend_own(first_row, first_kv, first_pieces, 0)
     first_next = passed_along(first_out, "section", 1)
-    second_row = lax.optimization_barrier((second_row, first_out))[0]
+    previous_hand = passed_along(hand_over[0], "section", 1)
+    second_row, _, previous_hand = lax.optimization_barrier((second_row, first_out, previous_hand))
     second_out = attend_own(second_row, second_kv, second_pieces, 1)
     second_next = passed_along(second_out, "section", 1)
 
-    previous_hand = passed_along(hand_over[0], "section", 1)
     own_hand = lax.dynamic_index_in_dim(previous_hand, replica, 0, keepdims=False)
     partner_hand = lax.dynamic_index_in_dim(previous_hand, partner, 0, keepdims=False)
     partner_first = swapped(first_next, "dp", 0)

time: 56.9 us -> 54.2 us (0.953)
  waiting for transfers between devices: 28.1 us -> 26 us
  starting transfers between devices: 12.3 us -> 11.7 us
    ppermute x2, waiting for transfers between devices: 7.7 us -> 6.12 us  [gathered(): over_y = lax.ppermute(block, 'seq', [(j, j ^ 2) for j in range(4)])]
  transfers between devices with their start and end apart: 9 -> 9, of which waited for: 7 -> 7; matrix products, arithmetic and copies ran while one was open for 19% -> 23% of each run, Pallas kernels for 0% -> 0%
where the time goes in v7:
time: 54.2 us; the launch traced here: 54 us
  waiting for transfers between devices  26 us (48%)
  starting transfers between devices  11.7 us (22%)
  local copies, waits for them, and re-layouts  6.59 us (12%)
  other arithmetic  6.46 us (12%)
  matrix products  1.84 us (3%)
  between operations  1.42 us (3%)
    ppermute x3, waiting for transfers between devices, passed_along(): return lax.ppermute(value, axis, pairs)  14.1 us
    ppermute x2, waiting for transfers between devices, gathered(): over_y = lax.ppermute(block, 'seq', [(j, j ^ 2) for j in range(4)])  6.12 us
    ppermute x3, starting transfers between devices, passed_along(): return lax.ppermute(value, axis, pairs)  4.77 us
    ppermute x2, starting transfers between devices, gathered(): over_y = lax.ppermute(block, 'seq', [(j, j ^ 2) for j in range(4)])  4.65 us
    ppermute x2, waiting for transfers between devices, gathered(): over_x = lax.ppermute(onward, 'seq', [(j, j ^ 1) for j in range(4)])  3.96 us
    ppermute x2, starting transfers between devices, gathered(): over_x = lax.ppermute(onward, 'seq', [(j, j ^ 1) for j in range(4)])  2.31 us
    sub x2, other arithmetic, attend_row(): weights = jnp.where(allowed, jnp.exp(scores - row_top), 0.0)  1.94 us
    ppermute x2, waiting for transfers between devices, swapped(): return lax.ppermute(block, axis, route)  1.84 us
  transfers between devices with their start and end apart: 9, of which 7 were waited for; matrix products, arithmetic and copies ran while one was open for 23% of the time, Pallas kernels for 0%

profile of v7, /device:TPU:0, one launch (start us, length us, event | category | flops | bytes accessed | tf_op | source)
XLA Modules:
  0.0 54.0 jit_solution(12755469350202748567)
XLA Ops:
  0.0 1.5 %slice_bitcast_fusion.1 = (bf16[64,6144]{1,0:T(8,128)(2,1)S(1)}, bf16[64,6144]{1,0:T(8,128)(2,1)S(1)}) fusion(bf16[1,2,64,6144]{3,2,1,0:T(8,128)(2,1)} %param.4), kind=kLoop, calls=%fused_computation.33 | loop fusion | bytes 3145728 | tf_op jit(solution)/shard_map/squeeze | solution.py:112
  1.6 3.1 %collective-permute-start = (bf16[64,2048]{1,0:T(8,128)(2,1)S(1)}, bf16[64,2048]{1,0:T(8,128)(2,1)S(1)}, u32[]{:S(2)}, u32[]{:S(2)}) collective-permute-start(bf16[64,2048]{1,0:T(8,128)(2,1)S(1)} %slice.42), channel_id=1, source_target_pairs={{0,2},{1,3},{2,0},{3,1},{4,6},{5,7},{6,4},{7,5},{8,10},{9,11},{10,... | collective-permute-start | bytes 786440 | tf_op jit(solution)/shard_map/ppermute | solution.py:60
  4.6 1.6 %collective-permute-start.2 = (s32[2]{0:T(128)S(1)}, s32[2]{0:T(128)S(1)}, u32[]{:S(2)}, u32[]{:S(2)}) collective-permute-start(s32[2]{0:T(128)S(1)} %bitcast.93), channel_id=1, source_target_pairs={{0,8},{8,16},{16,24},{24,0},{1,9},{9,17},{17,25},{25,1},{2,10},{10... | collective-permute-start | bytes 32 | tf_op jit(solution)/shard_map/ppermute | solution.py:26
  6.2 0.2 reduce_window_sum.11
  6.4 0.1 pad_add_fusion
  6.5 0.7 %constant_dynamic-slice_fusion = (s32[1,1]{1,0:T(1,128)}, s32[1,1]{1,0:T(1,128)}) fusion(s32[1,4]{1,0:T(1,128)S(1)} %copy-done, s32[]{:T(128)S(6)} %select_n.101, s32[]{:T(128)S(6)} %select_n.95), kind=kLoop, calls=%fused_computation.62 | loop fusion | bytes 24 | tf_op jit(solution)/shard_map/jit(dynamic_index_in_dim)/dynamic_slice | solution.py:101
  7.2 0.1 convert_reduce_fusion.2
  7.3 0.1 convert_reduce_fusion
  7.3 3.6 %collective-permute-done = bf16[64,2048]{1,0:T(8,128)(2,1)S(1)} collective-permute-done((bf16[64,2048]{1,0:T(8,128)(2,1)S(1)}, bf16[64,2048]{1,0:T(8,128)(2,1)S(1)}, u32[]{:S(2)}, u32[]{:S(2)}) %collective-permute-start) | collective-permute-done | bytes 262176 | tf_op jit(solution)/shard_map/ppermute | solution.py:60
  10.9 0.7 %broadcast_select_fusion.1 = bf16[64,2048]{1,0:T(8,128)(2,1)} fusion(bf16[64,2048]{1,0:T(8,128)(2,1)S(1)} %collective-permute-done, pred[]{:T(512)S(6)} %eq.45, bf16[64,6144]{1,0:T(8,128)(2,1)S(1)} %get-tuple-element.16), kind=kLoop, calls=%fused_computation.49 | loop fusion | flops 131072 | bytes 786433 | tf_op jit(solution)/shard_map/jit(_where)/select_n | solution.py:62
  11.7 1.7 %collective-permute-start.1 = (bf16[64,2048]{1,0:T(8,128)(2,1)}, bf16[64,2048]{1,0:T(8,128)(2,1)S(1)}, u32[]{:S(2)}, u32[]{:S(2)}) collective-permute-start(bf16[64,2048]{1,0:T(8,128)(2,1)} %broadcast_select_fusion.1), channel_id=1, source_target_pairs={{0,1},{1,0},{2,3},{3,2},{4,5},{5,4},{6,7},{7,6},{8,9},{9,8},{10,11... | collective-permute-start | bytes 786440 | tf_op jit(solution)/shard_map/ppermute | solution.py:63
  13.4 1.2 %compare_convert_fusion = (f32[64]{0:T(128)S(1)}, f32[64]{0:T(128)S(1)}) fusion(s32[]{:T(128)} %bitcast.18, s32[]{:T(128)S(6)} %mul.43, s32[]{:T(128)} %bitcast.9), kind=kLoop, calls=%fused_computation.59 | loop fusion | flops 320 | bytes 524 | tf_op jit(solution)/shard_map/convert_element_type | solution.py:53
  14.7 0.4 reshape.63
  15.1 0.1 compare_and_fusion
  15.2 1.6 %collective-permute-start.4 = (bf16[64,2048]{1,0:T(8,128)(2,1)S(1)}, bf16[64,2048]{1,0:T(8,128)(2,1)S(1)}, u32[]{:S(2)}, u32[]{:S(2)}) collective-permute-start(bf16[64,2048]{1,0:T(8,128)(2,1)S(1)} %slice.46), channel_id=1, source_target_pairs={{0,2},{1,3},{2,0},{3,1},{4,6},{5,7},{6,4},{7,5},{8,10},{9,11},{10,... | collective-permute-start | bytes 786440 | tf_op jit(solution)/shard_map/ppermute | solution.py:60
  16.8 2.6 %collective-permute-done.1 = bf16[64,2048]{1,0:T(8,128)(2,1)S(1)} collective-permute-done((bf16[64,2048]{1,0:T(8,128)(2,1)}, bf16[64,2048]{1,0:T(8,128)(2,1)S(1)}, u32[]{:S(2)}, u32[]{:S(2)}) %collective-permute-start.1) | collective-permute-done | bytes 262176 | tf_op jit(solution)/shard_map/ppermute | solution.py:63
  19.4 0.1 pad_maximum_fusion
  19.4 0.1 slice_bitcast_fusion.5
  19.5 0.1 copy.34
  19.6 0.1 copy.33
  19.6 2.5 %collective-permute-done.4 = bf16[64,2048]{1,0:T(8,128)(2,1)S(1)} collective-permute-done((bf16[64,2048]{1,0:T(8,128)(2,1)S(1)}, bf16[64,2048]{1,0:T(8,128)(2,1)S(1)}, u32[]{:S(2)}, u32[]{:S(2)}) %collective-permute-start.4) | collective-permute-done | bytes 262176 | tf_op jit(solution)/shard_map/ppermute | solution.py:60
  22.2 0.8 %broadcast_select_fusion = (bf16[64,2048]{1,0:T(8,128)(2,1)}, bf16[192,2048]{1,0:T(8,128)(2,1)S(1)}) fusion(bf16[64,2048]{1,0:T(8,128)(2,1)S(1)} %collective-permute-done.4, bf16[64,2048]{1,0:T(8,128)(2,1)S(1)} %slice.46, pred[]{:T(512)S(6)} %eq.45), kind=kLoop, calls=%fused_computation.48 | loop fusion | flops 131071 | bytes 1048577 | tf_op jit(solution)/shard_map/jit(_where)/select_n | solution.py:62
  22.9 0.6 %collective-permute-start.5 = (bf16[64,2048]{1,0:T(8,128)(2,1)}, bf16[64,2048]{1,0:T(8,128)(2,1)}, u32[]{:S(2)}, u32[]{:S(2)}) collective-permute-start(bf16[64,2048]{1,0:T(8,128)(2,1)} %get-tuple-element.21), channel_id=1, source_target_pairs={{0,1},{1,0},{2,3},{3,2},{4,5},{5,4},{6,7},{7,6},{8,9},{9,8},{10,11... | collective-permute-start | bytes 786440 | tf_op jit(solution)/shard_map/ppermute | solution.py:63
  23.5 0.5 fusion.26
  24.0 1.0 %fusion.39 = (f32[8,4,64]{2,1,0:T(4,128)S(1)}, bf16[8,4,64,192]{3,2,1,0:T(8,128)(2,1)S(1)}) fusion(f32[8,192,64,4]{1,2,3,0:T(8,128)S(1)} %fusion.26, pred[64,192]{1,0:T(8,128)(4,1)S(1)} %get-tuple-element.26), kind=kOutput, calls=%fused_computation.76 | output fusion | flops 2752703 | bytes 2379776 | tf_op jit(solution)/shard_map/sub | solution.py:48
  25.0 0.5 fusion.14
  25.4 0.4 copy.16
  25.8 0.4 convert_element_type.49
  26.2 1.6 %collective-permute-start.3 = (bf16[64,4096]{1,0:T(8,128)(2,1)S(1)}, bf16[64,4096]{1,0:T(8,128)(2,1)S(1)}, u32[]{:S(2)}, u32[]{:S(2)}) collective-permute-start(bf16[64,4096]{1,0:T(8,128)(2,1)S(1)} %convert_element_type.49), channel_id=1, source_target_pairs={{0,8},{8,16},{16,24},{24,0},{1,9},{9,17},{17,25},{25,1},{2,10},{10... | collective-permute-start | bytes 1572872 | tf_op jit(solution)/shard_map/ppermute | solution.py:26
  27.8 0.4 reshape.66
  28.2 1.4 %collective-permute-done.5 = bf16[64,2048]{1,0:T(8,128)(2,1)} collective-permute-done((bf16[64,2048]{1,0:T(8,128)(2,1)}, bf16[64,2048]{1,0:T(8,128)(2,1)}, u32[]{:S(2)}, u32[]{:S(2)}) %collective-permute-start.5) | collective-permute-done | bytes 262176 | tf_op jit(solution)/shard_map/ppermute | solution.py:63
  29.6 1.0 %constant_dynamic-update-slice_fusion = bf16[192,2048]{1,0:T(8,128)(2,1)S(1)} fusion(bf16[192,2048]{1,0:T(8,128)(2,1)S(1)} %constant_dynamic-update-slice_fusion.1, bf16[64,2048]{1,0:T(8,128)(2,1)} %collective-permute-done.5), kind=kLoop, calls=%fused_computation.52 | loop fusion | bytes 524288 | tf_op jit(solution)/shard_map/concatenate | solution.py:97
  30.6 0.1 slice_bitcast_fusion.3
  30.6 0.1 copy.36
  30.7 0.1 copy.35
  30.8 0.5 fusion.24
  31.3 1.0 %fusion.40 = (f32[8,4,64]{2,1,0:T(4,128)S(1)}, bf16[8,4,64,192]{3,2,1,0:T(8,128)(2,1)S(1)}) fusion(f32[8,192,64,4]{1,2,3,0:T(8,128)S(1)} %fusion.24, pred[64,192]{1,0:T(8,128)(4,1)S(1)} %get-tuple-element.25), kind=kOutput, calls=%fused_computation.77 | output fusion | flops 2752703 | bytes 2379776 | tf_op jit(solution)/shard_map/sub | solution.py:48
  32.2 0.5 fusion.15
  32.7 0.4 copy.20
  33.1 0.4 convert_element_type.55
  33.5 1.6 %collective-permute-start.6 = (bf16[64,4096]{1,0:T(8,128)(2,1)S(1)}, bf16[64,4096]{1,0:T(8,128)(2,1)S(1)}, u32[]{:S(2)}, u32[]{:S(2)}) collective-permute-start(bf16[64,4096]{1,0:T(8,128)(2,1)S(1)} %convert_element_type.55), channel_id=1, source_target_pairs={{0,8},{8,16},{16,24},{24,0},{1,9},{9,17},{17,25},{25,1},{2,10},{10... | collective-permute-start | bytes 1572872 | tf_op jit(solution)/shard_map/ppermute | solution.py:26
  35.1 0.6 %fusion.38 = (s32[1]{0:T(128)}, s32[1]{0:T(128)}) fusion(s32[2]{0:T(128)S(1)} %collective-permute-done.2, s32[]{:T(128)S(6)} %select_n.98, s32[]{:T(128)S(6)} %select_n.105), kind=kLoop, calls=%fused_computation.75 | loop fusion | bytes 24 | tf_op jit(solution)/shard_map/jit(dynamic_index_in_dim)/dynamic_slice | solution.py:124
  36.9 5.9 %collective-permute-done.3 = bf16[64,4096]{1,0:T(8,128)(2,1)S(1)} collective-permute-done((bf16[64,4096]{1,0:T(8,128)(2,1)S(1)}, bf16[64,4096]{1,0:T(8,128)(2,1)S(1)}, u32[]{:S(2)}, u32[]{:S(2)}) %collective-permute-start.3) | collective-permute-done | bytes 524320 | tf_op jit(solution)/shard_map/ppermute | solution.py:26
  42.9 8.1 %collective-permute-done.6 = bf16[64,4096]{1,0:T(8,128)(2,1)S(1)} collective-permute-done((bf16[64,4096]{1,0:T(8,128)(2,1)S(1)}, bf16[64,4096]{1,0:T(8,128)(2,1)S(1)}, u32[]{:S(2)}, u32[]{:S(2)}) %collective-permute-start.6) | collective-permute-done | bytes 524320 | tf_op jit(solution)/shard_map/ppermute | solution.py:26
  51.0 0.1 select_bitcast_fusion.1
  51.1 1.8 %collective-permute-done.8 = bf16[64,4096]{1,0:T(8,128)(2,1)S(1)} collective-permute-done((bf16[64,4096]{1,0:T(8,128)(2,1)S(1)}, bf16[64,4096]{1,0:T(8,128)(2,1)S(1)}, u32[]{:S(2)}, u32[]{:S(2)}) %collective-permute-start.8) | collective-permute-done | bytes 524320 | tf_op jit(solution)/shard_map/ppermute | solution.py:20
  52.9 0.1 select_bitcast_fusion
  53.0 1.1 %maximum_bitcast_fusion = bf16[1,2,64,4096]{3,2,1,0:T(8,128)(2,1)} fusion(bf16[1,64,4096]{2,1,0:T(8,128)(2,1)S(1)} %select_bitcast_fusion, bf16[1,64,4096]{2,1,0:T(8,128)(2,1)S(1)} %select_bitcast_fusion.1), kind=kLoop, calls=%fused_computation.22 | loop fusion | flops 524288 | bytes 2097152 | tf_op jit(solution)/shard_map/reshape | solution.py:133
  (18 shorter events, 0.2 us)
Async XLA Ops:
  0.0 4.6 %copy-start.2 = (s32[1,2]{1,0:T(1,128)S(1)}, s32[1,2]{1,0:T(1,128)}, u32[]{:S(2)}) copy-start(s32[1,2]{1,0:T(1,128)} %param.7) | copy-start | bytes 28
  0.0 6.2 %copy-start.1 = (s32[1,4,8]{2,1,0:T(4,128)S(1)}, s32[1,4,8]{2,1,0:T(4,128)}, u32[]{:S(2)}) copy-start(s32[1,4,8]{2,1,0:T(4,128)} %param.6) | copy-start | bytes 388
  0.0 6.5 %copy-start = (s32[1,4]{1,0:T(1,128)S(1)}, s32[1,4]{1,0:T(1,128)}, u32[]{:S(2)}) copy-start(s32[1,4]{1,0:T(1,128)} %param.5) | copy-start | bytes 52
  1.6 9.4 %collective-permute-start = (bf16[64,2048]{1,0:T(8,128)(2,1)S(1)}, bf16[64,2048]{1,0:T(8,128)(2,1)S(1)}, u32[]{:S(2)}, u32[]{:S(2)}) collective-permute-start(bf16[64,2048]{1,0:T(8,128)(2,1)S(1)} %slice.42), channel_id=1, source_target_pairs={{0,2},{1,3},{2,0},{3,1},{4,6},{5,7},{6,4},{7,5},{8,10},{9,11},{10,... | collective-permute-start | bytes 786440 | tf_op jit(solution)/shard_map/ppermute | solution.py:60
  4.6 23.2 %collective-permute-start.2 = (s32[2]{0:T(128)S(1)}, s32[2]{0:T(128)S(1)}, u32[]{:S(2)}, u32[]{:S(2)}) collective-permute-start(s32[2]{0:T(128)S(1)} %bitcast.93), channel_id=1, source_target_pairs={{0,8},{8,16},{16,24},{24,0},{1,9},{9,17},{17,25},{25,1},{2,10},{10... | collective-permute-start | bytes 32 | tf_op jit(solution)/shard_map/ppermute | solution.py:26
  11.7 7.7 %collective-permute-start.1 = (bf16[64,2048]{1,0:T(8,128)(2,1)}, bf16[64,2048]{1,0:T(8,128)(2,1)S(1)}, u32[]{:S(2)}, u32[]{:S(2)}) collective-permute-start(bf16[64,2048]{1,0:T(8,128)(2,1)} %broadcast_select_fusion.1), channel_id=1, source_target_pairs={{0,1},{1,0},{2,3},{3,2},{4,5},{5,4},{6,7},{7,6},{8,9},{9,8},{10,11... | collective-permute-start | bytes 786440 | tf_op jit(solution)/shard_map/ppermute | solution.py:63
  15.2 7.0 %collective-permute-start.4 = (bf16[64,2048]{1,0:T(8,128)(2,1)S(1)}, bf16[64,2048]{1,0:T(8,128)(2,1)S(1)}, u32[]{:S(2)}, u32[]{:S(2)}) collective-permute-start(bf16[64,2048]{1,0:T(8,128)(2,1)S(1)} %slice.46), channel_id=1, source_target_pairs={{0,2},{1,3},{2,0},{3,1},{4,6},{5,7},{6,4},{7,5},{8,10},{9,11},{10,... | collective-permute-start | bytes 786440 | tf_op jit(solution)/shard_map/ppermute | solution.py:60
  22.9 6.7 %collective-permute-start.5 = (bf16[64,2048]{1,0:T(8,128)(2,1)}, bf16[64,2048]{1,0:T(8,128)(2,1)}, u32[]{:S(2)}, u32[]{:S(2)}) collective-permute-start(bf16[64,2048]{1,0:T(8,128)(2,1)} %get-tuple-element.21), channel_id=1, source_target_pairs={{0,1},{1,0},{2,3},{3,2},{4,5},{5,4},{6,7},{7,6},{8,9},{9,8},{10,11... | collective-permute-start | bytes 786440 | tf_op jit(solution)/shard_map/ppermute | solution.py:63
  26.2 16.6 %collective-permute-start.3 = (bf16[64,4096]{1,0:T(8,128)(2,1)S(1)}, bf16[64,4096]{1,0:T(8,128)(2,1)S(1)}, u32[]{:S(2)}, u32[]{:S(2)}) collective-permute-start(bf16[64,4096]{1,0:T(8,128)(2,1)S(1)} %convert_element_type.49), channel_id=1, source_target_pairs={{0,8},{8,16},{16,24},{24,0},{1,9},{9,17},{17,25},{25,1},{2,10},{10... | collective-permute-start | bytes 1572872 | tf_op jit(solution)/shard_map/ppermute | solution.py:26
  33.5 17.5 %collective-permute-start.6 = (bf16[64,4096]{1,0:T(8,128)(2,1)S(1)}, bf16[64,4096]{1,0:T(8,128)(2,1)S(1)}, u32[]{:S(2)}, u32[]{:S(2)}) collective-permute-start(bf16[64,4096]{1,0:T(8,128)(2,1)S(1)} %convert_element_type.55), channel_id=1, source_target_pairs={{0,8},{8,16},{16,24},{24,0},{1,9},{9,17},{17,25},{25,1},{2,10},{10... | collective-permute-start | bytes 1572872 | tf_op jit(solution)/shard_map/ppermute | solution.py:26
  42.9 8.2 %collective-permute-start.7 = (bf16[64,4096]{1,0:T(8,128)(2,1)S(1)}, bf16[64,4096]{1,0:T(8,128)(2,1)S(1)}, u32[]{:S(2)}, u32[]{:S(2)}) collective-permute-start(bf16[64,4096]{1,0:T(8,128)(2,1)S(1)} %collective-permute-done.3), channel_id=1, source_target_pairs={{0,4},{4,0},{1,5},{5,1},{2,6},{6,2},{3,7},{7,3},{8,12},{12,8},{9,1... | collective-permute-start | bytes 1572872 | tf_op jit(solution)/shard_map/ppermute | solution.py:20
  51.0 1.9 %collective-permute-start.8 = (bf16[64,4096]{1,0:T(8,128)(2,1)S(1)}, bf16[64,4096]{1,0:T(8,128)(2,1)S(1)}, u32[]{:S(2)}, u32[]{:S(2)}) collective-permute-start(bf16[64,4096]{1,0:T(8,128)(2,1)S(1)} %collective-permute-done.6), channel_id=1, source_target_pairs={{0,4},{4,0},{1,5},{5,1},{2,6},{6,2},{3,7},{7,3},{8,12},{12,8},{9,1... | collective-permute-start | bytes 1572872 | tf_op jit(solution)/shard_map/ppermute | solution.py:20

commit v8 on v7

--- a/solution.py
+++ b/solution.py
@@ -37,9 +37,10 @@
     query_doc = doc_of(query_pos, ends)
     key_doc = doc_of(key_pos, ends)
     allowed = (key_pos[None, :] <= query_pos[:, None]) & (key_doc[None, :] == query_doc[:, None])
-    queries = query_rows.reshape(seg_len, KV_HEADS, group_size, HD)
-    keys = key_rows.reshape(key_len, KV_HEADS, HD)
-    values = value_rows.reshape(key_len, KV_HEADS, HD)
+    kv_heads = key_rows.shape[1] // HD
+    queries = query_rows.reshape(seg_len, kv_heads, group_size, HD)
+    keys = key_rows.reshape(key_len, kv_heads, HD)
+    values = value_rows.reshape(key_len, kv_heads, HD)
     scores = (
         jnp.einsum("qkgd,skd->kgqs", queries, keys, preferred_element_type=jnp.float32)
         * HD ** (-0.5)
@@ -52,7 +53,7 @@
     result = summed / jnp.transpose(row_total, (2, 0, 1))[..., None]
     valid = (query_pos < length).astype(jnp.float32)
     result = result * valid[:, None, None, None]
-    return result.reshape(seg_len, D).astype(jnp.bfloat16)
+    return result.reshape(seg_len, kv_heads * group_size * HD).astype(jnp.bfloat16)
 
 
 def gathered(block, seq_index, seq_count, reach):
@@ -88,7 +89,12 @@
     key_value_width = KV_HEADS * HD
     far = jnp.int32(4 * length_all)
 
-    def attend_own(row, kv_local, pieces_and_chunks, own_index):
+    groups = 2
+    group_kv = KV_HEADS // groups
+    group_q = group_kv * (H // KV_HEADS) * HD
+    group_width = group_kv * HD
+
+    def attend_piece(query_rows, kv_local, pieces_and_chunks, own_index):
         pieces = [kv_local]
         key_pos = [query_pos]
         for piece, chunk in pieces_and_chunks:
@@ -100,34 +106,46 @@
         ends = lax.dynamic_index_in_dim(doc_ends, row_id, 0, keepdims=False)
         length = lax.dynamic_index_in_dim(lengths_all, row_id, 0, keepdims=False)
         return attend_row(
-            row[:, :D],
-            kv_all[:, :key_value_width],
-            kv_all[:, key_value_width:],
+            query_rows,
+            kv_all[:, :group_width],
+            kv_all[:, group_width:],
             query_pos,
             key_pos,
             ends,
             length,
         )
 
-    first_row, second_row = own_rows[0], own_rows[1]
-    first_kv = first_row[:, D:]
-    first_pieces = gathered(first_kv, seq_index, seq_count, reach)
-    second_kv = lax.optimization_barrier((second_row[:, D:], first_pieces[0][0]))[0]
-    second_pieces = gathered(second_kv, seq_index, seq_count, reach)
-    first_out = attend_own(first_row, first_kv, first_pieces, 0)
-    first_next = passed_along(first_out, "section", 1)
     previous_hand = passed_along(hand_over[0], "section", 1)
-    second_row, _, previous_hand = lax.optimization_barrier((second_row, first_out, previous_hand))
-    second_out = attend_own(second_row, second_kv, second_pieces, 1)
-    second_next = passed_along(second_out, "section", 1)
+    arrived = {}
+    last_first = None
+    last_out = None
+    for own_index in range(RPR):
+        row = own_rows[own_index]
+        for group in range(groups):
+            keys = row[:, D + group * group_width : D + (group + 1) * group_width]
+            values = row[:, D + key_value_width + group * group_width :][:, :group_width]
+            kv_local = jnp.concatenate([keys, values], axis=1)
+            queries = row[:, group * group_q : (group + 1) * group_q]
+            if last_first is not None:
+                kv_local = lax.optimization_barrier((kv_local, last_first))[0]
+            pieces = gathered(kv_local, seq_index, seq_count, reach)
+            if last_out is not None:
+                queries, _, previous_hand = lax.optimization_barrier((queries, last_out, previous_hand))
+            out = attend_piece(queries, kv_local, pieces, own_index)
+            arrived[own_index, group] = passed_along(out, "section", 1)
+            last_first = pieces[0][0]
+            last_out = out
 
     own_hand = lax.dynamic_index_in_dim(previous_hand, replica, 0, keepdims=False)
     partner_hand = lax.dynamic_index_in_dim(previous_hand, partner, 0, keepdims=False)
-    partner_first = swapped(first_next, "dp", 0)
-    partner_second = swapped(second_next, "dp", 0)
+    partner_arrived = {key: swapped(value, "dp", 0) for key, value in arrived.items()}
+
+    def whole(parts, own_index):
+        return jnp.concatenate([parts[own_index, group] for group in range(groups)], axis=1)
+
     sent = [
-        jnp.where(own_hand == 1, first_next, second_next),
-        jnp.where(partner_hand == 0, partner_first, partner_second),
+        jnp.where(own_hand == 1, whole(arrived, 0), whole(arrived, 1)),
+        jnp.where(partner_hand == 0, whole(partner_arrived, 0), whole(partner_arrived, 1)),
     ]
     out = jnp.stack(sent, axis=0)
     return out.reshape(1, RPR, seg_len, D)

time: 54.2 us -> 54.1 us (level)
  waiting for transfers between devices: 26 us -> 14.4 us
  starting transfers between devices: 11.7 us -> 21 us
  matrix products: 1.84 us -> 2.91 us
  other arithmetic: 6.46 us -> 7.36 us
    ppermute x3 -> x5, waiting for transfers between devices: 14.1 us -> 4.13 us  [passed_along(): return lax.ppermute(value, axis, pairs)]
    ppermute x3 -> x5, starting transfers between devices: 4.77 us -> 8.32 us  [passed_along(): return lax.ppermute(value, axis, pairs)]
    ppermute x2 -> x4, starting transfers between devices: 4.65 us -> 7.82 us  [gathered(): over_y = lax.ppermute(block, 'seq', [(j, j ^ 2) for j in range(4)])]
    ppermute x2 -> x4, waiting for transfers between devices: 3.96 us -> 1.43 us  [gathered(): over_x = lax.ppermute(onward, 'seq', [(j, j ^ 1) for j in range(4)])]
    ppermute x2 -> x4, waiting for transfers between devices: 6.12 us -> 8.56 us  [gathered(): over_y = lax.ppermute(block, 'seq', [(j, j ^ 2) for j in range(4)])]
    ppermute x2 -> x4, starting transfers between devices: 2.31 us -> 4.19 us  [gathered(): over_x = lax.ppermute(onward, 'seq', [(j, j ^ 1) for j in range(4)])]
    ppermute x2 -> x4, waiting for transfers between devices: 1.84 us -> 0.27 us  [swapped(): return lax.ppermute(block, axis, route)]
    select_n x1 -> x3, other arithmetic: 0.01 us -> 1.36 us  [the longest x1 1.23 us: shards(): jnp.where(own_hand == 1, whole(arrived, 0), whole(arrived, 1))]
  transfers between devices with their start and end apart: 9 -> 17, of which waited for: 7 -> 8; matrix products, arithmetic and copies ran while one was open for 23% -> 26% of each run, Pallas kernels for 0% -> 0%
where the time goes in v8:
time: 54.1 us; the launch traced here: 53.9 us
  starting transfers between devices  21 us (39%)
  waiting for transfers between devices  14.4 us (27%)
  other arithmetic  7.36 us (14%)
  local copies, waits for them, and re-layouts  6.63 us (12%)
  matrix products  2.91 us (5%)
  between operations  1.65 us (3%)
    ppermute x4, waiting for transfers between devices, gathered(): over_y = lax.ppermute(block, 'seq', [(j, j ^ 2) for j in range(4)])  8.56 us
    ppermute x5, starting transfers between devices, passed_along(): return lax.ppermute(value, axis, pairs)  8.32 us
    ppermute x4, starting transfers between devices, gathered(): over_y = lax.ppermute(block, 'seq', [(j, j ^ 2) for j in range(4)])  7.82 us
    ppermute x4, starting transfers between devices, gathered(): over_x = lax.ppermute(onward, 'seq', [(j, j ^ 1) for j in range(4)])  4.19 us
    ppermute x5, waiting for transfers between devices, passed_along(): return lax.ppermute(value, axis, pairs)  4.13 us
    dot_general x4, matrix products, attend_row(): jnp.einsum('kgqs,skd->qkgd', rounded, values, preferred_element_type=jnp....  1.63 us
    convert_element_type x8, local copies, waits for them, and re-layouts, attend_row(): result.reshape(seg_len, kv_heads * group_size * HD).astype(jnp.bfloat16)  1.55 us
    sub x4, other arithmetic, attend_row(): weights = jnp.where(allowed, jnp.exp(scores - row_top), 0.0)  1.55 us
  transfers between devices with their start and end apart: 17, of which 8 were waited for; matrix products, arithmetic and copies ran while one was open for 26% of the time, Pallas kernels for 0%

profile of v8, /device:TPU:0, one launch (start us, length us, event | category | flops | bytes accessed | tf_op | source)
XLA Modules:
  0.0 53.9 jit_solution(1958658967661194670)
XLA Ops:
  0.0 1.5 %slice_bitcast_fusion.1 = (bf16[64,6144]{1,0:T(8,128)(2,1)S(1)}, bf16[64,6144]{1,0:T(8,128)(2,1)S(1)}) fusion(bf16[1,2,64,6144]{3,2,1,0:T(8,128)(2,1)} %param.4), kind=kLoop, calls=%fused_computation.50 | loop fusion | bytes 3145728 | tf_op jit(solution)/shard_map/squeeze | solution.py:123
  1.6 3.1 %collective-permute-start = (bf16[64,1024]{1,0:T(8,128)(2,1)S(1)}, bf16[64,1024]{1,0:T(8,128)(2,1)S(1)}, u32[]{:S(2)}, u32[]{:S(2)}) collective-permute-start(bf16[64,1024]{1,0:T(8,128)(2,1)S(1)} %pad_maximum_fusion.3), channel_id=1, source_target_pairs={{0,2},{1,3},{2,0},{3,1},{4,6},{5,7},{6,4},{7,5},{8,10},{9,11},{10,... | collective-permute-start | bytes 393224 | tf_op jit(solution)/shard_map/ppermute | solution.py:61
  4.7 1.6 %collective-permute-start.6 = (s32[2]{0:T(128)S(1)}, s32[2]{0:T(128)S(1)}, u32[]{:S(2)}, u32[]{:S(2)}) collective-permute-start(s32[2]{0:T(128)S(1)} %bitcast.90), channel_id=1, source_target_pairs={{0,8},{8,16},{16,24},{24,0},{1,9},{9,17},{17,25},{25,1},{2,10},{10... | collective-permute-start | bytes 32 | tf_op jit(solution)/shard_map/ppermute | solution.py:26
  6.4 0.2 reduce_window_sum.11
  7.0 0.7 %constant_dynamic-slice_fusion = (s32[1,1]{1,0:T(1,128)}, s32[1,1]{1,0:T(1,128)}) fusion(s32[1,4]{1,0:T(1,128)S(1)} %copy-done, s32[]{:T(128)S(6)} %select_n.147, s32[]{:T(128)S(6)} %select_n.149), kind=kLoop, calls=%fused_computation.112 | loop fusion | bytes 24 | tf_op jit(solution)/shard_map/jit(dynamic_index_in_dim)/dynamic_slice | solution.py:107
  7.7 0.5 collective-permute-done
  8.2 1.8 %collective-permute-start.5 = (bf16[64,1024]{1,0:T(8,128)(2,1)S(1)}, bf16[64,1024]{1,0:T(8,128)(2,1)S(1)}, u32[]{:S(2)}, u32[]{:S(2)}) collective-permute-start(bf16[64,1024]{1,0:T(8,128)(2,1)S(1)} %broadcast_select_fusion.1), channel_id=1, source_target_pairs={{0,1},{1,0},{2,3},{3,2},{4,5},{5,4},{6,7},{7,6},{8,9},{9,8},{10,11... | collective-permute-start | bytes 393224 | tf_op jit(solution)/shard_map/ppermute | solution.py:64
  10.0 1.3 %compare_convert_fusion = (f32[64]{0:T(128)S(1)}, f32[64]{0:T(128)S(1)}) fusion(s32[]{:T(128)} %bitcast.22, s32[]{:T(128)S(6)} %mul.73, s32[]{:T(128)} %bitcast.14), kind=kLoop, calls=%fused_computation.101 | loop fusion | flops 320 | bytes 524 | tf_op jit(solution)/shard_map/convert_element_type | solution.py:54
  11.5 1.6 %collective-permute-start.1 = (bf16[64,1024]{1,0:T(8,128)(2,1)S(1)}, bf16[64,1024]{1,0:T(8,128)(2,1)S(1)}, u32[]{:S(2)}, u32[]{:S(2)}) collective-permute-start(bf16[64,1024]{1,0:T(8,128)(2,1)S(1)} %pad_maximum_fusion.2), channel_id=1, source_target_pairs={{0,2},{1,3},{2,0},{3,1},{4,6},{5,7},{6,4},{7,5},{8,10},{9,11},{10,... | collective-permute-start | bytes 393224 | tf_op jit(solution)/shard_map/ppermute | solution.py:61
  13.4 3.1 %collective-permute-done.1 = bf16[64,1024]{1,0:T(8,128)(2,1)S(1)} collective-permute-done((bf16[64,1024]{1,0:T(8,128)(2,1)S(1)}, bf16[64,1024]{1,0:T(8,128)(2,1)S(1)}, u32[]{:S(2)}, u32[]{:S(2)}) %collective-permute-start.1) | collective-permute-done | bytes 131104 | tf_op jit(solution)/shard_map/ppermute | solution.py:61
  16.6 0.7 %broadcast_select_fusion.2 = (bf16[64,1024]{1,0:T(8,128)(2,1)}, bf16[192,1024]{1,0:T(8,128)(2,1)S(1)}) fusion(bf16[64,1024]{1,0:T(8,128)(2,1)S(1)} %collective-permute-done.1, bf16[64,1024]{1,0:T(8,128)(2,1)S(1)} %pad_maximum_fusion.2, pred[]{:T(512)S(6)} %eq.29), kind=kLoop, calls=%fused_computation.84 | loop fusion | flops 65535 | bytes 524289 | tf_op jit(solution)/shard_map/jit(_where)/select_n | solution.py:63
  17.2 0.3 collective-permute-start.4
  17.6 0.3 fusion.39
  17.9 0.4 fusion.119
  18.3 0.4 fusion.51
  18.7 0.2 copy.27
  18.9 0.2 convert_element_type.75
  19.1 1.8 %collective-permute-start.7 = (bf16[64,2048]{1,0:T(8,128)(2,1)S(1)}, bf16[64,2048]{1,0:T(8,128)(2,1)}, u32[]{:S(2)}, u32[]{:S(2)}) collective-permute-start(bf16[64,2048]{1,0:T(8,128)(2,1)S(1)} %convert_element_type.75), channel_id=1, source_target_pairs={{0,8},{8,16},{16,24},{24,0},{1,9},{9,17},{17,25},{25,1},{2,10},{10... | collective-permute-start | bytes 786440 | tf_op jit(solution)/shard_map/ppermute | solution.py:26
  21.1 1.6 %collective-permute-start.2 = (bf16[64,1024]{1,0:T(8,128)(2,1)S(1)}, bf16[64,1024]{1,0:T(8,128)(2,1)S(1)}, u32[]{:S(2)}, u32[]{:S(2)}) collective-permute-start(bf16[64,1024]{1,0:T(8,128)(2,1)S(1)} %pad_maximum_fusion.1), channel_id=1, source_target_pairs={{0,2},{1,3},{2,0},{3,1},{4,6},{5,7},{6,4},{7,5},{8,10},{9,11},{10,... | collective-permute-start | bytes 393224 | tf_op jit(solution)/shard_map/ppermute | solution.py:61
  22.7 0.9 %constant_dynamic-update-slice_fusion.3 = bf16[192,1024]{1,0:T(8,128)(2,1)S(1)} fusion(bf16[192,1024]{1,0:T(8,128)(2,1)S(1)} %constant_dynamic-update-slice_fusion.4, bf16[64,1024]{1,0:T(8,128)(2,1)} %collective-permute-done.4), kind=kLoop, calls=%fused_computation.91 | loop fusion | bytes 262144 | tf_op jit(solution)/shard_map/concatenate | solution.py:103
  23.8 0.3 fusion.38
  24.1 0.4 fusion.120
  24.5 1.6 %collective-permute-done.2 = bf16[64,1024]{1,0:T(8,128)(2,1)S(1)} collective-permute-done((bf16[64,1024]{1,0:T(8,128)(2,1)S(1)}, bf16[64,1024]{1,0:T(8,128)(2,1)S(1)}, u32[]{:S(2)}, u32[]{:S(2)}) %collective-permute-start.2) | collective-permute-done | bytes 131104 | tf_op jit(solution)/shard_map/ppermute | solution.py:61
  26.2 1.6 %collective-permute-start.3 = (bf16[64,1024]{1,0:T(8,128)(2,1)S(1)}, bf16[64,1024]{1,0:T(8,128)(2,1)S(1)}, u32[]{:S(2)}, u32[]{:S(2)}) collective-permute-start(bf16[64,1024]{1,0:T(8,128)(2,1)S(1)} %get-tuple-element.51), channel_id=1, source_target_pairs={{0,1},{1,0},{2,3},{3,2},{4,5},{5,4},{6,7},{7,6},{8,9},{9,8},{10,11... | collective-permute-start | bytes 393224 | tf_op jit(solution)/shard_map/ppermute | solution.py:64
  27.7 0.4 fusion.50
  28.2 0.2 copy.31
  28.6 1.6 %collective-permute-start.8 = (bf16[64,2048]{1,0:T(8,128)(2,1)S(1)}, bf16[64,2048]{1,0:T(8,128)(2,1)}, u32[]{:S(2)}, u32[]{:S(2)}) collective-permute-start(bf16[64,2048]{1,0:T(8,128)(2,1)S(1)} %convert_element_type.78), channel_id=1, source_target_pairs={{0,8},{8,16},{16,24},{24,0},{1,9},{9,17},{17,25},{25,1},{2,10},{10... | collective-permute-start | bytes 786440 | tf_op jit(solution)/shard_map/ppermute | solution.py:26
  30.4 1.6 %collective-permute-start.10 = (bf16[64,1024]{1,0:T(8,128)(2,1)S(1)}, bf16[64,1024]{1,0:T(8,128)(2,1)S(1)}, u32[]{:S(2)}, u32[]{:S(2)}) collective-permute-start(bf16[64,1024]{1,0:T(8,128)(2,1)S(1)} %pad_maximum_fusion.4), channel_id=1, source_target_pairs={{0,2},{1,3},{2,0},{3,1},{4,6},{5,7},{6,4},{7,5},{8,10},{9,11},{10,... | collective-permute-start | bytes 393224 | tf_op jit(solution)/shard_map/ppermute | solution.py:61
  32.1 3.3 %collective-permute-done.10 = bf16[64,1024]{1,0:T(8,128)(2,1)S(1)} collective-permute-done((bf16[64,1024]{1,0:T(8,128)(2,1)S(1)}, bf16[64,1024]{1,0:T(8,128)(2,1)S(1)}, u32[]{:S(2)}, u32[]{:S(2)}) %collective-permute-start.10) | collective-permute-done | bytes 131104 | tf_op jit(solution)/shard_map/ppermute | solution.py:61
  35.4 0.7 %broadcast_select_fusion = (bf16[64,1024]{1,0:T(8,128)(2,1)}, bf16[192,1024]{1,0:T(8,128)(2,1)S(1)}) fusion(bf16[64,1024]{1,0:T(8,128)(2,1)S(1)} %collective-permute-done.10, bf16[64,1024]{1,0:T(8,128)(2,1)S(1)} %pad_maximum_fusion.4, pred[]{:T(512)S(6)} %eq.29), kind=kLoop, calls=%fused_computation.82 | loop fusion | flops 65535 | bytes 524289 | tf_op jit(solution)/shard_map/jit(_where)/select_n | solution.py:63
  36.1 0.5 collective-permute-start.11
  36.6 0.3 fusion.37
  36.9 0.4 fusion.121
  37.3 0.4 fusion.49
  37.7 0.2 copy.35
  38.1 1.6 %collective-permute-start.9 = (bf16[64,2048]{1,0:T(8,128)(2,1)S(1)}, bf16[64,2048]{1,0:T(8,128)(2,1)}, u32[]{:S(2)}, u32[]{:S(2)}) collective-permute-start(bf16[64,2048]{1,0:T(8,128)(2,1)S(1)} %convert_element_type.82), channel_id=1, source_target_pairs={{0,8},{8,16},{16,24},{24,0},{1,9},{9,17},{17,25},{25,1},{2,10},{10... | collective-permute-start | bytes 786440 | tf_op jit(solution)/shard_map/ppermute | solution.py:26
  40.0 1.3 %collective-permute-done.11 = bf16[64,1024]{1,0:T(8,128)(2,1)S(1)} collective-permute-done((bf16[64,1024]{1,0:T(8,128)(2,1)}, bf16[64,1024]{1,0:T(8,128)(2,1)S(1)}, u32[]{:S(2)}, u32[]{:S(2)}) %collective-permute-start.11) | collective-permute-done | bytes 131104 | tf_op jit(solution)/shard_map/ppermute | solution.py:64
  41.4 0.3 fusion.36
  41.7 0.4 fusion.122
  42.1 0.4 fusion.48
  42.6 0.2 copy.39
  43.0 1.6 %collective-permute-start.12 = (bf16[64,2048]{1,0:T(8,128)(2,1)S(1)}, bf16[64,2048]{1,0:T(8,128)(2,1)S(1)}, u32[]{:S(2)}, u32[]{:S(2)}) collective-permute-start(bf16[64,2048]{1,0:T(8,128)(2,1)S(1)} %convert_element_type.85), channel_id=1, source_target_pairs={{0,8},{8,16},{16,24},{24,0},{1,9},{9,17},{17,25},{25,1},{2,10},{10... | collective-permute-start | bytes 786440 | tf_op jit(solution)/shard_map/ppermute | solution.py:26
  44.6 0.6 %fusion.118 = (s32[1]{0:T(128)}, s32[1]{0:T(128)}) fusion(s32[2]{0:T(128)S(1)} %collective-permute-done.6, s32[]{:T(128)S(6)} %select_n.157, s32[]{:T(128)S(6)} %select_n.163), kind=kLoop, calls=%fused_computation.133 | loop fusion | bytes 24 | tf_op jit(solution)/shard_map/jit(dynamic_index_in_dim)/dynamic_slice | solution.py:139
  46.5 0.5 collective-permute-start.14
  47.1 4.1 %collective-permute-done.12 = bf16[64,2048]{1,0:T(8,128)(2,1)S(1)} collective-permute-done((bf16[64,2048]{1,0:T(8,128)(2,1)S(1)}, bf16[64,2048]{1,0:T(8,128)(2,1)S(1)}, u32[]{:S(2)}, u32[]{:S(2)}) %collective-permute-start.12) | collective-permute-done | bytes 262176 | tf_op jit(solution)/shard_map/ppermute | solution.py:26
  51.2 1.2 %maximum_select_fusion = bf16[1,64,4096]{2,1,0:T(8,128)(2,1)S(1)} fusion(bf16[1,64,2048]{2,1,0:T(8,128)(2,1)} %bitcast.25, bf16[1,64,2048]{2,1,0:T(8,128)(2,1)} %bitcast.24, bf16[1,64,2048]{2,1,0:T(8,128)(2,1)S(1)} %bitcast.80, bf16[1,64,2048]{2,1,0:T(8,128)(2,1)} %bitcast.26, pred[]{:T(512)} %bitcast.23), kind=kLoop, calls=%fused_computation.51 | loop fusion | flops 2359296 | bytes 1572865 | tf_op jit(solution)/shard_map/jit(_where)/select_n | solution.py:147
  52.4 0.3 collective-permute-done.16
  52.8 1.1 %maximum_bitcast_fusion = bf16[1,2,64,4096]{3,2,1,0:T(8,128)(2,1)} fusion(bf16[1,64,4096]{2,1,0:T(8,128)(2,1)S(1)} %maximum_select_fusion.1, bf16[1,64,4096]{2,1,0:T(8,128)(2,1)S(1)} %maximum_select_fusion), kind=kLoop, calls=%fused_computation.48 | loop fusion | flops 524288 | bytes 2097152 | tf_op jit(solution)/shard_map/reshape | solution.py:151
  (60 shorter events, 2.9 us)
Async XLA Ops:
  0.0 4.7 %copy-start.2 = (s32[1,2]{1,0:T(1,128)S(1)}, s32[1,2]{1,0:T(1,128)}, u32[]{:S(2)}) copy-start(s32[1,2]{1,0:T(1,128)} %param.7) | copy-start | bytes 28
  1.5 4.8 %copy-start.1 = (s32[1,4,8]{2,1,0:T(4,128)S(1)}, s32[1,4,8]{2,1,0:T(4,128)}, u32[]{:S(2)}) copy-start(s32[1,4,8]{2,1,0:T(4,128)} %param.6) | copy-start | bytes 388
  1.6 5.4 %copy-start = (s32[1,4]{1,0:T(1,128)S(1)}, s32[1,4]{1,0:T(1,128)}, u32[]{:S(2)}) copy-start(s32[1,4]{1,0:T(1,128)} %param.5) | copy-start | bytes 52
  1.6 6.6 %collective-permute-start = (bf16[64,1024]{1,0:T(8,128)(2,1)S(1)}, bf16[64,1024]{1,0:T(8,128)(2,1)S(1)}, u32[]{:S(2)}, u32[]{:S(2)}) collective-permute-start(bf16[64,1024]{1,0:T(8,128)(2,1)S(1)} %pad_maximum_fusion.3), channel_id=1, source_target_pairs={{0,2},{1,3},{2,0},{3,1},{4,6},{5,7},{6,4},{7,5},{8,10},{9,11},{10,... | collective-permute-start | bytes 393224 | tf_op jit(solution)/shard_map/ppermute | solution.py:61
  4.7 16.3 %collective-permute-start.6 = (s32[2]{0:T(128)S(1)}, s32[2]{0:T(128)S(1)}, u32[]{:S(2)}, u32[]{:S(2)}) collective-permute-start(s32[2]{0:T(128)S(1)} %bitcast.90), channel_id=1, source_target_pairs={{0,8},{8,16},{16,24},{24,0},{1,9},{9,17},{17,25},{25,1},{2,10},{10... | collective-permute-start | bytes 32 | tf_op jit(solution)/shard_map/ppermute | solution.py:26
  8.2 5.0 %collective-permute-start.5 = (bf16[64,1024]{1,0:T(8,128)(2,1)S(1)}, bf16[64,1024]{1,0:T(8,128)(2,1)S(1)}, u32[]{:S(2)}, u32[]{:S(2)}) collective-permute-start(bf16[64,1024]{1,0:T(8,128)(2,1)S(1)} %broadcast_select_fusion.1), channel_id=1, source_target_pairs={{0,1},{1,0},{2,3},{3,2},{4,5},{5,4},{6,7},{7,6},{8,9},{9,8},{10,11... | collective-permute-start | bytes 393224 | tf_op jit(solution)/shard_map/ppermute | solution.py:64
  11.5 5.0 %collective-permute-start.1 = (bf16[64,1024]{1,0:T(8,128)(2,1)S(1)}, bf16[64,1024]{1,0:T(8,128)(2,1)S(1)}, u32[]{:S(2)}, u32[]{:S(2)}) collective-permute-start(bf16[64,1024]{1,0:T(8,128)(2,1)S(1)} %pad_maximum_fusion.2), channel_id=1, source_target_pairs={{0,2},{1,3},{2,0},{3,1},{4,6},{5,7},{6,4},{7,5},{8,10},{9,11},{10,... | collective-permute-start | bytes 393224 | tf_op jit(solution)/shard_map/ppermute | solution.py:61
  17.2 5.5 %collective-permute-start.4 = (bf16[64,1024]{1,0:T(8,128)(2,1)}, bf16[64,1024]{1,0:T(8,128)(2,1)}, u32[]{:S(2)}, u32[]{:S(2)}) collective-permute-start(bf16[64,1024]{1,0:T(8,128)(2,1)} %get-tuple-element.53), channel_id=1, source_target_pairs={{0,1},{1,0},{2,3},{3,2},{4,5},{5,4},{6,7},{7,6},{8,9},{9,8},{10,11... | collective-permute-start | bytes 393224 | tf_op jit(solution)/shard_map/ppermute | solution.py:64
  19.1 27.3 %collective-permute-start.7 = (bf16[64,2048]{1,0:T(8,128)(2,1)S(1)}, bf16[64,2048]{1,0:T(8,128)(2,1)}, u32[]{:S(2)}, u32[]{:S(2)}) collective-permute-start(bf16[64,2048]{1,0:T(8,128)(2,1)S(1)} %convert_element_type.75), channel_id=1, source_target_pairs={{0,8},{8,16},{16,24},{24,0},{1,9},{9,17},{17,25},{25,1},{2,10},{10... | collective-permute-start | bytes 786440 | tf_op jit(solution)/shard_map/ppermute | solution.py:26
  21.1 5.0 %collective-permute-start.2 = (bf16[64,1024]{1,0:T(8,128)(2,1)S(1)}, bf16[64,1024]{1,0:T(8,128)(2,1)S(1)}, u32[]{:S(2)}, u32[]{:S(2)}) collective-permute-start(bf16[64,1024]{1,0:T(8,128)(2,1)S(1)} %pad_maximum_fusion.1), channel_id=1, source_target_pairs={{0,2},{1,3},{2,0},{3,1},{4,6},{5,7},{6,4},{7,5},{8,10},{9,11},{10,... | collective-permute-start | bytes 393224 | tf_op jit(solution)/shard_map/ppermute | solution.py:61
  26.2 5.8 %collective-permute-start.3 = (bf16[64,1024]{1,0:T(8,128)(2,1)S(1)}, bf16[64,1024]{1,0:T(8,128)(2,1)S(1)}, u32[]{:S(2)}, u32[]{:S(2)}) collective-permute-start(bf16[64,1024]{1,0:T(8,128)(2,1)S(1)} %get-tuple-element.51), channel_id=1, source_target_pairs={{0,1},{1,0},{2,3},{3,2},{4,5},{5,4},{6,7},{7,6},{8,9},{9,8},{10,11... | collective-permute-start | bytes 393224 | tf_op jit(solution)/shard_map/ppermute | solution.py:64
  28.6 17.9 %collective-permute-start.8 = (bf16[64,2048]{1,0:T(8,128)(2,1)S(1)}, bf16[64,2048]{1,0:T(8,128)(2,1)}, u32[]{:S(2)}, u32[]{:S(2)}) collective-permute-start(bf16[64,2048]{1,0:T(8,128)(2,1)S(1)} %convert_element_type.78), channel_id=1, source_target_pairs={{0,8},{8,16},{16,24},{24,0},{1,9},{9,17},{17,25},{25,1},{2,10},{10... | collective-permute-start | bytes 786440 | tf_op jit(solution)/shard_map/ppermute | solution.py:26
  30.4 5.0 %collective-permute-start.10 = (bf16[64,1024]{1,0:T(8,128)(2,1)S(1)}, bf16[64,1024]{1,0:T(8,128)(2,1)S(1)}, u32[]{:S(2)}, u32[]{:S(2)}) collective-permute-start(bf16[64,1024]{1,0:T(8,128)(2,1)S(1)} %pad_maximum_fusion.4), channel_id=1, source_target_pairs={{0,2},{1,3},{2,0},{3,1},{4,6},{5,7},{6,4},{7,5},{8,10},{9,11},{10,... | collective-permute-start | bytes 393224 | tf_op jit(solution)/shard_map/ppermute | solution.py:61
  36.1 5.2 %collective-permute-start.11 = (bf16[64,1024]{1,0:T(8,128)(2,1)}, bf16[64,1024]{1,0:T(8,128)(2,1)S(1)}, u32[]{:S(2)}, u32[]{:S(2)}) collective-permute-start(bf16[64,1024]{1,0:T(8,128)(2,1)} %get-tuple-element.49), channel_id=1, source_target_pairs={{0,1},{1,0},{2,3},{3,2},{4,5},{5,4},{6,7},{7,6},{8,9},{9,8},{10,11... | collective-permute-start | bytes 393224 | tf_op jit(solution)/shard_map/ppermute | solution.py:64
  38.1 8.8 %collective-permute-start.9 = (bf16[64,2048]{1,0:T(8,128)(2,1)S(1)}, bf16[64,2048]{1,0:T(8,128)(2,1)}, u32[]{:S(2)}, u32[]{:S(2)}) collective-permute-start(bf16[64,2048]{1,0:T(8,128)(2,1)S(1)} %convert_element_type.82), channel_id=1, source_target_pairs={{0,8},{8,16},{16,24},{24,0},{1,9},{9,17},{17,25},{25,1},{2,10},{10... | collective-permute-start | bytes 786440 | tf_op jit(solution)/shard_map/ppermute | solution.py:26
  43.0 8.2 %collective-permute-start.12 = (bf16[64,2048]{1,0:T(8,128)(2,1)S(1)}, bf16[64,2048]{1,0:T(8,128)(2,1)S(1)}, u32[]{:S(2)}, u32[]{:S(2)}) collective-permute-start(bf16[64,2048]{1,0:T(8,128)(2,1)S(1)} %convert_element_type.85), channel_id=1, source_target_pairs={{0,8},{8,16},{16,24},{24,0},{1,9},{9,17},{17,25},{25,1},{2,10},{10... | collective-permute-start | bytes 786440 | tf_op jit(solution)/shard_map/ppermute | solution.py:26
  46.4 6.0 %collective-permute-start.13 = (bf16[64,2048]{1,0:T(8,128)(2,1)}, bf16[64,2048]{1,0:T(8,128)(2,1)S(1)}, u32[]{:S(2)}, u32[]{:S(2)}) collective-permute-start(bf16[64,2048]{1,0:T(8,128)(2,1)} %collective-permute-done.7), channel_id=1, source_target_pairs={{0,4},{4,0},{1,5},{5,1},{2,6},{6,2},{3,7},{7,3},{8,12},{12,8},{9,1... | collective-permute-start | bytes 786440 | tf_op jit(solution)/shard_map/ppermute | solution.py:20
  46.5 5.9 %collective-permute-start.14 = (bf16[64,2048]{1,0:T(8,128)(2,1)}, bf16[64,2048]{1,0:T(8,128)(2,1)S(1)}, u32[]{:S(2)}, u32[]{:S(2)}) collective-permute-start(bf16[64,2048]{1,0:T(8,128)(2,1)} %collective-permute-done.8), channel_id=1, source_target_pairs={{0,4},{4,0},{1,5},{5,1},{2,6},{6,2},{3,7},{7,3},{8,12},{12,8},{9,1... | collective-permute-start | bytes 786440 | tf_op jit(solution)/shard_map/ppermute | solution.py:20
  47.0 5.5 %collective-permute-start.15 = (bf16[64,2048]{1,0:T(8,128)(2,1)}, bf16[64,2048]{1,0:T(8,128)(2,1)S(1)}, u32[]{:S(2)}, u32[]{:S(2)}) collective-permute-start(bf16[64,2048]{1,0:T(8,128)(2,1)} %collective-permute-done.9), channel_id=1, source_target_pairs={{0,4},{4,0},{1,5},{5,1},{2,6},{6,2},{3,7},{7,3},{8,12},{12,8},{9,1... | collective-permute-start | bytes 786440 | tf_op jit(solution)/shard_map/ppermute | solution.py:20
  51.2 1.5 %collective-permute-start.16 = (bf16[64,2048]{1,0:T(8,128)(2,1)S(1)}, bf16[64,2048]{1,0:T(8,128)(2,1)S(1)}, u32[]{:S(2)}, u32[]{:S(2)}) collective-permute-start(bf16[64,2048]{1,0:T(8,128)(2,1)S(1)} %collective-permute-done.12), channel_id=1, source_target_pairs={{0,4},{4,0},{1,5},{5,1},{2,6},{6,2},{3,7},{7,3},{8,12},{12,8},{9,1... | collective-permute-start | bytes 786440 | tf_op jit(solution)/shard_map/ppermute | solution.py:20

commit v9 on v7

--- a/solution.py
+++ b/solution.py
@@ -55,11 +55,13 @@
     return result.reshape(seg_len, D).astype(jnp.bfloat16)
 
 
-def gathered(block, seq_index, seq_count, reach):
+def gathered(block, seq_index, seq_count, reach, hold=None):
     if seq_count == 4 and reach == 2:
         over_y = lax.ppermute(block, "seq", [(j, j ^ 2) for j in range(4)])
         odd = seq_index % 2 == 1
         onward = jnp.where(odd, over_y, block)
+        if hold is not None:
+            onward = lax.optimization_barrier((onward, hold))[0]
         over_x = lax.ppermute(onward, "seq", [(j, j ^ 1) for j in range(4)])
         return [
             (over_y, jnp.bitwise_xor(seq_index, 2)),
@@ -112,9 +114,9 @@
     first_row, second_row = own_rows[0], own_rows[1]
     first_kv = first_row[:, D:]
     first_pieces = gathered(first_kv, seq_index, seq_count, reach)
+    first_out = attend_own(first_row, first_kv, first_pieces, 0)
     second_kv = lax.optimization_barrier((second_row[:, D:], first_pieces[0][0]))[0]
-    second_pieces = gathered(second_kv, seq_index, seq_count, reach)
-    first_out = attend_own(first_row, first_kv, first_pieces, 0)
+    second_pieces = gathered(second_kv, seq_index, seq_count, reach, hold=first_out)
     first_next = passed_along(first_out, "section", 1)
     previous_hand = passed_along(hand_over[0], "section", 1)
     second_row, _, previous_hand = lax.optimization_barrier((second_row, first_out, previous_hand))

time: 54.2 us -> 52.9 us (0.976)
  local copies, waits for them, and re-layouts: 6.59 us -> 5.7 us
  other arithmetic: 6.46 us -> 5.85 us
    ppermute x3, waiting for transfers between devices: 14.1 us -> 16.4 us  [passed_along(): return lax.ppermute(value, axis, pairs)]
    ppermute x2, waiting for transfers between devices: 3.96 us -> 2.29 us  [gathered(): over_x = lax.ppermute(onward, 'seq', [(j, j ^ 1) for j in range(4)])]
    concatenate x1, local copies, waits for them, and re-layouts: 0.97 us -> 0.02 us  [attend_own(): kv_all = jnp.concatenate(pieces, axis=0)]
    ppermute x2, waiting for transfers between devices: 6.12 us -> 5.28 us  [gathered(): over_y = lax.ppermute(block, 'seq', [(j, j ^ 2) for j in range(4)])]
    ppermute x2, starting transfers between devices: 2.31 us -> 3.11 us  [gathered(): over_x = lax.ppermute(onward, 'seq', [(j, j ^ 1) for j in range(4)])]
    select_n x2, other arithmetic: 1.5 us -> 0.79 us  [gathered(): onward = jnp.where(odd, over_y, block)]
    ppermute x3, starting transfers between devices: 4.77 us -> 4.21 us  [passed_along(): return lax.ppermute(value, axis, pairs)]
  transfers between devices with their start and end apart: 9 -> 9, of which waited for: 7 -> 7; matrix products, arithmetic and copies ran while one was open for 23% -> 19% of each run, Pallas kernels for 0% -> 0%
where the time goes in v9:
time: 52.9 us; the launch traced here: 52.7 us
  waiting for transfers between devices  25.8 us (49%)
  starting transfers between devices  12 us (23%)
  other arithmetic  5.85 us (11%)
  local copies, waits for them, and re-layouts  5.7 us (11%)
  matrix products  1.83 us (3%)
  between operations  1.57 us (3%)
    ppermute x3, waiting for transfers between devices, passed_along(): return lax.ppermute(value, axis, pairs)  16.4 us
    ppermute x2, waiting for transfers between devices, gathered(): over_y = lax.ppermute(block, 'seq', [(j, j ^ 2) for j in range(4)])  5.28 us
    ppermute x2, starting transfers between devices, gathered(): over_y = lax.ppermute(block, 'seq', [(j, j ^ 2) for j in range(4)])  4.65 us
    ppermute x3, starting transfers between devices, passed_along(): return lax.ppermute(value, axis, pairs)  4.21 us
    ppermute x2, starting transfers between devices, gathered(): over_x = lax.ppermute(onward, 'seq', [(j, j ^ 1) for j in range(4)])  3.11 us
    ppermute x2, waiting for transfers between devices, gathered(): over_x = lax.ppermute(onward, 'seq', [(j, j ^ 1) for j in range(4)])  2.29 us
    sub x2, other arithmetic, attend_row(): weights = jnp.where(allowed, jnp.exp(scores - row_top), 0.0)  1.94 us
    ppermute x2, waiting for transfers between devices, swapped(): return lax.ppermute(block, axis, route)  1.84 us
  transfers between devices with their start and end apart: 9, of which 7 were waited for; matrix products, arithmetic and copies ran while one was open for 19% of the time, Pallas kernels for 0%

profile of v9, /device:TPU:0, one launch (start us, length us, event | category | flops | bytes accessed | tf_op | source)
XLA Modules:
  0.0 52.7 jit_solution(2706032686259603236)
XLA Ops:
  0.0 1.5 %slice_bitcast_fusion.1 = (bf16[64,6144]{1,0:T(8,128)(2,1)S(1)}, bf16[64,6144]{1,0:T(8,128)(2,1)S(1)}) fusion(bf16[1,2,64,6144]{3,2,1,0:T(8,128)(2,1)} %param.4), kind=kLoop, calls=%fused_computation.33 | loop fusion | bytes 3145728 | tf_op jit(solution)/shard_map/squeeze | solution.py:114
  1.5 3.1 %collective-permute-start = (bf16[64,2048]{1,0:T(8,128)(2,1)S(1)}, bf16[64,2048]{1,0:T(8,128)(2,1)S(1)}, u32[]{:S(2)}, u32[]{:S(2)}) collective-permute-start(bf16[64,2048]{1,0:T(8,128)(2,1)S(1)} %slice.42), channel_id=1, source_target_pairs={{0,2},{1,3},{2,0},{3,1},{4,6},{5,7},{6,4},{7,5},{8,10},{9,11},{10,... | collective-permute-start | bytes 786440 | tf_op jit(solution)/shard_map/ppermute | solution.py:60
  4.6 0.2 reduce_window_sum.11
  4.8 0.1 pad_add_fusion
  4.9 0.7 %constant_dynamic-slice_fusion = (s32[1,1]{1,0:T(1,128)}, s32[1,1]{1,0:T(1,128)}) fusion(s32[1,4]{1,0:T(1,128)S(1)} %copy-done, s32[]{:T(128)S(6)} %select_n.101, s32[]{:T(128)S(6)} %select_n.95), kind=kLoop, calls=%fused_computation.62 | loop fusion | bytes 24 | tf_op jit(solution)/shard_map/jit(dynamic_index_in_dim)/dynamic_slice | solution.py:103
  5.6 0.1 convert_reduce_fusion.2
  5.6 0.1 convert_reduce_fusion
  5.7 5.2 %collective-permute-done = bf16[64,2048]{1,0:T(8,128)(2,1)S(1)} collective-permute-done((bf16[64,2048]{1,0:T(8,128)(2,1)S(1)}, bf16[64,2048]{1,0:T(8,128)(2,1)S(1)}, u32[]{:S(2)}, u32[]{:S(2)}) %collective-permute-start) | collective-permute-done | bytes 262176 | tf_op jit(solution)/shard_map/ppermute | solution.py:60
  10.9 1.8 %collective-permute-start.1 = (bf16[64,2048]{1,0:T(8,128)(2,1)S(1)}, bf16[64,2048]{1,0:T(8,128)(2,1)S(1)}, u32[]{:S(2)}, u32[]{:S(2)}) collective-permute-start(bf16[64,2048]{1,0:T(8,128)(2,1)S(1)} %broadcast_select_fusion.1), channel_id=1, source_target_pairs={{0,1},{1,0},{2,3},{3,2},{4,5},{5,4},{6,7},{7,6},{8,9},{9,8},{10,11... | collective-permute-start | bytes 786440 | tf_op jit(solution)/shard_map/ppermute | solution.py:65
  12.7 1.3 %compare_convert_fusion = (f32[64]{0:T(128)S(1)}, f32[64]{0:T(128)S(1)}) fusion(s32[]{:T(128)} %bitcast.18, s32[]{:T(128)S(6)} %mul.43, s32[]{:T(128)} %bitcast.9), kind=kLoop, calls=%fused_computation.59 | loop fusion | flops 320 | bytes 524 | tf_op jit(solution)/shard_map/convert_element_type | solution.py:53
  14.1 0.4 reshape.63
  14.5 0.1 compare_and_fusion
  14.6 1.6 %collective-permute-start.4 = (bf16[64,2048]{1,0:T(8,128)(2,1)S(1)}, bf16[64,2048]{1,0:T(8,128)(2,1)S(1)}, u32[]{:S(2)}, u32[]{:S(2)}) collective-permute-start(bf16[64,2048]{1,0:T(8,128)(2,1)S(1)} %slice.46), channel_id=1, source_target_pairs={{0,2},{1,3},{2,0},{3,1},{4,6},{5,7},{6,4},{7,5},{8,10},{9,11},{10,... | collective-permute-start | bytes 786440 | tf_op jit(solution)/shard_map/ppermute | solution.py:60
  16.2 2.3 %collective-permute-done.1 = bf16[64,2048]{1,0:T(8,128)(2,1)S(1)} collective-permute-done((bf16[64,2048]{1,0:T(8,128)(2,1)S(1)}, bf16[64,2048]{1,0:T(8,128)(2,1)S(1)}, u32[]{:S(2)}, u32[]{:S(2)}) %collective-permute-start.1) | collective-permute-done | bytes 262176 | tf_op jit(solution)/shard_map/ppermute | solution.py:65
  18.5 0.1 pad_maximum_fusion
  18.5 0.1 slice_bitcast_fusion.5
  18.6 0.1 copy.34
  18.7 0.1 copy.33
  18.8 0.5 fusion.26
  19.2 1.0 %fusion.39 = (f32[8,4,64]{2,1,0:T(4,128)S(1)}, bf16[8,4,64,192]{3,2,1,0:T(8,128)(2,1)S(1)}) fusion(f32[8,192,64,4]{1,2,3,0:T(8,128)S(1)} %fusion.26, pred[64,192]{1,0:T(8,128)(4,1)S(1)} %get-tuple-element.28), kind=kOutput, calls=%fused_computation.76 | output fusion | flops 2752703 | bytes 2379776 | tf_op jit(solution)/shard_map/sub | solution.py:48
  20.2 0.5 fusion.14
  20.7 0.0 copy-start.2
  20.7 0.4 copy.16
  21.1 0.4 convert_element_type.49
  21.5 0.1 collective-permute-done.4
  21.6 0.8 %broadcast_select_fusion = (bf16[64,2048]{1,0:T(8,128)(2,1)}, bf16[192,2048]{1,0:T(8,128)(2,1)S(1)}) fusion(bf16[64,2048]{1,0:T(8,128)(2,1)S(1)} %collective-permute-done.4, bf16[64,2048]{1,0:T(8,128)(2,1)S(1)} %slice.46, pred[]{:T(512)S(6)} %eq.45), kind=kLoop, calls=%fused_computation.48 | loop fusion | flops 131071 | bytes 1048577 | tf_op jit(solution)/shard_map/jit(_where)/select_n | solution.py:62
  22.3 1.3 %collective-permute-start.5 = (bf16[64,2048]{1,0:T(8,128)(2,1)}, bf16[64,2048]{1,0:T(8,128)(2,1)S(1)}, u32[]{:S(2)}, u32[]{:S(2)}) collective-permute-start(bf16[64,2048]{1,0:T(8,128)(2,1)} %get-tuple-element.11), channel_id=1, source_target_pairs={{0,1},{1,0},{2,3},{3,2},{4,5},{5,4},{6,7},{7,6},{8,9},{9,8},{10,11... | collective-permute-start | bytes 786440 | tf_op jit(solution)/shard_map/ppermute | solution.py:65
  23.7 1.6 %collective-permute-start.2 = (s32[2]{0:T(128)S(1)}, s32[2]{0:T(128)S(1)}, u32[]{:S(2)}, u32[]{:S(2)}) collective-permute-start(s32[2]{0:T(128)S(1)} %bitcast.93), channel_id=1, source_target_pairs={{0,8},{8,16},{16,24},{24,0},{1,9},{9,17},{17,25},{25,1},{2,10},{10... | collective-permute-start | bytes 32 | tf_op jit(solution)/shard_map/ppermute | solution.py:26
  25.3 1.6 %collective-permute-start.3 = (bf16[64,4096]{1,0:T(8,128)(2,1)S(1)}, bf16[64,4096]{1,0:T(8,128)(2,1)}, u32[]{:S(2)}, u32[]{:S(2)}) collective-permute-start(bf16[64,4096]{1,0:T(8,128)(2,1)S(1)} %convert_element_type.49), channel_id=1, source_target_pairs={{0,8},{8,16},{16,24},{24,0},{1,9},{9,17},{17,25},{25,1},{2,10},{10... | collective-permute-start | bytes 1572872 | tf_op jit(solution)/shard_map/ppermute | solution.py:26
  26.8 2.2 %collective-permute-done.2 = s32[2]{0:T(128)S(1)} collective-permute-done((s32[2]{0:T(128)S(1)}, s32[2]{0:T(128)S(1)}, u32[]{:S(2)}, u32[]{:S(2)}) %collective-permute-start.2) | collective-permute-done | bytes 40 | tf_op jit(solution)/shard_map/ppermute | solution.py:26
  29.1 0.4 reshape.66
  29.5 0.1 slice_bitcast_fusion.3
  29.6 0.1 copy.36
  29.7 0.1 copy.35
  29.7 0.5 fusion.24
  30.2 1.0 %fusion.40 = (f32[8,4,64]{2,1,0:T(4,128)S(1)}, bf16[8,4,64,192]{3,2,1,0:T(8,128)(2,1)S(1)}) fusion(f32[8,192,64,4]{1,2,3,0:T(8,128)S(1)} %fusion.24, pred[64,192]{1,0:T(8,128)(4,1)S(1)} %get-tuple-element.27), kind=kOutput, calls=%fused_computation.77 | output fusion | flops 2752703 | bytes 2379776 | tf_op jit(solution)/shard_map/sub | solution.py:48
  31.2 0.4 fusion.15
  31.6 0.4 copy.20
  32.0 0.4 convert_element_type.55
  32.4 1.0 %collective-permute-start.6 = (bf16[64,4096]{1,0:T(8,128)(2,1)S(1)}, bf16[64,4096]{1,0:T(8,128)(2,1)S(1)}, u32[]{:S(2)}, u32[]{:S(2)}) collective-permute-start(bf16[64,4096]{1,0:T(8,128)(2,1)S(1)} %convert_element_type.55), channel_id=1, source_target_pairs={{0,8},{8,16},{16,24},{24,0},{1,9},{9,17},{17,25},{25,1},{2,10},{10... | collective-permute-start | bytes 1572872 | tf_op jit(solution)/shard_map/ppermute | solution.py:26
  33.5 0.7 %fusion.38 = (s32[1]{0:T(128)}, s32[1]{0:T(128)}) fusion(s32[2]{0:T(128)S(1)} %collective-permute-done.2, s32[]{:T(128)S(6)} %select_n.98, s32[]{:T(128)S(6)} %select_n.105), kind=kLoop, calls=%fused_computation.75 | loop fusion | bytes 24 | tf_op jit(solution)/shard_map/jit(dynamic_index_in_dim)/dynamic_slice | solution.py:126
  35.5 6.5 %collective-permute-done.3 = bf16[64,4096]{1,0:T(8,128)(2,1)} collective-permute-done((bf16[64,4096]{1,0:T(8,128)(2,1)S(1)}, bf16[64,4096]{1,0:T(8,128)(2,1)}, u32[]{:S(2)}, u32[]{:S(2)}) %collective-permute-start.3) | collective-permute-done | bytes 524320 | tf_op jit(solution)/shard_map/ppermute | solution.py:26
  42.0 0.0 collective-permute-start.7
  42.0 7.7 %collective-permute-done.6 = bf16[64,4096]{1,0:T(8,128)(2,1)S(1)} collective-permute-done((bf16[64,4096]{1,0:T(8,128)(2,1)S(1)}, bf16[64,4096]{1,0:T(8,128)(2,1)S(1)}, u32[]{:S(2)}, u32[]{:S(2)}) %collective-permute-start.6) | collective-permute-done | bytes 524320 | tf_op jit(solution)/shard_map/ppermute | solution.py:26
  49.7 0.1 select_bitcast_fusion.1
  49.8 1.8 %collective-permute-done.8 = bf16[64,4096]{1,0:T(8,128)(2,1)S(1)} collective-permute-done((bf16[64,4096]{1,0:T(8,128)(2,1)S(1)}, bf16[64,4096]{1,0:T(8,128)(2,1)S(1)}, u32[]{:S(2)}, u32[]{:S(2)}) %collective-permute-start.8) | collective-permute-done | bytes 524320 | tf_op jit(solution)/shard_map/ppermute | solution.py:20
  51.6 0.1 select_bitcast_fusion
  51.7 1.1 %maximum_bitcast_fusion = bf16[1,2,64,4096]{3,2,1,0:T(8,128)(2,1)} fusion(bf16[1,64,4096]{2,1,0:T(8,128)(2,1)S(1)} %select_bitcast_fusion, bf16[1,64,4096]{2,1,0:T(8,128)(2,1)S(1)} %select_bitcast_fusion.1), kind=kLoop, calls=%fused_computation.22 | loop fusion | flops 524288 | bytes 2097152 | tf_op jit(solution)/shard_map/reshape | solution.py:135
  (18 shorter events, 0.2 us)
Async XLA Ops:
  0.0 4.6 %copy-start.1 = (s32[1,4,8]{2,1,0:T(4,128)S(1)}, s32[1,4,8]{2,1,0:T(4,128)}, u32[]{:S(2)}) copy-start(s32[1,4,8]{2,1,0:T(4,128)} %param.6) | copy-start | bytes 388
  0.0 4.9 %copy-start = (s32[1,4]{1,0:T(1,128)S(1)}, s32[1,4]{1,0:T(1,128)}, u32[]{:S(2)}) copy-start(s32[1,4]{1,0:T(1,128)} %param.5) | copy-start | bytes 52
  1.5 9.4 %collective-permute-start = (bf16[64,2048]{1,0:T(8,128)(2,1)S(1)}, bf16[64,2048]{1,0:T(8,128)(2,1)S(1)}, u32[]{:S(2)}, u32[]{:S(2)}) collective-permute-start(bf16[64,2048]{1,0:T(8,128)(2,1)S(1)} %slice.42), channel_id=1, source_target_pairs={{0,2},{1,3},{2,0},{3,1},{4,6},{5,7},{6,4},{7,5},{8,10},{9,11},{10,... | collective-permute-start | bytes 786440 | tf_op jit(solution)/shard_map/ppermute | solution.py:60
  10.9 7.5 %collective-permute-start.1 = (bf16[64,2048]{1,0:T(8,128)(2,1)S(1)}, bf16[64,2048]{1,0:T(8,128)(2,1)S(1)}, u32[]{:S(2)}, u32[]{:S(2)}) collective-permute-start(bf16[64,2048]{1,0:T(8,128)(2,1)S(1)} %broadcast_select_fusion.1), channel_id=1, source_target_pairs={{0,1},{1,0},{2,3},{3,2},{4,5},{5,4},{6,7},{7,6},{8,9},{9,8},{10,11... | collective-permute-start | bytes 786440 | tf_op jit(solution)/shard_map/ppermute | solution.py:65
  14.6 7.0 %collective-permute-start.4 = (bf16[64,2048]{1,0:T(8,128)(2,1)S(1)}, bf16[64,2048]{1,0:T(8,128)(2,1)S(1)}, u32[]{:S(2)}, u32[]{:S(2)}) collective-permute-start(bf16[64,2048]{1,0:T(8,128)(2,1)S(1)} %slice.46), channel_id=1, source_target_pairs={{0,2},{1,3},{2,0},{3,1},{4,6},{5,7},{6,4},{7,5},{8,10},{9,11},{10,... | collective-permute-start | bytes 786440 | tf_op jit(solution)/shard_map/ppermute | solution.py:60
  20.7 3.0 %copy-start.2 = (s32[1,2]{1,0:T(1,128)S(1)}, s32[1,2]{1,0:T(1,128)}, u32[]{:S(2)}) copy-start(s32[1,2]{1,0:T(1,128)} %param.7) | copy-start | bytes 28
  22.3 7.1 %collective-permute-start.5 = (bf16[64,2048]{1,0:T(8,128)(2,1)}, bf16[64,2048]{1,0:T(8,128)(2,1)S(1)}, u32[]{:S(2)}, u32[]{:S(2)}) collective-permute-start(bf16[64,2048]{1,0:T(8,128)(2,1)} %get-tuple-element.11), channel_id=1, source_target_pairs={{0,1},{1,0},{2,3},{3,2},{4,5},{5,4},{6,7},{7,6},{8,9},{9,8},{10,11... | collective-permute-start | bytes 786440 | tf_op jit(solution)/shard_map/ppermute | solution.py:65
  23.7 5.4 %collective-permute-start.2 = (s32[2]{0:T(128)S(1)}, s32[2]{0:T(128)S(1)}, u32[]{:S(2)}, u32[]{:S(2)}) collective-permute-start(s32[2]{0:T(128)S(1)} %bitcast.93), channel_id=1, source_target_pairs={{0,8},{8,16},{16,24},{24,0},{1,9},{9,17},{17,25},{25,1},{2,10},{10... | collective-permute-start | bytes 32 | tf_op jit(solution)/shard_map/ppermute | solution.py:26
  25.3 16.7 %collective-permute-start.3 = (bf16[64,4096]{1,0:T(8,128)(2,1)S(1)}, bf16[64,4096]{1,0:T(8,128)(2,1)}, u32[]{:S(2)}, u32[]{:S(2)}) collective-permute-start(bf16[64,4096]{1,0:T(8,128)(2,1)S(1)} %convert_element_type.49), channel_id=1, source_target_pairs={{0,8},{8,16},{16,24},{24,0},{1,9},{9,17},{17,25},{25,1},{2,10},{10... | collective-permute-start | bytes 1572872 | tf_op jit(solution)/shard_map/ppermute | solution.py:26
  32.4 17.3 %collective-permute-start.6 = (bf16[64,4096]{1,0:T(8,128)(2,1)S(1)}, bf16[64,4096]{1,0:T(8,128)(2,1)S(1)}, u32[]{:S(2)}, u32[]{:S(2)}) collective-permute-start(bf16[64,4096]{1,0:T(8,128)(2,1)S(1)} %convert_element_type.55), channel_id=1, source_target_pairs={{0,8},{8,16},{16,24},{24,0},{1,9},{9,17},{17,25},{25,1},{2,10},{10... | collective-permute-start | bytes 1572872 | tf_op jit(solution)/shard_map/ppermute | solution.py:26
  42.0 7.8 %collective-permute-start.7 = (bf16[64,4096]{1,0:T(8,128)(2,1)}, bf16[64,4096]{1,0:T(8,128)(2,1)S(1)}, u32[]{:S(2)}, u32[]{:S(2)}) collective-permute-start(bf16[64,4096]{1,0:T(8,128)(2,1)} %collective-permute-done.3), channel_id=1, source_target_pairs={{0,4},{4,0},{1,5},{5,1},{2,6},{6,2},{3,7},{7,3},{8,12},{12,8},{9,1... | collective-permute-start | bytes 1572872 | tf_op jit(solution)/shard_map/ppermute | solution.py:20
  49.7 1.9 %collective-permute-start.8 = (bf16[64,4096]{1,0:T(8,128)(2,1)S(1)}, bf16[64,4096]{1,0:T(8,128)(2,1)S(1)}, u32[]{:S(2)}, u32[]{:S(2)}) collective-permute-start(bf16[64,4096]{1,0:T(8,128)(2,1)S(1)} %collective-permute-done.6), channel_id=1, source_target_pairs={{0,4},{4,0},{1,5},{5,1},{2,6},{6,2},{3,7},{7,3},{8,12},{12,8},{9,1... | collective-permute-start | bytes 1572872 | tf_op jit(solution)/shard_map/ppermute | solution.py:20

commit v10 on v9

--- a/solution.py
+++ b/solution.py
@@ -117,19 +117,19 @@
     first_out = attend_own(first_row, first_kv, first_pieces, 0)
     second_kv = lax.optimization_barrier((second_row[:, D:], first_pieces[0][0]))[0]
     second_pieces = gathered(second_kv, seq_index, seq_count, reach, hold=first_out)
-    first_next = passed_along(first_out, "section", 1)
-    previous_hand = passed_along(hand_over[0], "section", 1)
-    second_row, _, previous_hand = lax.optimization_barrier((second_row, first_out, previous_hand))
+    replicas = lax.axis_size("dp")
+    own_hand = jnp.sum(jnp.where(jnp.arange(replicas) == replica, hand_over[0], 0))
+    hand_block = jnp.full((seg_len, HD), own_hand, dtype=jnp.bfloat16)
+    first_next = passed_along(jnp.concatenate([first_out, hand_block], axis=1), "section", 1)
+    second_row = lax.optimization_barrier((second_row, first_out))[0]
     second_out = attend_own(second_row, second_kv, second_pieces, 1)
     second_next = passed_along(second_out, "section", 1)
 
-    own_hand = lax.dynamic_index_in_dim(previous_hand, replica, 0, keepdims=False)
-    partner_hand = lax.dynamic_index_in_dim(previous_hand, partner, 0, keepdims=False)
     partner_first = swapped(first_next, "dp", 0)
     partner_second = swapped(second_next, "dp", 0)
     sent = [
-        jnp.where(own_hand == 1, first_next, second_next),
-        jnp.where(partner_hand == 0, partner_first, partner_second),
+        jnp.where(first_next[0:1, D:D + 1] == 1, first_next[:, :D], second_next),
+        jnp.where(partner_first[0:1, D:D + 1] == 0, partner_first[:, :D], partner_second),
     ]
     out = jnp.stack(sent, axis=0)
     return out.reshape(1, RPR, seg_len, D)

time: 52.9 us -> 54.4 us (1.028)
  other arithmetic: 5.85 us -> 7.6 us
  starting transfers between devices: 12 us -> 10.9 us
  local copies, waits for them, and re-layouts: 5.7 us -> 6.75 us
  waiting for transfers between devices: 25.8 us -> 24.8 us
  between operations: 1.57 us -> 2.25 us
    ppermute x2, waiting for transfers between devices: 2.29 us -> 4.15 us  [gathered(): over_x = lax.ppermute(onward, 'seq', [(j, j ^ 1) for j in range(4)])]
    ppermute x2, waiting for transfers between devices: 1.84 us -> 0.01 us  [swapped(): return lax.ppermute(block, axis, route)]
    slice x0 -> x2, local copies, waits for them, and re-layouts: none -> 1.68 us  [the longest x1 1.17 us: shards(): first_next[0:1, D:D + 1] == 1]
    ppermute x3 -> x2, starting transfers between devices: 4.21 us -> 3.11 us  [passed_along(): return lax.ppermute(value, axis, pairs)]
    ppermute x3 -> x2, waiting for transfers between devices: 16.4 us -> 15.3 us  [passed_along(): return lax.ppermute(value, axis, pairs)]
    another operation x2, other arithmetic: 0.11 us -> 1.15 us  [shards(): out = jnp.stack(sent, axis=0)]
    reduce_sum x0 -> x1, other arithmetic: none -> 0.71 us  [shards(): jnp.sum(jnp.where(jnp.arange(replicas) == replica, hand_over[0], 0))]
    dynamic_slice x1 -> x0, local copies, waits for them, and re-layouts: 0.67 us -> none  [shards(): lax.dynamic_index_in_dim(previous_hand, replica, 0, keepdims=False)]
  transfers between devices with their start and end apart: 9 -> 8, of which waited for: 7 -> 6; matrix products, arithmetic and copies ran while one was open for 19% -> 23% of each run, Pallas kernels for 0% -> 0%
where the time goes in v10:
time: 54.4 us; the launch traced here: 54.2 us
  waiting for transfers between devices  24.8 us (46%)
  starting transfers between devices  10.9 us (20%)
  other arithmetic  7.6 us (14%)
  local copies, waits for them, and re-layouts  6.75 us (12%)
  between operations  2.25 us (4%)
  matrix products  1.83 us (3%)
    ppermute x2, waiting for transfers between devices, passed_along(): return lax.ppermute(value, axis, pairs)  15.3 us
    ppermute x2, waiting for transfers between devices, gathered(): over_y = lax.ppermute(block, 'seq', [(j, j ^ 2) for j in range(4)])  5.28 us
    ppermute x2, starting transfers between devices, gathered(): over_y = lax.ppermute(block, 'seq', [(j, j ^ 2) for j in range(4)])  4.65 us
    ppermute x2, waiting for transfers between devices, gathered(): over_x = lax.ppermute(onward, 'seq', [(j, j ^ 1) for j in range(4)])  4.15 us
    ppermute x2, starting transfers between devices, gathered(): over_x = lax.ppermute(onward, 'seq', [(j, j ^ 1) for j in range(4)])  3.11 us
    ppermute x2, starting transfers between devices, passed_along(): return lax.ppermute(value, axis, pairs)  3.11 us
    sub x2, other arithmetic, attend_row(): weights = jnp.where(allowed, jnp.exp(scores - row_top), 0.0)  1.94 us
    convert_element_type x4, local copies, waits for them, and re-layouts, attend_row(): return result.reshape(seg_len, D).astype(jnp.bfloat16)  1.59 us
  transfers between devices with their start and end apart: 8, of which 6 were waited for; matrix products, arithmetic and copies ran while one was open for 23% of the time, Pallas kernels for 0%

profile of v10, /device:TPU:0, one launch (start us, length us, event | category | flops | bytes accessed | tf_op | source)
XLA Modules:
  0.0 54.2 jit_solution(2410596027434050294)
XLA Ops:
  0.0 1.5 %slice_bitcast_fusion.1 = (bf16[64,6144]{1,0:T(8,128)(2,1)S(1)}, bf16[64,6144]{1,0:T(8,128)(2,1)S(1)}) fusion(bf16[1,2,64,6144]{3,2,1,0:T(8,128)(2,1)} %param.4), kind=kLoop, calls=%fused_computation.33 | loop fusion | bytes 3145728 | tf_op jit(solution)/shard_map/squeeze | solution.py:114
  1.5 3.1 %collective-permute-start = (bf16[64,2048]{1,0:T(8,128)(2,1)S(1)}, bf16[64,2048]{1,0:T(8,128)(2,1)S(1)}, u32[]{:S(2)}, u32[]{:S(2)}) collective-permute-start(bf16[64,2048]{1,0:T(8,128)(2,1)S(1)} %slice.58), channel_id=1, source_target_pairs={{0,2},{1,3},{2,0},{3,1},{4,6},{5,7},{6,4},{7,5},{8,10},{9,11},{10,... | collective-permute-start | bytes 786440 | tf_op jit(solution)/shard_map/ppermute | solution.py:60
  4.6 0.2 reduce_window_sum.11
  4.8 0.1 pad_add_fusion
  4.9 0.7 %constant_dynamic-slice_fusion = (s32[1,1]{1,0:T(1,128)}, s32[1,1]{1,0:T(1,128)}) fusion(s32[1,4]{1,0:T(1,128)S(1)} %copy-done, s32[]{:T(128)S(6)} %select_n.90, s32[]{:T(128)S(6)} %select_n.85), kind=kLoop, calls=%fused_computation.65 | loop fusion | bytes 24 | tf_op jit(solution)/shard_map/jit(dynamic_index_in_dim)/dynamic_slice | solution.py:103
  5.6 0.1 convert_reduce_fusion.2
  5.6 0.1 convert_reduce_fusion
  5.7 5.2 %collective-permute-done = bf16[64,2048]{1,0:T(8,128)(2,1)S(1)} collective-permute-done((bf16[64,2048]{1,0:T(8,128)(2,1)S(1)}, bf16[64,2048]{1,0:T(8,128)(2,1)S(1)}, u32[]{:S(2)}, u32[]{:S(2)}) %collective-permute-start) | collective-permute-done | bytes 262176 | tf_op jit(solution)/shard_map/ppermute | solution.py:60
  10.9 1.8 %collective-permute-start.1 = (bf16[64,2048]{1,0:T(8,128)(2,1)S(1)}, bf16[64,2048]{1,0:T(8,128)(2,1)S(1)}, u32[]{:S(2)}, u32[]{:S(2)}) collective-permute-start(bf16[64,2048]{1,0:T(8,128)(2,1)S(1)} %broadcast_select_fusion.1), channel_id=1, source_target_pairs={{0,1},{1,0},{2,3},{3,2},{4,5},{5,4},{6,7},{7,6},{8,9},{9,8},{10,11... | collective-permute-start | bytes 786440 | tf_op jit(solution)/shard_map/ppermute | solution.py:65
  12.7 1.3 %compare_convert_fusion = (f32[64]{0:T(128)S(1)}, f32[64]{0:T(128)S(1)}) fusion(s32[]{:T(128)} %bitcast.18, s32[]{:T(128)S(6)} %mul.43, s32[]{:T(128)} %bitcast.8), kind=kLoop, calls=%fused_computation.61 | loop fusion | flops 320 | bytes 524 | tf_op jit(solution)/shard_map/convert_element_type | solution.py:53
  14.1 0.4 reshape.59
  14.5 0.1 compare_and_fusion
  14.6 1.6 %collective-permute-start.3 = (bf16[64,2048]{1,0:T(8,128)(2,1)S(1)}, bf16[64,2048]{1,0:T(8,128)(2,1)S(1)}, u32[]{:S(2)}, u32[]{:S(2)}) collective-permute-start(bf16[64,2048]{1,0:T(8,128)(2,1)S(1)} %slice.64), channel_id=1, source_target_pairs={{0,2},{1,3},{2,0},{3,1},{4,6},{5,7},{6,4},{7,5},{8,10},{9,11},{10,... | collective-permute-start | bytes 786440 | tf_op jit(solution)/shard_map/ppermute | solution.py:60
  16.2 2.3 %collective-permute-done.1 = bf16[64,2048]{1,0:T(8,128)(2,1)S(1)} collective-permute-done((bf16[64,2048]{1,0:T(8,128)(2,1)S(1)}, bf16[64,2048]{1,0:T(8,128)(2,1)S(1)}, u32[]{:S(2)}, u32[]{:S(2)}) %collective-permute-start.1) | collective-permute-done | bytes 262176 | tf_op jit(solution)/shard_map/ppermute | solution.py:65
  18.5 0.1 pad_maximum_fusion
  18.5 0.1 slice_bitcast_fusion.5
  18.6 0.1 copy.34
  18.7 0.1 copy.33
  18.8 0.5 fusion.28
  19.2 1.0 %fusion.41 = (f32[8,4,64]{2,1,0:T(4,128)S(1)}, bf16[8,4,64,192]{3,2,1,0:T(8,128)(2,1)S(1)}) fusion(f32[8,192,64,4]{1,2,3,0:T(8,128)S(1)} %fusion.28, pred[64,192]{1,0:T(8,128)(4,1)S(1)} %get-tuple-element.26), kind=kOutput, calls=%fused_computation.79 | output fusion | flops 2752703 | bytes 2379776 | tf_op jit(solution)/shard_map/sub | solution.py:48
  20.2 0.5 fusion.14
  20.7 0.0 copy-start.2
  20.7 0.4 copy.16
  21.1 0.4 convert_element_type.52
  21.5 0.1 collective-permute-done.3
  21.6 0.8 %broadcast_select_fusion = (bf16[64,2048]{1,0:T(8,128)(2,1)}, bf16[192,2048]{1,0:T(8,128)(2,1)S(1)}) fusion(bf16[64,2048]{1,0:T(8,128)(2,1)S(1)} %collective-permute-done.3, bf16[64,2048]{1,0:T(8,128)(2,1)S(1)} %slice.64, pred[]{:T(512)S(6)} %eq.45), kind=kLoop, calls=%fused_computation.50 | loop fusion | flops 131071 | bytes 1048577 | tf_op jit(solution)/shard_map/jit(_where)/select_n | solution.py:62
  22.3 1.3 %collective-permute-start.4 = (bf16[64,2048]{1,0:T(8,128)(2,1)}, bf16[64,2048]{1,0:T(8,128)(2,1)S(1)}, u32[]{:S(2)}, u32[]{:S(2)}) collective-permute-start(bf16[64,2048]{1,0:T(8,128)(2,1)} %get-tuple-element.9), channel_id=1, source_target_pairs={{0,1},{1,0},{2,3},{3,2},{4,5},{5,4},{6,7},{7,6},{8,9},{9,8},{10,11... | collective-permute-start | bytes 786440 | tf_op jit(solution)/shard_map/ppermute | solution.py:65
  23.7 0.7 %fusion.36 = s32[]{:T(128)} fusion(s32[1,2]{1,0:T(1,128)S(1)} %copy-done.2, s32[]{:T(128)S(6)} %axis_index.25), kind=kLoop, calls=%fused_computation.73 | loop fusion | flops 5 | bytes 16 | tf_op jit(solution)/shard_map/reduce_sum | solution.py:121
  25.1 0.4 reshape.62
  25.6 1.6 %collective-permute-start.2 = (bf16[64,4224]{1,0:T(8,128)(2,1)S(1)}, bf16[64,4224]{1,0:T(8,128)(2,1)}, u32[]{:S(2)}, u32[]{:S(2)}) collective-permute-start(bf16[64,4224]{1,0:T(8,128)(2,1)S(1)} %concatenate.15), channel_id=1, source_target_pairs={{0,8},{8,16},{16,24},{24,0},{1,9},{9,17},{17,25},{25,1},{2,10},{10... | collective-permute-start | bytes 1622024 | tf_op jit(solution)/shard_map/ppermute | solution.py:26
  27.2 1.9 %collective-permute-done.4 = bf16[64,2048]{1,0:T(8,128)(2,1)S(1)} collective-permute-done((bf16[64,2048]{1,0:T(8,128)(2,1)}, bf16[64,2048]{1,0:T(8,128)(2,1)S(1)}, u32[]{:S(2)}, u32[]{:S(2)}) %collective-permute-start.4) | collective-permute-done | bytes 262176 | tf_op jit(solution)/shard_map/ppermute | solution.py:65
  29.1 0.1 slice_bitcast_fusion.3
  29.2 0.1 copy.36
  29.2 0.1 copy.35
  29.3 0.5 fusion.26
  29.8 1.0 %fusion.42 = (f32[8,4,64]{2,1,0:T(4,128)S(1)}, bf16[8,4,64,192]{3,2,1,0:T(8,128)(2,1)S(1)}) fusion(f32[8,192,64,4]{1,2,3,0:T(8,128)S(1)} %fusion.26, pred[64,192]{1,0:T(8,128)(4,1)S(1)} %get-tuple-element.25), kind=kOutput, calls=%fused_computation.80 | output fusion | flops 2752703 | bytes 2379776 | tf_op jit(solution)/shard_map/sub | solution.py:48
  30.7 0.4 fusion.15
  31.2 0.4 copy.20
  31.6 0.4 convert_element_type.59
  32.0 1.5 %collective-permute-start.5 = (bf16[64,4096]{1,0:T(8,128)(2,1)S(1)}, bf16[64,4096]{1,0:T(8,128)(2,1)S(1)}, u32[]{:S(2)}, u32[]{:S(2)}) collective-permute-start(bf16[64,4096]{1,0:T(8,128)(2,1)S(1)} %convert_element_type.59), channel_id=1, source_target_pairs={{0,8},{8,16},{16,24},{24,0},{1,9},{9,17},{17,25},{25,1},{2,10},{10... | collective-permute-start | bytes 1572872 | tf_op jit(solution)/shard_map/ppermute | solution.py:26
  33.5 9.2 %collective-permute-done.2 = bf16[64,4224]{1,0:T(8,128)(2,1)} collective-permute-done((bf16[64,4224]{1,0:T(8,128)(2,1)S(1)}, bf16[64,4224]{1,0:T(8,128)(2,1)}, u32[]{:S(2)}, u32[]{:S(2)}) %collective-permute-start.2) | collective-permute-done | bytes 540704 | tf_op jit(solution)/shard_map/ppermute | solution.py:26
  42.7 1.2 %slice.62 = bf16[1,1]{1,0:T(2,128)(2,1)} slice(bf16[64,4224]{1,0:T(8,128)(2,1)} %collective-permute-done.2), slice={[0:1], [4096:4097]} | slice | bytes 4 | tf_op jit(solution)/shard_map/slice | solution.py:131
  44.5 0.1 collective-permute-start.6
  44.6 6.2 %collective-permute-done.5 = bf16[64,4096]{1,0:T(8,128)(2,1)S(1)} collective-permute-done((bf16[64,4096]{1,0:T(8,128)(2,1)S(1)}, bf16[64,4096]{1,0:T(8,128)(2,1)S(1)}, u32[]{:S(2)}, u32[]{:S(2)}) %collective-permute-start.5) | collective-permute-done | bytes 524320 | tf_op jit(solution)/shard_map/ppermute | solution.py:26
  50.7 1.1 %fusion.25 = bf16[1,64,4096]{2,1,0:T(8,128)(2,1)S(1)} fusion(bf16[64,4096]{1,0:T(8,128)(2,1)S(1)} %collective-permute-done.5, bf16[64,4224]{1,0:T(8,128)(2,1)} %collective-permute-done.2, pred[]{:T(512)} %bitcast.10), kind=kLoop, calls=%fused_computation.37 | loop fusion | flops 262144 | bytes 1572865 | tf_op jit(solution)/shard_map/stack | solution.py:134
  51.8 0.5 slice.67
  53.0 0.1 fusion.24
  53.1 1.1 %maximum_bitcast_fusion = bf16[1,2,64,4096]{3,2,1,0:T(8,128)(2,1)} fusion(bf16[1,64,4096]{2,1,0:T(8,128)(2,1)S(1)} %fusion.24, bf16[1,64,4096]{2,1,0:T(8,128)(2,1)S(1)} %fusion.25), kind=kLoop, calls=%fused_computation.22 | loop fusion | flops 524288 | bytes 2097152 | tf_op jit(solution)/shard_map/reshape | solution.py:135
  (19 shorter events, 0.2 us)
Async XLA Ops:
  0.0 4.6 %copy-start.1 = (s32[1,4,8]{2,1,0:T(4,128)S(1)}, s32[1,4,8]{2,1,0:T(4,128)}, u32[]{:S(2)}) copy-start(s32[1,4,8]{2,1,0:T(4,128)} %param.6) | copy-start | bytes 388
  0.0 4.9 %copy-start = (s32[1,4]{1,0:T(1,128)S(1)}, s32[1,4]{1,0:T(1,128)}, u32[]{:S(2)}) copy-start(s32[1,4]{1,0:T(1,128)} %param.5) | copy-start | bytes 52
  1.5 9.4 %collective-permute-start = (bf16[64,2048]{1,0:T(8,128)(2,1)S(1)}, bf16[64,2048]{1,0:T(8,128)(2,1)S(1)}, u32[]{:S(2)}, u32[]{:S(2)}) collective-permute-start(bf16[64,2048]{1,0:T(8,128)(2,1)S(1)} %slice.58), channel_id=1, source_target_pairs={{0,2},{1,3},{2,0},{3,1},{4,6},{5,7},{6,4},{7,5},{8,10},{9,11},{10,... | collective-permute-start | bytes 786440 | tf_op jit(solution)/shard_map/ppermute | solution.py:60
  10.9 7.5 %collective-permute-start.1 = (bf16[64,2048]{1,0:T(8,128)(2,1)S(1)}, bf16[64,2048]{1,0:T(8,128)(2,1)S(1)}, u32[]{:S(2)}, u32[]{:S(2)}) collective-permute-start(bf16[64,2048]{1,0:T(8,128)(2,1)S(1)} %broadcast_select_fusion.1), channel_id=1, source_target_pairs={{0,1},{1,0},{2,3},{3,2},{4,5},{5,4},{6,7},{7,6},{8,9},{9,8},{10,11... | collective-permute-start | bytes 786440 | tf_op jit(solution)/shard_map/ppermute | solution.py:65
  14.6 7.0 %collective-permute-start.3 = (bf16[64,2048]{1,0:T(8,128)(2,1)S(1)}, bf16[64,2048]{1,0:T(8,128)(2,1)S(1)}, u32[]{:S(2)}, u32[]{:S(2)}) collective-permute-start(bf16[64,2048]{1,0:T(8,128)(2,1)S(1)} %slice.64), channel_id=1, source_target_pairs={{0,2},{1,3},{2,0},{3,1},{4,6},{5,7},{6,4},{7,5},{8,10},{9,11},{10,... | collective-permute-start | bytes 786440 | tf_op jit(solution)/shard_map/ppermute | solution.py:60
  20.7 3.0 %copy-start.2 = (s32[1,2]{1,0:T(1,128)S(1)}, s32[1,2]{1,0:T(1,128)}, u32[]{:S(2)}) copy-start(s32[1,2]{1,0:T(1,128)} %param.7) | copy-start | bytes 28
  22.3 6.7 %collective-permute-start.4 = (bf16[64,2048]{1,0:T(8,128)(2,1)}, bf16[64,2048]{1,0:T(8,128)(2,1)S(1)}, u32[]{:S(2)}, u32[]{:S(2)}) collective-permute-start(bf16[64,2048]{1,0:T(8,128)(2,1)} %get-tuple-element.9), channel_id=1, source_target_pairs={{0,1},{1,0},{2,3},{3,2},{4,5},{5,4},{6,7},{7,6},{8,9},{9,8},{10,11... | collective-permute-start | bytes 786440 | tf_op jit(solution)/shard_map/ppermute | solution.py:65
  25.6 17.1 %collective-permute-start.2 = (bf16[64,4224]{1,0:T(8,128)(2,1)S(1)}, bf16[64,4224]{1,0:T(8,128)(2,1)}, u32[]{:S(2)}, u32[]{:S(2)}) collective-permute-start(bf16[64,4224]{1,0:T(8,128)(2,1)S(1)} %concatenate.15), channel_id=1, source_target_pairs={{0,8},{8,16},{16,24},{24,0},{1,9},{9,17},{17,25},{25,1},{2,10},{10... | collective-permute-start | bytes 1622024 | tf_op jit(solution)/shard_map/ppermute | solution.py:26
  32.0 18.7 %collective-permute-start.5 = (bf16[64,4096]{1,0:T(8,128)(2,1)S(1)}, bf16[64,4096]{1,0:T(8,128)(2,1)S(1)}, u32[]{:S(2)}, u32[]{:S(2)}) collective-permute-start(bf16[64,4096]{1,0:T(8,128)(2,1)S(1)} %convert_element_type.59), channel_id=1, source_target_pairs={{0,8},{8,16},{16,24},{24,0},{1,9},{9,17},{17,25},{25,1},{2,10},{10... | collective-permute-start | bytes 1572872 | tf_op jit(solution)/shard_map/ppermute | solution.py:26
  44.5 7.4 %collective-permute-start.6 = (bf16[64,4224]{1,0:T(8,128)(2,1)}, bf16[64,4224]{1,0:T(8,128)(2,1)S(1)}, u32[]{:S(2)}, u32[]{:S(2)}) collective-permute-start(bf16[64,4224]{1,0:T(8,128)(2,1)} %collective-permute-done.2), channel_id=1, source_target_pairs={{0,4},{4,0},{1,5},{5,1},{2,6},{6,2},{3,7},{7,3},{8,12},{12,8},{9,1... | collective-permute-start | bytes 1622024 | tf_op jit(solution)/shard_map/ppermute | solution.py:20
  50.7 2.3 %collective-permute-start.7 = (bf16[64,4096]{1,0:T(8,128)(2,1)S(1)}, bf16[64,4096]{1,0:T(8,128)(2,1)S(1)}, u32[]{:S(2)}, u32[]{:S(2)}) collective-permute-start(bf16[64,4096]{1,0:T(8,128)(2,1)S(1)} %collective-permute-done.5), channel_id=1, source_target_pairs={{0,4},{4,0},{1,5},{5,1},{2,6},{6,2},{3,7},{7,3},{8,12},{12,8},{9,1... | collective-permute-start | bytes 1572872 | tf_op jit(solution)/shard_map/ppermute | solution.py:20

commit v11 on v5

--- a/solution.py
+++ b/solution.py
@@ -55,11 +55,13 @@
     return result.reshape(seg_len, D).astype(jnp.bfloat16)
 
 
-def gathered(block, seq_index, seq_count, reach):
+def gathered(block, seq_index, seq_count, reach, hold=None):
     if seq_count == 4 and reach == 2:
         over_y = lax.ppermute(block, "seq", [(j, j ^ 2) for j in range(4)])
         odd = seq_index % 2 == 1
         onward = jnp.where(odd, over_y, block)
+        if hold is not None:
+            onward = lax.optimization_barrier((onward, hold))[0]
         over_x = lax.ppermute(onward, "seq", [(j, j ^ 1) for j in range(4)])
         return [
             (over_y, jnp.bitwise_xor(seq_index, 2)),
@@ -77,7 +79,6 @@
     seq_index = lax.axis_index("seq")
     replica = lax.axis_index("dp")
     partner = jnp.bitwise_xor(replica, 1)
-    handed = lax.dynamic_index_in_dim(hand_over[0], replica, 0, keepdims=False)
     own_rows = qkv[0]
     seg_len = own_rows.shape[1]
     length_all = seg_len * seq_count
@@ -89,12 +90,12 @@
     key_value_width = KV_HEADS * HD
     far = jnp.int32(4 * length_all)
 
-    def prepare(own_index):
-        row = lax.dynamic_index_in_dim(own_rows, own_index, 0, keepdims=False)
-        kv_local = row[:, D:]
-        return row, kv_local
+    replicas = lax.axis_size("dp")
+    handed = jnp.sum(jnp.where(jnp.arange(replicas) == replica, hand_over[0], 0)) == 1
+    own_ends = lax.dynamic_slice_in_dim(doc_ends, 2 * replica, 2, 0)
+    own_lengths = lax.dynamic_slice_in_dim(lengths_all, 2 * replica, 2, 0)
 
-    def attend_own(row, kv_local, pieces_and_chunks, own_index):
+    def attend_own(query_rows, kv_local, pieces_and_chunks, first_is_kept):
         pieces = [kv_local]
         key_pos = [query_pos]
         for piece, chunk in pieces_and_chunks:
@@ -102,11 +103,10 @@
             key_pos.append(jnp.where(chunk >= 0, chunk * seg_len + local, far))
         kv_all = jnp.concatenate(pieces, axis=0)
         key_pos = jnp.concatenate(key_pos)
-        row_id = 2 * replica + own_index
-        ends = lax.dynamic_index_in_dim(doc_ends, row_id, 0, keepdims=False)
-        length = lax.dynamic_index_in_dim(lengths_all, row_id, 0, keepdims=False)
+        ends = jnp.where(first_is_kept, own_ends[0], own_ends[1])
+        length = jnp.where(first_is_kept, own_lengths[0], own_lengths[1])
         return attend_row(
-            row[:, :D],
+            query_rows,
             kv_all[:, :key_value_width],
             kv_all[:, key_value_width:],
             query_pos,
@@ -115,17 +115,18 @@
             length,
         )
 
-    kept_row, kept_kv = prepare(1 - handed)
-    given_row, given_kv = prepare(handed)
+    kept_kv = jnp.where(handed, own_rows[0, :, D:], own_rows[1, :, D:])
     kept_pieces = gathered(kept_kv, seq_index, seq_count, reach)
+    kept_queries = jnp.where(handed, own_rows[0, :, :D], own_rows[1, :, :D])
+    kept_out = attend_own(kept_queries, kept_kv, kept_pieces, handed)
+    given_kv = jnp.where(handed, own_rows[1, :, D:], own_rows[0, :, D:])
     given_kv = lax.optimization_barrier((given_kv, kept_pieces[0][0]))[0]
-    given_pieces = gathered(given_kv, seq_index, seq_count, reach)
-    kept_out = attend_own(kept_row, kept_kv, kept_pieces, 1 - handed)
+    given_pieces = gathered(given_kv, seq_index, seq_count, reach, hold=kept_out)
     sent = [passed_along(kept_out, "section", 1)]
-    given_row = lax.optimization_barrier((given_row, kept_out))[0]
-    given_out = attend_own(given_row, given_kv, given_pieces, handed)
+    given_queries = jnp.where(handed, own_rows[1, :, :D], own_rows[0, :, :D])
+    given_queries = lax.optimization_barrier((given_queries, kept_out))[0]
+    given_out = attend_own(given_queries, given_kv, given_pieces, jnp.logical_not(handed))
     sections = lax.axis_size("section")
-    replicas = lax.axis_size("dp")
     pairs = []
     for section in range(sections):
         for rep in range(replicas):

time: 56.6 us -> 51.1 us (0.903)
  the two profiles are of different devices: /device:TPU:1 before, /device:TPU:0 now
where the time goes in v11:
time: 51.1 us; the launch traced here: 50.8 us
  waiting for transfers between devices  24.1 us (47%)
  starting transfers between devices  9.55 us (19%)
  other arithmetic  8.42 us (16%)
  between operations  3.55 us (7%)
  local copies, waits for them, and re-layouts  3.41 us (7%)
  matrix products  1.83 us (4%)
    ppermute x1, waiting for transfers between devices, shards(): sent.append(lax.ppermute(given_out, ('section', 'dp'), pairs))  9.96 us
    ppermute x2, waiting for transfers between devices, gathered(): over_x = lax.ppermute(onward, 'seq', [(j, j ^ 1) for j in range(4)])  6.91 us
    ppermute x1, waiting for transfers between devices, passed_along(): return lax.ppermute(value, axis, pairs)  6.04 us
    ppermute x2, starting transfers between devices, gathered(): over_y = lax.ppermute(block, 'seq', [(j, j ^ 2) for j in range(4)])  4.65 us
    ppermute x2, starting transfers between devices, gathered(): over_x = lax.ppermute(onward, 'seq', [(j, j ^ 1) for j in range(4)])  3.28 us
    reshape x1, other arithmetic, shards(): return out.reshape(1, RPR, seg_len, D)  2.11 us
    sub x2, other arithmetic, attend_row(): weights = jnp.where(allowed, jnp.exp(scores - row_top), 0.0)  1.94 us
    convert_element_type x4, local copies, waits for them, and re-layouts, attend_row(): return result.reshape(seg_len, D).astype(jnp.bfloat16)  1.59 us
  transfers between devices with their start and end apart: 6, of which 5 were waited for; matrix products, arithmetic and copies ran while one was open for 18% of the time, Pallas kernels for 0%

profile of v11, /device:TPU:0, one launch (start us, length us, event | category | flops | bytes accessed | tf_op | source)
XLA Modules:
  0.0 50.8 jit_solution(4394657152667914696)
XLA Ops:
  0.0 0.0 copy-start
  0.0 0.0 copy-start.1
  0.0 1.3 %fusion.34 = s32[]{:T(128)} fusion(s32[1,2]{1,0:T(1,128)} %param.7, s32[]{:T(128)S(6)} %axis_index.23), kind=kLoop, calls=%fused_computation.69 | loop fusion | flops 5 | bytes 16 | tf_op jit(solution)/shard_map/reduce_sum | solution.py:94
  2.0 1.1 %select_bitcast_fusion.1 = (bf16[64,2048]{1,0:T(8,128)(2,1)S(1)}, bf16[64,2048]{1,0:T(8,128)(2,1)S(1)}) fusion(pred[]{:T(512)S(6)} %eq.44, bf16[2,64,6144]{2,1,0:T(8,128)(2,1)} %bitcast.88), kind=kLoop, calls=%fused_computation.46 | loop fusion | flops 262144 | bytes 1048577 | tf_op jit(solution)/shard_map/jit(_where)/select_n | solution.py:122
  3.1 3.1 %collective-permute-start = (bf16[64,2048]{1,0:T(8,128)(2,1)S(1)}, bf16[64,2048]{1,0:T(8,128)(2,1)S(1)}, u32[]{:S(2)}, u32[]{:S(2)}) collective-permute-start(bf16[64,2048]{1,0:T(8,128)(2,1)S(1)} %get-tuple-element.16), channel_id=1, source_target_pairs={{0,2},{1,3},{2,0},{3,1},{4,6},{5,7},{6,4},{7,5},{8,10},{9,11},{10,... | collective-permute-start | bytes 786440 | tf_op jit(solution)/shard_map/ppermute | solution.py:60
  6.1 1.3 %broadcast_select_fusion = (bf16[1,64,4096]{2,1,0:T(8,128)(2,1)S(1)}, bf16[64,4096]{1,0:T(8,128)(2,1)S(1)}) fusion(pred[]{:T(512)S(6)} %eq.44, bf16[2,64,6144]{2,1,0:T(8,128)(2,1)} %bitcast.89), kind=kLoop, calls=%fused_computation.37 | loop fusion | flops 524288 | bytes 2097153 | tf_op jit(solution)/shard_map/jit(_where)/select_n | solution.py:120
  7.4 0.0 copy-done.1
  7.4 0.2 reduce_window_sum.11
  7.6 0.0 copy-done
  7.6 0.1 constant_dynamic-slice_fusion
  7.7 0.6 %fusion.39 = (s32[1,1]{1,0:T(1,128)}, s32[1,1]{1,0:T(1,128)}) fusion(s32[1,2]{1,0:T(1,128)S(1)} %constant_dynamic-slice_fusion), kind=kLoop, calls=%fused_computation.77 | loop fusion | bytes 16 | tf_op jit(solution)/shard_map/slice | solution.py:107
  8.3 0.1 pad_add_fusion
  11.1 0.1 convert_reduce_fusion.2
  11.2 0.1 convert_reduce_fusion
  11.2 1.2 %collective-permute-done = bf16[64,2048]{1,0:T(8,128)(2,1)S(1)} collective-permute-done((bf16[64,2048]{1,0:T(8,128)(2,1)S(1)}, bf16[64,2048]{1,0:T(8,128)(2,1)S(1)}, u32[]{:S(2)}, u32[]{:S(2)}) %collective-permute-start) | collective-permute-done | bytes 262176 | tf_op jit(solution)/shard_map/ppermute | solution.py:60
  12.5 1.8 %collective-permute-start.1 = (bf16[64,2048]{1,0:T(8,128)(2,1)S(1)}, bf16[64,2048]{1,0:T(8,128)(2,1)S(1)}, u32[]{:S(2)}, u32[]{:S(2)}) collective-permute-start(bf16[64,2048]{1,0:T(8,128)(2,1)S(1)} %broadcast_select_fusion.2), channel_id=1, source_target_pairs={{0,1},{1,0},{2,3},{3,2},{4,5},{5,4},{6,7},{7,6},{8,9},{9,8},{10,11... | collective-permute-start | bytes 786440 | tf_op jit(solution)/shard_map/ppermute | solution.py:65
  14.2 0.4 select_n.138
  14.6 0.1 compare_and_fusion
  14.7 1.6 %collective-permute-start.3 = (bf16[64,2048]{1,0:T(8,128)(2,1)S(1)}, bf16[64,2048]{1,0:T(8,128)(2,1)S(1)}, u32[]{:S(2)}, u32[]{:S(2)}) collective-permute-start(bf16[64,2048]{1,0:T(8,128)(2,1)S(1)} %get-tuple-element.8), channel_id=1, source_target_pairs={{0,2},{1,3},{2,0},{3,1},{4,6},{5,7},{6,4},{7,5},{8,10},{9,11},{10,... | collective-permute-start | bytes 786440 | tf_op jit(solution)/shard_map/ppermute | solution.py:60
  16.3 3.7 %collective-permute-done.1 = bf16[64,2048]{1,0:T(8,128)(2,1)S(1)} collective-permute-done((bf16[64,2048]{1,0:T(8,128)(2,1)S(1)}, bf16[64,2048]{1,0:T(8,128)(2,1)S(1)}, u32[]{:S(2)}, u32[]{:S(2)}) %collective-permute-start.1) | collective-permute-done | bytes 262176 | tf_op jit(solution)/shard_map/ppermute | solution.py:65
  20.0 0.1 pad_maximum_fusion
  20.1 0.1 slice_bitcast_fusion.3
  20.1 0.1 copy.36
  20.2 0.1 copy.35
  20.3 0.5 fusion.26
  20.7 1.0 %fusion.40 = (f32[8,4,64]{2,1,0:T(4,128)S(1)}, bf16[8,4,64,192]{3,2,1,0:T(8,128)(2,1)S(1)}) fusion(f32[8,192,64,4]{1,2,3,0:T(8,128)S(1)} %fusion.26, pred[64,192]{1,0:T(8,128)(4,1)S(1)} %get-tuple-element.26), kind=kOutput, calls=%fused_computation.78 | output fusion | flops 2752703 | bytes 2379776 | tf_op jit(solution)/shard_map/sub | solution.py:48
  21.7 0.5 fusion.14
  22.2 0.4 copy.18
  22.6 0.4 convert_element_type.49
  23.0 0.0 collective-permute-done.3
  23.0 0.1 broadcast_select_fusion.1
  23.1 1.5 %collective-permute-start.4 = (bf16[64,2048]{1,0:T(8,128)(2,1)S(1)}, bf16[64,2048]{1,0:T(8,128)(2,1)S(1)}, u32[]{:S(2)}, u32[]{:S(2)}) collective-permute-start(bf16[64,2048]{1,0:T(8,128)(2,1)S(1)} %get-tuple-element.9), channel_id=1, source_target_pairs={{0,1},{1,0},{2,3},{3,2},{4,5},{5,4},{6,7},{7,6},{8,9},{9,8},{10,11... | collective-permute-start | bytes 786440 | tf_op jit(solution)/shard_map/ppermute | solution.py:65
  24.6 1.6 %collective-permute-start.2 = (bf16[64,4096]{1,0:T(8,128)(2,1)S(1)}, bf16[64,4096]{1,0:T(8,128)(2,1)}, u32[]{:S(2)}, u32[]{:S(2)}) collective-permute-start(bf16[64,4096]{1,0:T(8,128)(2,1)S(1)} %convert_element_type.49), channel_id=1, source_target_pairs={{0,8},{8,16},{16,24},{24,0},{1,9},{9,17},{17,25},{25,1},{2,10},{10... | collective-permute-start | bytes 1572872 | tf_op jit(solution)/shard_map/ppermute | solution.py:26
  26.1 0.4 reshape.66
  26.5 3.2 %collective-permute-done.4 = bf16[64,2048]{1,0:T(8,128)(2,1)S(1)} collective-permute-done((bf16[64,2048]{1,0:T(8,128)(2,1)S(1)}, bf16[64,2048]{1,0:T(8,128)(2,1)S(1)}, u32[]{:S(2)}, u32[]{:S(2)}) %collective-permute-start.4) | collective-permute-done | bytes 262176 | tf_op jit(solution)/shard_map/ppermute | solution.py:65
  29.8 0.1 slice_bitcast_fusion.1
  29.8 0.1 copy.38
  29.9 0.1 copy.37
  30.0 0.5 fusion.24
  30.4 1.0 %fusion.41 = (f32[8,4,64]{2,1,0:T(4,128)S(1)}, bf16[8,4,64,192]{3,2,1,0:T(8,128)(2,1)S(1)}) fusion(f32[8,192,64,4]{1,2,3,0:T(8,128)S(1)} %fusion.24, pred[64,192]{1,0:T(8,128)(4,1)S(1)} %get-tuple-element.25), kind=kOutput, calls=%fused_computation.79 | output fusion | flops 2752703 | bytes 2379776 | tf_op jit(solution)/shard_map/sub | solution.py:48
  31.4 0.5 fusion.15
  31.9 0.4 copy.22
  32.3 0.4 convert_element_type.55
  32.7 0.1 collective-permute-start.5
  32.7 6.0 %collective-permute-done.2 = bf16[64,4096]{1,0:T(8,128)(2,1)} collective-permute-done((bf16[64,4096]{1,0:T(8,128)(2,1)S(1)}, bf16[64,4096]{1,0:T(8,128)(2,1)}, u32[]{:S(2)}, u32[]{:S(2)}) %collective-permute-start.2) | collective-permute-done | bytes 524320 | tf_op jit(solution)/shard_map/ppermute | solution.py:26
  38.8 10.0 %collective-permute-done.5 = bf16[64,4096]{1,0:T(8,128)(2,1)S(1)} collective-permute-done((bf16[64,4096]{1,0:T(8,128)(2,1)S(1)}, bf16[64,4096]{1,0:T(8,128)(2,1)S(1)}, u32[]{:S(2)}, u32[]{:S(2)}) %collective-permute-start.5) | collective-permute-done | bytes 524320 | tf_op jit(solution)/shard_map/ppermute | solution.py:136
  48.7 2.1 %maximum_bitcast_fusion = bf16[1,2,64,4096]{3,2,1,0:T(8,128)(2,1)} fusion(bf16[1,64,4096]{2,1,0:T(8,128)(2,1)S(1)} %bitcast.92, bf16[1,64,4096]{2,1,0:T(8,128)(2,1)} %bitcast.12), kind=kLoop, calls=%fused_computation.22 | loop fusion | flops 524288 | bytes 2097152 | tf_op jit(solution)/shard_map/reshape | solution.py:138
  (8 shorter events, 0.1 us)
Async XLA Ops:
  0.0 7.6 %copy-start = (s32[1,4]{1,0:T(1,128)S(1)}, s32[1,4]{1,0:T(1,128)}, u32[]{:S(2)}) copy-start(s32[1,4]{1,0:T(1,128)} %param.5) | copy-start | bytes 52
  0.0 7.4 %copy-start.1 = (s32[1,4,8]{2,1,0:T(4,128)S(1)}, s32[1,4,8]{2,1,0:T(4,128)}, u32[]{:S(2)}) copy-start(s32[1,4,8]{2,1,0:T(4,128)} %param.6) | copy-start | bytes 388
  3.1 9.4 %collective-permute-start = (bf16[64,2048]{1,0:T(8,128)(2,1)S(1)}, bf16[64,2048]{1,0:T(8,128)(2,1)S(1)}, u32[]{:S(2)}, u32[]{:S(2)}) collective-permute-start(bf16[64,2048]{1,0:T(8,128)(2,1)S(1)} %get-tuple-element.16), channel_id=1, source_target_pairs={{0,2},{1,3},{2,0},{3,1},{4,6},{5,7},{6,4},{7,5},{8,10},{9,11},{10,... | collective-permute-start | bytes 786440 | tf_op jit(solution)/shard_map/ppermute | solution.py:60
  12.5 7.5 %collective-permute-start.1 = (bf16[64,2048]{1,0:T(8,128)(2,1)S(1)}, bf16[64,2048]{1,0:T(8,128)(2,1)S(1)}, u32[]{:S(2)}, u32[]{:S(2)}) collective-permute-start(bf16[64,2048]{1,0:T(8,128)(2,1)S(1)} %broadcast_select_fusion.2), channel_id=1, source_target_pairs={{0,1},{1,0},{2,3},{3,2},{4,5},{5,4},{6,7},{7,6},{8,9},{9,8},{10,11... | collective-permute-start | bytes 786440 | tf_op jit(solution)/shard_map/ppermute | solution.py:65
  14.7 8.3 %collective-permute-start.3 = (bf16[64,2048]{1,0:T(8,128)(2,1)S(1)}, bf16[64,2048]{1,0:T(8,128)(2,1)S(1)}, u32[]{:S(2)}, u32[]{:S(2)}) collective-permute-start(bf16[64,2048]{1,0:T(8,128)(2,1)S(1)} %get-tuple-element.8), channel_id=1, source_target_pairs={{0,2},{1,3},{2,0},{3,1},{4,6},{5,7},{6,4},{7,5},{8,10},{9,11},{10,... | collective-permute-start | bytes 786440 | tf_op jit(solution)/shard_map/ppermute | solution.py:60
  23.1 6.7 %collective-permute-start.4 = (bf16[64,2048]{1,0:T(8,128)(2,1)S(1)}, bf16[64,2048]{1,0:T(8,128)(2,1)S(1)}, u32[]{:S(2)}, u32[]{:S(2)}) collective-permute-start(bf16[64,2048]{1,0:T(8,128)(2,1)S(1)} %get-tuple-element.9), channel_id=1, source_target_pairs={{0,1},{1,0},{2,3},{3,2},{4,5},{5,4},{6,7},{7,6},{8,9},{9,8},{10,11... | collective-permute-start | bytes 786440 | tf_op jit(solution)/shard_map/ppermute | solution.py:65
  24.6 14.2 %collective-permute-start.2 = (bf16[64,4096]{1,0:T(8,128)(2,1)S(1)}, bf16[64,4096]{1,0:T(8,128)(2,1)}, u32[]{:S(2)}, u32[]{:S(2)}) collective-permute-start(bf16[64,4096]{1,0:T(8,128)(2,1)S(1)} %convert_element_type.49), channel_id=1, source_target_pairs={{0,8},{8,16},{16,24},{24,0},{1,9},{9,17},{17,25},{25,1},{2,10},{10... | collective-permute-start | bytes 1572872 | tf_op jit(solution)/shard_map/ppermute | solution.py:26
  32.7 16.1 %collective-permute-start.5 = (bf16[64,4096]{1,0:T(8,128)(2,1)S(1)}, bf16[64,4096]{1,0:T(8,128)(2,1)S(1)}, u32[]{:S(2)}, u32[]{:S(2)}) collective-permute-start(bf16[64,4096]{1,0:T(8,128)(2,1)S(1)} %convert_element_type.55), channel_id=1, source_target_pairs={{0,12},{4,8},{8,20},{12,16},{16,28},{20,24},{24,4},{28,0},{1,13},{... | collective-permute-start | bytes 1572872 | tf_op jit(solution)/shard_map/ppermute | solution.py:136

commit v12 on v11

--- a/solution.py
+++ b/solution.py
@@ -134,7 +134,8 @@
                 (section * replicas + rep, (section + 1) % sections * replicas + (rep ^ 1))
             )
     sent.append(lax.ppermute(given_out, ("section", "dp"), pairs))
-    out = jnp.stack(sent, axis=0)
+    out = lax.optimization_barrier(jnp.stack([sent[0], sent[0]], axis=0))
+    out = lax.dynamic_update_slice_in_dim(out, sent[1][None], 1, 0)
     return out.reshape(1, RPR, seg_len, D)
 
 

time: 51.1 us -> 50.6 us (level)
  waiting for transfers between devices: 24.1 us -> 23.2 us
  local copies, waits for them, and re-layouts: 3.41 us -> 4.24 us
    reshape x1 -> x0, other arithmetic: 2.11 us -> none  [shards(): return out.reshape(1, RPR, seg_len, D)]
    another operation x0 -> x1, other arithmetic: none -> 1.06 us  [shards(): out = lax.optimization_barrier(jnp.stack([sent[0], sent[0]], axis=0))]
    dynamic_update_slice x0 -> x1, local copies, waits for them, and re-layouts: none -> 0.83 us  [shards(): out = lax.dynamic_update_slice_in_dim(out, sent[1][None], 1, 0)]
    select_n x2, other arithmetic: 0.09 us -> 0.8 us  [gathered(): onward = jnp.where(odd, over_y, block)]
    ppermute x1, waiting for transfers between devices: 9.96 us -> 9.43 us  [shards(): sent.append(lax.ppermute(given_out, ('section', 'dp'), pairs))]
    ppermute x1, waiting for transfers between devices: 6.04 us -> 5.52 us  [passed_along(): return lax.ppermute(value, axis, pairs)]
  transfers between devices with their start and end apart: 6 -> 6, of which waited for: 5 -> 5; matrix products, arithmetic and copies ran while one was open for 18% -> 20% of each run, Pallas kernels for 0% -> 0%
where the time goes in v12:
time: 50.6 us; the launch traced here: 50.4 us
  waiting for transfers between devices  23.2 us (46%)
  starting transfers between devices  9.49 us (19%)
  other arithmetic  8.07 us (16%)
  local copies, waits for them, and re-layouts  4.24 us (8%)
  between operations  3.54 us (7%)
  matrix products  1.83 us (4%)
    ppermute x1, waiting for transfers between devices, shards(): sent.append(lax.ppermute(given_out, ('section', 'dp'), pairs))  9.43 us
    ppermute x2, waiting for transfers between devices, gathered(): over_x = lax.ppermute(onward, 'seq', [(j, j ^ 1) for j in range(4)])  7.12 us
    ppermute x1, waiting for transfers between devices, passed_along(): return lax.ppermute(value, axis, pairs)  5.52 us
    ppermute x2, starting transfers between devices, gathered(): over_y = lax.ppermute(block, 'seq', [(j, j ^ 2) for j in range(4)])  4.65 us
    ppermute x2, starting transfers between devices, gathered(): over_x = lax.ppermute(onward, 'seq', [(j, j ^ 1) for j in range(4)])  3.22 us
    sub x2, other arithmetic, attend_row(): weights = jnp.where(allowed, jnp.exp(scores - row_top), 0.0)  1.94 us
    convert_element_type x4, local copies, waits for them, and re-layouts, attend_row(): return result.reshape(seg_len, D).astype(jnp.bfloat16)  1.59 us
    ppermute x1, starting transfers between devices, passed_along(): return lax.ppermute(value, axis, pairs)  1.57 us
  transfers between devices with their start and end apart: 6, of which 5 were waited for; matrix products, arithmetic and copies ran while one was open for 20% of the time, Pallas kernels for 0%

profile of v12, /device:TPU:0, one launch (start us, length us, event | category | flops | bytes accessed | tf_op | source)
XLA Modules:
  0.0 50.4 jit_solution(159814634739980695)
XLA Ops:
  0.0 0.0 copy-start
  0.0 0.0 copy-start.1
  0.0 1.3 %fusion.34 = s32[]{:T(128)} fusion(s32[1,2]{1,0:T(1,128)} %param.7, s32[]{:T(128)S(6)} %axis_index.23), kind=kLoop, calls=%fused_computation.72 | loop fusion | flops 5 | bytes 16 | tf_op jit(solution)/shard_map/reduce_sum | solution.py:94
  2.0 1.1 %select_bitcast_fusion.1 = (bf16[64,2048]{1,0:T(8,128)(2,1)S(1)}, bf16[64,2048]{1,0:T(8,128)(2,1)S(1)}) fusion(pred[]{:T(512)S(6)} %eq.44, bf16[2,64,6144]{2,1,0:T(8,128)(2,1)} %bitcast.88), kind=kLoop, calls=%fused_computation.47 | loop fusion | flops 262144 | bytes 1048577 | tf_op jit(solution)/shard_map/jit(_where)/select_n | solution.py:122
  3.1 3.1 %collective-permute-start = (bf16[64,2048]{1,0:T(8,128)(2,1)S(1)}, bf16[64,2048]{1,0:T(8,128)(2,1)S(1)}, u32[]{:S(2)}, u32[]{:S(2)}) collective-permute-start(bf16[64,2048]{1,0:T(8,128)(2,1)S(1)} %get-tuple-element.16), channel_id=1, source_target_pairs={{0,2},{1,3},{2,0},{3,1},{4,6},{5,7},{6,4},{7,5},{8,10},{9,11},{10,... | collective-permute-start | bytes 786440 | tf_op jit(solution)/shard_map/ppermute | solution.py:60
  6.1 1.3 %select_bitcast_fusion = (bf16[64,4096]{1,0:T(8,128)(2,1)S(1)}, bf16[1,64,4096]{2,1,0:T(8,128)(2,1)S(1)}) fusion(pred[]{:T(512)S(6)} %eq.44, bf16[2,64,6144]{2,1,0:T(8,128)(2,1)} %bitcast.89), kind=kLoop, calls=%fused_computation.37 | loop fusion | flops 524288 | bytes 2097153 | tf_op jit(solution)/shard_map/jit(_where)/select_n | solution.py:126
  7.4 0.0 copy-done.1
  7.4 0.2 reduce_window_sum.11
  7.6 0.0 copy-done
  7.6 0.1 constant_dynamic-slice_fusion
  7.7 0.6 %fusion.39 = (s32[1,1]{1,0:T(1,128)}, s32[1,1]{1,0:T(1,128)}) fusion(s32[1,2]{1,0:T(1,128)S(1)} %constant_dynamic-slice_fusion), kind=kLoop, calls=%fused_computation.78 | loop fusion | bytes 16 | tf_op jit(solution)/shard_map/slice | solution.py:107
  8.3 0.1 pad_add_fusion
  11.1 0.1 convert_reduce_fusion.2
  11.2 0.1 convert_reduce_fusion
  11.2 1.2 %collective-permute-done = bf16[64,2048]{1,0:T(8,128)(2,1)S(1)} collective-permute-done((bf16[64,2048]{1,0:T(8,128)(2,1)S(1)}, bf16[64,2048]{1,0:T(8,128)(2,1)S(1)}, u32[]{:S(2)}, u32[]{:S(2)}) %collective-permute-start) | collective-permute-done | bytes 262176 | tf_op jit(solution)/shard_map/ppermute | solution.py:60
  12.5 1.8 %collective-permute-start.1 = (bf16[64,2048]{1,0:T(8,128)(2,1)S(1)}, bf16[64,2048]{1,0:T(8,128)(2,1)S(1)}, u32[]{:S(2)}, u32[]{:S(2)}) collective-permute-start(bf16[64,2048]{1,0:T(8,128)(2,1)S(1)} %broadcast_select_fusion.2), channel_id=1, source_target_pairs={{0,1},{1,0},{2,3},{3,2},{4,5},{5,4},{6,7},{7,6},{8,9},{9,8},{10,11... | collective-permute-start | bytes 786440 | tf_op jit(solution)/shard_map/ppermute | solution.py:65
  14.2 0.4 select_n.138
  14.6 0.1 compare_and_fusion
  14.7 1.6 %collective-permute-start.3 = (bf16[64,2048]{1,0:T(8,128)(2,1)S(1)}, bf16[64,2048]{1,0:T(8,128)(2,1)S(1)}, u32[]{:S(2)}, u32[]{:S(2)}) collective-permute-start(bf16[64,2048]{1,0:T(8,128)(2,1)S(1)} %get-tuple-element.8), channel_id=1, source_target_pairs={{0,2},{1,3},{2,0},{3,1},{4,6},{5,7},{6,4},{7,5},{8,10},{9,11},{10,... | collective-permute-start | bytes 786440 | tf_op jit(solution)/shard_map/ppermute | solution.py:60
  16.3 3.7 %collective-permute-done.1 = bf16[64,2048]{1,0:T(8,128)(2,1)S(1)} collective-permute-done((bf16[64,2048]{1,0:T(8,128)(2,1)S(1)}, bf16[64,2048]{1,0:T(8,128)(2,1)S(1)}, u32[]{:S(2)}, u32[]{:S(2)}) %collective-permute-start.1) | collective-permute-done | bytes 262176 | tf_op jit(solution)/shard_map/ppermute | solution.py:65
  20.0 0.1 pad_maximum_fusion.1
  20.1 0.1 slice_bitcast_fusion.3
  20.1 0.1 copy.36
  20.2 0.1 copy.35
  20.3 0.5 fusion.26
  20.7 1.0 %fusion.40 = (f32[8,4,64]{2,1,0:T(4,128)S(1)}, bf16[8,4,64,192]{3,2,1,0:T(8,128)(2,1)S(1)}) fusion(f32[8,192,64,4]{1,2,3,0:T(8,128)S(1)} %fusion.26, pred[64,192]{1,0:T(8,128)(4,1)S(1)} %get-tuple-element.26), kind=kOutput, calls=%fused_computation.79 | output fusion | flops 2752703 | bytes 2379776 | tf_op jit(solution)/shard_map/sub | solution.py:48
  21.7 0.5 fusion.14
  22.2 0.4 copy.18
  22.6 0.4 convert_element_type.49
  23.0 0.0 collective-permute-done.3
  23.0 0.8 %broadcast_select_fusion.1 = (bf16[64,2048]{1,0:T(8,128)(2,1)}, bf16[192,2048]{1,0:T(8,128)(2,1)S(1)}) fusion(bf16[64,2048]{1,0:T(8,128)(2,1)S(1)} %collective-permute-done.3, bf16[64,2048]{1,0:T(8,128)(2,1)S(1)} %get-tuple-element.8, pred[]{:T(512)S(6)} %eq.45), kind=kLoop, calls=%fused_computation.49 | loop fusion | flops 131071 | bytes 1048577 | tf_op jit(solution)/shard_map/jit(_where)/select_n | solution.py:62
  23.8 1.4 %collective-permute-start.4 = (bf16[64,2048]{1,0:T(8,128)(2,1)}, bf16[64,2048]{1,0:T(8,128)(2,1)S(1)}, u32[]{:S(2)}, u32[]{:S(2)}) collective-permute-start(bf16[64,2048]{1,0:T(8,128)(2,1)} %get-tuple-element.9), channel_id=1, source_target_pairs={{0,1},{1,0},{2,3},{3,2},{4,5},{5,4},{6,7},{7,6},{8,9},{9,8},{10,11... | collective-permute-start | bytes 786440 | tf_op jit(solution)/shard_map/ppermute | solution.py:65
  25.2 1.6 %collective-permute-start.2 = (bf16[64,4096]{1,0:T(8,128)(2,1)S(1)}, bf16[64,4096]{1,0:T(8,128)(2,1)S(1)}, u32[]{:S(2)}, u32[]{:S(2)}) collective-permute-start(bf16[64,4096]{1,0:T(8,128)(2,1)S(1)} %convert_element_type.49), channel_id=1, source_target_pairs={{0,8},{8,16},{16,24},{24,0},{1,9},{9,17},{17,25},{25,1},{2,10},{10... | collective-permute-start | bytes 1572872 | tf_op jit(solution)/shard_map/ppermute | solution.py:26
  26.8 0.4 reshape.72
  27.2 3.4 %collective-permute-done.4 = bf16[64,2048]{1,0:T(8,128)(2,1)S(1)} collective-permute-done((bf16[64,2048]{1,0:T(8,128)(2,1)}, bf16[64,2048]{1,0:T(8,128)(2,1)S(1)}, u32[]{:S(2)}, u32[]{:S(2)}) %collective-permute-start.4) | collective-permute-done | bytes 262176 | tf_op jit(solution)/shard_map/ppermute | solution.py:65
  30.6 0.1 slice_bitcast_fusion.1
  30.7 0.1 copy.38
  30.7 0.1 copy.37
  30.8 0.5 fusion.24
  31.3 1.0 %fusion.41 = (f32[8,4,64]{2,1,0:T(4,128)S(1)}, bf16[8,4,64,192]{3,2,1,0:T(8,128)(2,1)S(1)}) fusion(f32[8,192,64,4]{1,2,3,0:T(8,128)S(1)} %fusion.24, pred[64,192]{1,0:T(8,128)(4,1)S(1)} %get-tuple-element.25), kind=kOutput, calls=%fused_computation.80 | output fusion | flops 2752703 | bytes 2379776 | tf_op jit(solution)/shard_map/sub | solution.py:48
  32.2 0.5 fusion.15
  32.7 0.4 copy.22
  33.1 0.4 convert_element_type.55
  33.5 0.1 collective-permute-start.5
  33.6 5.5 %collective-permute-done.2 = bf16[64,4096]{1,0:T(8,128)(2,1)S(1)} collective-permute-done((bf16[64,4096]{1,0:T(8,128)(2,1)S(1)}, bf16[64,4096]{1,0:T(8,128)(2,1)S(1)}, u32[]{:S(2)}, u32[]{:S(2)}) %collective-permute-start.2) | collective-permute-done | bytes 524320 | tf_op jit(solution)/shard_map/ppermute | solution.py:26
  39.1 1.1 %pad_maximum_fusion = bf16[2,64,4096]{2,1,0:T(8,128)(2,1)} fusion(bf16[1,64,4096]{2,1,0:T(8,128)(2,1)S(1)} %bitcast.93), kind=kLoop, calls=%fused_computation.22 | loop fusion | flops 524288 | bytes 1572864 | tf_op jit(solution)/shard_map/stack | solution.py:137
  40.1 9.4 %collective-permute-done.5 = bf16[64,4096]{1,0:T(8,128)(2,1)S(1)} collective-permute-done((bf16[64,4096]{1,0:T(8,128)(2,1)S(1)}, bf16[64,4096]{1,0:T(8,128)(2,1)S(1)}, u32[]{:S(2)}, u32[]{:S(2)}) %collective-permute-start.5) | collective-permute-done | bytes 524320 | tf_op jit(solution)/shard_map/ppermute | solution.py:136
  49.6 0.8 %bitcast_dynamic-update-slice_fusion = bf16[1,2,64,4096]{3,2,1,0:T(8,128)(2,1)} fusion(bf16[1,2,64,4096]{3,2,1,0:T(8,128)(2,1)} %bitcast.92, bf16[64,4096]{1,0:T(8,128)(2,1)S(1)} %collective-permute-done.5), kind=kLoop, calls=%fused_computation.32 | loop fusion | bytes 1048576 | tf_op jit(solution)/shard_map/dynamic_update_slice | solution.py:138
  (8 shorter events, 0.1 us)
Async XLA Ops:
  0.0 7.6 %copy-start = (s32[1,4]{1,0:T(1,128)S(1)}, s32[1,4]{1,0:T(1,128)}, u32[]{:S(2)}) copy-start(s32[1,4]{1,0:T(1,128)} %param.5) | copy-start | bytes 52
  0.0 7.4 %copy-start.1 = (s32[1,4,8]{2,1,0:T(4,128)S(1)}, s32[1,4,8]{2,1,0:T(4,128)}, u32[]{:S(2)}) copy-start(s32[1,4,8]{2,1,0:T(4,128)} %param.6) | copy-start | bytes 388
  3.1 9.4 %collective-permute-start = (bf16[64,2048]{1,0:T(8,128)(2,1)S(1)}, bf16[64,2048]{1,0:T(8,128)(2,1)S(1)}, u32[]{:S(2)}, u32[]{:S(2)}) collective-permute-start(bf16[64,2048]{1,0:T(8,128)(2,1)S(1)} %get-tuple-element.16), channel_id=1, source_target_pairs={{0,2},{1,3},{2,0},{3,1},{4,6},{5,7},{6,4},{7,5},{8,10},{9,11},{10,... | collective-permute-start | bytes 786440 | tf_op jit(solution)/shard_map/ppermute | solution.py:60
  12.5 7.5 %collective-permute-start.1 = (bf16[64,2048]{1,0:T(8,128)(2,1)S(1)}, bf16[64,2048]{1,0:T(8,128)(2,1)S(1)}, u32[]{:S(2)}, u32[]{:S(2)}) collective-permute-start(bf16[64,2048]{1,0:T(8,128)(2,1)S(1)} %broadcast_select_fusion.2), channel_id=1, source_target_pairs={{0,1},{1,0},{2,3},{3,2},{4,5},{5,4},{6,7},{7,6},{8,9},{9,8},{10,11... | collective-permute-start | bytes 786440 | tf_op jit(solution)/shard_map/ppermute | solution.py:65
  14.7 8.3 %collective-permute-start.3 = (bf16[64,2048]{1,0:T(8,128)(2,1)S(1)}, bf16[64,2048]{1,0:T(8,128)(2,1)S(1)}, u32[]{:S(2)}, u32[]{:S(2)}) collective-permute-start(bf16[64,2048]{1,0:T(8,128)(2,1)S(1)} %get-tuple-element.8), channel_id=1, source_target_pairs={{0,2},{1,3},{2,0},{3,1},{4,6},{5,7},{6,4},{7,5},{8,10},{9,11},{10,... | collective-permute-start | bytes 786440 | tf_op jit(solution)/shard_map/ppermute | solution.py:60
  23.8 6.8 %collective-permute-start.4 = (bf16[64,2048]{1,0:T(8,128)(2,1)}, bf16[64,2048]{1,0:T(8,128)(2,1)S(1)}, u32[]{:S(2)}, u32[]{:S(2)}) collective-permute-start(bf16[64,2048]{1,0:T(8,128)(2,1)} %get-tuple-element.9), channel_id=1, source_target_pairs={{0,1},{1,0},{2,3},{3,2},{4,5},{5,4},{6,7},{7,6},{8,9},{9,8},{10,11... | collective-permute-start | bytes 786440 | tf_op jit(solution)/shard_map/ppermute | solution.py:65
  25.2 13.9 %collective-permute-start.2 = (bf16[64,4096]{1,0:T(8,128)(2,1)S(1)}, bf16[64,4096]{1,0:T(8,128)(2,1)S(1)}, u32[]{:S(2)}, u32[]{:S(2)}) collective-permute-start(bf16[64,4096]{1,0:T(8,128)(2,1)S(1)} %convert_element_type.49), channel_id=1, source_target_pairs={{0,8},{8,16},{16,24},{24,0},{1,9},{9,17},{17,25},{25,1},{2,10},{10... | collective-permute-start | bytes 1572872 | tf_op jit(solution)/shard_map/ppermute | solution.py:26
  33.5 16.1 %collective-permute-start.5 = (bf16[64,4096]{1,0:T(8,128)(2,1)S(1)}, bf16[64,4096]{1,0:T(8,128)(2,1)S(1)}, u32[]{:S(2)}, u32[]{:S(2)}) collective-permute-start(bf16[64,4096]{1,0:T(8,128)(2,1)S(1)} %convert_element_type.55), channel_id=1, source_target_pairs={{0,12},{4,8},{8,20},{12,16},{16,28},{20,24},{24,4},{28,0},{1,13},{... | collective-permute-start | bytes 1572872 | tf_op jit(solution)/shard_map/ppermute | solution.py:136

commit v13 on v12

--- a/solution.py
+++ b/solution.py
@@ -37,9 +37,10 @@
     query_doc = doc_of(query_pos, ends)
     key_doc = doc_of(key_pos, ends)
     allowed = (key_pos[None, :] <= query_pos[:, None]) & (key_doc[None, :] == query_doc[:, None])
-    queries = query_rows.reshape(seg_len, KV_HEADS, group_size, HD)
-    keys = key_rows.reshape(key_len, KV_HEADS, HD)
-    values = value_rows.reshape(key_len, KV_HEADS, HD)
+    kv_heads = key_rows.shape[1] // HD
+    queries = query_rows.reshape(seg_len, kv_heads, group_size, HD)
+    keys = key_rows.reshape(key_len, kv_heads, HD)
+    values = value_rows.reshape(key_len, kv_heads, HD)
     scores = (
         jnp.einsum("qkgd,skd->kgqs", queries, keys, preferred_element_type=jnp.float32)
         * HD ** (-0.5)
@@ -52,7 +53,7 @@
     result = summed / jnp.transpose(row_total, (2, 0, 1))[..., None]
     valid = (query_pos < length).astype(jnp.float32)
     result = result * valid[:, None, None, None]
-    return result.reshape(seg_len, D).astype(jnp.bfloat16)
+    return result.reshape(seg_len, kv_heads * group_size * HD).astype(jnp.bfloat16)
 
 
 def gathered(block, seq_index, seq_count, reach, hold=None):
@@ -96,6 +97,7 @@
     own_lengths = lax.dynamic_slice_in_dim(lengths_all, 2 * replica, 2, 0)
 
     def attend_own(query_rows, kv_local, pieces_and_chunks, first_is_kept):
+        width = kv_local.shape[1] // 2
         pieces = [kv_local]
         key_pos = [query_pos]
         for piece, chunk in pieces_and_chunks:
@@ -107,25 +109,46 @@
         length = jnp.where(first_is_kept, own_lengths[0], own_lengths[1])
         return attend_row(
             query_rows,
-            kv_all[:, :key_value_width],
-            kv_all[:, key_value_width:],
+            kv_all[:, :width],
+            kv_all[:, width:],
             query_pos,
             key_pos,
             ends,
             length,
         )
 
-    kept_kv = jnp.where(handed, own_rows[0, :, D:], own_rows[1, :, D:])
-    kept_pieces = gathered(kept_kv, seq_index, seq_count, reach)
-    kept_queries = jnp.where(handed, own_rows[0, :, :D], own_rows[1, :, :D])
-    kept_out = attend_own(kept_queries, kept_kv, kept_pieces, handed)
-    given_kv = jnp.where(handed, own_rows[1, :, D:], own_rows[0, :, D:])
-    given_kv = lax.optimization_barrier((given_kv, kept_pieces[0][0]))[0]
-    given_pieces = gathered(given_kv, seq_index, seq_count, reach, hold=kept_out)
-    sent = [passed_along(kept_out, "section", 1)]
-    given_queries = jnp.where(handed, own_rows[1, :, :D], own_rows[0, :, :D])
-    given_queries = lax.optimization_barrier((given_queries, kept_out))[0]
-    given_out = attend_own(given_queries, given_kv, given_pieces, jnp.logical_not(handed))
+    def columns(kv_from, kv_to):
+        per_kv = (H // KV_HEADS) * HD
+        queries = own_rows[:, :, kv_from * per_kv : kv_to * per_kv]
+        keys = own_rows[:, :, D + kv_from * HD : D + kv_to * HD]
+        values = own_rows[:, :, D + key_value_width + kv_from * HD : D + key_value_width + kv_to * HD]
+        return queries, jnp.concatenate([keys, values], axis=2)
+
+    half = KV_HEADS // 2
+    plan = [(True, 0, half), (True, half, KV_HEADS), (False, 0, KV_HEADS)]
+    outs = []
+    arrived = []
+    last_first = None
+    last_out = None
+    for is_kept, kv_from, kv_to in plan:
+        queries, kv_rows = columns(kv_from, kv_to)
+        pick = handed if is_kept else jnp.logical_not(handed)
+        kv_local = jnp.where(pick, kv_rows[0], kv_rows[1])
+        if last_first is not None:
+            kv_local = lax.optimization_barrier((kv_local, last_first))[0]
+        pieces = gathered(kv_local, seq_index, seq_count, reach, hold=last_out)
+        query_rows = jnp.where(pick, queries[0], queries[1])
+        if len(arrived) == 1:
+            query_rows = lax.optimization_barrier((query_rows, arrived[0]))[0]
+        elif last_out is not None:
+            query_rows = lax.optimization_barrier((query_rows, last_out))[0]
+        out = attend_own(query_rows, kv_local, pieces, pick)
+        if is_kept:
+            arrived.append(passed_along(out, "section", 1))
+        outs.append(out)
+        last_first = pieces[0][0]
+        last_out = out
+    sent = arrived
     sections = lax.axis_size("section")
     pairs = []
     for section in range(sections):
@@ -133,7 +156,8 @@
             pairs.append(
                 (section * replicas + rep, (section + 1) % sections * replicas + (rep ^ 1))
             )
-    sent.append(lax.ppermute(given_out, ("section", "dp"), pairs))
+    given_next = lax.ppermute(outs[2], ("section", "dp"), pairs)
+    sent = [jnp.concatenate(sent, axis=1), given_next]
     out = lax.optimization_barrier(jnp.stack([sent[0], sent[0]], axis=0))
     out = lax.dynamic_update_slice_in_dim(out, sent[1][None], 1, 0)
     return out.reshape(1, RPR, seg_len, D)

time: 50.6 us -> 58.2 us (1.15)
  waiting for transfers between devices: 23.2 us -> 26.9 us
  local copies, waits for them, and re-layouts: 4.24 us -> 7.41 us
  matrix products: 1.83 us -> 3.42 us
  other arithmetic: 8.07 us -> 7.1 us
    ppermute x1, waiting for transfers between devices: 9.43 us -> 13.4 us  [shards(): given_next = lax.ppermute(outs[2], ('section', 'dp'), pairs)]
    ppermute x2 -> x3, waiting for transfers between devices: 7.12 us -> 9.61 us  [gathered(): over_x = lax.ppermute(onward, 'seq', [(j, j ^ 1) for j in range(4)])]
    ppermute x1 -> x2, waiting for transfers between devices: 5.52 us -> 3.84 us  [passed_along(): return lax.ppermute(value, axis, pairs)]
    dot_general x2 -> x3, matrix products: 0.91 us -> 2.32 us  [attend_row(): jnp.einsum('kgqs,skd->qkgd', rounded, values, preferred_element_type=jnp....]
    slice x0 -> x3, local copies, waits for them, and re-layouts: none -> 1.21 us  [the longest x1 1.16 us: columns(): own_rows[:, :, D + key_value_width + kv_from * HD:D + key_value_width + k...]
    ppermute x2 -> x3, waiting for transfers between devices: 1.17 us -> 0.07 us  [gathered(): over_y = lax.ppermute(block, 'seq', [(j, j ^ 2) for j in range(4)])]
    reshape x1 -> x6, local copies, waits for them, and re-layouts: 0.37 us -> 1.42 us  [the longest x2 0.78 us: attend_row(): values = value_rows.reshape(key_len, kv_heads, HD)]
    select_n x2 -> x4, other arithmetic: 2.34 us -> 1.56 us  [the longest x3 1.5 us: shards(): kv_local = jnp.where(pick, kv_rows[0], kv_rows[1])]
  transfers between devices with their start and end apart: 6 -> 9, of which waited for: 5 -> 6; matrix products, arithmetic and copies ran while one was open for 20% -> 23% of each run, Pallas kernels for 0% -> 0%
where the time goes in v13:
time: 58.2 us; the launch traced here: 57.9 us
  waiting for transfers between devices  26.9 us (46%)
  starting transfers between devices  9.45 us (16%)
  local copies, waits for them, and re-layouts  7.41 us (13%)
  other arithmetic  7.1 us (12%)
  between operations  3.62 us (6%)
  matrix products  3.42 us (6%)
    ppermute x1, waiting for transfers between devices, shards(): given_next = lax.ppermute(outs[2], ('section', 'dp'), pairs)  13.4 us
    ppermute x3, waiting for transfers between devices, gathered(): over_x = lax.ppermute(onward, 'seq', [(j, j ^ 1) for j in range(4)])  9.61 us
    ppermute x3, starting transfers between devices, gathered(): over_y = lax.ppermute(block, 'seq', [(j, j ^ 2) for j in range(4)])  4.14 us
    ppermute x2, waiting for transfers between devices, passed_along(): return lax.ppermute(value, axis, pairs)  3.84 us
    ppermute x3, starting transfers between devices, gathered(): over_x = lax.ppermute(onward, 'seq', [(j, j ^ 1) for j in range(4)])  3.62 us
    dot_general x3, matrix products, attend_row(): jnp.einsum('kgqs,skd->qkgd', rounded, values, preferred_element_type=jnp....  2.32 us
    convert_element_type x6, local copies, waits for them, and re-layouts, attend_row(): result.reshape(seg_len, kv_heads * group_size * HD).astype(jnp.bfloat16)  2.27 us
    sub x3, other arithmetic, attend_row(): weights = jnp.where(allowed, jnp.exp(scores - row_top), 0.0)  1.76 us
  transfers between devices with their start and end apart: 9, of which 6 were waited for; matrix products, arithmetic and copies ran while one was open for 23% of the time, Pallas kernels for 0%

profile of v13, /device:TPU:0, one launch (start us, length us, event | category | flops | bytes accessed | tf_op | source)
XLA Modules:
  0.0 57.9 jit_solution(251733468426364407)
XLA Ops:
  0.0 1.2 %fusion.84 = (bf16[2,64,512]{2,1,0:T(8,128)(2,1)S(1)}, bf16[2,64,512]{2,1,0:T(8,128)(2,1)S(1)}, bf16[2,64,512]{2,1,0:T(8,128)(2,1)S(1)}, bf16[2,64,512]{2,1,0:T(8,128)(2,1)S(1)}) fusion(bf16[2,64,6144]{2,1,0:T(8,128)(2,1)} %bitcast.85), kind=kLoop, calls=%fused_computation.117 | loop fusion | bytes 1048576 | tf_op jit(solution)/shard_map/slice | solution.py:124
  1.2 1.3 %fusion.80 = s32[]{:T(128)} fusion(s32[1,2]{1,0:T(1,128)} %param.7, s32[]{:T(128)S(6)} %axis_index.23), kind=kLoop, calls=%fused_computation.112 | loop fusion | flops 5 | bytes 16 | tf_op jit(solution)/shard_map/reduce_sum | solution.py:95
  3.2 3.1 %collective-permute-start = (bf16[64,1024]{1,0:T(8,128)(2,1)S(1)}, bf16[64,1024]{1,0:T(8,128)(2,1)S(1)}, u32[]{:S(2)}, u32[]{:S(2)}) collective-permute-start(bf16[64,1024]{1,0:T(8,128)(2,1)S(1)} %fusion.62), channel_id=1, source_target_pairs={{0,2},{1,3},{2,0},{3,1},{4,6},{5,7},{6,4},{7,5},{8,10},{9,11},{10,... | collective-permute-start | bytes 393224 | tf_op jit(solution)/shard_map/ppermute | solution.py:61
  6.2 0.1 constant_dynamic-slice_fusion
  6.3 0.6 %fusion.87 = (s32[1,1]{1,0:T(1,128)}, s32[1,1]{1,0:T(1,128)}) fusion(s32[1,2]{1,0:T(1,128)S(1)} %constant_dynamic-slice_fusion), kind=kLoop, calls=%fused_computation.120 | loop fusion | bytes 16 | tf_op jit(solution)/shard_map/slice | solution.py:109
  9.6 1.4 %fusion.49 = (bf16[64,2048]{1,0:T(8,128)(2,1)S(1)}, bf16[64,2048]{1,0:T(8,128)(2,1)S(1)}, bf16[1,64,2048]{2,1,0:T(8,128)(2,1)S(1)}) fusion(bf16[2,64,6144]{2,1,0:T(8,128)(2,1)} %bitcast.86, pred[]{:T(512)S(6)} %not.3, pred[]{:T(512)S(6)} %eq.26), kind=kLoop, calls=%fused_computation.58 | loop fusion | flops 393216 | bytes 2359298 | tf_op jit(solution)/shard_map/jit(_where)/select_n | solution.py:136
  11.0 0.2 reduce_window_sum.11
  11.2 0.1 pad_add_fusion
  11.3 0.1 convert_reduce_fusion.2
  11.4 0.1 convert_reduce_fusion
  11.5 0.1 compare_and_fusion
  11.6 1.6 %collective-permute-start.1 = (bf16[64,1024]{1,0:T(8,128)(2,1)S(1)}, bf16[64,1024]{1,0:T(8,128)(2,1)S(1)}, u32[]{:S(2)}, u32[]{:S(2)}) collective-permute-start(bf16[64,1024]{1,0:T(8,128)(2,1)S(1)} %broadcast_select_fusion.2), channel_id=1, source_target_pairs={{0,1},{1,0},{2,3},{3,2},{4,5},{5,4},{6,7},{7,6},{8,9},{9,8},{10,11... | collective-permute-start | bytes 393224 | tf_op jit(solution)/shard_map/ppermute | solution.py:66
  13.2 0.2 select_n.181
  13.4 0.6 collective-permute-start.3
  14.0 2.7 %collective-permute-done.1 = bf16[64,1024]{1,0:T(8,128)(2,1)S(1)} collective-permute-done((bf16[64,1024]{1,0:T(8,128)(2,1)S(1)}, bf16[64,1024]{1,0:T(8,128)(2,1)S(1)}, u32[]{:S(2)}, u32[]{:S(2)}) %collective-permute-start.1) | collective-permute-done | bytes 131104 | tf_op jit(solution)/shard_map/ppermute | solution.py:66
  16.8 0.3 fusion.26
  17.2 0.4 fusion.88
  17.6 0.4 fusion.33
  18.0 0.2 copy.23
  18.2 0.2 convert_element_type.61
  18.4 0.1 collective-permute-done.3
  18.5 1.5 %collective-permute-start.4 = (bf16[64,1024]{1,0:T(8,128)(2,1)S(1)}, bf16[64,1024]{1,0:T(8,128)(2,1)S(1)}, u32[]{:S(2)}, u32[]{:S(2)}) collective-permute-start(bf16[64,1024]{1,0:T(8,128)(2,1)S(1)} %get-tuple-element.12), channel_id=1, source_target_pairs={{0,1},{1,0},{2,3},{3,2},{4,5},{5,4},{6,7},{7,6},{8,9},{9,8},{10,11... | collective-permute-start | bytes 393224 | tf_op jit(solution)/shard_map/ppermute | solution.py:66
  20.0 1.6 %collective-permute-start.2 = (bf16[64,2048]{1,0:T(8,128)(2,1)S(1)}, bf16[64,2048]{1,0:T(8,128)(2,1)S(1)}, u32[]{:S(2)}, u32[]{:S(2)}) collective-permute-start(bf16[64,2048]{1,0:T(8,128)(2,1)S(1)} %convert_element_type.61), channel_id=1, source_target_pairs={{0,8},{8,16},{16,24},{24,0},{1,9},{9,17},{17,25},{25,1},{2,10},{10... | collective-permute-start | bytes 786440 | tf_op jit(solution)/shard_map/ppermute | solution.py:26
  21.6 0.5 collective-permute-start.6
  22.1 1.4 %collective-permute-done.4 = bf16[64,1024]{1,0:T(8,128)(2,1)S(1)} collective-permute-done((bf16[64,1024]{1,0:T(8,128)(2,1)S(1)}, bf16[64,1024]{1,0:T(8,128)(2,1)S(1)}, u32[]{:S(2)}, u32[]{:S(2)}) %collective-permute-start.4) | collective-permute-done | bytes 131104 | tf_op jit(solution)/shard_map/ppermute | solution.py:66
  23.6 0.7 %reshape.86 = bf16[192,4,128]{2,1,0:T(4,128)(2,1)} reshape(bf16[192,512]{1,0:T(8,128)(2,1)S(1)} %get-tuple-element.30) | data formatting | bytes 393216 | tf_op jit(solution)/shard_map/reshape | solution.py:43
  24.3 3.8 %collective-permute-done.2 = bf16[64,2048]{1,0:T(8,128)(2,1)S(1)} collective-permute-done((bf16[64,2048]{1,0:T(8,128)(2,1)S(1)}, bf16[64,2048]{1,0:T(8,128)(2,1)S(1)}, u32[]{:S(2)}, u32[]{:S(2)}) %collective-permute-start.2) | collective-permute-done | bytes 262176 | tf_op jit(solution)/shard_map/ppermute | solution.py:26
  28.2 0.2 reshape.88
  28.4 0.5 copy-done.2
  28.9 0.3 fusion.25
  29.2 0.4 fusion.89
  29.6 1.5 %fusion.32 = bf16[64,4,4,128]{3,0,2,1:T(8,128)(2,1)S(1)} fusion(f32[64,4,4]{0,2,1:T(4,128)S(1)} %bitcast.97, f32[64]{0:T(128)S(1)} %get-tuple-element.47, bf16[192,4,128,1]{2,1,0,3:T(4,128)(2,1)} %bitcast.93, f32[4,4,64,192]{3,2,1,0:T(8,128)S(1)} %fusion.25, pred[64,192]{1,0:T(8,128)(4,1)S(1)} %get-tuple-element.39), kind=kOutput, calls=%fused_computation.33 | convolution fusion | flops 51512512 | bytes 1261824 | tf_op jit(solution)/shard_map/kgqs,skd->qkgd/dot_general | solution.py:52
  31.1 0.2 copy.27
  31.3 0.9 %convert_element_type.64 = bf16[64,2048]{1,0:T(8,128)(2,1)} reshape(bf16[64,4,4,128]{3,2,1,0:T(4,128)(2,1)S(1)} %copy.27) | data formatting | bytes 524288 | tf_op jit(solution)/shard_map/convert_element_type | solution.py:56
  32.2 0.8 %broadcast_select_fusion = (bf16[64,2048]{1,0:T(8,128)(2,1)}, bf16[192,2048]{1,0:T(8,128)(2,1)S(1)}) fusion(bf16[64,2048]{1,0:T(8,128)(2,1)S(1)} %collective-permute-done.6, bf16[64,2048]{1,0:T(8,128)(2,1)S(1)} %get-tuple-element.14, pred[]{:T(512)S(6)} %eq.27), kind=kLoop, calls=%fused_computation.68 | loop fusion | flops 131071 | bytes 1048577 | tf_op jit(solution)/shard_map/jit(_where)/select_n | solution.py:63
  32.9 0.6 collective-permute-start.7
  33.6 0.4 reshape.92
  34.0 5.5 %collective-permute-done.7 = bf16[64,2048]{1,0:T(8,128)(2,1)S(1)} collective-permute-done((bf16[64,2048]{1,0:T(8,128)(2,1)}, bf16[64,2048]{1,0:T(8,128)(2,1)S(1)}, u32[]{:S(2)}, u32[]{:S(2)}) %collective-permute-start.7) | collective-permute-done | bytes 262176 | tf_op jit(solution)/shard_map/ppermute | solution.py:66
  39.6 0.1 copy.51
  39.7 0.1 copy.50
  39.8 0.5 fusion.39
  40.2 1.0 %fusion.90 = (f32[8,4,64]{2,1,0:T(4,128)S(1)}, bf16[8,4,64,192]{3,2,1,0:T(8,128)(2,1)S(1)}) fusion(f32[8,192,64,4]{1,2,3,0:T(8,128)S(1)} %fusion.39, pred[64,192]{1,0:T(8,128)(4,1)S(1)} %get-tuple-element.38), kind=kOutput, calls=%fused_computation.123 | output fusion | flops 2752703 | bytes 2379776 | tf_op jit(solution)/shard_map/sub | solution.py:49
  41.2 0.5 fusion.27
  41.7 0.4 copy.31
  42.1 0.4 convert_element_type.70
  42.6 1.1 %pad_maximum_fusion = bf16[2,64,4096]{2,1,0:T(8,128)(2,1)} fusion(bf16[1,64,4096]{2,1,0:T(8,128)(2,1)S(1)} %maximum_bitcast_fusion), kind=kLoop, calls=%fused_computation.35 | loop fusion | flops 524288 | bytes 1572864 | tf_op jit(solution)/shard_map/stack | solution.py:161
  43.7 13.4 %collective-permute-done.8 = bf16[64,4096]{1,0:T(8,128)(2,1)S(1)} collective-permute-done((bf16[64,4096]{1,0:T(8,128)(2,1)S(1)}, bf16[64,4096]{1,0:T(8,128)(2,1)S(1)}, u32[]{:S(2)}, u32[]{:S(2)}) %collective-permute-start.8) | collective-permute-done | bytes 524320 | tf_op jit(solution)/shard_map/ppermute | solution.py:159
  57.1 0.8 %bitcast_dynamic-update-slice_fusion = bf16[1,2,64,4096]{3,2,1,0:T(8,128)(2,1)} fusion(bf16[1,2,64,4096]{3,2,1,0:T(8,128)(2,1)} %bitcast.89, bf16[64,4096]{1,0:T(8,128)(2,1)S(1)} %collective-permute-done.8), kind=kLoop, calls=%fused_computation.43 | loop fusion | bytes 1048576 | tf_op jit(solution)/shard_map/dynamic_update_slice | solution.py:162
  (36 shorter events, 0.8 us)
Async XLA Ops:
  0.0 6.2 %copy-start = (s32[1,4]{1,0:T(1,128)S(1)}, s32[1,4]{1,0:T(1,128)}, u32[]{:S(2)}) copy-start(s32[1,4]{1,0:T(1,128)} %param.5) | copy-start | bytes 52
  0.0 11.0 %copy-start.4 = (s32[1,4,8]{2,1,0:T(4,128)S(1)}, s32[1,4,8]{2,1,0:T(4,128)}, u32[]{:S(2)}) copy-start(s32[1,4,8]{2,1,0:T(4,128)} %param.6) | copy-start | bytes 388
  3.2 8.4 %collective-permute-start = (bf16[64,1024]{1,0:T(8,128)(2,1)S(1)}, bf16[64,1024]{1,0:T(8,128)(2,1)S(1)}, u32[]{:S(2)}, u32[]{:S(2)}) collective-permute-start(bf16[64,1024]{1,0:T(8,128)(2,1)S(1)} %fusion.62), channel_id=1, source_target_pairs={{0,2},{1,3},{2,0},{3,1},{4,6},{5,7},{6,4},{7,5},{8,10},{9,11},{10,... | collective-permute-start | bytes 393224 | tf_op jit(solution)/shard_map/ppermute | solution.py:61
  11.6 5.0 %collective-permute-start.1 = (bf16[64,1024]{1,0:T(8,128)(2,1)S(1)}, bf16[64,1024]{1,0:T(8,128)(2,1)S(1)}, u32[]{:S(2)}, u32[]{:S(2)}) collective-permute-start(bf16[64,1024]{1,0:T(8,128)(2,1)S(1)} %broadcast_select_fusion.2), channel_id=1, source_target_pairs={{0,1},{1,0},{2,3},{3,2},{4,5},{5,4},{6,7},{7,6},{8,9},{9,8},{10,11... | collective-permute-start | bytes 393224 | tf_op jit(solution)/shard_map/ppermute | solution.py:66
  13.4 5.0 %collective-permute-start.3 = (bf16[64,1024]{1,0:T(8,128)(2,1)S(1)}, bf16[64,1024]{1,0:T(8,128)(2,1)S(1)}, u32[]{:S(2)}, u32[]{:S(2)}) collective-permute-start(bf16[64,1024]{1,0:T(8,128)(2,1)S(1)} %fusion.59), channel_id=1, source_target_pairs={{0,2},{1,3},{2,0},{3,1},{4,6},{5,7},{6,4},{7,5},{8,10},{9,11},{10,... | collective-permute-start | bytes 393224 | tf_op jit(solution)/shard_map/ppermute | solution.py:61
  18.5 5.0 %collective-permute-start.4 = (bf16[64,1024]{1,0:T(8,128)(2,1)S(1)}, bf16[64,1024]{1,0:T(8,128)(2,1)S(1)}, u32[]{:S(2)}, u32[]{:S(2)}) collective-permute-start(bf16[64,1024]{1,0:T(8,128)(2,1)S(1)} %get-tuple-element.12), channel_id=1, source_target_pairs={{0,1},{1,0},{2,3},{3,2},{4,5},{5,4},{6,7},{7,6},{8,9},{9,8},{10,11... | collective-permute-start | bytes 393224 | tf_op jit(solution)/shard_map/ppermute | solution.py:66
  20.0 8.2 %collective-permute-start.2 = (bf16[64,2048]{1,0:T(8,128)(2,1)S(1)}, bf16[64,2048]{1,0:T(8,128)(2,1)S(1)}, u32[]{:S(2)}, u32[]{:S(2)}) collective-permute-start(bf16[64,2048]{1,0:T(8,128)(2,1)S(1)} %convert_element_type.61), channel_id=1, source_target_pairs={{0,8},{8,16},{16,24},{24,0},{1,9},{9,17},{17,25},{25,1},{2,10},{10... | collective-permute-start | bytes 786440 | tf_op jit(solution)/shard_map/ppermute | solution.py:26
  21.6 10.6 %collective-permute-start.6 = (bf16[64,2048]{1,0:T(8,128)(2,1)S(1)}, bf16[64,2048]{1,0:T(8,128)(2,1)S(1)}, u32[]{:S(2)}, u32[]{:S(2)}) collective-permute-start(bf16[64,2048]{1,0:T(8,128)(2,1)S(1)} %get-tuple-element.14), channel_id=1, source_target_pairs={{0,2},{1,3},{2,0},{3,1},{4,6},{5,7},{6,4},{7,5},{8,10},{9,11},{10,... | collective-permute-start | bytes 786440 | tf_op jit(solution)/shard_map/ppermute | solution.py:61
  28.2 0.7 %copy-start.2 = (bf16[64,2048]{1,0:T(8,128)(2,1)}, bf16[64,2048]{1,0:T(8,128)(2,1)S(1)}, u32[]{:S(2)}) copy-start(bf16[64,2048]{1,0:T(8,128)(2,1)S(1)} %collective-permute-done.2) | copy-start | bytes 786436
  29.6 3.9 %copy-start.1 = (bf16[1,2,64,6144]{3,2,1,0:T(8,128)(2,1)S(1)}, bf16[1,2,64,6144]{3,2,1,0:T(8,128)(2,1)}, u32[]{:S(2)}) copy-start(bf16[1,2,64,6144]{3,2,1,0:T(8,128)(2,1)} %param.4) | copy-start | bytes 4718596
  32.9 6.6 %collective-permute-start.7 = (bf16[64,2048]{1,0:T(8,128)(2,1)}, bf16[64,2048]{1,0:T(8,128)(2,1)S(1)}, u32[]{:S(2)}, u32[]{:S(2)}) collective-permute-start(bf16[64,2048]{1,0:T(8,128)(2,1)} %get-tuple-element.15), channel_id=1, source_target_pairs={{0,1},{1,0},{2,3},{3,2},{4,5},{5,4},{6,7},{7,6},{8,9},{9,8},{10,11... | collective-permute-start | bytes 786440 | tf_op jit(solution)/shard_map/ppermute | solution.py:66
  33.6 9.0 %collective-permute-start.5 = (bf16[64,2048]{1,0:T(8,128)(2,1)}, bf16[64,2048]{1,0:T(8,128)(2,1)S(1)}, u32[]{:S(2)}, u32[]{:S(2)}) collective-permute-start(bf16[64,2048]{1,0:T(8,128)(2,1)} %convert_element_type.64), channel_id=1, source_target_pairs={{0,8},{8,16},{16,24},{24,0},{1,9},{9,17},{17,25},{25,1},{2,10},{10... | collective-permute-start | bytes 786440 | tf_op jit(solution)/shard_map/ppermute | solution.py:26
  41.6 1.0 %copy-start.3 = (bf16[64,2048]{1,0:T(8,128)(2,1)S(1)}, bf16[64,2048]{1,0:T(8,128)(2,1)}, u32[]{:S(2)}) copy-start(bf16[64,2048]{1,0:T(8,128)(2,1)} %copy-done.2) | copy-start | bytes 786436
  42.5 14.6 %collective-permute-start.8 = (bf16[64,4096]{1,0:T(8,128)(2,1)S(1)}, bf16[64,4096]{1,0:T(8,128)(2,1)S(1)}, u32[]{:S(2)}, u32[]{:S(2)}) collective-permute-start(bf16[64,4096]{1,0:T(8,128)(2,1)S(1)} %convert_element_type.70), channel_id=1, source_target_pairs={{0,12},{4,8},{8,20},{12,16},{16,28},{20,24},{24,4},{28,0},{1,13},{... | collective-permute-start | bytes 1572872 | tf_op jit(solution)/shard_map/ppermute | solution.py:159

commit v14 on v12

--- a/solution.py
+++ b/solution.py
@@ -91,7 +91,9 @@
     far = jnp.int32(4 * length_all)
 
     replicas = lax.axis_size("dp")
-    handed = jnp.sum(jnp.where(jnp.arange(replicas) == replica, hand_over[0], 0)) == 1
+    handed = hand_over[0, 0] == 1
+    for rep in range(1, replicas):
+        handed = jnp.where(replica == rep, hand_over[0, rep] == 1, handed)
     own_ends = lax.dynamic_slice_in_dim(doc_ends, 2 * replica, 2, 0)
     own_lengths = lax.dynamic_slice_in_dim(lengths_all, 2 * replica, 2, 0)
 

time: 50.6 us -> 51.2 us (1.012)
  other arithmetic: 8.07 us -> 6.75 us
  local copies, waits for them, and re-layouts: 4.24 us -> 5.54 us
  between operations: 3.54 us -> 4.11 us
    reduce_sum x1 -> x0, other arithmetic: 1.32 us -> none  [shards(): jnp.sum(jnp.where(jnp.arange(replicas) == replica, hand_over[0], 0)) == 1]
    slice x0 -> x1, local copies, waits for them, and re-layouts: none -> 1.3 us  [shards(): handed = hand_over[0, 0] == 1]
where the time goes in v14:
time: 51.2 us; the launch traced here: 51 us
  waiting for transfers between devices  23.2 us (45%)
  starting transfers between devices  9.49 us (19%)
  other arithmetic  6.75 us (13%)
  local copies, waits for them, and re-layouts  5.54 us (11%)
  between operations  4.11 us (8%)
  matrix products  1.83 us (4%)
    ppermute x1, waiting for transfers between devices, shards(): sent.append(lax.ppermute(given_out, ('section', 'dp'), pairs))  9.43 us
    ppermute x2, waiting for transfers between devices, gathered(): over_x = lax.ppermute(onward, 'seq', [(j, j ^ 1) for j in range(4)])  7.12 us
    ppermute x1, waiting for transfers between devices, passed_along(): return lax.ppermute(value, axis, pairs)  5.52 us
    ppermute x2, starting transfers between devices, gathered(): over_y = lax.ppermute(block, 'seq', [(j, j ^ 2) for j in range(4)])  4.65 us
    ppermute x2, starting transfers between devices, gathered(): over_x = lax.ppermute(onward, 'seq', [(j, j ^ 1) for j in range(4)])  3.2 us
    sub x2, other arithmetic, attend_row(): weights = jnp.where(allowed, jnp.exp(scores - row_top), 0.0)  1.94 us
    convert_element_type x4, local copies, waits for them, and re-layouts, attend_row(): return result.reshape(seg_len, D).astype(jnp.bfloat16)  1.59 us
    ppermute x1, starting transfers between devices, passed_along(): return lax.ppermute(value, axis, pairs)  1.58 us
  transfers between devices with their start and end apart: 6, of which 5 were waited for; matrix products, arithmetic and copies ran while one was open for 20% of the time, Pallas kernels for 0%

profile of v14, /device:TPU:0, one launch (start us, length us, event | category | flops | bytes accessed | tf_op | source)
XLA Modules:
  0.0 51.0 jit_solution(10040035827573562985)
XLA Ops:
  0.0 0.0 copy-start
  0.0 0.0 copy-start.1
  0.0 1.3 %fusion.39 = (s32[1,1]{1,0:T(1,128)}, s32[1,1]{1,0:T(1,128)}) fusion(s32[1,2]{1,0:T(1,128)} %param.7), kind=kLoop, calls=%fused_computation.77 | loop fusion | bytes 16 | tf_op jit(solution)/shard_map/slice | solution.py:94
  2.5 1.1 %select_bitcast_fusion.1 = (bf16[64,2048]{1,0:T(8,128)(2,1)S(1)}, bf16[64,2048]{1,0:T(8,128)(2,1)S(1)}) fusion(pred[]{:T(512)S(6)} %select_n.121, bf16[2,64,6144]{2,1,0:T(8,128)(2,1)} %bitcast.88), kind=kLoop, calls=%fused_computation.47 | loop fusion | flops 262144 | bytes 1048577 | tf_op jit(solution)/shard_map/jit(_where)/select_n | solution.py:124
  3.6 3.1 %collective-permute-start = (bf16[64,2048]{1,0:T(8,128)(2,1)S(1)}, bf16[64,2048]{1,0:T(8,128)(2,1)S(1)}, u32[]{:S(2)}, u32[]{:S(2)}) collective-permute-start(bf16[64,2048]{1,0:T(8,128)(2,1)S(1)} %get-tuple-element.16), channel_id=1, source_target_pairs={{0,2},{1,3},{2,0},{3,1},{4,6},{5,7},{6,4},{7,5},{8,10},{9,11},{10,... | collective-permute-start | bytes 786440 | tf_op jit(solution)/shard_map/ppermute | solution.py:60
  6.7 1.3 %select_bitcast_fusion = (bf16[64,4096]{1,0:T(8,128)(2,1)S(1)}, bf16[1,64,4096]{2,1,0:T(8,128)(2,1)S(1)}) fusion(pred[]{:T(512)S(6)} %select_n.121, bf16[2,64,6144]{2,1,0:T(8,128)(2,1)} %bitcast.89), kind=kLoop, calls=%fused_computation.37 | loop fusion | flops 524288 | bytes 2097153 | tf_op jit(solution)/shard_map/jit(_where)/select_n | solution.py:128
  8.0 0.0 copy-done.1
  8.0 0.2 reduce_window_sum.11
  8.2 0.0 copy-done
  8.2 0.1 constant_dynamic-slice_fusion
  8.3 0.6 %fusion.38 = (s32[1,1]{1,0:T(1,128)}, s32[1,1]{1,0:T(1,128)}) fusion(s32[1,2]{1,0:T(1,128)S(1)} %constant_dynamic-slice_fusion), kind=kLoop, calls=%fused_computation.76 | loop fusion | bytes 16 | tf_op jit(solution)/shard_map/slice | solution.py:109
  8.9 0.1 pad_add_fusion
  11.6 0.1 convert_reduce_fusion.2
  11.7 0.1 convert_reduce_fusion
  11.8 1.2 %collective-permute-done = bf16[64,2048]{1,0:T(8,128)(2,1)S(1)} collective-permute-done((bf16[64,2048]{1,0:T(8,128)(2,1)S(1)}, bf16[64,2048]{1,0:T(8,128)(2,1)S(1)}, u32[]{:S(2)}, u32[]{:S(2)}) %collective-permute-start) | collective-permute-done | bytes 262176 | tf_op jit(solution)/shard_map/ppermute | solution.py:60
  13.0 1.8 %collective-permute-start.1 = (bf16[64,2048]{1,0:T(8,128)(2,1)S(1)}, bf16[64,2048]{1,0:T(8,128)(2,1)S(1)}, u32[]{:S(2)}, u32[]{:S(2)}) collective-permute-start(bf16[64,2048]{1,0:T(8,128)(2,1)S(1)} %broadcast_select_fusion.2), channel_id=1, source_target_pairs={{0,1},{1,0},{2,3},{3,2},{4,5},{5,4},{6,7},{7,6},{8,9},{9,8},{10,11... | collective-permute-start | bytes 786440 | tf_op jit(solution)/shard_map/ppermute | solution.py:65
  14.8 0.4 select_n.138
  15.2 0.1 compare_and_fusion
  15.3 1.6 %collective-permute-start.3 = (bf16[64,2048]{1,0:T(8,128)(2,1)S(1)}, bf16[64,2048]{1,0:T(8,128)(2,1)S(1)}, u32[]{:S(2)}, u32[]{:S(2)}) collective-permute-start(bf16[64,2048]{1,0:T(8,128)(2,1)S(1)} %get-tuple-element.8), channel_id=1, source_target_pairs={{0,2},{1,3},{2,0},{3,1},{4,6},{5,7},{6,4},{7,5},{8,10},{9,11},{10,... | collective-permute-start | bytes 786440 | tf_op jit(solution)/shard_map/ppermute | solution.py:60
  16.8 3.7 %collective-permute-done.1 = bf16[64,2048]{1,0:T(8,128)(2,1)S(1)} collective-permute-done((bf16[64,2048]{1,0:T(8,128)(2,1)S(1)}, bf16[64,2048]{1,0:T(8,128)(2,1)S(1)}, u32[]{:S(2)}, u32[]{:S(2)}) %collective-permute-start.1) | collective-permute-done | bytes 262176 | tf_op jit(solution)/shard_map/ppermute | solution.py:65
  20.5 0.1 pad_maximum_fusion.1
  20.6 0.1 slice_bitcast_fusion.3
  20.7 0.1 copy.36
  20.8 0.1 copy.35
  20.8 0.5 fusion.26
  21.3 1.0 %fusion.40 = (f32[8,4,64]{2,1,0:T(4,128)S(1)}, bf16[8,4,64,192]{3,2,1,0:T(8,128)(2,1)S(1)}) fusion(f32[8,192,64,4]{1,2,3,0:T(8,128)S(1)} %fusion.26, pred[64,192]{1,0:T(8,128)(4,1)S(1)} %get-tuple-element.26), kind=kOutput, calls=%fused_computation.78 | output fusion | flops 2752703 | bytes 2379776 | tf_op jit(solution)/shard_map/sub | solution.py:48
  22.3 0.5 fusion.14
  22.7 0.4 copy.18
  23.1 0.4 convert_element_type.49
  23.5 0.0 collective-permute-done.3
  23.5 0.8 %broadcast_select_fusion.1 = (bf16[64,2048]{1,0:T(8,128)(2,1)}, bf16[192,2048]{1,0:T(8,128)(2,1)S(1)}) fusion(bf16[64,2048]{1,0:T(8,128)(2,1)S(1)} %collective-permute-done.3, bf16[64,2048]{1,0:T(8,128)(2,1)S(1)} %get-tuple-element.8, pred[]{:T(512)S(6)} %eq.53), kind=kLoop, calls=%fused_computation.49 | loop fusion | flops 131071 | bytes 1048577 | tf_op jit(solution)/shard_map/jit(_where)/select_n | solution.py:62
  24.3 1.4 %collective-permute-start.4 = (bf16[64,2048]{1,0:T(8,128)(2,1)}, bf16[64,2048]{1,0:T(8,128)(2,1)S(1)}, u32[]{:S(2)}, u32[]{:S(2)}) collective-permute-start(bf16[64,2048]{1,0:T(8,128)(2,1)} %get-tuple-element.9), channel_id=1, source_target_pairs={{0,1},{1,0},{2,3},{3,2},{4,5},{5,4},{6,7},{7,6},{8,9},{9,8},{10,11... | collective-permute-start | bytes 786440 | tf_op jit(solution)/shard_map/ppermute | solution.py:65
  25.7 1.6 %collective-permute-start.2 = (bf16[64,4096]{1,0:T(8,128)(2,1)S(1)}, bf16[64,4096]{1,0:T(8,128)(2,1)S(1)}, u32[]{:S(2)}, u32[]{:S(2)}) collective-permute-start(bf16[64,4096]{1,0:T(8,128)(2,1)S(1)} %convert_element_type.49), channel_id=1, source_target_pairs={{0,8},{8,16},{16,24},{24,0},{1,9},{9,17},{17,25},{25,1},{2,10},{10... | collective-permute-start | bytes 1572872 | tf_op jit(solution)/shard_map/ppermute | solution.py:26
  27.3 0.4 reshape.76
  27.7 3.4 %collective-permute-done.4 = bf16[64,2048]{1,0:T(8,128)(2,1)S(1)} collective-permute-done((bf16[64,2048]{1,0:T(8,128)(2,1)}, bf16[64,2048]{1,0:T(8,128)(2,1)S(1)}, u32[]{:S(2)}, u32[]{:S(2)}) %collective-permute-start.4) | collective-permute-done | bytes 262176 | tf_op jit(solution)/shard_map/ppermute | solution.py:65
  31.2 0.1 slice_bitcast_fusion.1
  31.2 0.1 copy.38
  31.3 0.1 copy.37
  31.4 0.5 fusion.24
  31.8 1.0 %fusion.41 = (f32[8,4,64]{2,1,0:T(4,128)S(1)}, bf16[8,4,64,192]{3,2,1,0:T(8,128)(2,1)S(1)}) fusion(f32[8,192,64,4]{1,2,3,0:T(8,128)S(1)} %fusion.24, pred[64,192]{1,0:T(8,128)(4,1)S(1)} %get-tuple-element.25), kind=kOutput, calls=%fused_computation.79 | output fusion | flops 2752703 | bytes 2379776 | tf_op jit(solution)/shard_map/sub | solution.py:48
  32.8 0.5 fusion.15
  33.3 0.4 copy.22
  33.7 0.4 convert_element_type.55
  34.1 0.1 collective-permute-start.5
  34.1 5.5 %collective-permute-done.2 = bf16[64,4096]{1,0:T(8,128)(2,1)S(1)} collective-permute-done((bf16[64,4096]{1,0:T(8,128)(2,1)S(1)}, bf16[64,4096]{1,0:T(8,128)(2,1)S(1)}, u32[]{:S(2)}, u32[]{:S(2)}) %collective-permute-start.2) | collective-permute-done | bytes 524320 | tf_op jit(solution)/shard_map/ppermute | solution.py:26
  39.6 1.1 %pad_maximum_fusion = bf16[2,64,4096]{2,1,0:T(8,128)(2,1)} fusion(bf16[1,64,4096]{2,1,0:T(8,128)(2,1)S(1)} %bitcast.93), kind=kLoop, calls=%fused_computation.22 | loop fusion | flops 524288 | bytes 1572864 | tf_op jit(solution)/shard_map/stack | solution.py:139
  40.7 9.4 %collective-permute-done.5 = bf16[64,4096]{1,0:T(8,128)(2,1)S(1)} collective-permute-done((bf16[64,4096]{1,0:T(8,128)(2,1)S(1)}, bf16[64,4096]{1,0:T(8,128)(2,1)S(1)}, u32[]{:S(2)}, u32[]{:S(2)}) %collective-permute-start.5) | collective-permute-done | bytes 524320 | tf_op jit(solution)/shard_map/ppermute | solution.py:138
  50.1 0.8 %bitcast_dynamic-update-slice_fusion = bf16[1,2,64,4096]{3,2,1,0:T(8,128)(2,1)} fusion(bf16[1,2,64,4096]{3,2,1,0:T(8,128)(2,1)} %bitcast.92, bf16[64,4096]{1,0:T(8,128)(2,1)S(1)} %collective-permute-done.5), kind=kLoop, calls=%fused_computation.32 | loop fusion | bytes 1048576 | tf_op jit(solution)/shard_map/dynamic_update_slice | solution.py:140
  (8 shorter events, 0.1 us)
Async XLA Ops:
  0.0 8.2 %copy-start = (s32[1,4]{1,0:T(1,128)S(1)}, s32[1,4]{1,0:T(1,128)}, u32[]{:S(2)}) copy-start(s32[1,4]{1,0:T(1,128)} %param.5) | copy-start | bytes 52
  0.0 8.0 %copy-start.1 = (s32[1,4,8]{2,1,0:T(4,128)S(1)}, s32[1,4,8]{2,1,0:T(4,128)}, u32[]{:S(2)}) copy-start(s32[1,4,8]{2,1,0:T(4,128)} %param.6) | copy-start | bytes 388
  3.6 9.4 %collective-permute-start = (bf16[64,2048]{1,0:T(8,128)(2,1)S(1)}, bf16[64,2048]{1,0:T(8,128)(2,1)S(1)}, u32[]{:S(2)}, u32[]{:S(2)}) collective-permute-start(bf16[64,2048]{1,0:T(8,128)(2,1)S(1)} %get-tuple-element.16), channel_id=1, source_target_pairs={{0,2},{1,3},{2,0},{3,1},{4,6},{5,7},{6,4},{7,5},{8,10},{9,11},{10,... | collective-permute-start | bytes 786440 | tf_op jit(solution)/shard_map/ppermute | solution.py:60
  13.0 7.5 %collective-permute-start.1 = (bf16[64,2048]{1,0:T(8,128)(2,1)S(1)}, bf16[64,2048]{1,0:T(8,128)(2,1)S(1)}, u32[]{:S(2)}, u32[]{:S(2)}) collective-permute-start(bf16[64,2048]{1,0:T(8,128)(2,1)S(1)} %broadcast_select_fusion.2), channel_id=1, source_target_pairs={{0,1},{1,0},{2,3},{3,2},{4,5},{5,4},{6,7},{7,6},{8,9},{9,8},{10,11... | collective-permute-start | bytes 786440 | tf_op jit(solution)/shard_map/ppermute | solution.py:65
  15.3 8.3 %collective-permute-start.3 = (bf16[64,2048]{1,0:T(8,128)(2,1)S(1)}, bf16[64,2048]{1,0:T(8,128)(2,1)S(1)}, u32[]{:S(2)}, u32[]{:S(2)}) collective-permute-start(bf16[64,2048]{1,0:T(8,128)(2,1)S(1)} %get-tuple-element.8), channel_id=1, source_target_pairs={{0,2},{1,3},{2,0},{3,1},{4,6},{5,7},{6,4},{7,5},{8,10},{9,11},{10,... | collective-permute-start | bytes 786440 | tf_op jit(solution)/shard_map/ppermute | solution.py:60
  24.3 6.8 %collective-permute-start.4 = (bf16[64,2048]{1,0:T(8,128)(2,1)}, bf16[64,2048]{1,0:T(8,128)(2,1)S(1)}, u32[]{:S(2)}, u32[]{:S(2)}) collective-permute-start(bf16[64,2048]{1,0:T(8,128)(2,1)} %get-tuple-element.9), channel_id=1, source_target_pairs={{0,1},{1,0},{2,3},{3,2},{4,5},{5,4},{6,7},{7,6},{8,9},{9,8},{10,11... | collective-permute-start | bytes 786440 | tf_op jit(solution)/shard_map/ppermute | solution.py:65
  25.7 13.9 %collective-permute-start.2 = (bf16[64,4096]{1,0:T(8,128)(2,1)S(1)}, bf16[64,4096]{1,0:T(8,128)(2,1)S(1)}, u32[]{:S(2)}, u32[]{:S(2)}) collective-permute-start(bf16[64,4096]{1,0:T(8,128)(2,1)S(1)} %convert_element_type.49), channel_id=1, source_target_pairs={{0,8},{8,16},{16,24},{24,0},{1,9},{9,17},{17,25},{25,1},{2,10},{10... | collective-permute-start | bytes 1572872 | tf_op jit(solution)/shard_map/ppermute | solution.py:26
  34.1 16.1 %collective-permute-start.5 = (bf16[64,4096]{1,0:T(8,128)(2,1)S(1)}, bf16[64,4096]{1,0:T(8,128)(2,1)S(1)}, u32[]{:S(2)}, u32[]{:S(2)}) collective-permute-start(bf16[64,4096]{1,0:T(8,128)(2,1)S(1)} %convert_element_type.55), channel_id=1, source_target_pairs={{0,12},{4,8},{8,20},{12,16},{16,28},{20,24},{24,4},{28,0},{1,13},{... | collective-permute-start | bytes 1572872 | tf_op jit(solution)/shard_map/ppermute | solution.py:138

commit v15 on v12

--- a/solution.py
+++ b/solution.py
@@ -57,21 +57,37 @@
 
 def gathered(block, seq_index, seq_count, reach, hold=None):
     if seq_count == 4 and reach == 2:
-        over_y = lax.ppermute(block, "seq", [(j, j ^ 2) for j in range(4)])
-        odd = seq_index % 2 == 1
-        onward = jnp.where(odd, over_y, block)
+        replicas = lax.axis_size("dp")
+        axes = ("dp", "seq")
+        replica = lax.axis_index("dp")
+
+        def pairs(first):
+            route = []
+            for rep in range(replicas):
+                step = 2 if (rep % 2 == 0) == first else 1
+                route += [(rep * 4 + j, rep * 4 + (j ^ step)) for j in range(4)]
+            return route
+
+        over_first = lax.ppermute(block, axes, pairs(True))
+        both = jnp.concatenate([block, over_first], axis=0)
         if hold is not None:
-            onward = lax.optimization_barrier((onward, hold))[0]
-        over_x = lax.ppermute(onward, "seq", [(j, j ^ 1) for j in range(4)])
-        return [
-            (over_y, jnp.bitwise_xor(seq_index, 2)),
-            (over_x, jnp.where(odd, seq_index - 1, jnp.bitwise_xor(seq_index, 3))),
+            both = lax.optimization_barrier((both, hold))[0]
+        over_second = lax.ppermute(both, axes, pairs(False))
+        even = replica % 2 == 0
+        first_step = jnp.where(even, 2, 1)
+        second_step = jnp.where(even, 1, 2)
+        seg_len = block.shape[0]
+        pieces = [
+            (over_first, jnp.bitwise_xor(seq_index, first_step)),
+            (over_second[:seg_len], jnp.bitwise_xor(seq_index, second_step)),
+            (over_second[seg_len:], jnp.bitwise_xor(seq_index, 3)),
         ]
+        return pieces, over_second
     pieces = []
     for shift in range(1, reach + 1):
         pairs = [(source, source + shift) for source in range(seq_count - shift)]
         pieces.append((lax.ppermute(block, "seq", pairs), seq_index - shift))
-    return pieces
+    return pieces, pieces[-1][0]
 
 
 def shards(qkv, stream_lengths, doc_lengths, hand_over):
@@ -116,12 +132,12 @@
         )
 
     kept_kv = jnp.where(handed, own_rows[0, :, D:], own_rows[1, :, D:])
-    kept_pieces = gathered(kept_kv, seq_index, seq_count, reach)
+    kept_pieces, kept_last = gathered(kept_kv, seq_index, seq_count, reach)
     kept_queries = jnp.where(handed, own_rows[0, :, :D], own_rows[1, :, :D])
     kept_out = attend_own(kept_queries, kept_kv, kept_pieces, handed)
     given_kv = jnp.where(handed, own_rows[1, :, D:], own_rows[0, :, D:])
-    given_kv = lax.optimization_barrier((given_kv, kept_pieces[0][0]))[0]
-    given_pieces = gathered(given_kv, seq_index, seq_count, reach, hold=kept_out)
+    given_kv = lax.optimization_barrier((given_kv, kept_last))[0]
+    given_pieces, _ = gathered(given_kv, seq_index, seq_count, reach, hold=kept_out)
     sent = [passed_along(kept_out, "section", 1)]
     given_queries = jnp.where(handed, own_rows[1, :, :D], own_rows[0, :, :D])
     given_queries = lax.optimization_barrier((given_queries, kept_out))[0]

time: 50.6 us -> 69.2 us (1.37)
  waiting for transfers between devices: 23.2 us -> 31.3 us
  matrix products: 1.83 us -> 7.99 us
  local copies, waits for them, and re-layouts: 4.24 us -> 6.35 us
  starting transfers between devices: 9.49 us -> 10.8 us
  other arithmetic: 8.07 us -> 8.78 us
    ppermute x4, waiting for transfers between devices: 8.29 us -> 17.2 us  [the longest x2 12.4 us: gathered(): over_second = lax.ppermute(both, axes, pairs(False))]
    ppermute x1, waiting for transfers between devices: 5.52 us -> 0.06 us  [passed_along(): return lax.ppermute(value, axis, pairs)]
    sub x0 -> x2, matrix products: none -> 4.65 us  [attend_row(): weights = jnp.where(allowed, jnp.exp(scores - row_top), 0.0)]
    ppermute x1, waiting for transfers between devices: 9.43 us -> 14 us  [shards(): sent.append(lax.ppermute(given_out, ('section', 'dp'), pairs))]
    unnamed x11 -> x13, local copies, waits for them, and re-layouts: 0.39 us -> 3.11 us
    dot_general x2, matrix products: 0.91 us -> 3.34 us  [attend_row(): jnp.einsum('kgqs,skd->qkgd', rounded, values, preferred_element_type=jnp....]
    concatenate x1 -> x2, other arithmetic: 0.07 us -> 2.17 us  [attend_own(): kv_all = jnp.concatenate(pieces, axis=0)]
    sub x2 -> x0, other arithmetic: 1.94 us -> none  [attend_row(): weights = jnp.where(allowed, jnp.exp(scores - row_top), 0.0)]
  transfers between devices with their start and end apart: 6 -> 6, of which waited for: 5 -> 6; matrix products, arithmetic and copies ran while one was open for 20% -> 20% of each run, Pallas kernels for 0% -> 0%
where the time goes in v15:
time: 69.2 us; the launch traced here: 68.7 us
  waiting for transfers between devices  31.3 us (45%)
  starting transfers between devices  10.8 us (16%)
  other arithmetic  8.78 us (13%)
  matrix products  7.99 us (12%)
  local copies, waits for them, and re-layouts  6.35 us (9%)
  between operations  3.51 us (5%)
    ppermute x1, waiting for transfers between devices, shards(): sent.append(lax.ppermute(given_out, ('section', 'dp'), pairs))  14 us
    ppermute x2, waiting for transfers between devices, gathered(): over_second = lax.ppermute(both, axes, pairs(False))  12.4 us
    ppermute x2, starting transfers between devices, gathered(): over_first = lax.ppermute(block, axes, pairs(True))  5.08 us
    ppermute x2, waiting for transfers between devices, gathered(): over_first = lax.ppermute(block, axes, pairs(True))  4.73 us
    sub x2, matrix products, attend_row(): weights = jnp.where(allowed, jnp.exp(scores - row_top), 0.0)  4.65 us
    ppermute x2, starting transfers between devices, gathered(): over_second = lax.ppermute(both, axes, pairs(False))  4.12 us
    dot_general x2, matrix products, attend_row(): jnp.einsum('kgqs,skd->qkgd', rounded, values, preferred_element_type=jnp....  3.34 us
    unnamed x13, local copies, waits for them, and re-layouts  3.11 us
  transfers between devices with their start and end apart: 6, of which 6 were waited for; matrix products, arithmetic and copies ran while one was open for 20% of the time, Pallas kernels for 0%

profile of v15, /device:TPU:0, one launch (start us, length us, event | category | flops | bytes accessed | tf_op | source)
XLA Modules:
  0.0 68.7 jit_solution(6997251005079975086)
XLA Ops:
  0.0 0.0 copy-start
  0.0 3.1 %copy.16 = bf16[1,2,64,6144]{2,3,1,0:T(8,128)(2,1)S(1)} copy(bf16[1,2,64,6144]{3,2,1,0:T(8,128)(2,1)} %param.4) | data formatting | bytes 3145728 | tf_op args[0]
  3.1 0.0 copy-done.5
  3.1 0.6 fusion.30
  4.4 1.1 %select_bitcast_fusion.1 = (bf16[64,2048]{0,1:T(8,128)(2,1)}, bf16[64,2048]{0,1:T(8,128)(2,1)}) fusion(pred[]{:T(512)S(6)} %eq.44, bf16[2,64,6144]{1,2,0:T(8,128)(2,1)S(1)} %bitcast.100), kind=kLoop, calls=%fused_computation.38 | loop fusion | flops 262144 | bytes 1048577 | tf_op jit(solution)/shard_map/jit(_where)/select_n | solution.py:138
  5.5 3.0 %collective-permute-start = (bf16[64,2048]{0,1:T(8,128)(2,1)}, bf16[64,2048]{0,1:T(8,128)(2,1)}, u32[]{:S(2)}, u32[]{:S(2)}) collective-permute-start(bf16[64,2048]{0,1:T(8,128)(2,1)} %get-tuple-element.18), channel_id=1, source_target_pairs={{0,2},{1,3},{2,0},{3,1},{4,5},{5,4},{6,7},{7,6},{8,10},{9,11},{10,... | collective-permute-start | bytes 786440 | tf_op jit(solution)/shard_map/ppermute | solution.py:71
  8.5 0.0 copy-done
  8.5 0.1 constant_dynamic-slice_fusion
  8.6 0.6 fusion.37
  11.8 0.0 copy-start.4
  11.9 1.5 %select_bitcast_fusion = (bf16[64,4096]{0,1:T(8,128)(2,1)}, bf16[1,64,4096]{1,2,0:T(8,128)(2,1)}) fusion(pred[]{:T(512)S(6)} %eq.44, bf16[2,64,6144]{1,2,0:T(8,128)(2,1)S(1)} %bitcast.101), kind=kLoop, calls=%fused_computation.26 | loop fusion | flops 524288 | bytes 2097153 | tf_op jit(solution)/shard_map/jit(_where)/select_n | solution.py:142
  13.3 0.0 copy-done.4
  13.3 0.2 reduce_window_sum.11
  13.6 2.4 %collective-permute-done = bf16[64,2048]{0,1:T(8,128)(2,1)} collective-permute-done((bf16[64,2048]{0,1:T(8,128)(2,1)}, bf16[64,2048]{0,1:T(8,128)(2,1)}, u32[]{:S(2)}, u32[]{:S(2)}) %collective-permute-start) | collective-permute-done | bytes 262176 | tf_op jit(solution)/shard_map/ppermute | solution.py:71
  16.0 1.5 %pad_maximum_fusion.3 = bf16[128,2048]{0,1:T(8,128)(2,1)S(1)} fusion(bf16[64,2048]{0,1:T(8,128)(2,1)} %collective-permute-done, bf16[64,2048]{0,1:T(8,128)(2,1)} %get-tuple-element.18), kind=kLoop, calls=%fused_computation.35 | loop fusion | flops 1048576 | bytes 1048576 | tf_op jit(solution)/shard_map/concatenate | solution.py:72
  17.5 2.1 %collective-permute-start.1 = (bf16[128,2048]{0,1:T(8,128)(2,1)S(1)}, bf16[128,2048]{0,1:T(8,128)(2,1)S(1)}, u32[]{:S(2)}, u32[]{:S(2)}) collective-permute-start(bf16[128,2048]{0,1:T(8,128)(2,1)S(1)} %pad_maximum_fusion.3), channel_id=1, source_target_pairs={{0,1},{1,0},{2,3},{3,2},{4,6},{5,7},{6,4},{7,5},{8,9},{9,8},{10,11... | collective-permute-start | bytes 1572872 | tf_op jit(solution)/shard_map/ppermute | solution.py:75
  19.5 0.1 pad_add_fusion
  19.6 0.1 convert_reduce_fusion.2
  19.7 0.1 convert_reduce_fusion
  19.8 0.1 compare_and_fusion
  19.9 0.0 copy-start.1
  19.9 0.0 copy-start.3
  19.9 6.8 %collective-permute-done.1 = bf16[128,2048]{0,1:T(8,128)(2,1)S(1)} collective-permute-done((bf16[128,2048]{0,1:T(8,128)(2,1)S(1)}, bf16[128,2048]{0,1:T(8,128)(2,1)S(1)}, u32[]{:S(2)}, u32[]{:S(2)}) %collective-permute-start.1) | collective-permute-done | bytes 524320 | tf_op jit(solution)/shard_map/ppermute | solution.py:75
  26.7 1.7 %pad_maximum_fusion = bf16[256,2048]{0,1:T(8,128)(2,1)S(1)} fusion(bf16[128,2048]{0,1:T(8,128)(2,1)S(1)} %collective-permute-done.1, bf16[64,2048]{0,1:T(8,128)(2,1)} %collective-permute-done, bf16[64,2048]{0,1:T(8,128)(2,1)} %get-tuple-element.18), kind=kLoop, calls=%fused_computation.22 | loop fusion | flops 3145728 | bytes 2097152 | tf_op jit(solution)/shard_map/concatenate | solution.py:120
  28.4 0.1 fusion.36
  28.5 0.0 copy-done.1
  28.5 2.1 %collective-permute-start.3 = (bf16[64,2048]{0,1:T(8,128)(2,1)S(1)}, bf16[64,2048]{0,1:T(8,128)(2,1)S(1)}, u32[]{:S(2)}, u32[]{:S(2)}) collective-permute-start(bf16[64,2048]{0,1:T(8,128)(2,1)S(1)} %copy-done.1), channel_id=1, source_target_pairs={{0,2},{1,3},{2,0},{3,1},{4,5},{5,4},{6,7},{7,6},{8,10},{9,11},{10,... | collective-permute-start | bytes 786440 | tf_op jit(solution)/shard_map/ppermute | solution.py:71
  30.6 0.0 copy-done.3
  30.6 2.3 %fusion.38 = (f32[8,4,64]{2,1,0:T(4,128)S(1)}, bf16[8,4,64,256]{3,2,1,0:T(8,128)(2,1)}) fusion(pred[64,256]{1,0:T(8,128)(4,1)S(1)} %get-tuple-element.24, bf16[256,8,128,1]{0,2,3,1:T(8,128)(2,1)S(1)} %bitcast.107, bf16[64,8,4,128]{0,3,2,1:T(8,128)(2,1)S(1)} %bitcast.103), kind=kOutput, calls=%fused_computation.70 | convolution fusion | flops 272105728 | bytes 2121728 | tf_op jit(solution)/shard_map/sub | solution.py:48
  32.9 1.7 %fusion.14 = bf16[64,8,4,128]{3,0,2,1:T(8,128)(2,1)S(1)} fusion(bf16[256,8,128,1]{0,2,3,1:T(8,128)(2,1)S(1)} %bitcast.106, bf16[8,4,64,256]{3,2,1,0:T(8,128)(2,1)} %get-tuple-element.30, f32[64]{0:T(128)S(1)} %get-tuple-element.34, f32[64,8,4]{0,2,1:T(4,128)S(1)} %bitcast.112), kind=kOutput, calls=%fused_computation.20 | convolution fusion | flops 135004160 | bytes 2105600 | tf_op jit(solution)/shard_map/kgqs,skd->qkgd/dot_general | solution.py:51
  34.6 0.4 copy.20
  35.0 0.4 convert_element_type.49
  35.4 2.3 %collective-permute-done.3 = bf16[64,2048]{0,1:T(8,128)(2,1)S(1)} collective-permute-done((bf16[64,2048]{0,1:T(8,128)(2,1)S(1)}, bf16[64,2048]{0,1:T(8,128)(2,1)S(1)}, u32[]{:S(2)}, u32[]{:S(2)}) %collective-permute-start.3) | collective-permute-done | bytes 262176 | tf_op jit(solution)/shard_map/ppermute | solution.py:71
  37.7 0.3 pad_maximum_fusion.4
  38.0 2.1 %collective-permute-start.4 = (bf16[128,2048]{0,1:T(8,128)(2,1)S(1)}, bf16[128,2048]{0,1:T(8,128)(2,1)S(1)}, u32[]{:S(2)}, u32[]{:S(2)}) collective-permute-start(bf16[128,2048]{0,1:T(8,128)(2,1)S(1)} %pad_maximum_fusion.4), channel_id=1, source_target_pairs={{0,1},{1,0},{2,3},{3,2},{4,6},{5,7},{6,4},{7,5},{8,9},{9,8},{10,11... | collective-permute-start | bytes 1572872 | tf_op jit(solution)/shard_map/ppermute | solution.py:75
  40.1 1.6 %collective-permute-start.2 = (bf16[64,4096]{1,0:T(8,128)(2,1)S(1)}, bf16[64,4096]{1,0:T(8,128)(2,1)S(1)}, u32[]{:S(2)}, u32[]{:S(2)}) collective-permute-start(bf16[64,4096]{1,0:T(8,128)(2,1)S(1)} %convert_element_type.49), channel_id=1, source_target_pairs={{0,8},{8,16},{16,24},{24,0},{1,9},{9,17},{17,25},{25,1},{2,10},{10... | collective-permute-start | bytes 1572872 | tf_op jit(solution)/shard_map/ppermute | solution.py:26
  41.7 5.6 %collective-permute-done.4 = bf16[128,2048]{0,1:T(8,128)(2,1)S(1)} collective-permute-done((bf16[128,2048]{0,1:T(8,128)(2,1)S(1)}, bf16[128,2048]{0,1:T(8,128)(2,1)S(1)}, u32[]{:S(2)}, u32[]{:S(2)}) %collective-permute-start.4) | collective-permute-done | bytes 524320 | tf_op jit(solution)/shard_map/ppermute | solution.py:75
  47.3 0.5 pad_maximum_fusion.2
  47.8 0.1 fusion.35
  47.9 2.3 %fusion.39 = (f32[8,4,64]{2,1,0:T(4,128)S(1)}, bf16[8,4,64,256]{3,2,1,0:T(8,128)(2,1)}) fusion(pred[64,256]{1,0:T(8,128)(4,1)S(1)} %get-tuple-element.23, bf16[256,8,128,1]{0,2,3,1:T(8,128)(2,1)S(1)} %bitcast.109, bf16[64,8,4,128]{0,3,2,1:T(8,128)(2,1)S(1)} %bitcast.102), kind=kOutput, calls=%fused_computation.71 | convolution fusion | flops 272105728 | bytes 2121728 | tf_op jit(solution)/shard_map/sub | solution.py:48
  50.2 1.7 %fusion.15 = bf16[64,8,4,128]{3,0,2,1:T(8,128)(2,1)S(1)} fusion(bf16[256,8,128,1]{0,2,3,1:T(8,128)(2,1)S(1)} %bitcast.108, bf16[8,4,64,256]{3,2,1,0:T(8,128)(2,1)} %get-tuple-element.32, f32[64]{0:T(128)S(1)} %get-tuple-element.33, f32[64,8,4]{0,2,1:T(4,128)S(1)} %bitcast.111), kind=kOutput, calls=%fused_computation.21 | convolution fusion | flops 135004160 | bytes 2105600 | tf_op jit(solution)/shard_map/kgqs,skd->qkgd/dot_general | solution.py:51
  51.9 0.4 copy.24
  52.3 0.4 convert_element_type.55
  52.7 0.1 collective-permute-start.5
  52.7 0.1 collective-permute-done.2
  52.8 1.1 %pad_maximum_fusion.1 = bf16[2,64,4096]{2,1,0:T(8,128)(2,1)} fusion(bf16[1,64,4096]{2,1,0:T(8,128)(2,1)S(1)} %bitcast.105), kind=kLoop, calls=%fused_computation.23 | loop fusion | flops 524288 | bytes 1572864 | tf_op jit(solution)/shard_map/stack | solution.py:153
  53.8 14.0 %collective-permute-done.5 = bf16[64,4096]{1,0:T(8,128)(2,1)S(1)} collective-permute-done((bf16[64,4096]{1,0:T(8,128)(2,1)S(1)}, bf16[64,4096]{1,0:T(8,128)(2,1)S(1)}, u32[]{:S(2)}, u32[]{:S(2)}) %collective-permute-start.5) | collective-permute-done | bytes 524320 | tf_op jit(solution)/shard_map/ppermute | solution.py:152
  67.9 0.8 %bitcast_dynamic-update-slice_fusion = bf16[1,2,64,4096]{3,2,1,0:T(8,128)(2,1)} fusion(bf16[1,2,64,4096]{3,2,1,0:T(8,128)(2,1)} %bitcast.104, bf16[64,4096]{1,0:T(8,128)(2,1)S(1)} %collective-permute-done.5), kind=kLoop, calls=%fused_computation.37 | loop fusion | bytes 1048576 | tf_op jit(solution)/shard_map/dynamic_update_slice | solution.py:154
  (8 shorter events, 0.0 us)
Async XLA Ops:
  0.0 8.5 %copy-start = (s32[1,4]{1,0:T(1,128)S(1)}, s32[1,4]{1,0:T(1,128)}, u32[]{:S(2)}) copy-start(s32[1,4]{1,0:T(1,128)} %param.5) | copy-start | bytes 52
  0.0 3.1 %copy-start.5 = (s32[1,2]{1,0:T(1,128)S(1)}, s32[1,2]{1,0:T(1,128)}, u32[]{:S(2)}) copy-start(s32[1,2]{1,0:T(1,128)} %param.7) | copy-start | bytes 28
  5.5 10.5 %collective-permute-start = (bf16[64,2048]{0,1:T(8,128)(2,1)}, bf16[64,2048]{0,1:T(8,128)(2,1)}, u32[]{:S(2)}, u32[]{:S(2)}) collective-permute-start(bf16[64,2048]{0,1:T(8,128)(2,1)} %get-tuple-element.18), channel_id=1, source_target_pairs={{0,2},{1,3},{2,0},{3,1},{4,5},{5,4},{6,7},{7,6},{8,10},{9,11},{10,... | collective-permute-start | bytes 786440 | tf_op jit(solution)/shard_map/ppermute | solution.py:71
  11.8 1.5 %copy-start.4 = (s32[1,4,8]{2,1,0:T(4,128)S(1)}, s32[1,4,8]{2,1,0:T(4,128)}, u32[]{:S(2)}) copy-start(s32[1,4,8]{2,1,0:T(4,128)} %param.6) | copy-start | bytes 388
  17.5 9.2 %collective-permute-start.1 = (bf16[128,2048]{0,1:T(8,128)(2,1)S(1)}, bf16[128,2048]{0,1:T(8,128)(2,1)S(1)}, u32[]{:S(2)}, u32[]{:S(2)}) collective-permute-start(bf16[128,2048]{0,1:T(8,128)(2,1)S(1)} %pad_maximum_fusion.3), channel_id=1, source_target_pairs={{0,1},{1,0},{2,3},{3,2},{4,6},{5,7},{6,4},{7,5},{8,9},{9,8},{10,11... | collective-permute-start | bytes 1572872 | tf_op jit(solution)/shard_map/ppermute | solution.py:75
  19.9 8.6 %copy-start.1 = (bf16[64,2048]{0,1:T(8,128)(2,1)S(1)}, bf16[64,2048]{0,1:T(8,128)(2,1)}, u32[]{:S(2)}) copy-start(bf16[64,2048]{0,1:T(8,128)(2,1)} %get-tuple-element.8) | copy-start | bytes 786436
  19.9 10.7 %copy-start.3 = (bf16[1,64,4096]{1,2,0:T(8,128)(2,1)S(1)}, bf16[1,64,4096]{1,2,0:T(8,128)(2,1)}, u32[]{:S(2)}) copy-start(bf16[1,64,4096]{1,2,0:T(8,128)(2,1)} %get-tuple-element.16) | copy-start | bytes 1572868
  28.5 9.2 %collective-permute-start.3 = (bf16[64,2048]{0,1:T(8,128)(2,1)S(1)}, bf16[64,2048]{0,1:T(8,128)(2,1)S(1)}, u32[]{:S(2)}, u32[]{:S(2)}) collective-permute-start(bf16[64,2048]{0,1:T(8,128)(2,1)S(1)} %copy-done.1), channel_id=1, source_target_pairs={{0,2},{1,3},{2,0},{3,1},{4,5},{5,4},{6,7},{7,6},{8,10},{9,11},{10,... | collective-permute-start | bytes 786440 | tf_op jit(solution)/shard_map/ppermute | solution.py:71
  38.0 9.2 %collective-permute-start.4 = (bf16[128,2048]{0,1:T(8,128)(2,1)S(1)}, bf16[128,2048]{0,1:T(8,128)(2,1)S(1)}, u32[]{:S(2)}, u32[]{:S(2)}) collective-permute-start(bf16[128,2048]{0,1:T(8,128)(2,1)S(1)} %pad_maximum_fusion.4), channel_id=1, source_target_pairs={{0,1},{1,0},{2,3},{3,2},{4,6},{5,7},{6,4},{7,5},{8,9},{9,8},{10,11... | collective-permute-start | bytes 1572872 | tf_op jit(solution)/shard_map/ppermute | solution.py:75
  40.1 12.7 %collective-permute-start.2 = (bf16[64,4096]{1,0:T(8,128)(2,1)S(1)}, bf16[64,4096]{1,0:T(8,128)(2,1)S(1)}, u32[]{:S(2)}, u32[]{:S(2)}) collective-permute-start(bf16[64,4096]{1,0:T(8,128)(2,1)S(1)} %convert_element_type.49), channel_id=1, source_target_pairs={{0,8},{8,16},{16,24},{24,0},{1,9},{9,17},{17,25},{25,1},{2,10},{10... | collective-permute-start | bytes 1572872 | tf_op jit(solution)/shard_map/ppermute | solution.py:26
  41.7 6.2 %copy-start.2 = (bf16[64,4096]{0,1:T(8,128)(2,1)S(1)}, bf16[64,4096]{0,1:T(8,128)(2,1)}, u32[]{:S(2)}) copy-start(bf16[64,4096]{0,1:T(8,128)(2,1)} %get-tuple-element.10) | copy-start | bytes 1572868
  52.7 15.2 %collective-permute-start.5 = (bf16[64,4096]{1,0:T(8,128)(2,1)S(1)}, bf16[64,4096]{1,0:T(8,128)(2,1)S(1)}, u32[]{:S(2)}, u32[]{:S(2)}) collective-permute-start(bf16[64,4096]{1,0:T(8,128)(2,1)S(1)} %convert_element_type.55), channel_id=1, source_target_pairs={{0,12},{4,8},{8,20},{12,16},{16,28},{20,24},{24,4},{28,0},{1,13},{... | collective-permute-start | bytes 1572872 | tf_op jit(solution)/shard_map/ppermute | solution.py:152

commit v16 on v12

--- a/solution.py
+++ b/solution.py
@@ -74,6 +74,20 @@
     return pieces
 
 
+def gathered_mirrored(block, seq_index, seq_count, reach):
+    if seq_count == 4 and reach == 2:
+        over_x = lax.ppermute(block, "seq", [(j, j ^ 1) for j in range(4)])
+        both = jnp.concatenate([block, over_x], axis=0)
+        over_y = lax.ppermute(both, "seq", [(j, j ^ 2) for j in range(4)])
+        seg_len = block.shape[0]
+        return [
+            (over_x, jnp.bitwise_xor(seq_index, 1)),
+            (over_y[:seg_len], jnp.bitwise_xor(seq_index, 2)),
+            (over_y[seg_len:], jnp.bitwise_xor(seq_index, 3)),
+        ]
+    return gathered(block, seq_index, seq_count, reach)
+
+
 def shards(qkv, stream_lengths, doc_lengths, hand_over):
     seq_count = lax.axis_size("seq")
     seq_index = lax.axis_index("seq")
@@ -120,8 +134,7 @@
     kept_queries = jnp.where(handed, own_rows[0, :, :D], own_rows[1, :, :D])
     kept_out = attend_own(kept_queries, kept_kv, kept_pieces, handed)
     given_kv = jnp.where(handed, own_rows[1, :, D:], own_rows[0, :, D:])
-    given_kv = lax.optimization_barrier((given_kv, kept_pieces[0][0]))[0]
-    given_pieces = gathered(given_kv, seq_index, seq_count, reach, hold=kept_out)
+    given_pieces = gathered_mirrored(given_kv, seq_index, seq_count, reach)
     sent = [passed_along(kept_out, "section", 1)]
     given_queries = jnp.where(handed, own_rows[1, :, :D], own_rows[0, :, :D])
     given_queries = lax.optimization_barrier((given_queries, kept_out))[0]

time: 50.6 us -> 68.1 us (1.35)
  waiting for transfers between devices: 23.2 us -> 30.8 us
  matrix products: 1.83 us -> 8.03 us
  other arithmetic: 8.07 us -> 11.1 us
  local copies, waits for them, and re-layouts: 4.24 us -> 6.3 us
  starting transfers between devices: 9.49 us -> 8.36 us
    ppermute x2 -> x1, waiting for transfers between devices: 1.17 us -> 6.93 us  [gathered(): over_y = lax.ppermute(block, 'seq', [(j, j ^ 2) for j in range(4)])]
    ppermute x0 -> x2, starting transfers between devices: none -> 4.78 us  [the longest x1 2.97 us: gathered_mirrored(): over_x = lax.ppermute(block, 'seq', [(j, j ^ 1) for j in range(4)])]
    sub x0 -> x2, matrix products: none -> 4.7 us  [attend_row(): weights = jnp.where(allowed, jnp.exp(scores - row_top), 0.0)]
    concatenate x1 -> x2, other arithmetic: 0.07 us -> 3.5 us  [attend_own(): kv_all = jnp.concatenate(pieces, axis=0)]
    ppermute x2 -> x1, starting transfers between devices: 4.65 us -> 1.52 us  [gathered(): over_y = lax.ppermute(block, 'seq', [(j, j ^ 2) for j in range(4)])]
    ppermute x2 -> x1, starting transfers between devices: 3.22 us -> 0.38 us  [gathered(): over_x = lax.ppermute(onward, 'seq', [(j, j ^ 1) for j in range(4)])]
    unnamed x11, local copies, waits for them, and re-layouts: 0.39 us -> 3.11 us
    dot_general x2, matrix products: 0.91 us -> 3.33 us  [attend_row(): jnp.einsum('kgqs,skd->qkgd', rounded, values, preferred_element_type=jnp....]
  transfers between devices with their start and end apart: 6 -> 6, of which waited for: 5 -> 4; matrix products, arithmetic and copies ran while one was open for 20% -> 29% of each run, Pallas kernels for 0% -> 0%
where the time goes in v16:
time: 68.1 us; the launch traced here: 67.7 us
  waiting for transfers between devices  30.8 us (45%)
  other arithmetic  11.1 us (16%)
  starting transfers between devices  8.36 us (12%)
  matrix products  8.03 us (12%)
  local copies, waits for them, and re-layouts  6.3 us (9%)
  between operations  3.13 us (5%)
    ppermute x1, waiting for transfers between devices, shards(): sent.append(lax.ppermute(given_out, ('section', 'dp'), pairs))  9.25 us
    ppermute x1, waiting for transfers between devices, gathered(): over_x = lax.ppermute(onward, 'seq', [(j, j ^ 1) for j in range(4)])  8.89 us
    ppermute x1, waiting for transfers between devices, gathered(): over_y = lax.ppermute(block, 'seq', [(j, j ^ 2) for j in range(4)])  6.93 us
    ppermute x1, waiting for transfers between devices, passed_along(): return lax.ppermute(value, axis, pairs)  5.7 us
    sub x2, matrix products, attend_row(): weights = jnp.where(allowed, jnp.exp(scores - row_top), 0.0)  4.7 us
    concatenate x2, other arithmetic, attend_own(): kv_all = jnp.concatenate(pieces, axis=0)  3.5 us
    dot_general x2, matrix products, attend_row(): jnp.einsum('kgqs,skd->qkgd', rounded, values, preferred_element_type=jnp....  3.33 us
    unnamed x11, local copies, waits for them, and re-layouts  3.11 us
  transfers between devices with their start and end apart: 6, of which 4 were waited for; matrix products, arithmetic and copies ran while one was open for 29% of the time, Pallas kernels for 0%

profile of v16, /device:TPU:0, one launch (start us, length us, event | category | flops | bytes accessed | tf_op | source)
XLA Modules:
  0.0 67.7 jit_solution(4627918429556253259)
XLA Ops:
  0.0 0.0 copy-start
  0.0 3.1 %copy.18 = bf16[1,2,64,6144]{2,3,1,0:T(8,128)(2,1)S(1)} copy(bf16[1,2,64,6144]{3,2,1,0:T(8,128)(2,1)} %param.4) | data formatting | bytes 3145728 | tf_op args[0]
  3.1 0.0 copy-done.4
  3.1 0.6 fusion.30
  4.4 1.1 %select_bitcast_fusion.1 = (bf16[64,2048]{0,1:T(8,128)(2,1)}, bf16[64,2048]{0,1:T(8,128)(2,1)}) fusion(pred[]{:T(512)S(6)} %eq.42, bf16[2,64,6144]{1,2,0:T(8,128)(2,1)S(1)} %bitcast.100), kind=kLoop, calls=%fused_computation.37 | loop fusion | flops 262144 | bytes 1048577 | tf_op jit(solution)/shard_map/jit(_where)/select_n | solution.py:136
  5.5 3.0 %collective-permute-start.3 = (bf16[64,2048]{0,1:T(8,128)(2,1)}, bf16[64,2048]{0,1:T(8,128)(2,1)}, u32[]{:S(2)}, u32[]{:S(2)}) collective-permute-start(bf16[64,2048]{0,1:T(8,128)(2,1)} %get-tuple-element.11), channel_id=1, source_target_pairs={{0,1},{1,0},{2,3},{3,2},{4,5},{5,4},{6,7},{7,6},{8,9},{9,8},{10,11... | collective-permute-start | bytes 786440 | tf_op jit(solution)/shard_map/ppermute | solution.py:79
  8.4 1.5 %collective-permute-start = (bf16[64,2048]{0,1:T(8,128)(2,1)}, bf16[64,2048]{0,1:T(8,128)(2,1)}, u32[]{:S(2)}, u32[]{:S(2)}) collective-permute-start(bf16[64,2048]{0,1:T(8,128)(2,1)} %get-tuple-element.12), channel_id=1, source_target_pairs={{0,2},{1,3},{2,0},{3,1},{4,6},{5,7},{6,4},{7,5},{8,10},{9,11},{10,... | collective-permute-start | bytes 786440 | tf_op jit(solution)/shard_map/ppermute | solution.py:60
  9.9 1.5 %select_bitcast_fusion = (bf16[64,4096]{0,1:T(8,128)(2,1)}, bf16[1,64,4096]{1,2,0:T(8,128)(2,1)}) fusion(pred[]{:T(512)S(6)} %eq.42, bf16[2,64,6144]{1,2,0:T(8,128)(2,1)S(1)} %bitcast.101), kind=kLoop, calls=%fused_computation.28 | loop fusion | flops 524288 | bytes 2097153 | tf_op jit(solution)/shard_map/jit(_where)/select_n | solution.py:139
  11.4 0.0 copy-done.3
  11.4 0.2 reduce_window_sum.11
  11.6 0.0 copy-done
  11.6 0.1 constant_dynamic-slice_fusion
  11.7 0.1 pad_add_fusion
  11.8 0.1 pad_add_fusion.1
  11.9 0.1 convert_reduce_fusion
  11.9 0.1 convert_reduce_fusion.2
  12.0 0.1 convert_reduce_fusion.1
  12.1 0.1 compare_and_fusion.1
  12.2 0.6 fusion.37
  15.1 0.1 compare_and_fusion
  15.2 6.9 %collective-permute-done = bf16[64,2048]{0,1:T(8,128)(2,1)} collective-permute-done((bf16[64,2048]{0,1:T(8,128)(2,1)}, bf16[64,2048]{0,1:T(8,128)(2,1)}, u32[]{:S(2)}, u32[]{:S(2)}) %collective-permute-start) | collective-permute-done | bytes 262176 | tf_op jit(solution)/shard_map/ppermute | solution.py:60
  22.1 1.1 %broadcast_select_fusion.1 = bf16[64,2048]{0,1:T(8,128)(2,1)S(1)} fusion(bf16[64,2048]{0,1:T(8,128)(2,1)} %collective-permute-done, bf16[64,2048]{0,1:T(8,128)(2,1)} %get-tuple-element.12, pred[]{:T(512)S(6)} %eq.43), kind=kLoop, calls=%fused_computation.39 | loop fusion | flops 131072 | bytes 786433 | tf_op jit(solution)/shard_map/jit(_where)/select_n | solution.py:62
  23.2 0.4 collective-permute-start.1
  23.6 0.0 collective-permute-done.3
  23.6 1.5 %pad_maximum_fusion.3 = bf16[128,2048]{0,1:T(8,128)(2,1)S(1)} fusion(bf16[64,2048]{0,1:T(8,128)(2,1)} %collective-permute-done.3, bf16[64,2048]{0,1:T(8,128)(2,1)} %get-tuple-element.11), kind=kLoop, calls=%fused_computation.35 | loop fusion | flops 1048576 | bytes 1048576 | tf_op jit(solution)/shard_map/concatenate | solution.py:80
  25.1 0.0 copy-start.2
  25.1 1.8 %collective-permute-start.4 = (bf16[128,2048]{0,1:T(8,128)(2,1)S(1)}, bf16[128,2048]{0,1:T(8,128)(2,1)S(1)}, u32[]{:S(2)}, u32[]{:S(2)}) collective-permute-start(bf16[128,2048]{0,1:T(8,128)(2,1)S(1)} %pad_maximum_fusion.3), channel_id=1, source_target_pairs={{0,2},{1,3},{2,0},{3,1},{4,6},{5,7},{6,4},{7,5},{8,10},{9,11},{10,... | collective-permute-start | bytes 1572872 | tf_op jit(solution)/shard_map/ppermute | solution.py:81
  26.9 8.9 %collective-permute-done.1 = bf16[64,2048]{0,1:T(8,128)(2,1)S(1)} collective-permute-done((bf16[64,2048]{0,1:T(8,128)(2,1)S(1)}, bf16[64,2048]{0,1:T(8,128)(2,1)S(1)}, u32[]{:S(2)}, u32[]{:S(2)}) %collective-permute-start.1) | collective-permute-done | bytes 262176 | tf_op jit(solution)/shard_map/ppermute | solution.py:65
  35.8 1.7 %pad_maximum_fusion = bf16[192,2048]{0,1:T(8,128)(2,1)S(1)} fusion(bf16[64,2048]{0,1:T(8,128)(2,1)S(1)} %collective-permute-done.1, bf16[64,2048]{0,1:T(8,128)(2,1)} %collective-permute-done, bf16[64,2048]{0,1:T(8,128)(2,1)} %get-tuple-element.12), kind=kLoop, calls=%fused_computation.22 | loop fusion | flops 2359296 | bytes 1572864 | tf_op jit(solution)/shard_map/concatenate | solution.py:118
  37.5 0.1 fusion.36
  37.6 0.0 copy-done.2
  37.6 2.4 %fusion.38 = (f32[8,4,64]{2,1,0:T(4,128)S(1)}, bf16[8,4,64,192]{3,2,1,0:T(8,128)(2,1)}) fusion(pred[64,192]{1,0:T(8,128)(4,1)S(1)} %compare_and_fusion.1, bf16[192,8,128,1]{0,2,3,1:T(8,128)(2,1)S(1)} %bitcast.108, bf16[64,8,4,128]{0,3,2,1:T(8,128)(2,1)S(1)} %bitcast.103), kind=kOutput, calls=%fused_computation.72 | convolution fusion | flops 204079296 | bytes 1724416 | tf_op jit(solution)/shard_map/sub | solution.py:48
  40.0 1.7 %fusion.14 = bf16[64,8,4,128]{3,0,2,1:T(8,128)(2,1)S(1)} fusion(bf16[192,8,128,1]{0,2,3,1:T(8,128)(2,1)S(1)} %bitcast.107, bf16[8,4,64,192]{3,2,1,0:T(8,128)(2,1)} %get-tuple-element.22, f32[64]{0:T(128)S(1)} %get-tuple-element.26, f32[64,8,4]{0,2,1:T(4,128)S(1)} %bitcast.112), kind=kOutput, calls=%fused_computation.20 | convolution fusion | flops 101449728 | bytes 1712384 | tf_op jit(solution)/shard_map/kgqs,skd->qkgd/dot_general | solution.py:51
  41.7 0.4 copy.24
  42.1 0.4 convert_element_type.49
  42.5 1.6 %collective-permute-start.2 = (bf16[64,4096]{1,0:T(8,128)(2,1)S(1)}, bf16[64,4096]{1,0:T(8,128)(2,1)S(1)}, u32[]{:S(2)}, u32[]{:S(2)}) collective-permute-start(bf16[64,4096]{1,0:T(8,128)(2,1)S(1)} %convert_element_type.49), channel_id=1, source_target_pairs={{0,8},{8,16},{16,24},{24,0},{1,9},{9,17},{17,25},{25,1},{2,10},{10... | collective-permute-start | bytes 1572872 | tf_op jit(solution)/shard_map/ppermute | solution.py:26
  44.1 0.0 collective-permute-done.4
  44.1 1.8 %pad_maximum_fusion.2 = bf16[256,2048]{0,1:T(8,128)(2,1)S(1)} fusion(bf16[128,2048]{0,1:T(8,128)(2,1)S(1)} %collective-permute-done.4, bf16[64,2048]{0,1:T(8,128)(2,1)} %collective-permute-done.3, bf16[64,2048]{0,1:T(8,128)(2,1)} %get-tuple-element.11), kind=kLoop, calls=%fused_computation.24 | loop fusion | flops 3145728 | bytes 2097152 | tf_op jit(solution)/shard_map/concatenate | solution.py:118
  45.9 0.1 fusion.35
  46.0 2.3 %fusion.39 = (f32[8,4,64]{2,1,0:T(4,128)S(1)}, bf16[8,4,64,256]{3,2,1,0:T(8,128)(2,1)}) fusion(pred[64,256]{1,0:T(8,128)(4,1)S(1)} %compare_and_fusion, bf16[256,8,128,1]{0,2,3,1:T(8,128)(2,1)S(1)} %bitcast.109, bf16[64,8,4,128]{0,3,2,1:T(8,128)(2,1)S(1)} %bitcast.102), kind=kOutput, calls=%fused_computation.73 | convolution fusion | flops 272105728 | bytes 2121728 | tf_op jit(solution)/shard_map/sub | solution.py:48
  48.3 1.7 %fusion.15 = bf16[64,8,4,128]{3,0,2,1:T(8,128)(2,1)S(1)} fusion(bf16[256,8,128,1]{0,2,3,1:T(8,128)(2,1)S(1)} %bitcast.106, bf16[8,4,64,256]{3,2,1,0:T(8,128)(2,1)} %get-tuple-element.24, f32[64]{0:T(128)S(1)} %get-tuple-element.25, f32[64,8,4]{0,2,1:T(4,128)S(1)} %bitcast.111), kind=kOutput, calls=%fused_computation.21 | convolution fusion | flops 135004160 | bytes 2105600 | tf_op jit(solution)/shard_map/kgqs,skd->qkgd/dot_general | solution.py:51
  50.0 0.4 copy.28
  50.4 0.4 convert_element_type.55
  50.8 0.1 collective-permute-start.5
  50.9 5.7 %collective-permute-done.2 = bf16[64,4096]{1,0:T(8,128)(2,1)S(1)} collective-permute-done((bf16[64,4096]{1,0:T(8,128)(2,1)S(1)}, bf16[64,4096]{1,0:T(8,128)(2,1)S(1)}, u32[]{:S(2)}, u32[]{:S(2)}) %collective-permute-start.2) | collective-permute-done | bytes 524320 | tf_op jit(solution)/shard_map/ppermute | solution.py:26
  56.6 1.1 %pad_maximum_fusion.1 = bf16[2,64,4096]{2,1,0:T(8,128)(2,1)} fusion(bf16[1,64,4096]{2,1,0:T(8,128)(2,1)S(1)} %bitcast.105), kind=kLoop, calls=%fused_computation.23 | loop fusion | flops 524288 | bytes 1572864 | tf_op jit(solution)/shard_map/stack | solution.py:150
  57.6 9.3 %collective-permute-done.5 = bf16[64,4096]{1,0:T(8,128)(2,1)S(1)} collective-permute-done((bf16[64,4096]{1,0:T(8,128)(2,1)S(1)}, bf16[64,4096]{1,0:T(8,128)(2,1)S(1)}, u32[]{:S(2)}, u32[]{:S(2)}) %collective-permute-start.5) | collective-permute-done | bytes 524320 | tf_op jit(solution)/shard_map/ppermute | solution.py:149
  66.9 0.8 %bitcast_dynamic-update-slice_fusion = bf16[1,2,64,4096]{3,2,1,0:T(8,128)(2,1)} fusion(bf16[1,2,64,4096]{3,2,1,0:T(8,128)(2,1)} %bitcast.104, bf16[64,4096]{1,0:T(8,128)(2,1)S(1)} %collective-permute-done.5), kind=kLoop, calls=%fused_computation.36 | loop fusion | bytes 1048576 | tf_op jit(solution)/shard_map/dynamic_update_slice | solution.py:151
  (10 shorter events, 0.0 us)
Async XLA Ops:
  0.0 11.6 %copy-start = (s32[1,4]{1,0:T(1,128)S(1)}, s32[1,4]{1,0:T(1,128)}, u32[]{:S(2)}) copy-start(s32[1,4]{1,0:T(1,128)} %param.5) | copy-start | bytes 52
  0.0 3.1 %copy-start.4 = (s32[1,2]{1,0:T(1,128)S(1)}, s32[1,2]{1,0:T(1,128)}, u32[]{:S(2)}) copy-start(s32[1,2]{1,0:T(1,128)} %param.7) | copy-start | bytes 28
  5.5 18.2 %collective-permute-start.3 = (bf16[64,2048]{0,1:T(8,128)(2,1)}, bf16[64,2048]{0,1:T(8,128)(2,1)}, u32[]{:S(2)}, u32[]{:S(2)}) collective-permute-start(bf16[64,2048]{0,1:T(8,128)(2,1)} %get-tuple-element.11), channel_id=1, source_target_pairs={{0,1},{1,0},{2,3},{3,2},{4,5},{5,4},{6,7},{7,6},{8,9},{9,8},{10,11... | collective-permute-start | bytes 786440 | tf_op jit(solution)/shard_map/ppermute | solution.py:79
  8.4 13.7 %collective-permute-start = (bf16[64,2048]{0,1:T(8,128)(2,1)}, bf16[64,2048]{0,1:T(8,128)(2,1)}, u32[]{:S(2)}, u32[]{:S(2)}) collective-permute-start(bf16[64,2048]{0,1:T(8,128)(2,1)} %get-tuple-element.12), channel_id=1, source_target_pairs={{0,2},{1,3},{2,0},{3,1},{4,6},{5,7},{6,4},{7,5},{8,10},{9,11},{10,... | collective-permute-start | bytes 786440 | tf_op jit(solution)/shard_map/ppermute | solution.py:60
  9.9 1.5 %copy-start.3 = (s32[1,4,8]{2,1,0:T(4,128)S(1)}, s32[1,4,8]{2,1,0:T(4,128)}, u32[]{:S(2)}) copy-start(s32[1,4,8]{2,1,0:T(4,128)} %param.6) | copy-start | bytes 388
  23.2 12.6 %collective-permute-start.1 = (bf16[64,2048]{0,1:T(8,128)(2,1)S(1)}, bf16[64,2048]{0,1:T(8,128)(2,1)S(1)}, u32[]{:S(2)}, u32[]{:S(2)}) collective-permute-start(bf16[64,2048]{0,1:T(8,128)(2,1)S(1)} %broadcast_select_fusion.1), channel_id=1, source_target_pairs={{0,1},{1,0},{2,3},{3,2},{4,5},{5,4},{6,7},{7,6},{8,9},{9,8},{10,11... | collective-permute-start | bytes 786440 | tf_op jit(solution)/shard_map/ppermute | solution.py:65
  25.1 12.5 %copy-start.2 = (bf16[1,64,4096]{1,2,0:T(8,128)(2,1)S(1)}, bf16[1,64,4096]{1,2,0:T(8,128)(2,1)}, u32[]{:S(2)}) copy-start(bf16[1,64,4096]{1,2,0:T(8,128)(2,1)} %get-tuple-element.10) | copy-start | bytes 1572868
  25.1 19.0 %collective-permute-start.4 = (bf16[128,2048]{0,1:T(8,128)(2,1)S(1)}, bf16[128,2048]{0,1:T(8,128)(2,1)S(1)}, u32[]{:S(2)}, u32[]{:S(2)}) collective-permute-start(bf16[128,2048]{0,1:T(8,128)(2,1)S(1)} %pad_maximum_fusion.3), channel_id=1, source_target_pairs={{0,2},{1,3},{2,0},{3,1},{4,6},{5,7},{6,4},{7,5},{8,10},{9,11},{10,... | collective-permute-start | bytes 1572872 | tf_op jit(solution)/shard_map/ppermute | solution.py:81
  42.5 14.0 %collective-permute-start.2 = (bf16[64,4096]{1,0:T(8,128)(2,1)S(1)}, bf16[64,4096]{1,0:T(8,128)(2,1)S(1)}, u32[]{:S(2)}, u32[]{:S(2)}) collective-permute-start(bf16[64,4096]{1,0:T(8,128)(2,1)S(1)} %convert_element_type.49), channel_id=1, source_target_pairs={{0,8},{8,16},{16,24},{24,0},{1,9},{9,17},{17,25},{25,1},{2,10},{10... | collective-permute-start | bytes 1572872 | tf_op jit(solution)/shard_map/ppermute | solution.py:26
  44.1 1.9 %copy-start.1 = (bf16[64,4096]{0,1:T(8,128)(2,1)S(1)}, bf16[64,4096]{0,1:T(8,128)(2,1)}, u32[]{:S(2)}) copy-start(bf16[64,4096]{0,1:T(8,128)(2,1)} %get-tuple-element.6) | copy-start | bytes 1572868
  50.8 16.1 %collective-permute-start.5 = (bf16[64,4096]{1,0:T(8,128)(2,1)S(1)}, bf16[64,4096]{1,0:T(8,128)(2,1)S(1)}, u32[]{:S(2)}, u32[]{:S(2)}) collective-permute-start(bf16[64,4096]{1,0:T(8,128)(2,1)S(1)} %convert_element_type.55), channel_id=1, source_target_pairs={{0,12},{4,8},{8,20},{12,16},{16,28},{20,24},{24,4},{28,0},{1,13},{... | collective-permute-start | bytes 1572872 | tf_op jit(solution)/shard_map/ppermute | solution.py:149

commit v17 on v12

--- a/solution.py
+++ b/solution.py
@@ -95,37 +95,51 @@
     own_ends = lax.dynamic_slice_in_dim(doc_ends, 2 * replica, 2, 0)
     own_lengths = lax.dynamic_slice_in_dim(lengths_all, 2 * replica, 2, 0)
 
-    def attend_own(query_rows, kv_local, pieces_and_chunks, first_is_kept):
-        pieces = [kv_local]
+    def positions_of(pieces_and_chunks):
         key_pos = [query_pos]
-        for piece, chunk in pieces_and_chunks:
-            pieces.append(piece)
+        for _, chunk in pieces_and_chunks:
             key_pos.append(jnp.where(chunk >= 0, chunk * seg_len + local, far))
-        kv_all = jnp.concatenate(pieces, axis=0)
-        key_pos = jnp.concatenate(key_pos)
+        return jnp.concatenate(key_pos)
+
+    def attend_own(query_rows, key_pieces, value_pieces, key_pos, first_is_kept):
         ends = jnp.where(first_is_kept, own_ends[0], own_ends[1])
         length = jnp.where(first_is_kept, own_lengths[0], own_lengths[1])
         return attend_row(
             query_rows,
-            kv_all[:, :key_value_width],
-            kv_all[:, key_value_width:],
+            jnp.concatenate(key_pieces, axis=0),
+            jnp.concatenate(value_pieces, axis=0),
             query_pos,
             key_pos,
             ends,
             length,
         )
 
-    kept_kv = jnp.where(handed, own_rows[0, :, D:], own_rows[1, :, D:])
-    kept_pieces = gathered(kept_kv, seq_index, seq_count, reach)
+    kept_k = jnp.where(handed, own_rows[0, :, D:D + key_value_width], own_rows[1, :, D:D + key_value_width])
+    kept_v = jnp.where(handed, own_rows[0, :, D + key_value_width:], own_rows[1, :, D + key_value_width:])
+    k_pieces = gathered(kept_k, seq_index, seq_count, reach)
+    kept_v = lax.optimization_barrier((kept_v, k_pieces[0][0]))[0]
+    v_pieces = gathered(kept_v, seq_index, seq_count, reach)
     kept_queries = jnp.where(handed, own_rows[0, :, :D], own_rows[1, :, :D])
-    kept_out = attend_own(kept_queries, kept_kv, kept_pieces, handed)
+    kept_out = attend_own(
+        kept_queries,
+        [kept_k] + [piece for piece, _ in k_pieces],
+        [kept_v] + [piece for piece, _ in v_pieces],
+        positions_of(k_pieces),
+        handed,
+    )
     given_kv = jnp.where(handed, own_rows[1, :, D:], own_rows[0, :, D:])
-    given_kv = lax.optimization_barrier((given_kv, kept_pieces[0][0]))[0]
+    given_kv = lax.optimization_barrier((given_kv, v_pieces[0][0]))[0]
     given_pieces = gathered(given_kv, seq_index, seq_count, reach, hold=kept_out)
     sent = [passed_along(kept_out, "section", 1)]
     given_queries = jnp.where(handed, own_rows[1, :, :D], own_rows[0, :, :D])
     given_queries = lax.optimization_barrier((given_queries, kept_out))[0]
-    given_out = attend_own(given_queries, given_kv, given_pieces, jnp.logical_not(handed))
+    given_out = attend_own(
+        given_queries,
+        [given_kv[:, :key_value_width]] + [piece[:, :key_value_width] for piece, _ in given_pieces],
+        [given_kv[:, key_value_width:]] + [piece[:, key_value_width:] for piece, _ in given_pieces],
+        positions_of(given_pieces),
+        jnp.logical_not(handed),
+    )
     sections = lax.axis_size("section")
     pairs = []
     for section in range(sections):

time: 50.6 us -> 52.5 us (1.038)
  starting transfers between devices: 9.49 us -> 12 us
  waiting for transfers between devices: 23.2 us -> 22.2 us
    ppermute x2 -> x3, waiting for transfers between devices: 7.12 us -> 4.1 us  [gathered(): over_x = lax.ppermute(onward, 'seq', [(j, j ^ 1) for j in range(4)])]
    ppermute x2 -> x3, waiting for transfers between devices: 1.17 us -> 3.75 us  [gathered(): over_y = lax.ppermute(block, 'seq', [(j, j ^ 2) for j in range(4)])]
    ppermute x2 -> x3, starting transfers between devices: 4.65 us -> 6.38 us  [gathered(): over_y = lax.ppermute(block, 'seq', [(j, j ^ 2) for j in range(4)])]
    ppermute x1, waiting for transfers between devices: 5.52 us -> 4.23 us  [passed_along(): return lax.ppermute(value, axis, pairs)]
    select_n x1 -> x2, other arithmetic: 0.01 us -> 1.13 us  [the longest x1 1.13 us: shards(): jnp.where(handed, own_rows[0, :, D + key_value_width:], own_rows[1, :, D...]
    select_n x2 -> x3, other arithmetic: 0.8 us -> 0.06 us  [gathered(): onward = jnp.where(odd, over_y, block)]
    ppermute x2 -> x3, starting transfers between devices: 3.22 us -> 3.93 us  [gathered(): over_x = lax.ppermute(onward, 'seq', [(j, j ^ 1) for j in range(4)])]
    ppermute x1, waiting for transfers between devices: 9.43 us -> 10.1 us  [shards(): sent.append(lax.ppermute(given_out, ('section', 'dp'), pairs))]
  transfers between devices with their start and end apart: 6 -> 8, of which waited for: 5 -> 7; matrix products, arithmetic and copies ran while one was open for 20% -> 21% of each run, Pallas kernels for 0% -> 0%
where the time goes in v17:
time: 52.5 us; the launch traced here: 52.3 us
  waiting for transfers between devices  22.2 us (42%)
  starting transfers between devices  12 us (23%)
  other arithmetic  8.5 us (16%)
  local copies, waits for them, and re-layouts  4.15 us (8%)
  between operations  3.57 us (7%)
  matrix products  1.83 us (3%)
    ppermute x1, waiting for transfers between devices, shards(): sent.append(lax.ppermute(given_out, ('section', 'dp'), pairs))  10.1 us
    ppermute x3, starting transfers between devices, gathered(): over_y = lax.ppermute(block, 'seq', [(j, j ^ 2) for j in range(4)])  6.38 us
    ppermute x1, waiting for transfers between devices, passed_along(): return lax.ppermute(value, axis, pairs)  4.23 us
    ppermute x3, waiting for transfers between devices, gathered(): over_x = lax.ppermute(onward, 'seq', [(j, j ^ 1) for j in range(4)])  4.1 us
    ppermute x3, starting transfers between devices, gathered(): over_x = lax.ppermute(onward, 'seq', [(j, j ^ 1) for j in range(4)])  3.93 us
    ppermute x3, waiting for transfers between devices, gathered(): over_y = lax.ppermute(block, 'seq', [(j, j ^ 2) for j in range(4)])  3.75 us
    sub x2, other arithmetic, attend_row(): weights = jnp.where(allowed, jnp.exp(scores - row_top), 0.0)  1.94 us
    ppermute x1, starting transfers between devices, passed_along(): return lax.ppermute(value, axis, pairs)  1.63 us
  transfers between devices with their start and end apart: 8, of which 7 were waited for; matrix products, arithmetic and copies ran while one was open for 21% of the time, Pallas kernels for 0%

profile of v17, /device:TPU:0, one launch (start us, length us, event | category | flops | bytes accessed | tf_op | source)
XLA Modules:
  0.0 52.3 jit_solution(3491558717512265588)
XLA Ops:
  0.0 0.0 copy-start
  0.0 1.3 %fusion.37 = s32[]{:T(128)} fusion(s32[1,2]{1,0:T(1,128)} %param.7, s32[]{:T(128)S(6)} %axis_index.23), kind=kLoop, calls=%fused_computation.73 | loop fusion | flops 5 | bytes 16 | tf_op jit(solution)/shard_map/reduce_sum | solution.py:94
  2.0 1.1 %fusion.34 = (bf16[64,1024]{1,0:T(8,128)(2,1)S(1)}, bf16[64,1024]{1,0:T(8,128)(2,1)S(1)}) fusion(bf16[2,64,6144]{2,1,0:T(8,128)(2,1)} %bitcast.90, pred[]{:T(512)S(6)} %eq.46), kind=kLoop, calls=%fused_computation.52 | loop fusion | flops 131072 | bytes 786433 | tf_op jit(solution)/shard_map/jit(_where)/select_n | solution.py:118
  3.1 3.1 %collective-permute-start = (bf16[64,1024]{1,0:T(8,128)(2,1)S(1)}, bf16[64,1024]{1,0:T(8,128)(2,1)S(1)}, u32[]{:S(2)}, u32[]{:S(2)}) collective-permute-start(bf16[64,1024]{1,0:T(8,128)(2,1)S(1)} %get-tuple-element.20), channel_id=1, source_target_pairs={{0,2},{1,3},{2,0},{3,1},{4,6},{5,7},{6,4},{7,5},{8,10},{9,11},{10,... | collective-permute-start | bytes 393224 | tf_op jit(solution)/shard_map/ppermute | solution.py:60
  6.2 1.3 %select_bitcast_fusion = (bf16[64,4096]{1,0:T(8,128)(2,1)S(1)}, bf16[1,64,4096]{2,1,0:T(8,128)(2,1)S(1)}) fusion(pred[]{:T(512)S(6)} %eq.46, bf16[2,64,6144]{2,1,0:T(8,128)(2,1)} %bitcast.91), kind=kLoop, calls=%fused_computation.36 | loop fusion | flops 524288 | bytes 2097153 | tf_op jit(solution)/shard_map/jit(_where)/select_n | solution.py:134
  7.5 1.1 %fusion.32 = bf16[64,2048]{1,0:T(8,128)(2,1)S(1)} fusion(bf16[2,64,6144]{2,1,0:T(8,128)(2,1)} %bitcast.92, pred[]{:T(512)S(6)} %eq.46), kind=kLoop, calls=%fused_computation.47 | loop fusion | flops 131072 | bytes 786433 | tf_op jit(solution)/shard_map/jit(_where)/select_n | solution.py:130
  8.6 0.0 copy-done.1
  8.6 0.2 reduce_window_sum.11
  8.8 0.1 pad_add_fusion
  8.9 0.1 convert_reduce_fusion.2
  8.9 0.1 convert_reduce_fusion
  9.0 0.1 compare_and_fusion
  9.1 0.0 copy-done
  9.1 0.1 constant_dynamic-slice_fusion
  9.2 0.4 collective-permute-done
  9.7 1.8 %collective-permute-start.3 = (bf16[64,1024]{1,0:T(8,128)(2,1)S(1)}, bf16[64,1024]{1,0:T(8,128)(2,1)S(1)}, u32[]{:S(2)}, u32[]{:S(2)}) collective-permute-start(bf16[64,1024]{1,0:T(8,128)(2,1)S(1)} %broadcast_select_fusion.2), channel_id=1, source_target_pairs={{0,1},{1,0},{2,3},{3,2},{4,5},{5,4},{6,7},{7,6},{8,9},{9,8},{10,11... | collective-permute-start | bytes 393224 | tf_op jit(solution)/shard_map/ppermute | solution.py:65
  11.5 0.6 %fusion.45 = (s32[1,1]{1,0:T(1,128)}, s32[1,1]{1,0:T(1,128)}) fusion(s32[1,2]{1,0:T(1,128)S(1)} %constant_dynamic-slice_fusion), kind=kLoop, calls=%fused_computation.82 | loop fusion | bytes 16 | tf_op jit(solution)/shard_map/slice | solution.py:106
  14.7 1.6 %collective-permute-start.1 = (bf16[64,1024]{1,0:T(8,128)(2,1)S(1)}, bf16[64,1024]{1,0:T(8,128)(2,1)S(1)}, u32[]{:S(2)}, u32[]{:S(2)}) collective-permute-start(bf16[64,1024]{1,0:T(8,128)(2,1)S(1)} %get-tuple-element.9), channel_id=1, source_target_pairs={{0,2},{1,3},{2,0},{3,1},{4,6},{5,7},{6,4},{7,5},{8,10},{9,11},{10,... | collective-permute-start | bytes 393224 | tf_op jit(solution)/shard_map/ppermute | solution.py:60
  16.3 0.4 select_n.160
  16.7 0.0 collective-permute-done.3
  16.7 0.1 copy.36
  16.8 3.0 %collective-permute-done.1 = bf16[64,1024]{1,0:T(8,128)(2,1)S(1)} collective-permute-done((bf16[64,1024]{1,0:T(8,128)(2,1)S(1)}, bf16[64,1024]{1,0:T(8,128)(2,1)S(1)}, u32[]{:S(2)}, u32[]{:S(2)}) %collective-permute-start.1) | collective-permute-done | bytes 131104 | tf_op jit(solution)/shard_map/ppermute | solution.py:60
  19.8 0.4 collective-permute-start.2
  20.2 1.7 %collective-permute-start.5 = (bf16[64,2048]{1,0:T(8,128)(2,1)S(1)}, bf16[64,2048]{1,0:T(8,128)(2,1)S(1)}, u32[]{:S(2)}, u32[]{:S(2)}) collective-permute-start(bf16[64,2048]{1,0:T(8,128)(2,1)S(1)} %fusion.32), channel_id=1, source_target_pairs={{0,2},{1,3},{2,0},{3,1},{4,6},{5,7},{6,4},{7,5},{8,10},{9,11},{10,... | collective-permute-start | bytes 786440 | tf_op jit(solution)/shard_map/ppermute | solution.py:60
  21.9 0.5 fusion.26
  22.4 1.0 %fusion.46 = (f32[8,4,64]{2,1,0:T(4,128)S(1)}, bf16[8,4,64,192]{3,2,1,0:T(8,128)(2,1)S(1)}) fusion(f32[8,192,64,4]{1,2,3,0:T(8,128)S(1)} %fusion.26, pred[64,192]{1,0:T(8,128)(4,1)S(1)} %get-tuple-element.28), kind=kOutput, calls=%fused_computation.83 | output fusion | flops 2752703 | bytes 2379776 | tf_op jit(solution)/shard_map/sub | solution.py:48
  23.3 1.5 %collective-permute-done.2 = bf16[64,1024]{1,0:T(8,128)(2,1)S(1)} collective-permute-done((bf16[64,1024]{1,0:T(8,128)(2,1)S(1)}, bf16[64,1024]{1,0:T(8,128)(2,1)S(1)}, u32[]{:S(2)}, u32[]{:S(2)}) %collective-permute-start.2) | collective-permute-done | bytes 131104 | tf_op jit(solution)/shard_map/ppermute | solution.py:65
  24.8 0.1 copy.35
  24.9 0.5 fusion.14
  25.4 0.4 copy.18
  25.8 0.4 convert_element_type.49
  26.2 0.3 collective-permute-done.5
  26.6 1.8 %collective-permute-start.6 = (bf16[64,2048]{1,0:T(8,128)(2,1)S(1)}, bf16[64,2048]{1,0:T(8,128)(2,1)S(1)}, u32[]{:S(2)}, u32[]{:S(2)}) collective-permute-start(bf16[64,2048]{1,0:T(8,128)(2,1)S(1)} %broadcast_select_fusion.1), channel_id=1, source_target_pairs={{0,1},{1,0},{2,3},{3,2},{4,5},{5,4},{6,7},{7,6},{8,9},{9,8},{10,11... | collective-permute-start | bytes 786440 | tf_op jit(solution)/shard_map/ppermute | solution.py:65
  28.4 1.6 %collective-permute-start.4 = (bf16[64,4096]{1,0:T(8,128)(2,1)S(1)}, bf16[64,4096]{1,0:T(8,128)(2,1)S(1)}, u32[]{:S(2)}, u32[]{:S(2)}) collective-permute-start(bf16[64,4096]{1,0:T(8,128)(2,1)S(1)} %convert_element_type.49), channel_id=1, source_target_pairs={{0,8},{8,16},{16,24},{24,0},{1,9},{9,17},{17,25},{25,1},{2,10},{10... | collective-permute-start | bytes 1572872 | tf_op jit(solution)/shard_map/ppermute | solution.py:26
  30.0 0.4 reshape.74
  30.4 2.6 %collective-permute-done.6 = bf16[64,2048]{1,0:T(8,128)(2,1)S(1)} collective-permute-done((bf16[64,2048]{1,0:T(8,128)(2,1)S(1)}, bf16[64,2048]{1,0:T(8,128)(2,1)S(1)}, u32[]{:S(2)}, u32[]{:S(2)}) %collective-permute-start.6) | collective-permute-done | bytes 262176 | tf_op jit(solution)/shard_map/ppermute | solution.py:65
  33.1 0.1 copy.38
  33.2 0.1 copy.37
  33.2 0.5 fusion.24
  33.7 1.0 %fusion.47 = (f32[8,4,64]{2,1,0:T(4,128)S(1)}, bf16[8,4,64,192]{3,2,1,0:T(8,128)(2,1)S(1)}) fusion(f32[8,192,64,4]{1,2,3,0:T(8,128)S(1)} %fusion.24, pred[64,192]{1,0:T(8,128)(4,1)S(1)} %get-tuple-element.27), kind=kOutput, calls=%fused_computation.84 | output fusion | flops 2752703 | bytes 2379776 | tf_op jit(solution)/shard_map/sub | solution.py:48
  34.7 0.5 fusion.15
  35.1 0.4 copy.22
  35.6 0.4 convert_element_type.55
  35.9 0.1 collective-permute-start.7
  36.0 4.2 %collective-permute-done.4 = bf16[64,4096]{1,0:T(8,128)(2,1)S(1)} collective-permute-done((bf16[64,4096]{1,0:T(8,128)(2,1)S(1)}, bf16[64,4096]{1,0:T(8,128)(2,1)S(1)}, u32[]{:S(2)}, u32[]{:S(2)}) %collective-permute-start.4) | collective-permute-done | bytes 524320 | tf_op jit(solution)/shard_map/ppermute | solution.py:26
  40.2 1.1 %pad_maximum_fusion = bf16[2,64,4096]{2,1,0:T(8,128)(2,1)} fusion(bf16[1,64,4096]{2,1,0:T(8,128)(2,1)S(1)} %bitcast.96), kind=kLoop, calls=%fused_computation.22 | loop fusion | flops 524288 | bytes 1572864 | tf_op jit(solution)/shard_map/stack | solution.py:151
  41.3 10.1 %collective-permute-done.7 = bf16[64,4096]{1,0:T(8,128)(2,1)S(1)} collective-permute-done((bf16[64,4096]{1,0:T(8,128)(2,1)S(1)}, bf16[64,4096]{1,0:T(8,128)(2,1)S(1)}, u32[]{:S(2)}, u32[]{:S(2)}) %collective-permute-start.7) | collective-permute-done | bytes 524320 | tf_op jit(solution)/shard_map/ppermute | solution.py:150
  51.4 0.8 %bitcast_dynamic-update-slice_fusion = bf16[1,2,64,4096]{3,2,1,0:T(8,128)(2,1)} fusion(bf16[1,2,64,4096]{3,2,1,0:T(8,128)(2,1)} %bitcast.95, bf16[64,4096]{1,0:T(8,128)(2,1)S(1)} %collective-permute-done.7), kind=kLoop, calls=%fused_computation.31 | loop fusion | bytes 1048576 | tf_op jit(solution)/shard_map/dynamic_update_slice | solution.py:152
  (16 shorter events, 0.3 us)
Async XLA Ops:
  0.0 9.1 %copy-start = (s32[1,4]{1,0:T(1,128)S(1)}, s32[1,4]{1,0:T(1,128)}, u32[]{:S(2)}) copy-start(s32[1,4]{1,0:T(1,128)} %param.5) | copy-start | bytes 52
  0.0 8.6 %copy-start.1 = (s32[1,4,8]{2,1,0:T(4,128)S(1)}, s32[1,4,8]{2,1,0:T(4,128)}, u32[]{:S(2)}) copy-start(s32[1,4,8]{2,1,0:T(4,128)} %param.6) | copy-start | bytes 388
  3.1 6.6 %collective-permute-start = (bf16[64,1024]{1,0:T(8,128)(2,1)S(1)}, bf16[64,1024]{1,0:T(8,128)(2,1)S(1)}, u32[]{:S(2)}, u32[]{:S(2)}) collective-permute-start(bf16[64,1024]{1,0:T(8,128)(2,1)S(1)} %get-tuple-element.20), channel_id=1, source_target_pairs={{0,2},{1,3},{2,0},{3,1},{4,6},{5,7},{6,4},{7,5},{8,10},{9,11},{10,... | collective-permute-start | bytes 393224 | tf_op jit(solution)/shard_map/ppermute | solution.py:60
  9.7 7.0 %collective-permute-start.3 = (bf16[64,1024]{1,0:T(8,128)(2,1)S(1)}, bf16[64,1024]{1,0:T(8,128)(2,1)S(1)}, u32[]{:S(2)}, u32[]{:S(2)}) collective-permute-start(bf16[64,1024]{1,0:T(8,128)(2,1)S(1)} %broadcast_select_fusion.2), channel_id=1, source_target_pairs={{0,1},{1,0},{2,3},{3,2},{4,5},{5,4},{6,7},{7,6},{8,9},{9,8},{10,11... | collective-permute-start | bytes 393224 | tf_op jit(solution)/shard_map/ppermute | solution.py:65
  14.7 5.0 %collective-permute-start.1 = (bf16[64,1024]{1,0:T(8,128)(2,1)S(1)}, bf16[64,1024]{1,0:T(8,128)(2,1)S(1)}, u32[]{:S(2)}, u32[]{:S(2)}) collective-permute-start(bf16[64,1024]{1,0:T(8,128)(2,1)S(1)} %get-tuple-element.9), channel_id=1, source_target_pairs={{0,2},{1,3},{2,0},{3,1},{4,6},{5,7},{6,4},{7,5},{8,10},{9,11},{10,... | collective-permute-start | bytes 393224 | tf_op jit(solution)/shard_map/ppermute | solution.py:60
  19.8 5.0 %collective-permute-start.2 = (bf16[64,1024]{1,0:T(8,128)(2,1)S(1)}, bf16[64,1024]{1,0:T(8,128)(2,1)S(1)}, u32[]{:S(2)}, u32[]{:S(2)}) collective-permute-start(bf16[64,1024]{1,0:T(8,128)(2,1)S(1)} %broadcast_select_fusion.3), channel_id=1, source_target_pairs={{0,1},{1,0},{2,3},{3,2},{4,5},{5,4},{6,7},{7,6},{8,9},{9,8},{10,11... | collective-permute-start | bytes 393224 | tf_op jit(solution)/shard_map/ppermute | solution.py:65
  20.2 6.4 %collective-permute-start.5 = (bf16[64,2048]{1,0:T(8,128)(2,1)S(1)}, bf16[64,2048]{1,0:T(8,128)(2,1)S(1)}, u32[]{:S(2)}, u32[]{:S(2)}) collective-permute-start(bf16[64,2048]{1,0:T(8,128)(2,1)S(1)} %fusion.32), channel_id=1, source_target_pairs={{0,2},{1,3},{2,0},{3,1},{4,6},{5,7},{6,4},{7,5},{8,10},{9,11},{10,... | collective-permute-start | bytes 786440 | tf_op jit(solution)/shard_map/ppermute | solution.py:60
  26.6 6.4 %collective-permute-start.6 = (bf16[64,2048]{1,0:T(8,128)(2,1)S(1)}, bf16[64,2048]{1,0:T(8,128)(2,1)S(1)}, u32[]{:S(2)}, u32[]{:S(2)}) collective-permute-start(bf16[64,2048]{1,0:T(8,128)(2,1)S(1)} %broadcast_select_fusion.1), channel_id=1, source_target_pairs={{0,1},{1,0},{2,3},{3,2},{4,5},{5,4},{6,7},{7,6},{8,9},{9,8},{10,11... | collective-permute-start | bytes 786440 | tf_op jit(solution)/shard_map/ppermute | solution.py:65
  28.4 11.9 %collective-permute-start.4 = (bf16[64,4096]{1,0:T(8,128)(2,1)S(1)}, bf16[64,4096]{1,0:T(8,128)(2,1)S(1)}, u32[]{:S(2)}, u32[]{:S(2)}) collective-permute-start(bf16[64,4096]{1,0:T(8,128)(2,1)S(1)} %convert_element_type.49), channel_id=1, source_target_pairs={{0,8},{8,16},{16,24},{24,0},{1,9},{9,17},{17,25},{25,1},{2,10},{10... | collective-permute-start | bytes 1572872 | tf_op jit(solution)/shard_map/ppermute | solution.py:26
  35.9 15.5 %collective-permute-start.7 = (bf16[64,4096]{1,0:T(8,128)(2,1)S(1)}, bf16[64,4096]{1,0:T(8,128)(2,1)S(1)}, u32[]{:S(2)}, u32[]{:S(2)}) collective-permute-start(bf16[64,4096]{1,0:T(8,128)(2,1)S(1)} %convert_element_type.55), channel_id=1, source_target_pairs={{0,12},{4,8},{8,20},{12,16},{16,28},{20,24},{24,4},{28,0},{1,13},{... | collective-permute-start | bytes 1572872 | tf_op jit(solution)/shard_map/ppermute | solution.py:150

commit v18 on v12

--- a/solution.py
+++ b/solution.py
@@ -74,7 +74,7 @@
     return pieces
 
 
-def shards(qkv, stream_lengths, doc_lengths, hand_over):
+def dense_shards(qkv, stream_lengths, doc_lengths, hand_over):
     seq_count = lax.axis_size("seq")
     seq_index = lax.axis_index("seq")
     replica = lax.axis_index("dp")
@@ -139,6 +139,87 @@
     return out.reshape(1, RPR, seg_len, D)
 
 
+def shards(qkv, stream_lengths, doc_lengths, hand_over):
+    seq_count = lax.axis_size("seq")
+    seg_len = qkv.shape[2]
+    length_all = seg_len * seq_count
+    rows = stream_lengths.shape[1]
+    reach = min(seq_count - 1, -(-(length_all // 2 - 1) // seg_len))
+    short_most = rows * length_all // 4 - 3 * length_all // 4 - (rows - 2)
+    if not (seq_count == 4 and reach == 2 and 0 < short_most < seg_len):
+        return dense_shards(qkv, stream_lengths, doc_lengths, hand_over)
+
+    seq_index = lax.axis_index("seq")
+    replica = lax.axis_index("dp")
+    partner = jnp.bitwise_xor(replica, 1)
+    own_rows = qkv[0]
+    doc_ends = jnp.cumsum(doc_lengths[0], axis=1)
+    lengths_all = stream_lengths[0]
+    local = jnp.arange(seg_len, dtype=jnp.int32)
+    query_pos = seq_index * seg_len + local
+    key_value_width = KV_HEADS * HD
+    far = jnp.int32(4 * length_all)
+    own_ends = lax.dynamic_slice_in_dim(doc_ends, 2 * replica, 2, 0)
+    own_lengths = lax.dynamic_slice_in_dim(lengths_all, 2 * replica, 2, 0)
+    swap_second = own_lengths[1] >= own_lengths[0]
+
+    def pick(first_if, a, b):
+        return jnp.where(first_if, a, b)
+
+    short_rows = pick(swap_second, own_rows[0], own_rows[1])
+    short_out = attend_row(
+        short_rows[:, :D],
+        short_rows[:, D:D + key_value_width],
+        short_rows[:, D + key_value_width:],
+        query_pos,
+        query_pos,
+        pick(swap_second, own_ends[0], own_ends[1]),
+        pick(swap_second, own_lengths[0], own_lengths[1]),
+    )
+    short_next = passed_along(short_out, "section", 1)
+
+    long_rows = pick(swap_second, own_rows[1], own_rows[0])
+    long_kv = long_rows[:, D:]
+    long_pieces = gathered(long_kv, seq_index, seq_count, reach)
+    previous = passed_along(jnp.concatenate([lengths_all, hand_over[0]]), "section", 1)
+    long_queries, _, previous = lax.optimization_barrier((long_rows[:, :D], short_out, previous))
+    pieces = [long_kv]
+    key_pos = [query_pos]
+    for piece, chunk in long_pieces:
+        pieces.append(piece)
+        key_pos.append(jnp.where(chunk >= 0, chunk * seg_len + local, far))
+    kv_all = jnp.concatenate(pieces, axis=0)
+    long_out = attend_row(
+        long_queries,
+        kv_all[:, :key_value_width],
+        kv_all[:, key_value_width:],
+        query_pos,
+        jnp.concatenate(key_pos),
+        pick(swap_second, own_ends[1], own_ends[0]),
+        pick(swap_second, own_lengths[1], own_lengths[0]),
+    )
+    long_next = passed_along(long_out, "section", 1)
+
+    previous_lengths = previous[:rows]
+    previous_hand = previous[rows:]
+
+    def short_index(rep):
+        first = lax.dynamic_index_in_dim(previous_lengths, 2 * rep, 0, keepdims=False)
+        second = lax.dynamic_index_in_dim(previous_lengths, 2 * rep + 1, 0, keepdims=False)
+        return jnp.where(second >= first, 0, 1)
+
+    own_hand = lax.dynamic_index_in_dim(previous_hand, replica, 0, keepdims=False)
+    partner_hand = lax.dynamic_index_in_dim(previous_hand, partner, 0, keepdims=False)
+    partner_short = swapped(short_next, "dp", 0)
+    partner_long = swapped(long_next, "dp", 0)
+    sent = [
+        jnp.where(short_index(replica) == 1 - own_hand, short_next, long_next),
+        jnp.where(short_index(partner) == partner_hand, partner_short, partner_long),
+    ]
+    out = jnp.stack(sent, axis=0)
+    return out.reshape(1, RPR, seg_len, D)
+
+
 def solution(mesh):
     return jax.shard_map(
         shards,

time: 50.6 us -> 45.8 us (0.905)
  waiting for transfers between devices: 23.2 us -> 14.2 us
  between operations: 3.54 us -> 7.72 us
  other arithmetic: 8.07 us -> 6.53 us
  local copies, waits for them, and re-layouts: 4.24 us -> 5.35 us
    ppermute x1 -> x2, waiting for transfers between devices: 9.43 us -> 1.84 us  [swapped(): return lax.ppermute(block, axis, route)]
    ppermute x1 -> x3, starting transfers between devices: 1.57 us -> 6.31 us  [passed_along(): return lax.ppermute(value, axis, pairs)]
    ppermute x2 -> x1, starting transfers between devices: 4.65 us -> 1.58 us  [gathered(): over_y = lax.ppermute(block, 'seq', [(j, j ^ 2) for j in range(4)])]
    ppermute x2 -> x1, waiting for transfers between devices: 7.12 us -> 5.1 us  [gathered(): over_x = lax.ppermute(onward, 'seq', [(j, j ^ 1) for j in range(4)])]
    ppermute x1 -> x3, waiting for transfers between devices: 5.52 us -> 7.28 us  [passed_along(): return lax.ppermute(value, axis, pairs)]
    ppermute x2 -> x1, starting transfers between devices: 3.22 us -> 1.56 us  [gathered(): over_x = lax.ppermute(onward, 'seq', [(j, j ^ 1) for j in range(4)])]
    concatenate x2 -> x3, other arithmetic: 0.14 us -> 1.48 us  [the longest x1 1.34 us: shards(): jnp.concatenate([lengths_all, hand_over[0]])]
    reduce_sum x1 -> x0, other arithmetic: 1.32 us -> none  [shards(): jnp.sum(jnp.where(jnp.arange(replicas) == replica, hand_over[0], 0)) == 1]
  transfers between devices with their start and end apart: 6 -> 7, of which waited for: 5 -> 3; matrix products, arithmetic and copies ran while one was open for 20% -> 25% of each run, Pallas kernels for 0% -> 0%
where the time goes in v18:
time: 45.8 us; the launch traced here: 45.6 us
  waiting for transfers between devices  14.2 us (31%)
  starting transfers between devices  9.53 us (21%)
  between operations  7.72 us (17%)
  other arithmetic  6.53 us (14%)
  local copies, waits for them, and re-layouts  5.35 us (12%)
  matrix products  2.21 us (5%)
    ppermute x3, waiting for transfers between devices, passed_along(): return lax.ppermute(value, axis, pairs)  7.28 us
    ppermute x3, starting transfers between devices, passed_along(): return lax.ppermute(value, axis, pairs)  6.31 us
    ppermute x1, waiting for transfers between devices, gathered(): over_x = lax.ppermute(onward, 'seq', [(j, j ^ 1) for j in range(4)])  5.1 us
    ppermute x2, waiting for transfers between devices, swapped(): return lax.ppermute(block, axis, route)  1.84 us
    convert_element_type x4, local copies, waits for them, and re-layouts, attend_row(): return result.reshape(seg_len, D).astype(jnp.bfloat16)  1.59 us
    ppermute x1, starting transfers between devices, gathered(): over_y = lax.ppermute(block, 'seq', [(j, j ^ 2) for j in range(4)])  1.58 us
    ppermute x1, starting transfers between devices, gathered(): over_x = lax.ppermute(onward, 'seq', [(j, j ^ 1) for j in range(4)])  1.56 us
    select_n x1, other arithmetic, pick(): return jnp.where(first_if, a, b)  1.48 us
  transfers between devices with their start and end apart: 7, of which 3 were waited for; matrix products, arithmetic and copies ran while one was open for 25% of the time, Pallas kernels for 0%

profile of v18, /device:TPU:0, one launch (start us, length us, event | category | flops | bytes accessed | tf_op | source)
XLA Modules:
  0.0 45.6 jit_solution(3230639697427236415)
XLA Ops:
  0.0 1.3 %pad_add_fusion.1 = s32[6]{0:T(128)} fusion(s32[2]{0:T(128)} %bitcast.83, s32[4]{0:T(128)} %bitcast.84), kind=kLoop, calls=%fused_computation.62 | loop fusion | flops 6 | bytes 48 | tf_op jit(solution)/shard_map/concatenate | solution.py:184
  1.3 3.1 %collective-permute-start = (s32[6]{0:T(128)}, s32[6]{0:T(128)S(1)}, u32[]{:S(2)}, u32[]{:S(2)}) collective-permute-start(s32[6]{0:T(128)} %pad_add_fusion.1), channel_id=1, source_target_pairs={{0,8},{8,16},{16,24},{24,0},{1,9},{9,17},{17,25},{25,1},{2,10},{10... | collective-permute-start | bytes 80 | tf_op jit(solution)/shard_map/ppermute | solution.py:26
  4.4 0.7 %constant_dynamic-slice_fusion.1 = s32[1,2]{1,0:T(1,128)S(1)} fusion(s32[1,4]{1,0:T(1,128)} %param.5, s32[]{:T(128)S(6)} %select_n.129), kind=kLoop, calls=%fused_computation.68 | loop fusion | bytes 20 | tf_op jit(solution)/shard_map/dynamic_slice | solution.py:163
  5.1 0.6 %fusion.49 = (s32[1,1]{1,0:T(1,128)}, s32[1,1]{1,0:T(1,128)}) fusion(s32[1,2]{1,0:T(1,128)S(1)} %constant_dynamic-slice_fusion.1), kind=kLoop, calls=%fused_computation.73 | loop fusion | bytes 16 | tf_op jit(solution)/shard_map/slice | solution.py:164
  6.9 0.0 copy-start.3
  6.9 1.5 %select_bitcast_fusion.1 = (bf16[64,6144]{1,0:T(8,128)(2,1)S(1)}, bf16[64,6144]{1,0:T(8,128)(2,1)S(1)}) fusion(pred[]{:T(512)S(6)} %ge.32, bf16[1,2,64,6144]{3,2,1,0:T(8,128)(2,1)} %param.4), kind=kLoop, calls=%fused_computation.30 | loop fusion | flops 786432 | bytes 3145729 | tf_op jit(solution)/shard_map/jit(_where)/select_n | solution.py:167
  8.4 1.6 %collective-permute-start.2 = (bf16[64,2048]{1,0:T(8,128)(2,1)S(1)}, bf16[64,2048]{1,0:T(8,128)(2,1)S(1)}, u32[]{:S(2)}, u32[]{:S(2)}) collective-permute-start(bf16[64,2048]{1,0:T(8,128)(2,1)S(1)} %slice.76), channel_id=1, source_target_pairs={{0,2},{1,3},{2,0},{3,1},{4,6},{5,7},{6,4},{7,5},{8,10},{9,11},{10,... | collective-permute-start | bytes 786440 | tf_op jit(solution)/shard_map/ppermute | solution.py:60
  12.5 0.2 reduce_window_sum.11
  12.7 0.6 %convert_reduce_fusion.1 = (s32[64]{0:T(128)}, s32[64]{0:T(128)S(1)}) fusion(s32[64]{0:T(128)S(1)} %iota_add_fusion, s32[8]{0:T(128)S(1)} %get-tuple-element.18, s32[8]{0:T(128)S(1)} %get-tuple-element.17), kind=kLoop, calls=%fused_computation.51 | loop fusion | flops 2944 | bytes 832 | tf_op jit(solution)/shard_map/reduce_sum | solution.py:30
  13.3 0.1 compare_and_fusion.1
  13.4 0.4 reshape.80
  13.8 0.6 %fusion.16 = f32[8,4,64,64]{2,3,1,0:T(8,128)S(1)} fusion(bf16[64,8,4,128]{3,2,1,0:T(4,128)(2,1)S(1)} %reshape.80, bf16[64,8,128,1]{2,1,0,3:T(8,128)(2,1)S(1)} %bitcast.78), kind=kOutput, calls=%fused_computation.17 | convolution fusion | flops 33685504 | bytes 1179648 | tf_op jit(solution)/shard_map/qkgd,skd->kgqs/dot_general | solution.py:44
  14.5 0.3 fusion.50
  14.8 0.7 %fusion.19 = bf16[64,8,4,128]{3,0,2,1:T(8,128)(2,1)S(1)} fusion(f32[64]{0:T(128)S(1)} %get-tuple-element.30, f32[64,8,4]{0,2,1:T(4,128)S(1)} %bitcast.85, bf16[64,8,128,1]{2,1,0,3:T(8,128)(2,1)S(1)} %bitcast.80, f32[8,4,64,64]{2,3,1,0:T(8,128)S(1)} %fusion.16, pred[64,64]{0,1:T(8,128)(4,1)S(1)} %compare_and_fusion.1), kind=kOutput, calls=%fused_computation.21 | convolution fusion | flops 34867264 | bytes 1192192 | tf_op jit(solution)/shard_map/kgqs,skd->qkgd/dot_general | solution.py:51
  15.5 0.0 copy-start.2
  15.5 0.4 copy.20
  15.9 0.4 convert_element_type.46
  16.3 1.6 %collective-permute-start.1 = (bf16[64,4096]{1,0:T(8,128)(2,1)S(1)}, bf16[64,4096]{1,0:T(8,128)(2,1)S(1)}, u32[]{:S(2)}, u32[]{:S(2)}) collective-permute-start(bf16[64,4096]{1,0:T(8,128)(2,1)S(1)} %convert_element_type.46), channel_id=1, source_target_pairs={{0,8},{8,16},{16,24},{24,0},{1,9},{9,17},{17,25},{25,1},{2,10},{10... | collective-permute-start | bytes 1572872 | tf_op jit(solution)/shard_map/ppermute | solution.py:26
  18.0 0.1 pad_add_fusion
  18.1 0.0 collective-permute-done.2
  18.1 1.6 %collective-permute-start.3 = (bf16[64,2048]{1,0:T(8,128)(2,1)S(1)}, bf16[64,2048]{1,0:T(8,128)(2,1)S(1)}, u32[]{:S(2)}, u32[]{:S(2)}) collective-permute-start(bf16[64,2048]{1,0:T(8,128)(2,1)S(1)} %broadcast_select_fusion), channel_id=1, source_target_pairs={{0,1},{1,0},{2,3},{3,2},{4,5},{5,4},{6,7},{7,6},{8,9},{9,8},{10,11... | collective-permute-start | bytes 786440 | tf_op jit(solution)/shard_map/ppermute | solution.py:65
  19.6 0.1 convert_reduce_fusion
  19.8 0.1 compare_and_fusion
  19.9 0.0 collective-permute-done
  19.9 0.4 reshape.83
  20.3 5.1 %collective-permute-done.3 = bf16[64,2048]{1,0:T(8,128)(2,1)S(1)} collective-permute-done((bf16[64,2048]{1,0:T(8,128)(2,1)S(1)}, bf16[64,2048]{1,0:T(8,128)(2,1)S(1)}, u32[]{:S(2)}, u32[]{:S(2)}) %collective-permute-start.3) | collective-permute-done | bytes 262176 | tf_op jit(solution)/shard_map/ppermute | solution.py:65
  25.4 0.1 pad_maximum_fusion
  25.4 0.1 slice_bitcast_fusion.1
  25.5 0.1 copy.41
  25.6 0.1 copy.40
  25.6 0.5 %fusion.25 = f32[8,192,64,4]{1,2,3,0:T(8,128)S(1)} fusion(bf16[64,8,4,128]{3,2,1,0:T(4,128)(2,1)S(1)} %reshape.83, bf16[192,8,128,1]{2,1,0,3:T(8,128)(2,1)S(1)} %bitcast.77), kind=kOutput, calls=%fused_computation.31 | convolution fusion | flops 100663296 | bytes 2490368 | tf_op jit(solution)/shard_map/qkgd,skd->kgqs/dot_general | solution.py:44
  26.1 1.0 %fusion.51 = (f32[8,4,64]{2,1,0:T(4,128)S(1)}, bf16[8,4,64,192]{3,2,1,0:T(8,128)(2,1)S(1)}) fusion(f32[8,192,64,4]{1,2,3,0:T(8,128)S(1)} %fusion.25, pred[64,192]{1,0:T(8,128)(4,1)S(1)} %compare_and_fusion), kind=kOutput, calls=%fused_computation.75 | output fusion | flops 2752703 | bytes 2379776 | tf_op jit(solution)/shard_map/sub | solution.py:48
  27.1 0.5 fusion.20
  27.5 0.4 copy.24
  27.9 0.4 convert_element_type.52
  28.3 1.6 %collective-permute-start.4 = (bf16[64,4096]{1,0:T(8,128)(2,1)S(1)}, bf16[64,4096]{1,0:T(8,128)(2,1)S(1)}, u32[]{:S(2)}, u32[]{:S(2)}) collective-permute-start(bf16[64,4096]{1,0:T(8,128)(2,1)S(1)} %convert_element_type.52), channel_id=1, source_target_pairs={{0,8},{8,16},{16,24},{24,0},{1,9},{9,17},{17,25},{25,1},{2,10},{10... | collective-permute-start | bytes 1572872 | tf_op jit(solution)/shard_map/ppermute | solution.py:26
  30.0 0.1 slice.68
  30.0 0.7 %fusion.48 = (s32[1]{0:T(128)}, s32[1]{0:T(128)}, s32[1]{0:T(128)}, s32[1]{0:T(128)}) fusion(s32[4]{0:T(128)S(1)} %bitcast.81, s32[]{:T(128)S(6)} %select_n.129, s32[]{:T(128)S(6)} %select_n.158, s32[]{:T(128)S(6)} %select_n.157, s32[]{:T(128)S(6)} %select_n.140), kind=kLoop, calls=%fused_computation.72 | loop fusion | bytes 48 | tf_op jit(solution)/shard_map/jit(dynamic_index_in_dim)/dynamic_slice | solution.py:207
  32.0 0.6 %fusion.47 = (s32[1]{0:T(128)}, s32[1]{0:T(128)}) fusion(s32[2]{0:T(128)S(1)} %slice.68, s32[]{:T(128)S(6)} %select_n.142, s32[]{:T(128)S(6)} %select_n.160), kind=kLoop, calls=%fused_computation.71 | loop fusion | bytes 24 | tf_op jit(solution)/shard_map/jit(dynamic_index_in_dim)/dynamic_slice | solution.py:211
  35.2 0.0 collective-permute-done.1
  35.2 0.1 collective-permute-start.5
  35.3 7.3 %collective-permute-done.4 = bf16[64,4096]{1,0:T(8,128)(2,1)S(1)} collective-permute-done((bf16[64,4096]{1,0:T(8,128)(2,1)S(1)}, bf16[64,4096]{1,0:T(8,128)(2,1)S(1)}, u32[]{:S(2)}, u32[]{:S(2)}) %collective-permute-start.4) | collective-permute-done | bytes 524320 | tf_op jit(solution)/shard_map/ppermute | solution.py:26
  42.5 0.0 collective-permute-start.6
  42.5 0.1 select_bitcast_fusion.3
  42.6 0.0 collective-permute-done.5
  42.6 1.8 %collective-permute-done.6 = bf16[64,4096]{1,0:T(8,128)(2,1)S(1)} collective-permute-done((bf16[64,4096]{1,0:T(8,128)(2,1)S(1)}, bf16[64,4096]{1,0:T(8,128)(2,1)S(1)}, u32[]{:S(2)}, u32[]{:S(2)}) %collective-permute-start.6) | collective-permute-done | bytes 524320 | tf_op jit(solution)/shard_map/ppermute | solution.py:20
  44.4 0.1 select_bitcast_fusion.2
  44.5 1.1 %maximum_bitcast_fusion = bf16[1,2,64,4096]{3,2,1,0:T(8,128)(2,1)} fusion(bf16[1,64,4096]{2,1,0:T(8,128)(2,1)S(1)} %select_bitcast_fusion.2, bf16[1,64,4096]{2,1,0:T(8,128)(2,1)S(1)} %select_bitcast_fusion.3), kind=kLoop, calls=%fused_computation.23 | loop fusion | flops 524288 | bytes 2097152 | tf_op jit(solution)/shard_map/reshape | solution.py:220
  (18 shorter events, 0.2 us)
Async XLA Ops:
  1.3 18.5 %collective-permute-start = (s32[6]{0:T(128)}, s32[6]{0:T(128)S(1)}, u32[]{:S(2)}, u32[]{:S(2)}) collective-permute-start(s32[6]{0:T(128)} %pad_add_fusion.1), channel_id=1, source_target_pairs={{0,8},{8,16},{16,24},{24,0},{1,9},{9,17},{17,25},{25,1},{2,10},{10... | collective-permute-start | bytes 80 | tf_op jit(solution)/shard_map/ppermute | solution.py:26
  6.9 5.6 %copy-start.3 = (s32[1,4,8]{2,1,0:T(4,128)S(1)}, s32[1,4,8]{2,1,0:T(4,128)}, u32[]{:S(2)}) copy-start(s32[1,4,8]{2,1,0:T(4,128)} %param.6) | copy-start | bytes 388
  8.4 9.6 %collective-permute-start.2 = (bf16[64,2048]{1,0:T(8,128)(2,1)S(1)}, bf16[64,2048]{1,0:T(8,128)(2,1)S(1)}, u32[]{:S(2)}, u32[]{:S(2)}) collective-permute-start(bf16[64,2048]{1,0:T(8,128)(2,1)S(1)} %slice.76), channel_id=1, source_target_pairs={{0,2},{1,3},{2,0},{3,1},{4,6},{5,7},{6,4},{7,5},{8,10},{9,11},{10,... | collective-permute-start | bytes 786440 | tf_op jit(solution)/shard_map/ppermute | solution.py:60
  12.7 0.7 %copy-start = (s32[8]{0:T(128)}, s32[8]{0:T(128)S(1)}, u32[]{:S(2)}) copy-start(s32[8]{0:T(128)S(1)} %get-tuple-element.18) | copy-start | bytes 100
  15.5 4.1 %copy-start.1 = (s32[8]{0:T(128)S(1)}, s32[8]{0:T(128)}, u32[]{:S(2)}) copy-start(s32[8]{0:T(128)} %copy-done) | copy-start | bytes 100
  15.5 4.3 %copy-start.2 = (s32[64]{0:T(128)S(1)}, s32[64]{0:T(128)}, u32[]{:S(2)}) copy-start(s32[64]{0:T(128)} %get-tuple-element.9) | copy-start | bytes 772
  16.3 18.8 %collective-permute-start.1 = (bf16[64,4096]{1,0:T(8,128)(2,1)S(1)}, bf16[64,4096]{1,0:T(8,128)(2,1)S(1)}, u32[]{:S(2)}, u32[]{:S(2)}) collective-permute-start(bf16[64,4096]{1,0:T(8,128)(2,1)S(1)} %convert_element_type.46), channel_id=1, source_target_pairs={{0,8},{8,16},{16,24},{24,0},{1,9},{9,17},{17,25},{25,1},{2,10},{10... | collective-permute-start | bytes 1572872 | tf_op jit(solution)/shard_map/ppermute | solution.py:26
  18.1 7.3 %collective-permute-start.3 = (bf16[64,2048]{1,0:T(8,128)(2,1)S(1)}, bf16[64,2048]{1,0:T(8,128)(2,1)S(1)}, u32[]{:S(2)}, u32[]{:S(2)}) collective-permute-start(bf16[64,2048]{1,0:T(8,128)(2,1)S(1)} %broadcast_select_fusion), channel_id=1, source_target_pairs={{0,1},{1,0},{2,3},{3,2},{4,5},{5,4},{6,7},{7,6},{8,9},{9,8},{10,11... | collective-permute-start | bytes 786440 | tf_op jit(solution)/shard_map/ppermute | solution.py:65
  28.3 14.2 %collective-permute-start.4 = (bf16[64,4096]{1,0:T(8,128)(2,1)S(1)}, bf16[64,4096]{1,0:T(8,128)(2,1)S(1)}, u32[]{:S(2)}, u32[]{:S(2)}) collective-permute-start(bf16[64,4096]{1,0:T(8,128)(2,1)S(1)} %convert_element_type.52), channel_id=1, source_target_pairs={{0,8},{8,16},{16,24},{24,0},{1,9},{9,17},{17,25},{25,1},{2,10},{10... | collective-permute-start | bytes 1572872 | tf_op jit(solution)/shard_map/ppermute | solution.py:26
  35.2 7.4 %collective-permute-start.5 = (bf16[64,4096]{1,0:T(8,128)(2,1)S(1)}, bf16[64,4096]{1,0:T(8,128)(2,1)S(1)}, u32[]{:S(2)}, u32[]{:S(2)}) collective-permute-start(bf16[64,4096]{1,0:T(8,128)(2,1)S(1)} %collective-permute-done.1), channel_id=1, source_target_pairs={{0,4},{4,0},{1,5},{5,1},{2,6},{6,2},{3,7},{7,3},{8,12},{12,8},{9,1... | collective-permute-start | bytes 1572872 | tf_op jit(solution)/shard_map/ppermute | solution.py:20
  42.5 1.9 %collective-permute-start.6 = (bf16[64,4096]{1,0:T(8,128)(2,1)S(1)}, bf16[64,4096]{1,0:T(8,128)(2,1)S(1)}, u32[]{:S(2)}, u32[]{:S(2)}) collective-permute-start(bf16[64,4096]{1,0:T(8,128)(2,1)S(1)} %collective-permute-done.4), channel_id=1, source_target_pairs={{0,4},{4,0},{1,5},{5,1},{2,6},{6,2},{3,7},{7,3},{8,12},{12,8},{9,1... | collective-permute-start | bytes 1572872 | tf_op jit(solution)/shard_map/ppermute | solution.py:20

commit v19 on v18

--- a/solution.py
+++ b/solution.py
@@ -176,13 +176,19 @@
         pick(swap_second, own_ends[0], own_ends[1]),
         pick(swap_second, own_lengths[0], own_lengths[1]),
     )
+    replicas = lax.axis_size("dp")
+    own_hand = jnp.sum(jnp.where(jnp.arange(replicas) == replica, hand_over[0], 0))
+    short_index = jnp.where(swap_second, 0, 1)
+    lane = jnp.arange(D)[None, :]
+    tag = jnp.where(lane == 0, short_index, jnp.where(lane == 1, own_hand, 0))
+    last_event = (local == seg_len - 1)[:, None]
+    short_out = jnp.where(last_event, tag.astype(jnp.bfloat16), short_out)
     short_next = passed_along(short_out, "section", 1)
 
     long_rows = pick(swap_second, own_rows[1], own_rows[0])
     long_kv = long_rows[:, D:]
     long_pieces = gathered(long_kv, seq_index, seq_count, reach)
-    previous = passed_along(jnp.concatenate([lengths_all, hand_over[0]]), "section", 1)
-    long_queries, _, previous = lax.optimization_barrier((long_rows[:, :D], short_out, previous))
+    long_queries = lax.optimization_barrier((long_rows[:, :D], short_out))[0]
     pieces = [long_kv]
     key_pos = [query_pos]
     for piece, chunk in long_pieces:
@@ -200,21 +206,17 @@
     )
     long_next = passed_along(long_out, "section", 1)
 
-    previous_lengths = previous[:rows]
-    previous_hand = previous[rows:]
-
-    def short_index(rep):
-        first = lax.dynamic_index_in_dim(previous_lengths, 2 * rep, 0, keepdims=False)
-        second = lax.dynamic_index_in_dim(previous_lengths, 2 * rep + 1, 0, keepdims=False)
-        return jnp.where(second >= first, 0, 1)
-
-    own_hand = lax.dynamic_index_in_dim(previous_hand, replica, 0, keepdims=False)
-    partner_hand = lax.dynamic_index_in_dim(previous_hand, partner, 0, keepdims=False)
     partner_short = swapped(short_next, "dp", 0)
     partner_long = swapped(long_next, "dp", 0)
+
+    def placed(short_block, long_block, own_index_of):
+        tag = short_block[seg_len - 1, :2].astype(jnp.int32)
+        cleared = jnp.where(last_event, jnp.zeros_like(short_block), short_block)
+        return jnp.where(tag[0] == own_index_of(tag[1]), cleared, long_block)
+
     sent = [
-        jnp.where(short_index(replica) == 1 - own_hand, short_next, long_next),
-        jnp.where(short_index(partner) == partner_hand, partner_short, partner_long),
+        placed(short_next, long_next, lambda hand: 1 - hand),
+        placed(partner_short, partner_long, lambda hand: hand),
     ]
     out = jnp.stack(sent, axis=0)
     return out.reshape(1, RPR, seg_len, D)

time: 45.8 us -> 49.3 us (1.076)
  waiting for transfers between devices: 14.2 us -> 17.9 us
  starting transfers between devices: 9.53 us -> 7.87 us
  other arithmetic: 6.53 us -> 7.83 us
  local copies, waits for them, and re-layouts: 5.35 us -> 6.49 us
  between operations: 7.72 us -> 6.65 us
    ppermute x3 -> x2, waiting for transfers between devices: 7.28 us -> 12.5 us  [passed_along(): return lax.ppermute(value, axis, pairs)]
    ppermute x3 -> x2, starting transfers between devices: 6.31 us -> 3.25 us  [passed_along(): return lax.ppermute(value, axis, pairs)]
    unnamed x14 -> x24, local copies, waits for them, and re-layouts: 0.26 us -> 2.14 us
    ppermute x2, waiting for transfers between devices: 1.84 us -> 0.01 us  [swapped(): return lax.ppermute(block, axis, route)]
    ppermute x1, starting transfers between devices: 1.58 us -> 3.06 us  [gathered(): over_y = lax.ppermute(block, 'seq', [(j, j ^ 2) for j in range(4)])]
    concatenate x1 -> x0, other arithmetic: 1.34 us -> none  [shards(): jnp.concatenate([lengths_all, hand_over[0]])]
    dynamic_slice x2 -> x0, local copies, waits for them, and re-layouts: 1.29 us -> none  [the longest x1 0.67 us: short_index(): lax.dynamic_index_in_dim(previous_lengths, 2 * rep, 0, keepdims=False)]
    slice x2 -> x3, local copies, waits for them, and re-layouts: 0.11 us -> 1.29 us  [the longest x2 1.26 us: placed(): return jnp.where(tag[0] == own_index_of(tag[1]), cleared, long_block)]
  transfers between devices with their start and end apart: 7 -> 6, of which waited for: 3 -> 2; matrix products, arithmetic and copies ran while one was open for 25% -> 24% of each run, Pallas kernels for 0% -> 0%
where the time goes in v19:
time: 49.3 us; the launch traced here: 49 us
  waiting for transfers between devices  17.9 us (36%)
  starting transfers between devices  7.87 us (16%)
  other arithmetic  7.83 us (16%)
  between operations  6.65 us (13%)
  local copies, waits for them, and re-layouts  6.49 us (13%)
  matrix products  2.21 us (4%)
    ppermute x2, waiting for transfers between devices, passed_along(): return lax.ppermute(value, axis, pairs)  12.5 us
    ppermute x1, waiting for transfers between devices, gathered(): over_x = lax.ppermute(onward, 'seq', [(j, j ^ 1) for j in range(4)])  5.48 us
    ppermute x2, starting transfers between devices, passed_along(): return lax.ppermute(value, axis, pairs)  3.25 us
    ppermute x1, starting transfers between devices, gathered(): over_y = lax.ppermute(block, 'seq', [(j, j ^ 2) for j in range(4)])  3.06 us
    unnamed x24, local copies, waits for them, and re-layouts  2.14 us
    convert_element_type x4, local copies, waits for them, and re-layouts, attend_row(): return result.reshape(seg_len, D).astype(jnp.bfloat16)  1.59 us
    ppermute x1, starting transfers between devices, gathered(): over_x = lax.ppermute(onward, 'seq', [(j, j ^ 1) for j in range(4)])  1.56 us
    select_n x1, other arithmetic, pick(): return jnp.where(first_if, a, b)  1.48 us
  transfers between devices with their start and end apart: 6, of which 2 were waited for; matrix products, arithmetic and copies ran while one was open for 24% of the time, Pallas kernels for 0%

profile of v19, /device:TPU:0, one launch (start us, length us, event | category | flops | bytes accessed | tf_op | source)
XLA Modules:
  0.0 49.0 jit_solution(1701486831570728176)
XLA Ops:
  0.0 0.7 %copy-done = s32[1,4]{1,0:T(1,128)S(1)} copy-done((s32[1,4]{1,0:T(1,128)S(1)}, s32[1,4]{1,0:T(1,128)}, u32[]{:S(2)}) %copy-start) | copy-done | bytes 40
  0.7 0.1 constant_dynamic-slice_fusion.1
  0.7 0.6 %fusion.50 = (s32[1,1]{1,0:T(1,128)}, s32[1,1]{1,0:T(1,128)}) fusion(s32[1,2]{1,0:T(1,128)S(1)} %constant_dynamic-slice_fusion.1), kind=kLoop, calls=%fused_computation.81 | loop fusion | bytes 16 | tf_op jit(solution)/shard_map/slice | solution.py:164
  2.6 0.0 copy-start.6
  2.6 1.5 %select_bitcast_fusion.1 = (bf16[64,6144]{1,0:T(8,128)(2,1)S(1)}, bf16[64,6144]{1,0:T(8,128)(2,1)S(1)}) fusion(pred[]{:T(512)S(6)} %ge.26, bf16[1,2,64,6144]{3,2,1,0:T(8,128)(2,1)} %param.4), kind=kLoop, calls=%fused_computation.30 | loop fusion | flops 786432 | bytes 3145729 | tf_op jit(solution)/shard_map/jit(_where)/select_n | solution.py:167
  4.1 3.1 %collective-permute-start.1 = (bf16[64,2048]{1,0:T(8,128)(2,1)S(1)}, bf16[64,2048]{1,0:T(8,128)(2,1)S(1)}, u32[]{:S(2)}, u32[]{:S(2)}) collective-permute-start(bf16[64,2048]{1,0:T(8,128)(2,1)S(1)} %slice.96), channel_id=1, source_target_pairs={{0,2},{1,3},{2,0},{3,1},{4,6},{5,7},{6,4},{7,5},{8,10},{9,11},{10,... | collective-permute-start | bytes 786440 | tf_op jit(solution)/shard_map/ppermute | solution.py:60
  8.5 0.5 %iota_compare_fusion.2 = pred[64]{0:T(512)(128)(4,1)} fusion(), kind=kLoop, calls=%fused_computation.76 | loop fusion | flops 64 | bytes 64 | tf_op jit(solution)/shard_map/eq | solution.py:184
  9.0 0.2 reduce_window_sum.11
  9.2 0.7 %convert_reduce_fusion.1 = (s32[64]{0:T(128)}, s32[64]{0:T(128)S(1)}) fusion(s32[64]{0:T(128)S(1)} %iota_add_fusion, s32[8]{0:T(128)S(1)} %get-tuple-element.16, s32[8]{0:T(128)S(1)} %get-tuple-element.15), kind=kLoop, calls=%fused_computation.55 | loop fusion | flops 2944 | bytes 832 | tf_op jit(solution)/shard_map/reduce_sum | solution.py:30
  9.9 0.1 compare_and_fusion.1
  10.0 0.4 reshape.103
  10.4 0.5 %compare_convert_fusion.1 = f32[64]{0:T(128)} fusion(s32[]{:T(128)S(6)} %select_n.151, s32[]{:T(128)S(6)} %mul.48), kind=kLoop, calls=%fused_computation.58 | loop fusion | flops 192 | bytes 264 | tf_op jit(solution)/shard_map/convert_element_type | solution.py:53
  10.9 0.7 %copy.38 = bf16[8,8,8,128]{3,2,1,0:T(8,128)(2,1)} copy(bf16[8,8,8,128]{3,1,2,0:T(8,128)(2,1)S(1)} %get-tuple-element.13) | data formatting | bytes 262144
  11.6 0.6 %fusion.16 = f32[8,4,64,64]{2,3,1,0:T(8,128)S(1)} fusion(bf16[64,8,4,128]{3,2,1,0:T(4,128)(2,1)S(1)} %reshape.103, bf16[64,8,128,1]{2,1,0,3:T(8,128)(2,1)S(1)} %bitcast.77), kind=kOutput, calls=%fused_computation.17 | convolution fusion | flops 33685504 | bytes 1179648 | tf_op jit(solution)/shard_map/qkgd,skd->kgqs/dot_general | solution.py:44
  12.3 0.3 fusion.51
  12.6 0.5 %copy-done.1 = bf16[8,8,8,128]{3,2,1,0:T(8,128)(2,1)S(1)} copy-done((bf16[8,8,8,128]{3,2,1,0:T(8,128)(2,1)S(1)}, bf16[8,8,8,128]{3,2,1,0:T(8,128)(2,1)}, u32[]{:S(2)}) %copy-start.1) | copy-done | bytes 131096
  13.2 0.7 %fusion.19 = bf16[64,8,4,128]{3,0,2,1:T(8,128)(2,1)S(1)} fusion(f32[64]{0:T(128)S(1)} %copy-done.8, f32[64,8,4]{0,2,1:T(4,128)S(1)} %bitcast.82, bf16[64,8,128,1]{2,1,0,3:T(8,128)(2,1)S(1)} %bitcast.79, f32[8,4,64,64]{2,3,1,0:T(8,128)S(1)} %fusion.16, pred[64,64]{0,1:T(8,128)(4,1)S(1)} %compare_and_fusion.1), kind=kOutput, calls=%fused_computation.21 | convolution fusion | flops 34867264 | bytes 1192192 | tf_op jit(solution)/shard_map/kgqs,skd->qkgd/dot_general | solution.py:51
  13.8 0.0 copy-start.7
  13.9 0.4 copy.20
  14.3 0.4 convert_element_type.63
  14.7 0.6 %fusion.41 = s32[]{:T(128)} fusion(s32[1,2]{1,0:T(1,128)S(1)} %copy-done.7, s32[]{:T(128)S(6)} %axis_index.23), kind=kLoop, calls=%fused_computation.67 | loop fusion | flops 5 | bytes 16 | tf_op jit(solution)/shard_map/reduce_sum | solution.py:180
  15.3 0.6 %select_convert_fusion = bf16[4096]{0:T(1024)(128)(2,1)S(1)} fusion(s32[]{:T(128)} %fusion.41, s32[]{:T(128)S(6)} %select_n.140), kind=kLoop, calls=%fused_computation.51 | loop fusion | flops 20480 | bytes 8200 | tf_op jit(solution)/shard_map/convert_element_type | solution.py:185
  16.0 0.1 broadcast_select_fusion
  16.1 1.6 %collective-permute-start = (bf16[64,4096]{1,0:T(8,128)(2,1)S(1)}, bf16[64,4096]{1,0:T(8,128)(2,1)S(1)}, u32[]{:S(2)}, u32[]{:S(2)}) collective-permute-start(bf16[64,4096]{1,0:T(8,128)(2,1)S(1)} %broadcast_select_fusion), channel_id=1, source_target_pairs={{0,8},{8,16},{16,24},{24,0},{1,9},{9,17},{17,25},{25,1},{2,10},{10... | collective-permute-start | bytes 1572872 | tf_op jit(solution)/shard_map/ppermute | solution.py:26
  19.0 0.1 pad_add_fusion
  19.1 0.1 convert_reduce_fusion
  19.2 0.0 collective-permute-done.1
  19.2 1.6 %collective-permute-start.2 = (bf16[64,2048]{1,0:T(8,128)(2,1)S(1)}, bf16[64,2048]{1,0:T(8,128)(2,1)S(1)}, u32[]{:S(2)}, u32[]{:S(2)}) collective-permute-start(bf16[64,2048]{1,0:T(8,128)(2,1)S(1)} %broadcast_select_fusion.1), channel_id=1, source_target_pairs={{0,1},{1,0},{2,3},{3,2},{4,5},{5,4},{6,7},{7,6},{8,9},{9,8},{10,11... | collective-permute-start | bytes 786440 | tf_op jit(solution)/shard_map/ppermute | solution.py:65
  20.8 0.4 reshape.106
  21.2 0.1 compare_and_fusion
  21.3 5.5 %collective-permute-done.2 = bf16[64,2048]{1,0:T(8,128)(2,1)S(1)} collective-permute-done((bf16[64,2048]{1,0:T(8,128)(2,1)S(1)}, bf16[64,2048]{1,0:T(8,128)(2,1)S(1)}, u32[]{:S(2)}, u32[]{:S(2)}) %collective-permute-start.2) | collective-permute-done | bytes 262176 | tf_op jit(solution)/shard_map/ppermute | solution.py:65
  26.8 0.1 pad_maximum_fusion
  26.8 0.1 slice_bitcast_fusion.1
  26.9 0.1 copy.41
  27.0 0.1 copy.40
  27.0 0.5 fusion.25
  27.5 1.0 %fusion.52 = (f32[8,4,64]{2,1,0:T(4,128)S(1)}, bf16[8,4,64,192]{3,2,1,0:T(8,128)(2,1)S(1)}) fusion(f32[8,192,64,4]{1,2,3,0:T(8,128)S(1)} %fusion.25, pred[64,192]{1,0:T(8,128)(4,1)S(1)} %compare_and_fusion), kind=kOutput, calls=%fused_computation.83 | output fusion | flops 2752703 | bytes 2379776 | tf_op jit(solution)/shard_map/sub | solution.py:48
  28.5 0.5 fusion.20
  28.9 0.4 copy.24
  29.4 0.4 convert_element_type.70
  29.7 1.6 %collective-permute-start.3 = (bf16[64,4096]{1,0:T(8,128)(2,1)S(1)}, bf16[64,4096]{1,0:T(8,128)(2,1)S(1)}, u32[]{:S(2)}, u32[]{:S(2)}) collective-permute-start(bf16[64,4096]{1,0:T(8,128)(2,1)S(1)} %convert_element_type.70), channel_id=1, source_target_pairs={{0,8},{8,16},{16,24},{24,0},{1,9},{9,17},{17,25},{25,1},{2,10},{10... | collective-permute-start | bytes 1572872 | tf_op jit(solution)/shard_map/ppermute | solution.py:26
  31.4 0.0 collective-permute-done
  31.4 0.0 collective-permute-start.4
  31.4 12.4 %collective-permute-done.3 = bf16[64,4096]{1,0:T(8,128)(2,1)S(1)} collective-permute-done((bf16[64,4096]{1,0:T(8,128)(2,1)S(1)}, bf16[64,4096]{1,0:T(8,128)(2,1)S(1)}, u32[]{:S(2)}, u32[]{:S(2)}) %collective-permute-start.3) | collective-permute-done | bytes 524320 | tf_op jit(solution)/shard_map/ppermute | solution.py:26
  43.8 0.6 %fusion.48 = (s32[1,1]{1,0:T(1,128)}, s32[1,1]{1,0:T(1,128)}) fusion(s32[1,2]{1,0:T(1,128)S(1)} %slice_convert_fusion.1), kind=kLoop, calls=%fused_computation.79 | loop fusion | bytes 16 | tf_op jit(solution)/shard_map/slice | solution.py:215
  45.8 0.7 %fusion.49 = (s32[1,1]{1,0:T(1,128)}, s32[1,1]{1,0:T(1,128)}) fusion(s32[1,2]{1,0:T(1,128)S(1)} %slice_convert_fusion), kind=kLoop, calls=%fused_computation.80 | loop fusion | bytes 16 | tf_op jit(solution)/shard_map/slice | solution.py:215
  47.7 0.2 select_bitcast_fusion.3
  47.9 1.1 %maximum_bitcast_fusion = bf16[1,2,64,4096]{3,2,1,0:T(8,128)(2,1)} fusion(bf16[1,64,4096]{2,1,0:T(8,128)(2,1)S(1)} %get-tuple-element.18, bf16[1,64,4096]{2,1,0:T(8,128)(2,1)S(1)} %get-tuple-element.17), kind=kLoop, calls=%fused_computation.23 | loop fusion | flops 524288 | bytes 2097152 | tf_op jit(solution)/shard_map/reshape | solution.py:222
  (30 shorter events, 0.2 us)
Async XLA Ops:
  0.0 0.7 %copy-start = (s32[1,4]{1,0:T(1,128)S(1)}, s32[1,4]{1,0:T(1,128)}, u32[]{:S(2)}) copy-start(s32[1,4]{1,0:T(1,128)} %param.5) | copy-start | bytes 52
  2.6 6.4 %copy-start.6 = (s32[1,4,8]{2,1,0:T(4,128)S(1)}, s32[1,4,8]{2,1,0:T(4,128)}, u32[]{:S(2)}) copy-start(s32[1,4,8]{2,1,0:T(4,128)} %param.6) | copy-start | bytes 388
  4.1 15.1 %collective-permute-start.1 = (bf16[64,2048]{1,0:T(8,128)(2,1)S(1)}, bf16[64,2048]{1,0:T(8,128)(2,1)S(1)}, u32[]{:S(2)}, u32[]{:S(2)}) collective-permute-start(bf16[64,2048]{1,0:T(8,128)(2,1)S(1)} %slice.96), channel_id=1, source_target_pairs={{0,2},{1,3},{2,0},{3,1},{4,6},{5,7},{6,4},{7,5},{8,10},{9,11},{10,... | collective-permute-start | bytes 786440 | tf_op jit(solution)/shard_map/ppermute | solution.py:60
  9.2 0.8 %copy-start.2 = (s32[8]{0:T(128)}, s32[8]{0:T(128)S(1)}, u32[]{:S(2)}) copy-start(s32[8]{0:T(128)S(1)} %get-tuple-element.16) | copy-start | bytes 100
  12.2 0.9 %copy-start.1 = (bf16[8,8,8,128]{3,2,1,0:T(8,128)(2,1)S(1)}, bf16[8,8,8,128]{3,2,1,0:T(8,128)(2,1)}, u32[]{:S(2)}) copy-start(bf16[8,8,8,128]{3,2,1,0:T(8,128)(2,1)} %copy.38) | copy-start | bytes 393220
  12.3 0.9 %copy-start.8 = (f32[64]{0:T(128)S(1)}, f32[64]{0:T(128)}, u32[]{:S(2)}) copy-start(f32[64]{0:T(128)} %compare_convert_fusion.1) | copy-start | bytes 772
  13.8 0.9 %copy-start.7 = (s32[1,2]{1,0:T(1,128)S(1)}, s32[1,2]{1,0:T(1,128)}, u32[]{:S(2)}) copy-start(s32[1,2]{1,0:T(1,128)} %param.7) | copy-start | bytes 28
  13.8 2.1 %copy-start.4 = (pred[64]{0:T(512)(128)(4,1)S(1)}, pred[64]{0:T(512)(128)(4,1)}, u32[]{:S(2)}) copy-start(pred[64]{0:T(512)(128)(4,1)} %iota_compare_fusion.2) | copy-start | bytes 196
  13.8 5.2 %copy-start.3 = (s32[8]{0:T(128)S(1)}, s32[8]{0:T(128)}, u32[]{:S(2)}) copy-start(s32[8]{0:T(128)} %copy-done.2) | copy-start | bytes 100
  14.7 6.5 %copy-start.5 = (s32[64]{0:T(128)S(1)}, s32[64]{0:T(128)}, u32[]{:S(2)}) copy-start(s32[64]{0:T(128)} %get-tuple-element.7) | copy-start | bytes 772
  16.1 15.3 %collective-permute-start = (bf16[64,4096]{1,0:T(8,128)(2,1)S(1)}, bf16[64,4096]{1,0:T(8,128)(2,1)S(1)}, u32[]{:S(2)}, u32[]{:S(2)}) collective-permute-start(bf16[64,4096]{1,0:T(8,128)(2,1)S(1)} %broadcast_select_fusion), channel_id=1, source_target_pairs={{0,8},{8,16},{16,24},{24,0},{1,9},{9,17},{17,25},{25,1},{2,10},{10... | collective-permute-start | bytes 1572872 | tf_op jit(solution)/shard_map/ppermute | solution.py:26
  19.2 7.6 %collective-permute-start.2 = (bf16[64,2048]{1,0:T(8,128)(2,1)S(1)}, bf16[64,2048]{1,0:T(8,128)(2,1)S(1)}, u32[]{:S(2)}, u32[]{:S(2)}) collective-permute-start(bf16[64,2048]{1,0:T(8,128)(2,1)S(1)} %broadcast_select_fusion.1), channel_id=1, source_target_pairs={{0,1},{1,0},{2,3},{3,2},{4,5},{5,4},{6,7},{7,6},{8,9},{9,8},{10,11... | collective-permute-start | bytes 786440 | tf_op jit(solution)/shard_map/ppermute | solution.py:65
  29.7 14.1 %collective-permute-start.3 = (bf16[64,4096]{1,0:T(8,128)(2,1)S(1)}, bf16[64,4096]{1,0:T(8,128)(2,1)S(1)}, u32[]{:S(2)}, u32[]{:S(2)}) collective-permute-start(bf16[64,4096]{1,0:T(8,128)(2,1)S(1)} %convert_element_type.70), channel_id=1, source_target_pairs={{0,8},{8,16},{16,24},{24,0},{1,9},{9,17},{17,25},{25,1},{2,10},{10... | collective-permute-start | bytes 1572872 | tf_op jit(solution)/shard_map/ppermute | solution.py:26
  31.4 14.4 %collective-permute-start.4 = (bf16[64,4096]{1,0:T(8,128)(2,1)S(1)}, bf16[64,4096]{1,0:T(8,128)(2,1)S(1)}, u32[]{:S(2)}, u32[]{:S(2)}) collective-permute-start(bf16[64,4096]{1,0:T(8,128)(2,1)S(1)} %collective-permute-done), channel_id=1, source_target_pairs={{0,4},{4,0},{1,5},{5,1},{2,6},{6,2},{3,7},{7,3},{8,12},{12,8},{9,1... | collective-permute-start | bytes 1572872 | tf_op jit(solution)/shard_map/ppermute | solution.py:20
  43.8 3.9 %collective-permute-start.5 = (bf16[64,4096]{1,0:T(8,128)(2,1)S(1)}, bf16[64,4096]{1,0:T(8,128)(2,1)S(1)}, u32[]{:S(2)}, u32[]{:S(2)}) collective-permute-start(bf16[64,4096]{1,0:T(8,128)(2,1)S(1)} %collective-permute-done.3), channel_id=1, source_target_pairs={{0,4},{4,0},{1,5},{5,1},{2,6},{6,2},{3,7},{7,3},{8,12},{12,8},{9,1... | collective-permute-start | bytes 1572872 | tf_op jit(solution)/shard_map/ppermute | solution.py:20

commit v20 on v18

--- a/solution.py
+++ b/solution.py
@@ -181,8 +181,9 @@
     long_rows = pick(swap_second, own_rows[1], own_rows[0])
     long_kv = long_rows[:, D:]
     long_pieces = gathered(long_kv, seq_index, seq_count, reach)
-    previous = passed_along(jnp.concatenate([lengths_all, hand_over[0]]), "section", 1)
-    long_queries, _, previous = lax.optimization_barrier((long_rows[:, :D], short_out, previous))
+    meta = lax.optimization_barrier((jnp.concatenate([lengths_all, hand_over[0]]), long_pieces[0][0]))[0]
+    previous = passed_along(meta, "section", 1)
+    long_queries = lax.optimization_barrier((long_rows[:, :D], short_out))[0]
     pieces = [long_kv]
     key_pos = [query_pos]
     for piece, chunk in long_pieces:
@@ -198,6 +199,7 @@
         pick(swap_second, own_ends[1], own_ends[0]),
         pick(swap_second, own_lengths[1], own_lengths[0]),
     )
+    long_out, previous = lax.optimization_barrier((long_out, previous))
     long_next = passed_along(long_out, "section", 1)
 
     previous_lengths = previous[:rows]

time: 45.8 us -> 46.9 us (1.024)
  waiting for transfers between devices: 14.2 us -> 17.6 us
  starting transfers between devices: 9.53 us -> 7.95 us
  other arithmetic: 6.53 us -> 5.28 us
    ppermute x3, waiting for transfers between devices: 7.28 us -> 12 us  [passed_along(): return lax.ppermute(value, axis, pairs)]
    ppermute x3, starting transfers between devices: 6.31 us -> 3.26 us  [passed_along(): return lax.ppermute(value, axis, pairs)]
    ppermute x1, starting transfers between devices: 1.58 us -> 3.06 us  [gathered(): over_y = lax.ppermute(block, 'seq', [(j, j ^ 2) for j in range(4)])]
    ppermute x1, waiting for transfers between devices: 5.1 us -> 3.77 us  [gathered(): over_x = lax.ppermute(onward, 'seq', [(j, j ^ 1) for j in range(4)])]
    concatenate x1, other arithmetic: 1.34 us -> 0.07 us  [shards(): jnp.concatenate([lengths_all, hand_over[0]])]
  transfers between devices with their start and end apart: 7 -> 7, of which waited for: 3 -> 4; matrix products, arithmetic and copies ran while one was open for 25% -> 19% of each run, Pallas kernels for 0% -> 0%
where the time goes in v20:
time: 46.9 us; the launch traced here: 46.6 us
  waiting for transfers between devices  17.6 us (38%)
  between operations  8.11 us (17%)
  starting transfers between devices  7.95 us (17%)
  local copies, waits for them, and re-layouts  5.44 us (12%)
  other arithmetic  5.28 us (11%)
  matrix products  2.21 us (5%)
    ppermute x3, waiting for transfers between devices, passed_along(): return lax.ppermute(value, axis, pairs)  12 us
    ppermute x1, waiting for transfers between devices, gathered(): over_x = lax.ppermute(onward, 'seq', [(j, j ^ 1) for j in range(4)])  3.77 us
    ppermute x3, starting transfers between devices, passed_along(): return lax.ppermute(value, axis, pairs)  3.26 us
    ppermute x1, starting transfers between devices, gathered(): over_y = lax.ppermute(block, 'seq', [(j, j ^ 2) for j in range(4)])  3.06 us
    ppermute x2, waiting for transfers between devices, swapped(): return lax.ppermute(block, axis, route)  1.84 us
    convert_element_type x4, local copies, waits for them, and re-layouts, attend_row(): return result.reshape(seg_len, D).astype(jnp.bfloat16)  1.59 us
    ppermute x1, starting transfers between devices, gathered(): over_x = lax.ppermute(onward, 'seq', [(j, j ^ 1) for j in range(4)])  1.56 us
    select_n x1, other arithmetic, pick(): return jnp.where(first_if, a, b)  1.48 us
  transfers between devices with their start and end apart: 7, of which 4 were waited for; matrix products, arithmetic and copies ran while one was open for 19% of the time, Pallas kernels for 0%

profile of v20, /device:TPU:0, one launch (start us, length us, event | category | flops | bytes accessed | tf_op | source)
XLA Modules:
  0.0 46.6 jit_solution(2235339509852175650)
XLA Ops:
  0.0 0.7 %constant_dynamic-slice_fusion.1 = s32[1,2]{1,0:T(1,128)S(1)} fusion(s32[1,4]{1,0:T(1,128)} %param.5, s32[]{:T(128)S(6)} %select_n.129), kind=kLoop, calls=%fused_computation.68 | loop fusion | bytes 20 | tf_op jit(solution)/shard_map/dynamic_slice | solution.py:163
  0.7 0.7 %fusion.49 = (s32[1,1]{1,0:T(1,128)}, s32[1,1]{1,0:T(1,128)}) fusion(s32[1,2]{1,0:T(1,128)S(1)} %constant_dynamic-slice_fusion.1), kind=kLoop, calls=%fused_computation.73 | loop fusion | bytes 16 | tf_op jit(solution)/shard_map/slice | solution.py:164
  2.7 0.0 copy-start.1
  2.7 1.5 %select_bitcast_fusion.1 = (bf16[64,6144]{1,0:T(8,128)(2,1)S(1)}, bf16[64,6144]{1,0:T(8,128)(2,1)S(1)}) fusion(pred[]{:T(512)S(6)} %ge.32, bf16[1,2,64,6144]{3,2,1,0:T(8,128)(2,1)} %param.4), kind=kLoop, calls=%fused_computation.30 | loop fusion | flops 786432 | bytes 3145729 | tf_op jit(solution)/shard_map/jit(_where)/select_n | solution.py:167
  4.3 3.1 %collective-permute-start = (bf16[64,2048]{1,0:T(8,128)(2,1)S(1)}, bf16[64,2048]{1,0:T(8,128)(2,1)S(1)}, u32[]{:S(2)}, u32[]{:S(2)}) collective-permute-start(bf16[64,2048]{1,0:T(8,128)(2,1)S(1)} %slice.72), channel_id=1, source_target_pairs={{0,2},{1,3},{2,0},{3,1},{4,6},{5,7},{6,4},{7,5},{8,10},{9,11},{10,... | collective-permute-start | bytes 786440 | tf_op jit(solution)/shard_map/ppermute | solution.py:60
  10.1 0.2 reduce_window_sum.11
  10.3 0.6 %convert_reduce_fusion.2 = (s32[64]{0:T(128)}, s32[64]{0:T(128)S(1)}) fusion(s32[64]{0:T(128)S(1)} %iota_add_fusion, s32[8]{0:T(128)S(1)} %get-tuple-element.22, s32[8]{0:T(128)S(1)} %get-tuple-element.21), kind=kLoop, calls=%fused_computation.52 | loop fusion | flops 2944 | bytes 832 | tf_op jit(solution)/shard_map/reduce_sum | solution.py:30
  10.9 0.1 compare_and_fusion.1
  11.0 0.4 reshape.82
  11.4 0.6 %fusion.16 = f32[8,4,64,64]{2,3,1,0:T(8,128)S(1)} fusion(bf16[64,8,4,128]{3,2,1,0:T(4,128)(2,1)S(1)} %reshape.82, bf16[64,8,128,1]{2,1,0,3:T(8,128)(2,1)S(1)} %bitcast.78), kind=kOutput, calls=%fused_computation.17 | convolution fusion | flops 33685504 | bytes 1179648 | tf_op jit(solution)/shard_map/qkgd,skd->kgqs/dot_general | solution.py:44
  12.0 0.3 fusion.50
  12.4 0.7 %fusion.19 = bf16[64,8,4,128]{3,0,2,1:T(8,128)(2,1)S(1)} fusion(f32[64]{0:T(128)S(1)} %get-tuple-element.34, f32[64,8,4]{0,2,1:T(4,128)S(1)} %bitcast.85, bf16[64,8,128,1]{2,1,0,3:T(8,128)(2,1)S(1)} %bitcast.80, f32[8,4,64,64]{2,3,1,0:T(8,128)S(1)} %fusion.16, pred[64,64]{0,1:T(8,128)(4,1)S(1)} %compare_and_fusion.1), kind=kOutput, calls=%fused_computation.21 | convolution fusion | flops 34867264 | bytes 1192192 | tf_op jit(solution)/shard_map/kgqs,skd->qkgd/dot_general | solution.py:51
  13.1 0.0 copy-start.2
  13.1 0.0 copy-start.3
  13.1 0.4 copy.20
  13.5 0.0 copy-start
  13.5 0.4 convert_element_type.48
  13.9 1.6 %collective-permute-start.3 = (bf16[64,4096]{1,0:T(8,128)(2,1)S(1)}, bf16[64,4096]{1,0:T(8,128)(2,1)S(1)}, u32[]{:S(2)}, u32[]{:S(2)}) collective-permute-start(bf16[64,4096]{1,0:T(8,128)(2,1)S(1)} %convert_element_type.48), channel_id=1, source_target_pairs={{0,8},{8,16},{16,24},{24,0},{1,9},{9,17},{17,25},{25,1},{2,10},{10... | collective-permute-start | bytes 1572872 | tf_op jit(solution)/shard_map/ppermute | solution.py:26
  15.5 0.1 pad_add_fusion
  15.6 0.1 convert_reduce_fusion
  15.8 1.6 %collective-permute-start.1 = (bf16[64,2048]{1,0:T(8,128)(2,1)S(1)}, bf16[64,2048]{1,0:T(8,128)(2,1)S(1)}, u32[]{:S(2)}, u32[]{:S(2)}) collective-permute-start(bf16[64,2048]{1,0:T(8,128)(2,1)S(1)} %broadcast_select_fusion), channel_id=1, source_target_pairs={{0,1},{1,0},{2,3},{3,2},{4,5},{5,4},{6,7},{7,6},{8,9},{9,8},{10,11... | collective-permute-start | bytes 786440 | tf_op jit(solution)/shard_map/ppermute | solution.py:65
  17.3 0.1 pad_add_fusion.1
  17.4 0.4 reshape.83
  17.8 0.1 compare_and_fusion
  17.9 1.6 %collective-permute-start.2 = (s32[6]{0:T(128)S(1)}, s32[6]{0:T(128)S(1)}, u32[]{:S(2)}, u32[]{:S(2)}) collective-permute-start(s32[6]{0:T(128)S(1)} %pad_add_fusion.1), channel_id=1, source_target_pairs={{0,8},{8,16},{16,24},{24,0},{1,9},{9,17},{17,25},{25,1},{2,10},{10... | collective-permute-start | bytes 80 | tf_op jit(solution)/shard_map/ppermute | solution.py:26
  19.5 3.8 %collective-permute-done.1 = bf16[64,2048]{1,0:T(8,128)(2,1)S(1)} collective-permute-done((bf16[64,2048]{1,0:T(8,128)(2,1)S(1)}, bf16[64,2048]{1,0:T(8,128)(2,1)S(1)}, u32[]{:S(2)}, u32[]{:S(2)}) %collective-permute-start.1) | collective-permute-done | bytes 262176 | tf_op jit(solution)/shard_map/ppermute | solution.py:65
  23.3 0.1 pad_maximum_fusion
  23.4 0.1 slice_bitcast_fusion.1
  23.4 0.1 copy.39
  23.5 0.1 copy.38
  23.6 0.5 fusion.25
  24.0 1.0 %fusion.51 = (f32[8,4,64]{2,1,0:T(4,128)S(1)}, bf16[8,4,64,192]{3,2,1,0:T(8,128)(2,1)S(1)}) fusion(f32[8,192,64,4]{1,2,3,0:T(8,128)S(1)} %fusion.25, pred[64,192]{1,0:T(8,128)(4,1)S(1)} %compare_and_fusion), kind=kOutput, calls=%fused_computation.75 | output fusion | flops 2752703 | bytes 2379776 | tf_op jit(solution)/shard_map/sub | solution.py:48
  25.0 0.5 fusion.20
  25.5 0.4 copy.24
  25.9 0.4 convert_element_type.52
  26.3 3.0 %collective-permute-done.2 = s32[6]{0:T(128)S(1)} collective-permute-done((s32[6]{0:T(128)S(1)}, s32[6]{0:T(128)S(1)}, u32[]{:S(2)}, u32[]{:S(2)}) %collective-permute-start.2) | collective-permute-done | bytes 56 | tf_op jit(solution)/shard_map/ppermute | solution.py:26
  29.3 0.1 slice.71
  29.4 0.7 %fusion.48 = (s32[1]{0:T(128)}, s32[1]{0:T(128)}, s32[1]{0:T(128)}, s32[1]{0:T(128)}) fusion(s32[4]{0:T(128)S(1)} %bitcast.81, s32[]{:T(128)S(6)} %select_n.129, s32[]{:T(128)S(6)} %select_n.158, s32[]{:T(128)S(6)} %select_n.157, s32[]{:T(128)S(6)} %select_n.152), kind=kLoop, calls=%fused_computation.72 | loop fusion | bytes 48 | tf_op jit(solution)/shard_map/jit(dynamic_index_in_dim)/dynamic_slice | solution.py:209
  31.3 0.6 %fusion.47 = (s32[1]{0:T(128)}, s32[1]{0:T(128)}) fusion(s32[2]{0:T(128)S(1)} %slice.71, s32[]{:T(128)S(6)} %select_n.154, s32[]{:T(128)S(6)} %select_n.160), kind=kLoop, calls=%fused_computation.71 | loop fusion | bytes 24 | tf_op jit(solution)/shard_map/jit(dynamic_index_in_dim)/dynamic_slice | solution.py:213
  34.5 0.0 collective-permute-done.3
  34.5 0.1 collective-permute-start.5
  34.6 9.0 %collective-permute-done.4 = bf16[64,4096]{1,0:T(8,128)(2,1)S(1)} collective-permute-done((bf16[64,4096]{1,0:T(8,128)(2,1)S(1)}, bf16[64,4096]{1,0:T(8,128)(2,1)S(1)}, u32[]{:S(2)}, u32[]{:S(2)}) %collective-permute-start.4) | collective-permute-done | bytes 524320 | tf_op jit(solution)/shard_map/ppermute | solution.py:26
  43.6 0.0 collective-permute-start.6
  43.6 0.1 select_bitcast_fusion.3
  43.7 0.0 collective-permute-done.5
  43.7 1.8 %collective-permute-done.6 = bf16[64,4096]{1,0:T(8,128)(2,1)S(1)} collective-permute-done((bf16[64,4096]{1,0:T(8,128)(2,1)S(1)}, bf16[64,4096]{1,0:T(8,128)(2,1)S(1)}, u32[]{:S(2)}, u32[]{:S(2)}) %collective-permute-start.6) | collective-permute-done | bytes 524320 | tf_op jit(solution)/shard_map/ppermute | solution.py:20
  45.5 0.1 select_bitcast_fusion.2
  45.6 1.1 %maximum_bitcast_fusion = bf16[1,2,64,4096]{3,2,1,0:T(8,128)(2,1)} fusion(bf16[1,64,4096]{2,1,0:T(8,128)(2,1)S(1)} %select_bitcast_fusion.2, bf16[1,64,4096]{2,1,0:T(8,128)(2,1)S(1)} %select_bitcast_fusion.3), kind=kLoop, calls=%fused_computation.23 | loop fusion | flops 524288 | bytes 2097152 | tf_op jit(solution)/shard_map/reshape | solution.py:222
  (18 shorter events, 0.2 us)
Async XLA Ops:
  2.7 7.3 %copy-start.1 = (s32[1,4,8]{2,1,0:T(4,128)S(1)}, s32[1,4,8]{2,1,0:T(4,128)}, u32[]{:S(2)}) copy-start(s32[1,4,8]{2,1,0:T(4,128)} %param.6) | copy-start | bytes 388
  4.3 11.4 %collective-permute-start = (bf16[64,2048]{1,0:T(8,128)(2,1)S(1)}, bf16[64,2048]{1,0:T(8,128)(2,1)S(1)}, u32[]{:S(2)}, u32[]{:S(2)}) collective-permute-start(bf16[64,2048]{1,0:T(8,128)(2,1)S(1)} %slice.72), channel_id=1, source_target_pairs={{0,2},{1,3},{2,0},{3,1},{4,6},{5,7},{6,4},{7,5},{8,10},{9,11},{10,... | collective-permute-start | bytes 786440 | tf_op jit(solution)/shard_map/ppermute | solution.py:60
  13.1 4.3 %copy-start.2 = (s32[1,4]{1,0:T(1,128)S(1)}, s32[1,4]{1,0:T(1,128)}, u32[]{:S(2)}) copy-start(s32[1,4]{1,0:T(1,128)} %param.5) | copy-start | bytes 52
  13.1 4.2 %copy-start.3 = (s32[1,2]{1,0:T(1,128)S(1)}, s32[1,2]{1,0:T(1,128)}, u32[]{:S(2)}) copy-start(s32[1,2]{1,0:T(1,128)} %param.7) | copy-start | bytes 28
  13.5 4.3 %copy-start = (s32[64]{0:T(128)S(1)}, s32[64]{0:T(128)}, u32[]{:S(2)}) copy-start(s32[64]{0:T(128)} %get-tuple-element.13) | copy-start | bytes 772
  13.9 20.6 %collective-permute-start.3 = (bf16[64,4096]{1,0:T(8,128)(2,1)S(1)}, bf16[64,4096]{1,0:T(8,128)(2,1)S(1)}, u32[]{:S(2)}, u32[]{:S(2)}) collective-permute-start(bf16[64,4096]{1,0:T(8,128)(2,1)S(1)} %convert_element_type.48), channel_id=1, source_target_pairs={{0,8},{8,16},{16,24},{24,0},{1,9},{9,17},{17,25},{25,1},{2,10},{10... | collective-permute-start | bytes 1572872 | tf_op jit(solution)/shard_map/ppermute | solution.py:26
  15.8 7.5 %collective-permute-start.1 = (bf16[64,2048]{1,0:T(8,128)(2,1)S(1)}, bf16[64,2048]{1,0:T(8,128)(2,1)S(1)}, u32[]{:S(2)}, u32[]{:S(2)}) collective-permute-start(bf16[64,2048]{1,0:T(8,128)(2,1)S(1)} %broadcast_select_fusion), channel_id=1, source_target_pairs={{0,1},{1,0},{2,3},{3,2},{4,5},{5,4},{6,7},{7,6},{8,9},{9,8},{10,11... | collective-permute-start | bytes 786440 | tf_op jit(solution)/shard_map/ppermute | solution.py:65
  17.9 11.4 %collective-permute-start.2 = (s32[6]{0:T(128)S(1)}, s32[6]{0:T(128)S(1)}, u32[]{:S(2)}, u32[]{:S(2)}) collective-permute-start(s32[6]{0:T(128)S(1)} %pad_add_fusion.1), channel_id=1, source_target_pairs={{0,8},{8,16},{16,24},{24,0},{1,9},{9,17},{17,25},{25,1},{2,10},{10... | collective-permute-start | bytes 80 | tf_op jit(solution)/shard_map/ppermute | solution.py:26
  29.3 14.3 %collective-permute-start.4 = (bf16[64,4096]{1,0:T(8,128)(2,1)S(1)}, bf16[64,4096]{1,0:T(8,128)(2,1)S(1)}, u32[]{:S(2)}, u32[]{:S(2)}) collective-permute-start(bf16[64,4096]{1,0:T(8,128)(2,1)S(1)} %convert_element_type.52), channel_id=1, source_target_pairs={{0,8},{8,16},{16,24},{24,0},{1,9},{9,17},{17,25},{25,1},{2,10},{10... | collective-permute-start | bytes 1572872 | tf_op jit(solution)/shard_map/ppermute | solution.py:26
  34.5 9.2 %collective-permute-start.5 = (bf16[64,4096]{1,0:T(8,128)(2,1)S(1)}, bf16[64,4096]{1,0:T(8,128)(2,1)S(1)}, u32[]{:S(2)}, u32[]{:S(2)}) collective-permute-start(bf16[64,4096]{1,0:T(8,128)(2,1)S(1)} %collective-permute-done.3), channel_id=1, source_target_pairs={{0,4},{4,0},{1,5},{5,1},{2,6},{6,2},{3,7},{7,3},{8,12},{12,8},{9,1... | collective-permute-start | bytes 1572872 | tf_op jit(solution)/shard_map/ppermute | solution.py:20
  43.6 1.9 %collective-permute-start.6 = (bf16[64,4096]{1,0:T(8,128)(2,1)S(1)}, bf16[64,4096]{1,0:T(8,128)(2,1)S(1)}, u32[]{:S(2)}, u32[]{:S(2)}) collective-permute-start(bf16[64,4096]{1,0:T(8,128)(2,1)S(1)} %collective-permute-done.4), channel_id=1, source_target_pairs={{0,4},{4,0},{1,5},{5,1},{2,6},{6,2},{3,7},{7,3},{8,12},{12,8},{9,1... | collective-permute-start | bytes 1572872 | tf_op jit(solution)/shard_map/ppermute | solution.py:20

commit v21 on v20

--- a/solution.py
+++ b/solution.py
@@ -166,7 +166,13 @@
     def pick(first_if, a, b):
         return jnp.where(first_if, a, b)
 
+    long_rows = pick(swap_second, own_rows[1], own_rows[0])
+    long_kv = long_rows[:, D:]
+    long_pieces = gathered(long_kv, seq_index, seq_count, reach)
+    meta = lax.optimization_barrier((jnp.concatenate([lengths_all, hand_over[0]]), long_kv))[0]
+    previous = passed_along(meta, "section", 1)
     short_rows = pick(swap_second, own_rows[0], own_rows[1])
+    short_rows, previous = lax.optimization_barrier((short_rows, previous))
     short_out = attend_row(
         short_rows[:, :D],
         short_rows[:, D:D + key_value_width],
@@ -178,11 +184,6 @@
     )
     short_next = passed_along(short_out, "section", 1)
 
-    long_rows = pick(swap_second, own_rows[1], own_rows[0])
-    long_kv = long_rows[:, D:]
-    long_pieces = gathered(long_kv, seq_index, seq_count, reach)
-    meta = lax.optimization_barrier((jnp.concatenate([lengths_all, hand_over[0]]), long_pieces[0][0]))[0]
-    previous = passed_along(meta, "section", 1)
     long_queries = lax.optimization_barrier((long_rows[:, :D], short_out))[0]
     pieces = [long_kv]
     key_pos = [query_pos]
@@ -199,7 +200,6 @@
         pick(swap_second, own_ends[1], own_ends[0]),
         pick(swap_second, own_lengths[1], own_lengths[0]),
     )
-    long_out, previous = lax.optimization_barrier((long_out, previous))
     long_next = passed_along(long_out, "section", 1)
 
     previous_lengths = previous[:rows]

time: 46.9 us -> 49.3 us (1.051)
  waiting for transfers between devices: 17.6 us -> 14.9 us
  other arithmetic: 5.28 us -> 7.64 us
  starting transfers between devices: 7.95 us -> 10.3 us
  local copies, waits for them, and re-layouts: 5.44 us -> 6.07 us
    ppermute x3, starting transfers between devices: 3.26 us -> 4.84 us  [passed_along(): return lax.ppermute(value, axis, pairs)]
    ppermute x1, waiting for transfers between devices: 3.77 us -> 2.2 us  [gathered(): over_x = lax.ppermute(onward, 'seq', [(j, j ^ 1) for j in range(4)])]
    ppermute x3, waiting for transfers between devices: 12 us -> 10.9 us  [passed_along(): return lax.ppermute(value, axis, pairs)]
    concatenate x1, other arithmetic: 0.07 us -> 1.08 us  [shards(): kv_all = jnp.concatenate(pieces, axis=0)]
    ppermute x1, starting transfers between devices: 1.56 us -> 2.44 us  [gathered(): over_x = lax.ppermute(onward, 'seq', [(j, j ^ 1) for j in range(4)])]
    select_n x1, other arithmetic: 0.03 us -> 0.74 us  [gathered(): onward = jnp.where(odd, over_y, block)]
    and x2, other arithmetic: 0.17 us -> 0.77 us  [attend_row(): (key_pos[None, :] <= query_pos[:, None]) & (key_doc[None, :] == query_doc...]
    unnamed x14 -> x22, local copies, waits for them, and re-layouts: 0.27 us -> 0.84 us
  transfers between devices with their start and end apart: 7 -> 7, of which waited for: 4 -> 4; matrix products, arithmetic and copies ran while one was open for 19% -> 21% of each run, Pallas kernels for 0% -> 0%
where the time goes in v21:
time: 49.3 us; the launch traced here: 49.1 us
  waiting for transfers between devices  14.9 us (30%)
  starting transfers between devices  10.3 us (21%)
  between operations  7.92 us (16%)
  other arithmetic  7.64 us (15%)
  local copies, waits for them, and re-layouts  6.07 us (12%)
  matrix products  2.21 us (4%)
    ppermute x3, waiting for transfers between devices, passed_along(): return lax.ppermute(value, axis, pairs)  10.9 us
    ppermute x3, starting transfers between devices, passed_along(): return lax.ppermute(value, axis, pairs)  4.84 us
    ppermute x1, starting transfers between devices, gathered(): over_y = lax.ppermute(block, 'seq', [(j, j ^ 2) for j in range(4)])  3.06 us
    ppermute x1, starting transfers between devices, gathered(): over_x = lax.ppermute(onward, 'seq', [(j, j ^ 1) for j in range(4)])  2.44 us
    ppermute x1, waiting for transfers between devices, gathered(): over_x = lax.ppermute(onward, 'seq', [(j, j ^ 1) for j in range(4)])  2.2 us
    ppermute x2, waiting for transfers between devices, swapped(): return lax.ppermute(block, axis, route)  1.84 us
    convert_element_type x4, local copies, waits for them, and re-layouts, attend_row(): return result.reshape(seg_len, D).astype(jnp.bfloat16)  1.59 us
    select_n x1, other arithmetic, pick(): return jnp.where(first_if, a, b)  1.48 us
  transfers between devices with their start and end apart: 7, of which 4 were waited for; matrix products, arithmetic and copies ran while one was open for 21% of the time, Pallas kernels for 0%

profile of v21, /device:TPU:0, one launch (start us, length us, event | category | flops | bytes accessed | tf_op | source)
XLA Modules:
  0.0 49.1 jit_solution(14005463210623700958)
XLA Ops:
  0.0 0.8 %constant_dynamic-slice_fusion.1 = s32[1,2]{1,0:T(1,128)S(1)} fusion(s32[1,4]{1,0:T(1,128)} %param.5, s32[]{:T(128)S(6)} %select_n.129), kind=kLoop, calls=%fused_computation.68 | loop fusion | bytes 20 | tf_op jit(solution)/shard_map/dynamic_slice | solution.py:163
  0.8 0.6 %fusion.49 = (s32[1,1]{1,0:T(1,128)}, s32[1,1]{1,0:T(1,128)}) fusion(s32[1,2]{1,0:T(1,128)S(1)} %constant_dynamic-slice_fusion.1), kind=kLoop, calls=%fused_computation.73 | loop fusion | bytes 16 | tf_op jit(solution)/shard_map/slice | solution.py:164
  2.7 0.0 copy-start.3
  2.7 1.5 %select_bitcast_fusion = (bf16[64,6144]{1,0:T(8,128)(2,1)S(1)}, bf16[64,6144]{1,0:T(8,128)(2,1)S(1)}) fusion(pred[]{:T(512)S(6)} %ge.32, bf16[1,2,64,6144]{3,2,1,0:T(8,128)(2,1)} %param.4), kind=kLoop, calls=%fused_computation.29 | loop fusion | flops 786432 | bytes 3145729 | tf_op jit(solution)/shard_map/jit(_where)/select_n | solution.py:167
  4.2 3.1 %collective-permute-start.2 = (bf16[64,2048]{1,0:T(8,128)(2,1)S(1)}, bf16[64,2048]{1,0:T(8,128)(2,1)}, u32[]{:S(2)}, u32[]{:S(2)}) collective-permute-start(bf16[64,2048]{1,0:T(8,128)(2,1)S(1)} %slice.72), channel_id=1, source_target_pairs={{0,2},{1,3},{2,0},{3,1},{4,6},{5,7},{6,4},{7,5},{8,10},{9,11},{10,... | collective-permute-start | bytes 786440 | tf_op jit(solution)/shard_map/ppermute | solution.py:60
  7.3 0.1 pad_add_fusion.1
  7.4 1.6 %collective-permute-start = (s32[6]{0:T(128)S(1)}, s32[6]{0:T(128)S(1)}, u32[]{:S(2)}, u32[]{:S(2)}) collective-permute-start(s32[6]{0:T(128)S(1)} %pad_add_fusion.1), channel_id=1, source_target_pairs={{0,8},{8,16},{16,24},{24,0},{1,9},{9,17},{17,25},{25,1},{2,10},{10... | collective-permute-start | bytes 80 | tf_op jit(solution)/shard_map/ppermute | solution.py:26
  11.6 0.2 reduce_window_sum.11
  11.8 0.1 convert_reduce_fusion.1
  11.9 0.7 %compare_and_fusion.1 = pred[64,64]{0,1:T(8,128)(4,1)} fusion(s32[64]{0:T(128)S(1)} %get-tuple-element.14, s32[64]{0:T(128)S(1)} %iota_add_fusion), kind=kLoop, calls=%fused_computation.49 | loop fusion | flops 12288 | bytes 4608 | tf_op jit(solution)/shard_map/and | solution.py:39
  12.6 0.1 pad_add_fusion
  12.6 0.1 convert_reduce_fusion
  12.7 0.6 %compare_convert_fusion = (f32[64]{0:T(128)}, f32[64]{0:T(128)}) fusion(s32[]{:T(128)S(6)} %select_n.155, s32[]{:T(128)S(6)} %mul.54, s32[]{:T(128)S(6)} %select_n.143), kind=kLoop, calls=%fused_computation.53 | loop fusion | flops 320 | bytes 524 | tf_op jit(solution)/shard_map/convert_element_type | solution.py:53
  13.3 0.1 compare_and_fusion
  13.4 0.0 collective-permute-done
  13.4 0.6 %copy-done = s32[6]{0:T(128)} copy-done((s32[6]{0:T(128)}, s32[6]{0:T(128)S(1)}, u32[]{:S(2)}) %copy-start) | copy-done | bytes 48
  14.1 0.4 reshape.80
  14.5 0.6 %fusion.16 = f32[8,4,64,64]{2,3,1,0:T(8,128)S(1)} fusion(bf16[64,8,4,128]{3,2,1,0:T(4,128)(2,1)S(1)} %reshape.80, bf16[64,8,128,1]{2,1,0,3:T(8,128)(2,1)S(1)} %bitcast.78), kind=kOutput, calls=%fused_computation.17 | convolution fusion | flops 33685504 | bytes 1179648 | tf_op jit(solution)/shard_map/qkgd,skd->kgqs/dot_general | solution.py:44
  15.1 0.0 collective-permute-done.2
  15.1 0.7 %broadcast_select_fusion = bf16[64,2048]{1,0:T(8,128)(2,1)} fusion(bf16[64,2048]{1,0:T(8,128)(2,1)} %collective-permute-done.2, pred[]{:T(512)S(6)} %eq.48, bf16[64,6144]{1,0:T(8,128)(2,1)S(1)} %get-tuple-element.15), kind=kLoop, calls=%fused_computation.43 | loop fusion | flops 131072 | bytes 786433 | tf_op jit(solution)/shard_map/jit(_where)/select_n | solution.py:62
  15.8 2.4 %collective-permute-start.3 = (bf16[64,2048]{1,0:T(8,128)(2,1)}, bf16[64,2048]{1,0:T(8,128)(2,1)}, u32[]{:S(2)}, u32[]{:S(2)}) collective-permute-start(bf16[64,2048]{1,0:T(8,128)(2,1)} %broadcast_select_fusion), channel_id=1, source_target_pairs={{0,1},{1,0},{2,3},{3,2},{4,5},{5,4},{6,7},{7,6},{8,9},{9,8},{10,11... | collective-permute-start | bytes 786440 | tf_op jit(solution)/shard_map/ppermute | solution.py:65
  18.3 0.3 fusion.50
  18.7 0.7 %fusion.19 = bf16[64,8,4,128]{3,0,2,1:T(8,128)(2,1)S(1)} fusion(f32[64]{0:T(128)S(1)} %copy-done.5, f32[64,8,4]{0,2,1:T(4,128)S(1)} %bitcast.86, bf16[64,8,128,1]{2,1,0,3:T(8,128)(2,1)S(1)} %bitcast.80, f32[8,4,64,64]{2,3,1,0:T(8,128)S(1)} %fusion.16, pred[64,64]{0,1:T(8,128)(4,1)S(1)} %copy-done.2), kind=kOutput, calls=%fused_computation.21 | convolution fusion | flops 34867264 | bytes 1192192 | tf_op jit(solution)/shard_map/kgqs,skd->qkgd/dot_general | solution.py:51
  19.3 0.4 copy.20
  19.7 0.4 convert_element_type.46
  20.1 1.6 %collective-permute-start.1 = (bf16[64,4096]{1,0:T(8,128)(2,1)S(1)}, bf16[64,4096]{1,0:T(8,128)(2,1)S(1)}, u32[]{:S(2)}, u32[]{:S(2)}) collective-permute-start(bf16[64,4096]{1,0:T(8,128)(2,1)S(1)} %convert_element_type.46), channel_id=1, source_target_pairs={{0,8},{8,16},{16,24},{24,0},{1,9},{9,17},{17,25},{25,1},{2,10},{10... | collective-permute-start | bytes 1572872 | tf_op jit(solution)/shard_map/ppermute | solution.py:26
  21.8 0.4 reshape.83
  22.1 2.2 %collective-permute-done.3 = bf16[64,2048]{1,0:T(8,128)(2,1)} collective-permute-done((bf16[64,2048]{1,0:T(8,128)(2,1)}, bf16[64,2048]{1,0:T(8,128)(2,1)}, u32[]{:S(2)}, u32[]{:S(2)}) %collective-permute-start.3) | collective-permute-done | bytes 262176 | tf_op jit(solution)/shard_map/ppermute | solution.py:65
  24.3 1.1 %pad_maximum_fusion = bf16[192,2048]{1,0:T(8,128)(2,1)S(1)} fusion(bf16[64,2048]{1,0:T(8,128)(2,1)} %collective-permute-done.3, bf16[64,2048]{1,0:T(8,128)(2,1)} %collective-permute-done.2, bf16[64,2048]{1,0:T(8,128)(2,1)S(1)} %slice.72), kind=kLoop, calls=%fused_computation.28 | loop fusion | flops 2359296 | bytes 1572864 | tf_op jit(solution)/shard_map/concatenate | solution.py:193
  25.4 0.1 slice_bitcast_fusion.1
  25.5 0.1 copy.41
  25.6 0.1 copy.40
  25.6 0.5 fusion.25
  26.1 1.0 %fusion.51 = (f32[8,4,64]{2,1,0:T(4,128)S(1)}, bf16[8,4,64,192]{3,2,1,0:T(8,128)(2,1)S(1)}) fusion(f32[8,192,64,4]{1,2,3,0:T(8,128)S(1)} %fusion.25, pred[64,192]{1,0:T(8,128)(4,1)S(1)} %compare_and_fusion), kind=kOutput, calls=%fused_computation.75 | output fusion | flops 2752703 | bytes 2379776 | tf_op jit(solution)/shard_map/sub | solution.py:48
  27.1 0.4 fusion.20
  27.5 0.4 copy.24
  28.0 0.4 convert_element_type.52
  28.4 1.6 %collective-permute-start.4 = (bf16[64,4096]{1,0:T(8,128)(2,1)S(1)}, bf16[64,4096]{1,0:T(8,128)(2,1)S(1)}, u32[]{:S(2)}, u32[]{:S(2)}) collective-permute-start(bf16[64,4096]{1,0:T(8,128)(2,1)S(1)} %convert_element_type.52), channel_id=1, source_target_pairs={{0,8},{8,16},{16,24},{24,0},{1,9},{9,17},{17,25},{25,1},{2,10},{10... | collective-permute-start | bytes 1572872 | tf_op jit(solution)/shard_map/ppermute | solution.py:26
  30.0 0.1 slice.63
  30.1 0.7 %fusion.48 = (s32[1]{0:T(128)}, s32[1]{0:T(128)}, s32[1]{0:T(128)}, s32[1]{0:T(128)}) fusion(s32[4]{0:T(128)S(1)} %bitcast.81, s32[]{:T(128)S(6)} %select_n.129, s32[]{:T(128)S(6)} %select_n.158, s32[]{:T(128)S(6)} %select_n.157, s32[]{:T(128)S(6)} %select_n.135), kind=kLoop, calls=%fused_computation.72 | loop fusion | bytes 48 | tf_op jit(solution)/shard_map/jit(dynamic_index_in_dim)/dynamic_slice | solution.py:209
  32.0 0.6 %fusion.47 = (s32[1]{0:T(128)}, s32[1]{0:T(128)}) fusion(s32[2]{0:T(128)S(1)} %slice.63, s32[]{:T(128)S(6)} %select_n.137, s32[]{:T(128)S(6)} %select_n.160), kind=kLoop, calls=%fused_computation.71 | loop fusion | bytes 24 | tf_op jit(solution)/shard_map/jit(dynamic_index_in_dim)/dynamic_slice | solution.py:213
  35.2 1.6 %collective-permute-done.1 = bf16[64,4096]{1,0:T(8,128)(2,1)S(1)} collective-permute-done((bf16[64,4096]{1,0:T(8,128)(2,1)S(1)}, bf16[64,4096]{1,0:T(8,128)(2,1)S(1)}, u32[]{:S(2)}, u32[]{:S(2)}) %collective-permute-start.1) | collective-permute-done | bytes 524320 | tf_op jit(solution)/shard_map/ppermute | solution.py:26
  36.8 0.0 collective-permute-start.5
  36.8 9.3 %collective-permute-done.4 = bf16[64,4096]{1,0:T(8,128)(2,1)S(1)} collective-permute-done((bf16[64,4096]{1,0:T(8,128)(2,1)S(1)}, bf16[64,4096]{1,0:T(8,128)(2,1)S(1)}, u32[]{:S(2)}, u32[]{:S(2)}) %collective-permute-start.4) | collective-permute-done | bytes 524320 | tf_op jit(solution)/shard_map/ppermute | solution.py:26
  46.0 0.1 select_bitcast_fusion.3
  46.1 1.8 %collective-permute-done.6 = bf16[64,4096]{1,0:T(8,128)(2,1)S(1)} collective-permute-done((bf16[64,4096]{1,0:T(8,128)(2,1)S(1)}, bf16[64,4096]{1,0:T(8,128)(2,1)S(1)}, u32[]{:S(2)}, u32[]{:S(2)}) %collective-permute-start.6) | collective-permute-done | bytes 524320 | tf_op jit(solution)/shard_map/ppermute | solution.py:20
  48.0 0.1 select_bitcast_fusion.2
  48.0 1.1 %maximum_bitcast_fusion = bf16[1,2,64,4096]{3,2,1,0:T(8,128)(2,1)} fusion(bf16[1,64,4096]{2,1,0:T(8,128)(2,1)S(1)} %select_bitcast_fusion.2, bf16[1,64,4096]{2,1,0:T(8,128)(2,1)S(1)} %select_bitcast_fusion.3), kind=kLoop, calls=%fused_computation.23 | loop fusion | flops 524288 | bytes 2097152 | tf_op jit(solution)/shard_map/reshape | solution.py:222
  (26 shorter events, 0.2 us)
Async XLA Ops:
  0.0 7.3 %copy-start.6 = (s32[1,4]{1,0:T(1,128)S(1)}, s32[1,4]{1,0:T(1,128)}, u32[]{:S(2)}) copy-start(s32[1,4]{1,0:T(1,128)} %param.5) | copy-start | bytes 52
  0.0 7.3 %copy-start.7 = (s32[1,2]{1,0:T(1,128)S(1)}, s32[1,2]{1,0:T(1,128)}, u32[]{:S(2)}) copy-start(s32[1,2]{1,0:T(1,128)} %param.7) | copy-start | bytes 28
  2.7 8.8 %copy-start.3 = (s32[1,4,8]{2,1,0:T(4,128)S(1)}, s32[1,4,8]{2,1,0:T(4,128)}, u32[]{:S(2)}) copy-start(s32[1,4,8]{2,1,0:T(4,128)} %param.6) | copy-start | bytes 388
  4.2 10.8 %collective-permute-start.2 = (bf16[64,2048]{1,0:T(8,128)(2,1)S(1)}, bf16[64,2048]{1,0:T(8,128)(2,1)}, u32[]{:S(2)}, u32[]{:S(2)}) collective-permute-start(bf16[64,2048]{1,0:T(8,128)(2,1)S(1)} %slice.72), channel_id=1, source_target_pairs={{0,2},{1,3},{2,0},{3,1},{4,6},{5,7},{6,4},{7,5},{8,10},{9,11},{10,... | collective-permute-start | bytes 786440 | tf_op jit(solution)/shard_map/ppermute | solution.py:60
  7.4 6.0 %collective-permute-start = (s32[6]{0:T(128)S(1)}, s32[6]{0:T(128)S(1)}, u32[]{:S(2)}, u32[]{:S(2)}) collective-permute-start(s32[6]{0:T(128)S(1)} %pad_add_fusion.1), channel_id=1, source_target_pairs={{0,8},{8,16},{16,24},{24,0},{1,9},{9,17},{17,25},{25,1},{2,10},{10... | collective-permute-start | bytes 80 | tf_op jit(solution)/shard_map/ppermute | solution.py:26
  13.4 0.6 %copy-start = (s32[6]{0:T(128)}, s32[6]{0:T(128)S(1)}, u32[]{:S(2)}) copy-start(s32[6]{0:T(128)S(1)} %collective-permute-done) | copy-start | bytes 76
  14.0 4.2 %copy-start.2 = (pred[64,64]{0,1:T(8,128)(4,1)S(1)}, pred[64,64]{0,1:T(8,128)(4,1)}, u32[]{:S(2)}) copy-start(pred[64,64]{0,1:T(8,128)(4,1)} %compare_and_fusion.1) | copy-start | bytes 12292
  14.4 4.2 %copy-start.5 = (f32[64]{0:T(128)S(1)}, f32[64]{0:T(128)}, u32[]{:S(2)}) copy-start(f32[64]{0:T(128)} %get-tuple-element.34) | copy-start | bytes 772
  15.8 8.5 %collective-permute-start.3 = (bf16[64,2048]{1,0:T(8,128)(2,1)}, bf16[64,2048]{1,0:T(8,128)(2,1)}, u32[]{:S(2)}, u32[]{:S(2)}) collective-permute-start(bf16[64,2048]{1,0:T(8,128)(2,1)} %broadcast_select_fusion), channel_id=1, source_target_pairs={{0,1},{1,0},{2,3},{3,2},{4,5},{5,4},{6,7},{7,6},{8,9},{9,8},{10,11... | collective-permute-start | bytes 786440 | tf_op jit(solution)/shard_map/ppermute | solution.py:65
  20.1 16.6 %collective-permute-start.1 = (bf16[64,4096]{1,0:T(8,128)(2,1)S(1)}, bf16[64,4096]{1,0:T(8,128)(2,1)S(1)}, u32[]{:S(2)}, u32[]{:S(2)}) collective-permute-start(bf16[64,4096]{1,0:T(8,128)(2,1)S(1)} %convert_element_type.46), channel_id=1, source_target_pairs={{0,8},{8,16},{16,24},{24,0},{1,9},{9,17},{17,25},{25,1},{2,10},{10... | collective-permute-start | bytes 1572872 | tf_op jit(solution)/shard_map/ppermute | solution.py:26
  26.1 1.0 %copy-start.4 = (f32[64]{0:T(128)S(1)}, f32[64]{0:T(128)}, u32[]{:S(2)}) copy-start(f32[64]{0:T(128)} %get-tuple-element.33) | copy-start | bytes 772
  27.5 2.5 %copy-start.1 = (s32[6]{0:T(128)S(1)}, s32[6]{0:T(128)}, u32[]{:S(2)}) copy-start(s32[6]{0:T(128)} %copy-done) | copy-start | bytes 76
  28.4 17.7 %collective-permute-start.4 = (bf16[64,4096]{1,0:T(8,128)(2,1)S(1)}, bf16[64,4096]{1,0:T(8,128)(2,1)S(1)}, u32[]{:S(2)}, u32[]{:S(2)}) collective-permute-start(bf16[64,4096]{1,0:T(8,128)(2,1)S(1)} %convert_element_type.52), channel_id=1, source_target_pairs={{0,8},{8,16},{16,24},{24,0},{1,9},{9,17},{17,25},{25,1},{2,10},{10... | collective-permute-start | bytes 1572872 | tf_op jit(solution)/shard_map/ppermute | solution.py:26
  36.8 9.3 %collective-permute-start.5 = (bf16[64,4096]{1,0:T(8,128)(2,1)S(1)}, bf16[64,4096]{1,0:T(8,128)(2,1)S(1)}, u32[]{:S(2)}, u32[]{:S(2)}) collective-permute-start(bf16[64,4096]{1,0:T(8,128)(2,1)S(1)} %collective-permute-done.1), channel_id=1, source_target_pairs={{0,4},{4,0},{1,5},{5,1},{2,6},{6,2},{3,7},{7,3},{8,12},{12,8},{9,1... | collective-permute-start | bytes 1572872 | tf_op jit(solution)/shard_map/ppermute | solution.py:20
  46.0 1.9 %collective-permute-start.6 = (bf16[64,4096]{1,0:T(8,128)(2,1)S(1)}, bf16[64,4096]{1,0:T(8,128)(2,1)S(1)}, u32[]{:S(2)}, u32[]{:S(2)}) collective-permute-start(bf16[64,4096]{1,0:T(8,128)(2,1)S(1)} %collective-permute-done.4), channel_id=1, source_target_pairs={{0,4},{4,0},{1,5},{5,1},{2,6},{6,2},{3,7},{7,3},{8,12},{12,8},{9,1... | collective-permute-start | bytes 1572872 | tf_op jit(solution)/shard_map/ppermute | solution.py:20

commit v22 on v20

--- a/solution.py
+++ b/solution.py
@@ -181,7 +181,7 @@
     long_rows = pick(swap_second, own_rows[1], own_rows[0])
     long_kv = long_rows[:, D:]
     long_pieces = gathered(long_kv, seq_index, seq_count, reach)
-    meta = lax.optimization_barrier((jnp.concatenate([lengths_all, hand_over[0]]), long_pieces[0][0]))[0]
+    meta = lax.optimization_barrier((jnp.concatenate([lengths_all, hand_over[0]]), long_kv))[0]
     previous = passed_along(meta, "section", 1)
     long_queries = lax.optimization_barrier((long_rows[:, :D], short_out))[0]
     pieces = [long_kv]

time: 46.9 us -> 45.2 us (0.964)
  waiting for transfers between devices: 17.6 us -> 14.2 us
  starting transfers between devices: 7.95 us -> 9.53 us
  other arithmetic: 5.28 us -> 5.86 us
    ppermute x3, waiting for transfers between devices: 12 us -> 7.27 us  [passed_along(): return lax.ppermute(value, axis, pairs)]
    ppermute x3, starting transfers between devices: 3.26 us -> 4.84 us  [passed_along(): return lax.ppermute(value, axis, pairs)]
    ppermute x1, waiting for transfers between devices: 3.77 us -> 5.11 us  [gathered(): over_x = lax.ppermute(onward, 'seq', [(j, j ^ 1) for j in range(4)])]
    concatenate x1, other arithmetic: 0.07 us -> 0.66 us  [shards(): jnp.concatenate([lengths_all, hand_over[0]])]
  transfers between devices with their start and end apart: 7 -> 7, of which waited for: 4 -> 3; matrix products, arithmetic and copies ran while one was open for 19% -> 21% of each run, Pallas kernels for 0% -> 0%
where the time goes in v22:
time: 45.2 us; the launch traced here: 45 us
  waiting for transfers between devices  14.2 us (31%)
  starting transfers between devices  9.53 us (21%)
  between operations  7.73 us (17%)
  other arithmetic  5.86 us (13%)
  local copies, waits for them, and re-layouts  5.43 us (12%)
  matrix products  2.21 us (5%)
    ppermute x3, waiting for transfers between devices, passed_along(): return lax.ppermute(value, axis, pairs)  7.27 us
    ppermute x1, waiting for transfers between devices, gathered(): over_x = lax.ppermute(onward, 'seq', [(j, j ^ 1) for j in range(4)])  5.11 us
    ppermute x3, starting transfers between devices, passed_along(): return lax.ppermute(value, axis, pairs)  4.84 us
    ppermute x1, starting transfers between devices, gathered(): over_y = lax.ppermute(block, 'seq', [(j, j ^ 2) for j in range(4)])  3.06 us
    ppermute x2, waiting for transfers between devices, swapped(): return lax.ppermute(block, axis, route)  1.84 us
    convert_element_type x4, local copies, waits for them, and re-layouts, attend_row(): return result.reshape(seg_len, D).astype(jnp.bfloat16)  1.59 us
    ppermute x1, starting transfers between devices, gathered(): over_x = lax.ppermute(onward, 'seq', [(j, j ^ 1) for j in range(4)])  1.56 us
    select_n x1, other arithmetic, pick(): return jnp.where(first_if, a, b)  1.48 us
  transfers between devices with their start and end apart: 7, of which 3 were waited for; matrix products, arithmetic and copies ran while one was open for 21% of the time, Pallas kernels for 0%

profile of v22, /device:TPU:0, one launch (start us, length us, event | category | flops | bytes accessed | tf_op | source)
XLA Modules:
  0.0 45.0 jit_solution(38978052608242968)
XLA Ops:
  0.0 0.8 %constant_dynamic-slice_fusion.1 = s32[1,2]{1,0:T(1,128)S(1)} fusion(s32[1,4]{1,0:T(1,128)} %param.5, s32[]{:T(128)S(6)} %select_n.129), kind=kLoop, calls=%fused_computation.68 | loop fusion | bytes 20 | tf_op jit(solution)/shard_map/dynamic_slice | solution.py:163
  0.8 0.6 %fusion.49 = (s32[1,1]{1,0:T(1,128)}, s32[1,1]{1,0:T(1,128)}) fusion(s32[1,2]{1,0:T(1,128)S(1)} %constant_dynamic-slice_fusion.1), kind=kLoop, calls=%fused_computation.73 | loop fusion | bytes 16 | tf_op jit(solution)/shard_map/slice | solution.py:164
  2.6 0.0 copy-start.3
  2.6 1.5 %select_bitcast_fusion.1 = (bf16[64,6144]{1,0:T(8,128)(2,1)S(1)}, bf16[64,6144]{1,0:T(8,128)(2,1)S(1)}) fusion(pred[]{:T(512)S(6)} %ge.32, bf16[1,2,64,6144]{3,2,1,0:T(8,128)(2,1)} %param.4), kind=kLoop, calls=%fused_computation.30 | loop fusion | flops 786432 | bytes 3145729 | tf_op jit(solution)/shard_map/jit(_where)/select_n | solution.py:167
  4.1 3.1 %collective-permute-start = (bf16[64,2048]{1,0:T(8,128)(2,1)S(1)}, bf16[64,2048]{1,0:T(8,128)(2,1)S(1)}, u32[]{:S(2)}, u32[]{:S(2)}) collective-permute-start(bf16[64,2048]{1,0:T(8,128)(2,1)S(1)} %slice.72), channel_id=1, source_target_pairs={{0,2},{1,3},{2,0},{3,1},{4,6},{5,7},{6,4},{7,5},{8,10},{9,11},{10,... | collective-permute-start | bytes 786440 | tf_op jit(solution)/shard_map/ppermute | solution.py:60
  7.2 0.7 %pad_add_fusion.1 = s32[6]{0:T(128)} fusion(s32[2]{0:T(128)S(1)} %bitcast.84, s32[4]{0:T(128)S(1)} %bitcast.83), kind=kLoop, calls=%fused_computation.62 | loop fusion | flops 6 | bytes 48 | tf_op jit(solution)/shard_map/concatenate | solution.py:184
  7.8 1.6 %collective-permute-start.2 = (s32[6]{0:T(128)}, s32[6]{0:T(128)S(1)}, u32[]{:S(2)}, u32[]{:S(2)}) collective-permute-start(s32[6]{0:T(128)} %pad_add_fusion.1), channel_id=1, source_target_pairs={{0,8},{8,16},{16,24},{24,0},{1,9},{9,17},{17,25},{25,1},{2,10},{10... | collective-permute-start | bytes 80 | tf_op jit(solution)/shard_map/ppermute | solution.py:26
  11.9 0.2 reduce_window_sum.11
  12.1 0.6 %convert_reduce_fusion.2 = (s32[64]{0:T(128)}, s32[64]{0:T(128)S(1)}) fusion(s32[64]{0:T(128)S(1)} %iota_add_fusion, s32[8]{0:T(128)S(1)} %get-tuple-element.22, s32[8]{0:T(128)S(1)} %get-tuple-element.21), kind=kLoop, calls=%fused_computation.52 | loop fusion | flops 2944 | bytes 832 | tf_op jit(solution)/shard_map/reduce_sum | solution.py:30
  12.7 0.1 compare_and_fusion.1
  12.9 0.4 reshape.82
  13.3 0.6 %fusion.16 = f32[8,4,64,64]{2,3,1,0:T(8,128)S(1)} fusion(bf16[64,8,4,128]{3,2,1,0:T(4,128)(2,1)S(1)} %reshape.82, bf16[64,8,128,1]{2,1,0,3:T(8,128)(2,1)S(1)} %bitcast.78), kind=kOutput, calls=%fused_computation.17 | convolution fusion | flops 33685504 | bytes 1179648 | tf_op jit(solution)/shard_map/qkgd,skd->kgqs/dot_general | solution.py:44
  13.9 0.3 fusion.50
  14.3 0.7 %fusion.19 = bf16[64,8,4,128]{3,0,2,1:T(8,128)(2,1)S(1)} fusion(f32[64]{0:T(128)S(1)} %get-tuple-element.34, f32[64,8,4]{0,2,1:T(4,128)S(1)} %bitcast.85, bf16[64,8,128,1]{2,1,0,3:T(8,128)(2,1)S(1)} %bitcast.80, f32[8,4,64,64]{2,3,1,0:T(8,128)S(1)} %fusion.16, pred[64,64]{0,1:T(8,128)(4,1)S(1)} %compare_and_fusion.1), kind=kOutput, calls=%fused_computation.21 | convolution fusion | flops 34867264 | bytes 1192192 | tf_op jit(solution)/shard_map/kgqs,skd->qkgd/dot_general | solution.py:51
  14.9 0.4 copy.20
  15.3 0.0 copy-start.2
  15.4 0.4 convert_element_type.48
  15.7 1.6 %collective-permute-start.3 = (bf16[64,4096]{1,0:T(8,128)(2,1)S(1)}, bf16[64,4096]{1,0:T(8,128)(2,1)S(1)}, u32[]{:S(2)}, u32[]{:S(2)}) collective-permute-start(bf16[64,4096]{1,0:T(8,128)(2,1)S(1)} %convert_element_type.48), channel_id=1, source_target_pairs={{0,8},{8,16},{16,24},{24,0},{1,9},{9,17},{17,25},{25,1},{2,10},{10... | collective-permute-start | bytes 1572872 | tf_op jit(solution)/shard_map/ppermute | solution.py:26
  17.4 0.1 pad_add_fusion
  17.5 0.0 collective-permute-done
  17.5 1.6 %collective-permute-start.1 = (bf16[64,2048]{1,0:T(8,128)(2,1)S(1)}, bf16[64,2048]{1,0:T(8,128)(2,1)S(1)}, u32[]{:S(2)}, u32[]{:S(2)}) collective-permute-start(bf16[64,2048]{1,0:T(8,128)(2,1)S(1)} %broadcast_select_fusion), channel_id=1, source_target_pairs={{0,1},{1,0},{2,3},{3,2},{4,5},{5,4},{6,7},{7,6},{8,9},{9,8},{10,11... | collective-permute-start | bytes 786440 | tf_op jit(solution)/shard_map/ppermute | solution.py:65
  19.1 0.1 convert_reduce_fusion
  19.2 0.4 reshape.83
  19.6 0.1 compare_and_fusion
  19.7 5.1 %collective-permute-done.1 = bf16[64,2048]{1,0:T(8,128)(2,1)S(1)} collective-permute-done((bf16[64,2048]{1,0:T(8,128)(2,1)S(1)}, bf16[64,2048]{1,0:T(8,128)(2,1)S(1)}, u32[]{:S(2)}, u32[]{:S(2)}) %collective-permute-start.1) | collective-permute-done | bytes 262176 | tf_op jit(solution)/shard_map/ppermute | solution.py:65
  24.8 0.1 pad_maximum_fusion
  24.8 0.1 slice_bitcast_fusion.1
  24.9 0.1 copy.39
  25.0 0.1 copy.38
  25.1 0.5 %fusion.25 = f32[8,192,64,4]{1,2,3,0:T(8,128)S(1)} fusion(bf16[64,8,4,128]{3,2,1,0:T(4,128)(2,1)S(1)} %reshape.83, bf16[192,8,128,1]{2,1,0,3:T(8,128)(2,1)S(1)} %bitcast.77), kind=kOutput, calls=%fused_computation.31 | convolution fusion | flops 100663296 | bytes 2490368 | tf_op jit(solution)/shard_map/qkgd,skd->kgqs/dot_general | solution.py:44
  25.5 1.0 %fusion.51 = (f32[8,4,64]{2,1,0:T(4,128)S(1)}, bf16[8,4,64,192]{3,2,1,0:T(8,128)(2,1)S(1)}) fusion(f32[8,192,64,4]{1,2,3,0:T(8,128)S(1)} %fusion.25, pred[64,192]{1,0:T(8,128)(4,1)S(1)} %compare_and_fusion), kind=kOutput, calls=%fused_computation.75 | output fusion | flops 2752703 | bytes 2379776 | tf_op jit(solution)/shard_map/sub | solution.py:48
  26.5 0.5 %fusion.20 = bf16[64,8,4,128]{3,0,2,1:T(8,128)(2,1)S(1)} fusion(bf16[8,4,64,192]{3,2,1,0:T(8,128)(2,1)S(1)} %get-tuple-element.32, f32[64]{0:T(128)S(1)} %get-tuple-element.33, f32[64,8,4]{0,2,1:T(4,128)S(1)} %bitcast.86, bf16[192,8,128,1]{2,1,0,3:T(8,128)(2,1)S(1)} %bitcast.79), kind=kOutput, calls=%fused_computation.22 | convolution fusion | flops 101449728 | bytes 1712384 | tf_op jit(solution)/shard_map/kgqs,skd->qkgd/dot_general | solution.py:51
  26.9 0.4 copy.24
  27.4 0.4 convert_element_type.52
  27.8 0.0 collective-permute-done.2
  27.8 1.6 %collective-permute-start.4 = (bf16[64,4096]{1,0:T(8,128)(2,1)S(1)}, bf16[64,4096]{1,0:T(8,128)(2,1)S(1)}, u32[]{:S(2)}, u32[]{:S(2)}) collective-permute-start(bf16[64,4096]{1,0:T(8,128)(2,1)S(1)} %convert_element_type.52), channel_id=1, source_target_pairs={{0,8},{8,16},{16,24},{24,0},{1,9},{9,17},{17,25},{25,1},{2,10},{10... | collective-permute-start | bytes 1572872 | tf_op jit(solution)/shard_map/ppermute | solution.py:26
  29.4 0.1 slice.71
  29.5 0.7 %fusion.48 = (s32[1]{0:T(128)}, s32[1]{0:T(128)}, s32[1]{0:T(128)}, s32[1]{0:T(128)}) fusion(s32[4]{0:T(128)S(1)} %bitcast.81, s32[]{:T(128)S(6)} %select_n.129, s32[]{:T(128)S(6)} %select_n.158, s32[]{:T(128)S(6)} %select_n.157, s32[]{:T(128)S(6)} %select_n.152), kind=kLoop, calls=%fused_computation.72 | loop fusion | bytes 48 | tf_op jit(solution)/shard_map/jit(dynamic_index_in_dim)/dynamic_slice | solution.py:209
  31.4 0.6 %fusion.47 = (s32[1]{0:T(128)}, s32[1]{0:T(128)}) fusion(s32[2]{0:T(128)S(1)} %slice.71, s32[]{:T(128)S(6)} %select_n.154, s32[]{:T(128)S(6)} %select_n.160), kind=kLoop, calls=%fused_computation.71 | loop fusion | bytes 24 | tf_op jit(solution)/shard_map/jit(dynamic_index_in_dim)/dynamic_slice | solution.py:213
  34.6 0.0 collective-permute-done.3
  34.6 0.1 collective-permute-start.5
  34.7 7.3 %collective-permute-done.4 = bf16[64,4096]{1,0:T(8,128)(2,1)S(1)} collective-permute-done((bf16[64,4096]{1,0:T(8,128)(2,1)S(1)}, bf16[64,4096]{1,0:T(8,128)(2,1)S(1)}, u32[]{:S(2)}, u32[]{:S(2)}) %collective-permute-start.4) | collective-permute-done | bytes 524320 | tf_op jit(solution)/shard_map/ppermute | solution.py:26
  41.9 0.0 collective-permute-start.6
  41.9 0.1 select_bitcast_fusion.3
  42.0 0.0 collective-permute-done.5
  42.0 1.8 %collective-permute-done.6 = bf16[64,4096]{1,0:T(8,128)(2,1)S(1)} collective-permute-done((bf16[64,4096]{1,0:T(8,128)(2,1)S(1)}, bf16[64,4096]{1,0:T(8,128)(2,1)S(1)}, u32[]{:S(2)}, u32[]{:S(2)}) %collective-permute-start.6) | collective-permute-done | bytes 524320 | tf_op jit(solution)/shard_map/ppermute | solution.py:20
  43.8 0.1 select_bitcast_fusion.2
  43.9 1.1 %maximum_bitcast_fusion = bf16[1,2,64,4096]{3,2,1,0:T(8,128)(2,1)} fusion(bf16[1,64,4096]{2,1,0:T(8,128)(2,1)S(1)} %select_bitcast_fusion.2, bf16[1,64,4096]{2,1,0:T(8,128)(2,1)S(1)} %select_bitcast_fusion.3), kind=kLoop, calls=%fused_computation.23 | loop fusion | flops 524288 | bytes 2097152 | tf_op jit(solution)/shard_map/reshape | solution.py:222
  (22 shorter events, 0.2 us)
Async XLA Ops:
  0.0 7.2 %copy-start.4 = (s32[1,4]{1,0:T(1,128)S(1)}, s32[1,4]{1,0:T(1,128)}, u32[]{:S(2)}) copy-start(s32[1,4]{1,0:T(1,128)} %param.5) | copy-start | bytes 52
  0.0 7.2 %copy-start.5 = (s32[1,2]{1,0:T(1,128)S(1)}, s32[1,2]{1,0:T(1,128)}, u32[]{:S(2)}) copy-start(s32[1,2]{1,0:T(1,128)} %param.7) | copy-start | bytes 28
  2.6 9.3 %copy-start.3 = (s32[1,4,8]{2,1,0:T(4,128)S(1)}, s32[1,4,8]{2,1,0:T(4,128)}, u32[]{:S(2)}) copy-start(s32[1,4,8]{2,1,0:T(4,128)} %param.6) | copy-start | bytes 388
  4.1 13.4 %collective-permute-start = (bf16[64,2048]{1,0:T(8,128)(2,1)S(1)}, bf16[64,2048]{1,0:T(8,128)(2,1)S(1)}, u32[]{:S(2)}, u32[]{:S(2)}) collective-permute-start(bf16[64,2048]{1,0:T(8,128)(2,1)S(1)} %slice.72), channel_id=1, source_target_pairs={{0,2},{1,3},{2,0},{3,1},{4,6},{5,7},{6,4},{7,5},{8,10},{9,11},{10,... | collective-permute-start | bytes 786440 | tf_op jit(solution)/shard_map/ppermute | solution.py:60
  7.8 19.9 %collective-permute-start.2 = (s32[6]{0:T(128)}, s32[6]{0:T(128)S(1)}, u32[]{:S(2)}, u32[]{:S(2)}) collective-permute-start(s32[6]{0:T(128)} %pad_add_fusion.1), channel_id=1, source_target_pairs={{0,8},{8,16},{16,24},{24,0},{1,9},{9,17},{17,25},{25,1},{2,10},{10... | collective-permute-start | bytes 80 | tf_op jit(solution)/shard_map/ppermute | solution.py:26
  12.1 0.7 %copy-start = (s32[8]{0:T(128)}, s32[8]{0:T(128)S(1)}, u32[]{:S(2)}) copy-start(s32[8]{0:T(128)S(1)} %get-tuple-element.22) | copy-start | bytes 100
  14.9 4.1 %copy-start.1 = (s32[8]{0:T(128)S(1)}, s32[8]{0:T(128)}, u32[]{:S(2)}) copy-start(s32[8]{0:T(128)} %copy-done) | copy-start | bytes 100
  15.3 4.2 %copy-start.2 = (s32[64]{0:T(128)S(1)}, s32[64]{0:T(128)}, u32[]{:S(2)}) copy-start(s32[64]{0:T(128)} %get-tuple-element.13) | copy-start | bytes 772
  15.7 18.8 %collective-permute-start.3 = (bf16[64,4096]{1,0:T(8,128)(2,1)S(1)}, bf16[64,4096]{1,0:T(8,128)(2,1)S(1)}, u32[]{:S(2)}, u32[]{:S(2)}) collective-permute-start(bf16[64,4096]{1,0:T(8,128)(2,1)S(1)} %convert_element_type.48), channel_id=1, source_target_pairs={{0,8},{8,16},{16,24},{24,0},{1,9},{9,17},{17,25},{25,1},{2,10},{10... | collective-permute-start | bytes 1572872 | tf_op jit(solution)/shard_map/ppermute | solution.py:26
  17.5 7.3 %collective-permute-start.1 = (bf16[64,2048]{1,0:T(8,128)(2,1)S(1)}, bf16[64,2048]{1,0:T(8,128)(2,1)S(1)}, u32[]{:S(2)}, u32[]{:S(2)}) collective-permute-start(bf16[64,2048]{1,0:T(8,128)(2,1)S(1)} %broadcast_select_fusion), channel_id=1, source_target_pairs={{0,1},{1,0},{2,3},{3,2},{4,5},{5,4},{6,7},{7,6},{8,9},{9,8},{10,11... | collective-permute-start | bytes 786440 | tf_op jit(solution)/shard_map/ppermute | solution.py:65
  27.8 14.2 %collective-permute-start.4 = (bf16[64,4096]{1,0:T(8,128)(2,1)S(1)}, bf16[64,4096]{1,0:T(8,128)(2,1)S(1)}, u32[]{:S(2)}, u32[]{:S(2)}) collective-permute-start(bf16[64,4096]{1,0:T(8,128)(2,1)S(1)} %convert_element_type.52), channel_id=1, source_target_pairs={{0,8},{8,16},{16,24},{24,0},{1,9},{9,17},{17,25},{25,1},{2,10},{10... | collective-permute-start | bytes 1572872 | tf_op jit(solution)/shard_map/ppermute | solution.py:26
  34.6 7.4 %collective-permute-start.5 = (bf16[64,4096]{1,0:T(8,128)(2,1)S(1)}, bf16[64,4096]{1,0:T(8,128)(2,1)S(1)}, u32[]{:S(2)}, u32[]{:S(2)}) collective-permute-start(bf16[64,4096]{1,0:T(8,128)(2,1)S(1)} %collective-permute-done.3), channel_id=1, source_target_pairs={{0,4},{4,0},{1,5},{5,1},{2,6},{6,2},{3,7},{7,3},{8,12},{12,8},{9,1... | collective-permute-start | bytes 1572872 | tf_op jit(solution)/shard_map/ppermute | solution.py:20
  41.9 1.9 %collective-permute-start.6 = (bf16[64,4096]{1,0:T(8,128)(2,1)S(1)}, bf16[64,4096]{1,0:T(8,128)(2,1)S(1)}, u32[]{:S(2)}, u32[]{:S(2)}) collective-permute-start(bf16[64,4096]{1,0:T(8,128)(2,1)S(1)} %collective-permute-done.4), channel_id=1, source_target_pairs={{0,4},{4,0},{1,5},{5,1},{2,6},{6,2},{3,7},{7,3},{8,12},{12,8},{9,1... | collective-permute-start | bytes 1572872 | tf_op jit(solution)/shard_map/ppermute | solution.py:20

commit v23 on v22

--- a/solution.py
+++ b/solution.py
@@ -181,7 +181,7 @@
     long_rows = pick(swap_second, own_rows[1], own_rows[0])
     long_kv = long_rows[:, D:]
     long_pieces = gathered(long_kv, seq_index, seq_count, reach)
-    meta = lax.optimization_barrier((jnp.concatenate([lengths_all, hand_over[0]]), long_kv))[0]
+    meta = lax.optimization_barrier((jnp.concatenate([lengths_all, hand_over[0]]), short_out))[0]
     previous = passed_along(meta, "section", 1)
     long_queries = lax.optimization_barrier((long_rows[:, :D], short_out))[0]
     pieces = [long_kv]

time: 45.2 us -> 46.9 us (1.038)
  waiting for transfers between devices: 14.2 us -> 17.7 us
  starting transfers between devices: 9.53 us -> 7.9 us
  other arithmetic: 5.86 us -> 5.27 us
    ppermute x3, waiting for transfers between devices: 7.27 us -> 10.8 us  [passed_along(): return lax.ppermute(value, axis, pairs)]
    ppermute x3, starting transfers between devices: 4.84 us -> 3.21 us  [passed_along(): return lax.ppermute(value, axis, pairs)]
    concatenate x1, other arithmetic: 0.66 us -> 0.07 us  [shards(): jnp.concatenate([lengths_all, hand_over[0]])]
  transfers between devices with their start and end apart: 7 -> 7, of which waited for: 3 -> 4; matrix products, arithmetic and copies ran while one was open for 21% -> 19% of each run, Pallas kernels for 0% -> 0%
where the time goes in v23:
time: 46.9 us; the launch traced here: 46.6 us
  waiting for transfers between devices  17.7 us (38%)
  between operations  8.1 us (17%)
  starting transfers between devices  7.9 us (17%)
  local copies, waits for them, and re-layouts  5.44 us (12%)
  other arithmetic  5.27 us (11%)
  matrix products  2.21 us (5%)
    ppermute x3, waiting for transfers between devices, passed_along(): return lax.ppermute(value, axis, pairs)  10.8 us
    ppermute x1, waiting for transfers between devices, gathered(): over_x = lax.ppermute(onward, 'seq', [(j, j ^ 1) for j in range(4)])  5.11 us
    ppermute x3, starting transfers between devices, passed_along(): return lax.ppermute(value, axis, pairs)  3.21 us
    ppermute x1, starting transfers between devices, gathered(): over_y = lax.ppermute(block, 'seq', [(j, j ^ 2) for j in range(4)])  3.06 us
    ppermute x2, waiting for transfers between devices, swapped(): return lax.ppermute(block, axis, route)  1.84 us
    convert_element_type x4, local copies, waits for them, and re-layouts, attend_row(): return result.reshape(seg_len, D).astype(jnp.bfloat16)  1.59 us
    ppermute x1, starting transfers between devices, gathered(): over_x = lax.ppermute(onward, 'seq', [(j, j ^ 1) for j in range(4)])  1.56 us
    select_n x1, other arithmetic, pick(): return jnp.where(first_if, a, b)  1.48 us
  transfers between devices with their start and end apart: 7, of which 4 were waited for; matrix products, arithmetic and copies ran while one was open for 19% of the time, Pallas kernels for 0%

profile of v23, /device:TPU:0, one launch (start us, length us, event | category | flops | bytes accessed | tf_op | source)
XLA Modules:
  0.0 46.6 jit_solution(2251139571985743604)
XLA Ops:
  0.0 0.7 %constant_dynamic-slice_fusion.1 = s32[1,2]{1,0:T(1,128)S(1)} fusion(s32[1,4]{1,0:T(1,128)} %param.5, s32[]{:T(128)S(6)} %select_n.129), kind=kLoop, calls=%fused_computation.68 | loop fusion | bytes 20 | tf_op jit(solution)/shard_map/dynamic_slice | solution.py:163
  0.7 0.7 %fusion.49 = (s32[1,1]{1,0:T(1,128)}, s32[1,1]{1,0:T(1,128)}) fusion(s32[1,2]{1,0:T(1,128)S(1)} %constant_dynamic-slice_fusion.1), kind=kLoop, calls=%fused_computation.73 | loop fusion | bytes 16 | tf_op jit(solution)/shard_map/slice | solution.py:164
  2.7 0.0 copy-start.1
  2.7 1.5 %select_bitcast_fusion.1 = (bf16[64,6144]{1,0:T(8,128)(2,1)S(1)}, bf16[64,6144]{1,0:T(8,128)(2,1)S(1)}) fusion(pred[]{:T(512)S(6)} %ge.32, bf16[1,2,64,6144]{3,2,1,0:T(8,128)(2,1)} %param.4), kind=kLoop, calls=%fused_computation.30 | loop fusion | flops 786432 | bytes 3145729 | tf_op jit(solution)/shard_map/jit(_where)/select_n | solution.py:167
  4.3 3.1 %collective-permute-start = (bf16[64,2048]{1,0:T(8,128)(2,1)S(1)}, bf16[64,2048]{1,0:T(8,128)(2,1)S(1)}, u32[]{:S(2)}, u32[]{:S(2)}) collective-permute-start(bf16[64,2048]{1,0:T(8,128)(2,1)S(1)} %slice.72), channel_id=1, source_target_pairs={{0,2},{1,3},{2,0},{3,1},{4,6},{5,7},{6,4},{7,5},{8,10},{9,11},{10,... | collective-permute-start | bytes 786440 | tf_op jit(solution)/shard_map/ppermute | solution.py:60
  10.1 0.2 reduce_window_sum.11
  10.3 0.6 %convert_reduce_fusion.2 = (s32[64]{0:T(128)}, s32[64]{0:T(128)S(1)}) fusion(s32[64]{0:T(128)S(1)} %iota_add_fusion, s32[8]{0:T(128)S(1)} %get-tuple-element.22, s32[8]{0:T(128)S(1)} %get-tuple-element.21), kind=kLoop, calls=%fused_computation.52 | loop fusion | flops 2944 | bytes 832 | tf_op jit(solution)/shard_map/reduce_sum | solution.py:30
  10.9 0.1 compare_and_fusion.1
  11.0 0.4 reshape.82
  11.4 0.6 %fusion.16 = f32[8,4,64,64]{2,3,1,0:T(8,128)S(1)} fusion(bf16[64,8,4,128]{3,2,1,0:T(4,128)(2,1)S(1)} %reshape.82, bf16[64,8,128,1]{2,1,0,3:T(8,128)(2,1)S(1)} %bitcast.78), kind=kOutput, calls=%fused_computation.17 | convolution fusion | flops 33685504 | bytes 1179648 | tf_op jit(solution)/shard_map/qkgd,skd->kgqs/dot_general | solution.py:44
  12.0 0.3 fusion.50
  12.4 0.7 %fusion.19 = bf16[64,8,4,128]{3,0,2,1:T(8,128)(2,1)S(1)} fusion(f32[64]{0:T(128)S(1)} %get-tuple-element.34, f32[64,8,4]{0,2,1:T(4,128)S(1)} %bitcast.85, bf16[64,8,128,1]{2,1,0,3:T(8,128)(2,1)S(1)} %bitcast.80, f32[8,4,64,64]{2,3,1,0:T(8,128)S(1)} %fusion.16, pred[64,64]{0,1:T(8,128)(4,1)S(1)} %compare_and_fusion.1), kind=kOutput, calls=%fused_computation.21 | convolution fusion | flops 34867264 | bytes 1192192 | tf_op jit(solution)/shard_map/kgqs,skd->qkgd/dot_general | solution.py:51
  13.1 0.0 copy-start.2
  13.1 0.0 copy-start.3
  13.1 0.4 copy.20
  13.5 0.0 copy-start
  13.5 0.4 convert_element_type.48
  13.9 1.6 %collective-permute-start.3 = (bf16[64,4096]{1,0:T(8,128)(2,1)S(1)}, bf16[64,4096]{1,0:T(8,128)(2,1)S(1)}, u32[]{:S(2)}, u32[]{:S(2)}) collective-permute-start(bf16[64,4096]{1,0:T(8,128)(2,1)S(1)} %convert_element_type.48), channel_id=1, source_target_pairs={{0,8},{8,16},{16,24},{24,0},{1,9},{9,17},{17,25},{25,1},{2,10},{10... | collective-permute-start | bytes 1572872 | tf_op jit(solution)/shard_map/ppermute | solution.py:26
  15.5 0.1 pad_add_fusion.1
  15.6 1.6 %collective-permute-start.2 = (s32[6]{0:T(128)S(1)}, s32[6]{0:T(128)S(1)}, u32[]{:S(2)}, u32[]{:S(2)}) collective-permute-start(s32[6]{0:T(128)S(1)} %pad_add_fusion.1), channel_id=1, source_target_pairs={{0,8},{8,16},{16,24},{24,0},{1,9},{9,17},{17,25},{25,1},{2,10},{10... | collective-permute-start | bytes 80 | tf_op jit(solution)/shard_map/ppermute | solution.py:26
  17.2 0.1 pad_add_fusion
  17.3 0.0 collective-permute-done
  17.3 1.6 %collective-permute-start.1 = (bf16[64,2048]{1,0:T(8,128)(2,1)S(1)}, bf16[64,2048]{1,0:T(8,128)(2,1)S(1)}, u32[]{:S(2)}, u32[]{:S(2)}) collective-permute-start(bf16[64,2048]{1,0:T(8,128)(2,1)S(1)} %broadcast_select_fusion), channel_id=1, source_target_pairs={{0,1},{1,0},{2,3},{3,2},{4,5},{5,4},{6,7},{7,6},{8,9},{9,8},{10,11... | collective-permute-start | bytes 786440 | tf_op jit(solution)/shard_map/ppermute | solution.py:65
  18.9 0.1 convert_reduce_fusion
  19.0 0.4 reshape.83
  19.4 0.1 compare_and_fusion
  19.5 5.1 %collective-permute-done.1 = bf16[64,2048]{1,0:T(8,128)(2,1)S(1)} collective-permute-done((bf16[64,2048]{1,0:T(8,128)(2,1)S(1)}, bf16[64,2048]{1,0:T(8,128)(2,1)S(1)}, u32[]{:S(2)}, u32[]{:S(2)}) %collective-permute-start.1) | collective-permute-done | bytes 262176 | tf_op jit(solution)/shard_map/ppermute | solution.py:65
  24.6 0.1 pad_maximum_fusion
  24.7 0.1 slice_bitcast_fusion.1
  24.7 0.1 copy.39
  24.8 0.1 copy.38
  24.9 0.5 fusion.25
  25.3 1.0 %fusion.51 = (f32[8,4,64]{2,1,0:T(4,128)S(1)}, bf16[8,4,64,192]{3,2,1,0:T(8,128)(2,1)S(1)}) fusion(f32[8,192,64,4]{1,2,3,0:T(8,128)S(1)} %fusion.25, pred[64,192]{1,0:T(8,128)(4,1)S(1)} %compare_and_fusion), kind=kOutput, calls=%fused_computation.75 | output fusion | flops 2752703 | bytes 2379776 | tf_op jit(solution)/shard_map/sub | solution.py:48
  26.3 0.5 fusion.20
  26.8 0.4 copy.24
  27.2 0.4 convert_element_type.52
  27.6 1.7 %collective-permute-done.2 = s32[6]{0:T(128)S(1)} collective-permute-done((s32[6]{0:T(128)S(1)}, s32[6]{0:T(128)S(1)}, u32[]{:S(2)}, u32[]{:S(2)}) %collective-permute-start.2) | collective-permute-done | bytes 56 | tf_op jit(solution)/shard_map/ppermute | solution.py:26
  29.3 0.0 collective-permute-start.4
  29.3 0.1 slice.71
  29.4 0.7 %fusion.48 = (s32[1]{0:T(128)}, s32[1]{0:T(128)}, s32[1]{0:T(128)}, s32[1]{0:T(128)}) fusion(s32[4]{0:T(128)S(1)} %bitcast.81, s32[]{:T(128)S(6)} %select_n.129, s32[]{:T(128)S(6)} %select_n.158, s32[]{:T(128)S(6)} %select_n.157, s32[]{:T(128)S(6)} %select_n.152), kind=kLoop, calls=%fused_computation.72 | loop fusion | bytes 48 | tf_op jit(solution)/shard_map/jit(dynamic_index_in_dim)/dynamic_slice | solution.py:209
  31.3 0.6 %fusion.47 = (s32[1]{0:T(128)}, s32[1]{0:T(128)}) fusion(s32[2]{0:T(128)S(1)} %slice.71, s32[]{:T(128)S(6)} %select_n.154, s32[]{:T(128)S(6)} %select_n.160), kind=kLoop, calls=%fused_computation.71 | loop fusion | bytes 24 | tf_op jit(solution)/shard_map/jit(dynamic_index_in_dim)/dynamic_slice | solution.py:213
  34.5 0.1 collective-permute-start.5
  34.6 9.0 %collective-permute-done.4 = bf16[64,4096]{1,0:T(8,128)(2,1)S(1)} collective-permute-done((bf16[64,4096]{1,0:T(8,128)(2,1)S(1)}, bf16[64,4096]{1,0:T(8,128)(2,1)S(1)}, u32[]{:S(2)}, u32[]{:S(2)}) %collective-permute-start.4) | collective-permute-done | bytes 524320 | tf_op jit(solution)/shard_map/ppermute | solution.py:26
  43.6 0.0 collective-permute-start.6
  43.6 0.1 select_bitcast_fusion.3
  43.7 1.8 %collective-permute-done.6 = bf16[64,4096]{1,0:T(8,128)(2,1)S(1)} collective-permute-done((bf16[64,4096]{1,0:T(8,128)(2,1)S(1)}, bf16[64,4096]{1,0:T(8,128)(2,1)S(1)}, u32[]{:S(2)}, u32[]{:S(2)}) %collective-permute-start.6) | collective-permute-done | bytes 524320 | tf_op jit(solution)/shard_map/ppermute | solution.py:20
  45.5 0.1 select_bitcast_fusion.2
  45.6 1.1 %maximum_bitcast_fusion = bf16[1,2,64,4096]{3,2,1,0:T(8,128)(2,1)} fusion(bf16[1,64,4096]{2,1,0:T(8,128)(2,1)S(1)} %select_bitcast_fusion.2, bf16[1,64,4096]{2,1,0:T(8,128)(2,1)S(1)} %select_bitcast_fusion.3), kind=kLoop, calls=%fused_computation.23 | loop fusion | flops 524288 | bytes 2097152 | tf_op jit(solution)/shard_map/reshape | solution.py:222
  (18 shorter events, 0.2 us)
Async XLA Ops:
  2.7 7.3 %copy-start.1 = (s32[1,4,8]{2,1,0:T(4,128)S(1)}, s32[1,4,8]{2,1,0:T(4,128)}, u32[]{:S(2)}) copy-start(s32[1,4,8]{2,1,0:T(4,128)} %param.6) | copy-start | bytes 388
  4.3 13.0 %collective-permute-start = (bf16[64,2048]{1,0:T(8,128)(2,1)S(1)}, bf16[64,2048]{1,0:T(8,128)(2,1)S(1)}, u32[]{:S(2)}, u32[]{:S(2)}) collective-permute-start(bf16[64,2048]{1,0:T(8,128)(2,1)S(1)} %slice.72), channel_id=1, source_target_pairs={{0,2},{1,3},{2,0},{3,1},{4,6},{5,7},{6,4},{7,5},{8,10},{9,11},{10,... | collective-permute-start | bytes 786440 | tf_op jit(solution)/shard_map/ppermute | solution.py:60
  13.1 2.5 %copy-start.2 = (s32[1,4]{1,0:T(1,128)S(1)}, s32[1,4]{1,0:T(1,128)}, u32[]{:S(2)}) copy-start(s32[1,4]{1,0:T(1,128)} %param.5) | copy-start | bytes 52
  13.1 2.5 %copy-start.3 = (s32[1,2]{1,0:T(1,128)S(1)}, s32[1,2]{1,0:T(1,128)}, u32[]{:S(2)}) copy-start(s32[1,2]{1,0:T(1,128)} %param.7) | copy-start | bytes 28
  13.5 5.9 %copy-start = (s32[64]{0:T(128)S(1)}, s32[64]{0:T(128)}, u32[]{:S(2)}) copy-start(s32[64]{0:T(128)} %get-tuple-element.13) | copy-start | bytes 772
  13.9 20.6 %collective-permute-start.3 = (bf16[64,4096]{1,0:T(8,128)(2,1)S(1)}, bf16[64,4096]{1,0:T(8,128)(2,1)S(1)}, u32[]{:S(2)}, u32[]{:S(2)}) collective-permute-start(bf16[64,4096]{1,0:T(8,128)(2,1)S(1)} %convert_element_type.48), channel_id=1, source_target_pairs={{0,8},{8,16},{16,24},{24,0},{1,9},{9,17},{17,25},{25,1},{2,10},{10... | collective-permute-start | bytes 1572872 | tf_op jit(solution)/shard_map/ppermute | solution.py:26
  15.6 13.7 %collective-permute-start.2 = (s32[6]{0:T(128)S(1)}, s32[6]{0:T(128)S(1)}, u32[]{:S(2)}, u32[]{:S(2)}) collective-permute-start(s32[6]{0:T(128)S(1)} %pad_add_fusion.1), channel_id=1, source_target_pairs={{0,8},{8,16},{16,24},{24,0},{1,9},{9,17},{17,25},{25,1},{2,10},{10... | collective-permute-start | bytes 80 | tf_op jit(solution)/shard_map/ppermute | solution.py:26
  17.3 7.3 %collective-permute-start.1 = (bf16[64,2048]{1,0:T(8,128)(2,1)S(1)}, bf16[64,2048]{1,0:T(8,128)(2,1)S(1)}, u32[]{:S(2)}, u32[]{:S(2)}) collective-permute-start(bf16[64,2048]{1,0:T(8,128)(2,1)S(1)} %broadcast_select_fusion), channel_id=1, source_target_pairs={{0,1},{1,0},{2,3},{3,2},{4,5},{5,4},{6,7},{7,6},{8,9},{9,8},{10,11... | collective-permute-start | bytes 786440 | tf_op jit(solution)/shard_map/ppermute | solution.py:65
  29.3 14.3 %collective-permute-start.4 = (bf16[64,4096]{1,0:T(8,128)(2,1)S(1)}, bf16[64,4096]{1,0:T(8,128)(2,1)S(1)}, u32[]{:S(2)}, u32[]{:S(2)}) collective-permute-start(bf16[64,4096]{1,0:T(8,128)(2,1)S(1)} %convert_element_type.52), channel_id=1, source_target_pairs={{0,8},{8,16},{16,24},{24,0},{1,9},{9,17},{17,25},{25,1},{2,10},{10... | collective-permute-start | bytes 1572872 | tf_op jit(solution)/shard_map/ppermute | solution.py:26
  34.5 9.2 %collective-permute-start.5 = (bf16[64,4096]{1,0:T(8,128)(2,1)S(1)}, bf16[64,4096]{1,0:T(8,128)(2,1)S(1)}, u32[]{:S(2)}, u32[]{:S(2)}) collective-permute-start(bf16[64,4096]{1,0:T(8,128)(2,1)S(1)} %collective-permute-done.3), channel_id=1, source_target_pairs={{0,4},{4,0},{1,5},{5,1},{2,6},{6,2},{3,7},{7,3},{8,12},{12,8},{9,1... | collective-permute-start | bytes 1572872 | tf_op jit(solution)/shard_map/ppermute | solution.py:20
  43.6 1.9 %collective-permute-start.6 = (bf16[64,4096]{1,0:T(8,128)(2,1)S(1)}, bf16[64,4096]{1,0:T(8,128)(2,1)S(1)}, u32[]{:S(2)}, u32[]{:S(2)}) collective-permute-start(bf16[64,4096]{1,0:T(8,128)(2,1)S(1)} %collective-permute-done.4), channel_id=1, source_target_pairs={{0,4},{4,0},{1,5},{5,1},{2,6},{6,2},{3,7},{7,3},{8,12},{12,8},{9,1... | collective-permute-start | bytes 1572872 | tf_op jit(solution)/shard_map/ppermute | solution.py:20

commit v24 on v22

--- a/solution.py
+++ b/solution.py
@@ -159,8 +159,13 @@
     query_pos = seq_index * seg_len + local
     key_value_width = KV_HEADS * HD
     far = jnp.int32(4 * length_all)
-    own_ends = lax.dynamic_slice_in_dim(doc_ends, 2 * replica, 2, 0)
-    own_lengths = lax.dynamic_slice_in_dim(lengths_all, 2 * replica, 2, 0)
+    row_ids = jnp.arange(rows)
+    own_ends = jnp.stack(
+        [jnp.sum(jnp.where((row_ids == 2 * replica + k)[:, None], doc_ends, 0), axis=0) for k in range(2)]
+    )
+    own_lengths = jnp.stack(
+        [jnp.sum(jnp.where(row_ids == 2 * replica + k, lengths_all, 0)) for k in range(2)]
+    )
     swap_second = own_lengths[1] >= own_lengths[0]
 
     def pick(first_if, a, b):

time: 45.2 us -> 45.3 us (level)
  other arithmetic: 5.86 us -> 7.33 us
  local copies, waits for them, and re-layouts: 5.43 us -> 4.05 us
    reduce_sum x0 -> x2, other arithmetic: none -> 1.45 us  [the longest x1 1.36 us: shards(): jnp.sum(jnp.where(row_ids == 2 * replica + k, lengths_all, 0))]
    dynamic_slice x2 -> x0, local copies, waits for them, and re-layouts: 0.8 us -> none  [the longest x1 0.8 us: shards(): own_lengths = lax.dynamic_slice_in_dim(lengths_all, 2 * replica, 2, 0)]
    slice x1 -> x0, local copies, waits for them, and re-layouts: 0.58 us -> none  [shards(): swap_second = own_lengths[1] >= own_lengths[0]]
    select_n x1 -> x2, other arithmetic: 1.48 us -> 1.49 us  [pick(): return jnp.where(first_if, a, b)]
where the time goes in v24:
time: 45.3 us; the launch traced here: 45.1 us
  waiting for transfers between devices  14.2 us (31%)
  starting transfers between devices  9.52 us (21%)
  between operations  7.74 us (17%)
  other arithmetic  7.33 us (16%)
  local copies, waits for them, and re-layouts  4.05 us (9%)
  matrix products  2.21 us (5%)
    ppermute x3, waiting for transfers between devices, passed_along(): return lax.ppermute(value, axis, pairs)  7.27 us
    ppermute x1, waiting for transfers between devices, gathered(): over_x = lax.ppermute(onward, 'seq', [(j, j ^ 1) for j in range(4)])  5.11 us
    ppermute x3, starting transfers between devices, passed_along(): return lax.ppermute(value, axis, pairs)  4.83 us
    ppermute x1, starting transfers between devices, gathered(): over_y = lax.ppermute(block, 'seq', [(j, j ^ 2) for j in range(4)])  3.06 us
    ppermute x2, waiting for transfers between devices, swapped(): return lax.ppermute(block, axis, route)  1.84 us
    convert_element_type x4, local copies, waits for them, and re-layouts, attend_row(): return result.reshape(seg_len, D).astype(jnp.bfloat16)  1.59 us
    ppermute x1, starting transfers between devices, gathered(): over_x = lax.ppermute(onward, 'seq', [(j, j ^ 1) for j in range(4)])  1.56 us
    select_n x2, other arithmetic, pick(): return jnp.where(first_if, a, b)  1.49 us
  transfers between devices with their start and end apart: 7, of which 3 were waited for; matrix products, arithmetic and copies ran while one was open for 21% of the time, Pallas kernels for 0%

profile of v24, /device:TPU:0, one launch (start us, length us, event | category | flops | bytes accessed | tf_op | source)
XLA Modules:
  0.0 45.1 jit_solution(8099568103270761251)
XLA Ops:
  0.0 1.4 %select_reduce_fusion.3 = (s32[]{:T(128)}, s32[]{:T(128)}) fusion(s32[1,4]{1,0:T(1,128)} %param.5, s32[]{:T(128)S(6)} %mul.55, s32[]{:T(128)S(6)} %add.70), kind=kLoop, calls=%fused_computation.67 | loop fusion | flops 22 | bytes 32 | tf_op jit(solution)/shard_map/reduce_sum | solution.py:167
  2.6 0.0 copy-start.3
  2.6 1.5 %select_bitcast_fusion.1 = (bf16[64,6144]{1,0:T(8,128)(2,1)S(1)}, bf16[64,6144]{1,0:T(8,128)(2,1)S(1)}) fusion(pred[]{:T(512)S(6)} %ge.28, bf16[1,2,64,6144]{3,2,1,0:T(8,128)(2,1)} %param.4), kind=kLoop, calls=%fused_computation.30 | loop fusion | flops 786432 | bytes 3145729 | tf_op jit(solution)/shard_map/jit(_where)/select_n | solution.py:172
  4.1 3.1 %collective-permute-start = (bf16[64,2048]{1,0:T(8,128)(2,1)S(1)}, bf16[64,2048]{1,0:T(8,128)(2,1)S(1)}, u32[]{:S(2)}, u32[]{:S(2)}) collective-permute-start(bf16[64,2048]{1,0:T(8,128)(2,1)S(1)} %slice.48), channel_id=1, source_target_pairs={{0,2},{1,3},{2,0},{3,1},{4,6},{5,7},{6,4},{7,5},{8,10},{9,11},{10,... | collective-permute-start | bytes 786440 | tf_op jit(solution)/shard_map/ppermute | solution.py:60
  7.2 0.7 %pad_add_fusion.1 = s32[6]{0:T(128)} fusion(s32[2]{0:T(128)S(1)} %bitcast.80, s32[4]{0:T(128)S(1)} %bitcast.79), kind=kLoop, calls=%fused_computation.62 | loop fusion | flops 6 | bytes 48 | tf_op jit(solution)/shard_map/concatenate | solution.py:189
  7.8 1.6 %collective-permute-start.2 = (s32[6]{0:T(128)}, s32[6]{0:T(128)S(1)}, u32[]{:S(2)}, u32[]{:S(2)}) collective-permute-start(s32[6]{0:T(128)} %pad_add_fusion.1), channel_id=1, source_target_pairs={{0,8},{8,16},{16,24},{24,0},{1,9},{9,17},{17,25},{25,1},{2,10},{10... | collective-permute-start | bytes 80 | tf_op jit(solution)/shard_map/ppermute | solution.py:26
  11.9 0.2 reduce_window_sum.11
  12.1 0.1 select_reduce_fusion.2
  12.2 0.6 %convert_reduce_fusion.2 = (s32[64]{0:T(128)}, s32[64]{0:T(128)S(1)}) fusion(s32[64]{0:T(128)S(1)} %iota_add_fusion, s32[8]{0:T(128)S(1)} %get-tuple-element.26, s32[8]{0:T(128)S(1)} %get-tuple-element.25), kind=kLoop, calls=%fused_computation.52 | loop fusion | flops 2944 | bytes 832 | tf_op jit(solution)/shard_map/reduce_sum | solution.py:30
  12.8 0.1 compare_and_fusion.1
  12.9 0.4 reshape.95
  13.3 0.6 %fusion.16 = f32[8,4,64,64]{2,3,1,0:T(8,128)S(1)} fusion(bf16[64,8,4,128]{3,2,1,0:T(4,128)(2,1)S(1)} %reshape.95, bf16[64,8,128,1]{2,1,0,3:T(8,128)(2,1)S(1)} %bitcast.74), kind=kOutput, calls=%fused_computation.17 | convolution fusion | flops 33685504 | bytes 1179648 | tf_op jit(solution)/shard_map/qkgd,skd->kgqs/dot_general | solution.py:44
  14.0 0.3 fusion.47
  14.3 0.7 %fusion.19 = bf16[64,8,4,128]{3,0,2,1:T(8,128)(2,1)S(1)} fusion(f32[64]{0:T(128)S(1)} %get-tuple-element.36, f32[64,8,4]{0,2,1:T(4,128)S(1)} %bitcast.81, bf16[64,8,128,1]{2,1,0,3:T(8,128)(2,1)S(1)} %bitcast.76, f32[8,4,64,64]{2,3,1,0:T(8,128)S(1)} %fusion.16, pred[64,64]{0,1:T(8,128)(4,1)S(1)} %compare_and_fusion.1), kind=kOutput, calls=%fused_computation.21 | convolution fusion | flops 34867264 | bytes 1192192 | tf_op jit(solution)/shard_map/kgqs,skd->qkgd/dot_general | solution.py:51
  15.0 0.4 copy.20
  15.4 0.0 copy-start.2
  15.4 0.4 convert_element_type.48
  15.8 1.6 %collective-permute-start.3 = (bf16[64,4096]{1,0:T(8,128)(2,1)S(1)}, bf16[64,4096]{1,0:T(8,128)(2,1)S(1)}, u32[]{:S(2)}, u32[]{:S(2)}) collective-permute-start(bf16[64,4096]{1,0:T(8,128)(2,1)S(1)} %convert_element_type.48), channel_id=1, source_target_pairs={{0,8},{8,16},{16,24},{24,0},{1,9},{9,17},{17,25},{25,1},{2,10},{10... | collective-permute-start | bytes 1572872 | tf_op jit(solution)/shard_map/ppermute | solution.py:26
  17.5 0.1 pad_add_fusion
  17.6 0.0 collective-permute-done
  17.6 1.6 %collective-permute-start.1 = (bf16[64,2048]{1,0:T(8,128)(2,1)S(1)}, bf16[64,2048]{1,0:T(8,128)(2,1)S(1)}, u32[]{:S(2)}, u32[]{:S(2)}) collective-permute-start(bf16[64,2048]{1,0:T(8,128)(2,1)S(1)} %broadcast_select_fusion), channel_id=1, source_target_pairs={{0,1},{1,0},{2,3},{3,2},{4,5},{5,4},{6,7},{7,6},{8,9},{9,8},{10,11... | collective-permute-start | bytes 786440 | tf_op jit(solution)/shard_map/ppermute | solution.py:65
  19.1 0.1 convert_reduce_fusion
  19.3 0.4 reshape.96
  19.7 0.1 compare_and_fusion
  19.8 5.1 %collective-permute-done.1 = bf16[64,2048]{1,0:T(8,128)(2,1)S(1)} collective-permute-done((bf16[64,2048]{1,0:T(8,128)(2,1)S(1)}, bf16[64,2048]{1,0:T(8,128)(2,1)S(1)}, u32[]{:S(2)}, u32[]{:S(2)}) %collective-permute-start.1) | collective-permute-done | bytes 262176 | tf_op jit(solution)/shard_map/ppermute | solution.py:65
  24.9 0.1 pad_maximum_fusion
  24.9 0.1 slice_bitcast_fusion.1
  25.0 0.1 copy.39
  25.1 0.1 copy.38
  25.1 0.5 %fusion.25 = f32[8,192,64,4]{1,2,3,0:T(8,128)S(1)} fusion(bf16[64,8,4,128]{3,2,1,0:T(4,128)(2,1)S(1)} %reshape.96, bf16[192,8,128,1]{2,1,0,3:T(8,128)(2,1)S(1)} %bitcast.73), kind=kOutput, calls=%fused_computation.31 | convolution fusion | flops 100663296 | bytes 2490368 | tf_op jit(solution)/shard_map/qkgd,skd->kgqs/dot_general | solution.py:44
  25.6 1.0 %fusion.48 = (f32[8,4,64]{2,1,0:T(4,128)S(1)}, bf16[8,4,64,192]{3,2,1,0:T(8,128)(2,1)S(1)}) fusion(f32[8,192,64,4]{1,2,3,0:T(8,128)S(1)} %fusion.25, pred[64,192]{1,0:T(8,128)(4,1)S(1)} %compare_and_fusion), kind=kOutput, calls=%fused_computation.76 | output fusion | flops 2752703 | bytes 2379776 | tf_op jit(solution)/shard_map/sub | solution.py:48
  26.6 0.5 %fusion.20 = bf16[64,8,4,128]{3,0,2,1:T(8,128)(2,1)S(1)} fusion(bf16[8,4,64,192]{3,2,1,0:T(8,128)(2,1)S(1)} %get-tuple-element.34, f32[64]{0:T(128)S(1)} %get-tuple-element.35, f32[64,8,4]{0,2,1:T(4,128)S(1)} %bitcast.82, bf16[192,8,128,1]{2,1,0,3:T(8,128)(2,1)S(1)} %bitcast.75), kind=kOutput, calls=%fused_computation.22 | convolution fusion | flops 101449728 | bytes 1712384 | tf_op jit(solution)/shard_map/kgqs,skd->qkgd/dot_general | solution.py:51
  27.0 0.4 copy.24
  27.5 0.4 convert_element_type.52
  27.8 0.0 collective-permute-done.2
  27.9 1.6 %collective-permute-start.4 = (bf16[64,4096]{1,0:T(8,128)(2,1)S(1)}, bf16[64,4096]{1,0:T(8,128)(2,1)S(1)}, u32[]{:S(2)}, u32[]{:S(2)}) collective-permute-start(bf16[64,4096]{1,0:T(8,128)(2,1)S(1)} %convert_element_type.52), channel_id=1, source_target_pairs={{0,8},{8,16},{16,24},{24,0},{1,9},{9,17},{17,25},{25,1},{2,10},{10... | collective-permute-start | bytes 1572872 | tf_op jit(solution)/shard_map/ppermute | solution.py:26
  29.5 0.1 slice.47
  29.6 0.7 %fusion.46 = (s32[1]{0:T(128)}, s32[1]{0:T(128)}, s32[1]{0:T(128)}, s32[1]{0:T(128)}) fusion(s32[4]{0:T(128)S(1)} %bitcast.77, s32[]{:T(128)S(6)} %select_n.174, s32[]{:T(128)S(6)} %select_n.180, s32[]{:T(128)S(6)} %select_n.179, s32[]{:T(128)S(6)} %select_n.173), kind=kLoop, calls=%fused_computation.74 | loop fusion | bytes 48 | tf_op jit(solution)/shard_map/jit(dynamic_index_in_dim)/dynamic_slice | solution.py:214
  31.5 0.6 %fusion.45 = (s32[1]{0:T(128)}, s32[1]{0:T(128)}) fusion(s32[2]{0:T(128)S(1)} %slice.47, s32[]{:T(128)S(6)} %select_n.176, s32[]{:T(128)S(6)} %select_n.182), kind=kLoop, calls=%fused_computation.73 | loop fusion | bytes 24 | tf_op jit(solution)/shard_map/jit(dynamic_index_in_dim)/dynamic_slice | solution.py:218
  34.7 0.0 collective-permute-done.3
  34.7 0.1 collective-permute-start.5
  34.8 7.3 %collective-permute-done.4 = bf16[64,4096]{1,0:T(8,128)(2,1)S(1)} collective-permute-done((bf16[64,4096]{1,0:T(8,128)(2,1)S(1)}, bf16[64,4096]{1,0:T(8,128)(2,1)S(1)}, u32[]{:S(2)}, u32[]{:S(2)}) %collective-permute-start.4) | collective-permute-done | bytes 524320 | tf_op jit(solution)/shard_map/ppermute | solution.py:26
  42.0 0.0 collective-permute-start.6
  42.0 0.1 select_bitcast_fusion.3
  42.1 0.0 collective-permute-done.5
  42.1 1.8 %collective-permute-done.6 = bf16[64,4096]{1,0:T(8,128)(2,1)S(1)} collective-permute-done((bf16[64,4096]{1,0:T(8,128)(2,1)S(1)}, bf16[64,4096]{1,0:T(8,128)(2,1)S(1)}, u32[]{:S(2)}, u32[]{:S(2)}) %collective-permute-start.6) | collective-permute-done | bytes 524320 | tf_op jit(solution)/shard_map/ppermute | solution.py:20
  43.9 0.1 select_bitcast_fusion.2
  44.0 1.1 %maximum_bitcast_fusion = bf16[1,2,64,4096]{3,2,1,0:T(8,128)(2,1)} fusion(bf16[1,64,4096]{2,1,0:T(8,128)(2,1)S(1)} %select_bitcast_fusion.2, bf16[1,64,4096]{2,1,0:T(8,128)(2,1)S(1)} %select_bitcast_fusion.3), kind=kLoop, calls=%fused_computation.23 | loop fusion | flops 524288 | bytes 2097152 | tf_op jit(solution)/shard_map/reshape | solution.py:227
  (23 shorter events, 0.2 us)
Async XLA Ops:
  0.0 7.2 %copy-start.4 = (s32[1,4]{1,0:T(1,128)S(1)}, s32[1,4]{1,0:T(1,128)}, u32[]{:S(2)}) copy-start(s32[1,4]{1,0:T(1,128)} %param.5) | copy-start | bytes 52
  0.0 7.2 %copy-start.5 = (s32[1,2]{1,0:T(1,128)S(1)}, s32[1,2]{1,0:T(1,128)}, u32[]{:S(2)}) copy-start(s32[1,2]{1,0:T(1,128)} %param.7) | copy-start | bytes 28
  2.6 9.3 %copy-start.3 = (s32[1,4,8]{2,1,0:T(4,128)S(1)}, s32[1,4,8]{2,1,0:T(4,128)}, u32[]{:S(2)}) copy-start(s32[1,4,8]{2,1,0:T(4,128)} %param.6) | copy-start | bytes 388
  4.1 13.5 %collective-permute-start = (bf16[64,2048]{1,0:T(8,128)(2,1)S(1)}, bf16[64,2048]{1,0:T(8,128)(2,1)S(1)}, u32[]{:S(2)}, u32[]{:S(2)}) collective-permute-start(bf16[64,2048]{1,0:T(8,128)(2,1)S(1)} %slice.48), channel_id=1, source_target_pairs={{0,2},{1,3},{2,0},{3,1},{4,6},{5,7},{6,4},{7,5},{8,10},{9,11},{10,... | collective-permute-start | bytes 786440 | tf_op jit(solution)/shard_map/ppermute | solution.py:60
  7.8 20.0 %collective-permute-start.2 = (s32[6]{0:T(128)}, s32[6]{0:T(128)S(1)}, u32[]{:S(2)}, u32[]{:S(2)}) collective-permute-start(s32[6]{0:T(128)} %pad_add_fusion.1), channel_id=1, source_target_pairs={{0,8},{8,16},{16,24},{24,0},{1,9},{9,17},{17,25},{25,1},{2,10},{10... | collective-permute-start | bytes 80 | tf_op jit(solution)/shard_map/ppermute | solution.py:26
  12.2 0.7 %copy-start = (s32[8]{0:T(128)}, s32[8]{0:T(128)S(1)}, u32[]{:S(2)}) copy-start(s32[8]{0:T(128)S(1)} %get-tuple-element.26) | copy-start | bytes 100
  15.0 4.1 %copy-start.1 = (s32[8]{0:T(128)S(1)}, s32[8]{0:T(128)}, u32[]{:S(2)}) copy-start(s32[8]{0:T(128)} %copy-done) | copy-start | bytes 100
  15.4 4.2 %copy-start.2 = (s32[64]{0:T(128)S(1)}, s32[64]{0:T(128)}, u32[]{:S(2)}) copy-start(s32[64]{0:T(128)} %get-tuple-element.15) | copy-start | bytes 772
  15.8 18.8 %collective-permute-start.3 = (bf16[64,4096]{1,0:T(8,128)(2,1)S(1)}, bf16[64,4096]{1,0:T(8,128)(2,1)S(1)}, u32[]{:S(2)}, u32[]{:S(2)}) collective-permute-start(bf16[64,4096]{1,0:T(8,128)(2,1)S(1)} %convert_element_type.48), channel_id=1, source_target_pairs={{0,8},{8,16},{16,24},{24,0},{1,9},{9,17},{17,25},{25,1},{2,10},{10... | collective-permute-start | bytes 1572872 | tf_op jit(solution)/shard_map/ppermute | solution.py:26
  17.6 7.3 %collective-permute-start.1 = (bf16[64,2048]{1,0:T(8,128)(2,1)S(1)}, bf16[64,2048]{1,0:T(8,128)(2,1)S(1)}, u32[]{:S(2)}, u32[]{:S(2)}) collective-permute-start(bf16[64,2048]{1,0:T(8,128)(2,1)S(1)} %broadcast_select_fusion), channel_id=1, source_target_pairs={{0,1},{1,0},{2,3},{3,2},{4,5},{5,4},{6,7},{7,6},{8,9},{9,8},{10,11... | collective-permute-start | bytes 786440 | tf_op jit(solution)/shard_map/ppermute | solution.py:65
  27.9 14.2 %collective-permute-start.4 = (bf16[64,4096]{1,0:T(8,128)(2,1)S(1)}, bf16[64,4096]{1,0:T(8,128)(2,1)S(1)}, u32[]{:S(2)}, u32[]{:S(2)}) collective-permute-start(bf16[64,4096]{1,0:T(8,128)(2,1)S(1)} %convert_element_type.52), channel_id=1, source_target_pairs={{0,8},{8,16},{16,24},{24,0},{1,9},{9,17},{17,25},{25,1},{2,10},{10... | collective-permute-start | bytes 1572872 | tf_op jit(solution)/shard_map/ppermute | solution.py:26
  34.7 7.4 %collective-permute-start.5 = (bf16[64,4096]{1,0:T(8,128)(2,1)S(1)}, bf16[64,4096]{1,0:T(8,128)(2,1)S(1)}, u32[]{:S(2)}, u32[]{:S(2)}) collective-permute-start(bf16[64,4096]{1,0:T(8,128)(2,1)S(1)} %collective-permute-done.3), channel_id=1, source_target_pairs={{0,4},{4,0},{1,5},{5,1},{2,6},{6,2},{3,7},{7,3},{8,12},{12,8},{9,1... | collective-permute-start | bytes 1572872 | tf_op jit(solution)/shard_map/ppermute | solution.py:20
  42.0 1.9 %collective-permute-start.6 = (bf16[64,4096]{1,0:T(8,128)(2,1)S(1)}, bf16[64,4096]{1,0:T(8,128)(2,1)S(1)}, u32[]{:S(2)}, u32[]{:S(2)}) collective-permute-start(bf16[64,4096]{1,0:T(8,128)(2,1)S(1)} %collective-permute-done.4), channel_id=1, source_target_pairs={{0,4},{4,0},{1,5},{5,1},{2,6},{6,2},{3,7},{7,3},{8,12},{12,8},{9,1... | collective-permute-start | bytes 1572872 | tf_op jit(solution)/shard_map/ppermute | solution.py:20

commit v25 on v22

--- a/solution.py
+++ b/solution.py
@@ -218,7 +218,8 @@
         jnp.where(short_index(replica) == 1 - own_hand, short_next, long_next),
         jnp.where(short_index(partner) == partner_hand, partner_short, partner_long),
     ]
-    out = jnp.stack(sent, axis=0)
+    out = lax.optimization_barrier(jnp.stack([sent[0], sent[0]], axis=0))
+    out = lax.dynamic_update_slice_in_dim(out, sent[1][None], 1, 0)
     return out.reshape(1, RPR, seg_len, D)
 
 

time: 45.2 us -> 45 us (level)
  waiting for transfers between devices: 14.2 us -> 13.1 us
  other arithmetic: 5.86 us -> 6.71 us
    reshape x1 -> x0, other arithmetic: 1.06 us -> none  [shards(): return out.reshape(1, RPR, seg_len, D)]
    ppermute x2, waiting for transfers between devices: 1.84 us -> 0.79 us  [swapped(): return lax.ppermute(block, axis, route)]
    another operation x2, other arithmetic: 0.11 us -> 1.11 us  [shards(): out = lax.optimization_barrier(jnp.stack([sent[0], sent[0]], axis=0))]
    dynamic_update_slice x0 -> x1, other arithmetic: none -> 0.92 us  [shards(): out = lax.dynamic_update_slice_in_dim(out, sent[1][None], 1, 0)]
  transfers between devices with their start and end apart: 7 -> 7, of which waited for: 3 -> 3; matrix products, arithmetic and copies ran while one was open for 21% -> 24% of each run, Pallas kernels for 0% -> 0%
where the time goes in v25:
time: 45 us; the launch traced here: 44.8 us
  waiting for transfers between devices  13.1 us (29%)
  starting transfers between devices  9.53 us (21%)
  between operations  7.78 us (17%)
  other arithmetic  6.71 us (15%)
  local copies, waits for them, and re-layouts  5.48 us (12%)
  matrix products  2.21 us (5%)
    ppermute x3, waiting for transfers between devices, passed_along(): return lax.ppermute(value, axis, pairs)  7.16 us
    ppermute x1, waiting for transfers between devices, gathered(): over_x = lax.ppermute(onward, 'seq', [(j, j ^ 1) for j in range(4)])  5.11 us
    ppermute x3, starting transfers between devices, passed_along(): return lax.ppermute(value, axis, pairs)  4.84 us
    ppermute x1, starting transfers between devices, gathered(): over_y = lax.ppermute(block, 'seq', [(j, j ^ 2) for j in range(4)])  3.06 us
    convert_element_type x4, local copies, waits for them, and re-layouts, attend_row(): return result.reshape(seg_len, D).astype(jnp.bfloat16)  1.59 us
    ppermute x1, starting transfers between devices, gathered(): over_x = lax.ppermute(onward, 'seq', [(j, j ^ 1) for j in range(4)])  1.56 us
    select_n x1, other arithmetic, pick(): return jnp.where(first_if, a, b)  1.48 us
    sub x2, other arithmetic, attend_row(): weights = jnp.where(allowed, jnp.exp(scores - row_top), 0.0)  1.31 us
  transfers between devices with their start and end apart: 7, of which 3 were waited for; matrix products, arithmetic and copies ran while one was open for 24% of the time, Pallas kernels for 0%

profile of v25, /device:TPU:0, one launch (start us, length us, event | category | flops | bytes accessed | tf_op | source)
XLA Modules:
  0.0 44.8 jit_solution(18294456996411061680)
XLA Ops:
  0.0 0.8 %constant_dynamic-slice_fusion.1 = s32[1,2]{1,0:T(1,128)S(1)} fusion(s32[1,4]{1,0:T(1,128)} %param.5, s32[]{:T(128)S(6)} %select_n.129), kind=kLoop, calls=%fused_computation.61 | loop fusion | bytes 20 | tf_op jit(solution)/shard_map/dynamic_slice | solution.py:163
  0.8 0.6 %fusion.49 = (s32[1,1]{1,0:T(1,128)}, s32[1,1]{1,0:T(1,128)}) fusion(s32[1,2]{1,0:T(1,128)S(1)} %constant_dynamic-slice_fusion.1), kind=kLoop, calls=%fused_computation.73 | loop fusion | bytes 16 | tf_op jit(solution)/shard_map/slice | solution.py:164
  2.6 0.0 copy-start.3
  2.6 1.5 %select_bitcast_fusion.1 = (bf16[64,6144]{1,0:T(8,128)(2,1)S(1)}, bf16[64,6144]{1,0:T(8,128)(2,1)S(1)}) fusion(pred[]{:T(512)S(6)} %ge.32, bf16[1,2,64,6144]{3,2,1,0:T(8,128)(2,1)} %param.4), kind=kLoop, calls=%fused_computation.30 | loop fusion | flops 786432 | bytes 3145729 | tf_op jit(solution)/shard_map/jit(_where)/select_n | solution.py:167
  4.1 3.1 %collective-permute-start = (bf16[64,2048]{1,0:T(8,128)(2,1)S(1)}, bf16[64,2048]{1,0:T(8,128)(2,1)S(1)}, u32[]{:S(2)}, u32[]{:S(2)}) collective-permute-start(bf16[64,2048]{1,0:T(8,128)(2,1)S(1)} %slice.72), channel_id=1, source_target_pairs={{0,2},{1,3},{2,0},{3,1},{4,6},{5,7},{6,4},{7,5},{8,10},{9,11},{10,... | collective-permute-start | bytes 786440 | tf_op jit(solution)/shard_map/ppermute | solution.py:60
  7.2 0.7 %pad_add_fusion.1 = s32[6]{0:T(128)} fusion(s32[2]{0:T(128)S(1)} %bitcast.84, s32[4]{0:T(128)S(1)} %bitcast.83), kind=kLoop, calls=%fused_computation.64 | loop fusion | flops 6 | bytes 48 | tf_op jit(solution)/shard_map/concatenate | solution.py:184
  7.8 1.6 %collective-permute-start.2 = (s32[6]{0:T(128)}, s32[6]{0:T(128)S(1)}, u32[]{:S(2)}, u32[]{:S(2)}) collective-permute-start(s32[6]{0:T(128)} %pad_add_fusion.1), channel_id=1, source_target_pairs={{0,8},{8,16},{16,24},{24,0},{1,9},{9,17},{17,25},{25,1},{2,10},{10... | collective-permute-start | bytes 80 | tf_op jit(solution)/shard_map/ppermute | solution.py:26
  11.9 0.2 reduce_window_sum.11
  12.1 0.6 %convert_reduce_fusion.2 = (s32[64]{0:T(128)}, s32[64]{0:T(128)S(1)}) fusion(s32[64]{0:T(128)S(1)} %iota_add_fusion, s32[8]{0:T(128)S(1)} %get-tuple-element.22, s32[8]{0:T(128)S(1)} %get-tuple-element.21), kind=kLoop, calls=%fused_computation.52 | loop fusion | flops 2944 | bytes 832 | tf_op jit(solution)/shard_map/reduce_sum | solution.py:30
  12.7 0.1 compare_and_fusion.1
  12.9 0.4 reshape.87
  13.3 0.6 %fusion.16 = f32[8,4,64,64]{2,3,1,0:T(8,128)S(1)} fusion(bf16[64,8,4,128]{3,2,1,0:T(4,128)(2,1)S(1)} %reshape.87, bf16[64,8,128,1]{2,1,0,3:T(8,128)(2,1)S(1)} %bitcast.78), kind=kOutput, calls=%fused_computation.17 | convolution fusion | flops 33685504 | bytes 1179648 | tf_op jit(solution)/shard_map/qkgd,skd->kgqs/dot_general | solution.py:44
  13.9 0.3 fusion.50
  14.3 0.7 %fusion.19 = bf16[64,8,4,128]{3,0,2,1:T(8,128)(2,1)S(1)} fusion(f32[64]{0:T(128)S(1)} %get-tuple-element.34, f32[64,8,4]{0,2,1:T(4,128)S(1)} %bitcast.85, bf16[64,8,128,1]{2,1,0,3:T(8,128)(2,1)S(1)} %bitcast.80, f32[8,4,64,64]{2,3,1,0:T(8,128)S(1)} %fusion.16, pred[64,64]{0,1:T(8,128)(4,1)S(1)} %compare_and_fusion.1), kind=kOutput, calls=%fused_computation.21 | convolution fusion | flops 34867264 | bytes 1192192 | tf_op jit(solution)/shard_map/kgqs,skd->qkgd/dot_general | solution.py:51
  14.9 0.4 copy.20
  15.3 0.0 copy-start.2
  15.4 0.4 convert_element_type.48
  15.7 1.6 %collective-permute-start.3 = (bf16[64,4096]{1,0:T(8,128)(2,1)S(1)}, bf16[64,4096]{1,0:T(8,128)(2,1)S(1)}, u32[]{:S(2)}, u32[]{:S(2)}) collective-permute-start(bf16[64,4096]{1,0:T(8,128)(2,1)S(1)} %convert_element_type.48), channel_id=1, source_target_pairs={{0,8},{8,16},{16,24},{24,0},{1,9},{9,17},{17,25},{25,1},{2,10},{10... | collective-permute-start | bytes 1572872 | tf_op jit(solution)/shard_map/ppermute | solution.py:26
  17.4 0.1 pad_add_fusion
  17.5 0.0 collective-permute-done
  17.5 1.6 %collective-permute-start.1 = (bf16[64,2048]{1,0:T(8,128)(2,1)S(1)}, bf16[64,2048]{1,0:T(8,128)(2,1)S(1)}, u32[]{:S(2)}, u32[]{:S(2)}) collective-permute-start(bf16[64,2048]{1,0:T(8,128)(2,1)S(1)} %broadcast_select_fusion), channel_id=1, source_target_pairs={{0,1},{1,0},{2,3},{3,2},{4,5},{5,4},{6,7},{7,6},{8,9},{9,8},{10,11... | collective-permute-start | bytes 786440 | tf_op jit(solution)/shard_map/ppermute | solution.py:65
  19.1 0.1 convert_reduce_fusion
  19.2 0.4 reshape.88
  19.6 0.1 compare_and_fusion
  19.7 5.1 %collective-permute-done.1 = bf16[64,2048]{1,0:T(8,128)(2,1)S(1)} collective-permute-done((bf16[64,2048]{1,0:T(8,128)(2,1)S(1)}, bf16[64,2048]{1,0:T(8,128)(2,1)S(1)}, u32[]{:S(2)}, u32[]{:S(2)}) %collective-permute-start.1) | collective-permute-done | bytes 262176 | tf_op jit(solution)/shard_map/ppermute | solution.py:65
  24.8 0.1 pad_maximum_fusion.1
  24.8 0.1 slice_bitcast_fusion.1
  24.9 0.1 copy.39
  25.0 0.1 copy.38
  25.1 0.5 %fusion.25 = f32[8,192,64,4]{1,2,3,0:T(8,128)S(1)} fusion(bf16[64,8,4,128]{3,2,1,0:T(4,128)(2,1)S(1)} %reshape.88, bf16[192,8,128,1]{2,1,0,3:T(8,128)(2,1)S(1)} %bitcast.76), kind=kOutput, calls=%fused_computation.32 | convolution fusion | flops 100663296 | bytes 2490368 | tf_op jit(solution)/shard_map/qkgd,skd->kgqs/dot_general | solution.py:44
  25.5 1.0 %fusion.51 = (f32[8,4,64]{2,1,0:T(4,128)S(1)}, bf16[8,4,64,192]{3,2,1,0:T(8,128)(2,1)S(1)}) fusion(f32[8,192,64,4]{1,2,3,0:T(8,128)S(1)} %fusion.25, pred[64,192]{1,0:T(8,128)(4,1)S(1)} %compare_and_fusion), kind=kOutput, calls=%fused_computation.75 | output fusion | flops 2752703 | bytes 2379776 | tf_op jit(solution)/shard_map/sub | solution.py:48
  26.5 0.5 %fusion.20 = bf16[64,8,4,128]{3,0,2,1:T(8,128)(2,1)S(1)} fusion(bf16[8,4,64,192]{3,2,1,0:T(8,128)(2,1)S(1)} %get-tuple-element.32, f32[64]{0:T(128)S(1)} %get-tuple-element.33, f32[64,8,4]{0,2,1:T(4,128)S(1)} %bitcast.86, bf16[192,8,128,1]{2,1,0,3:T(8,128)(2,1)S(1)} %bitcast.79), kind=kOutput, calls=%fused_computation.22 | convolution fusion | flops 101449728 | bytes 1712384 | tf_op jit(solution)/shard_map/kgqs,skd->qkgd/dot_general | solution.py:51
  26.9 0.4 copy.24
  27.4 0.4 convert_element_type.52
  27.8 0.0 collective-permute-done.2
  27.8 1.6 %collective-permute-start.4 = (bf16[64,4096]{1,0:T(8,128)(2,1)S(1)}, bf16[64,4096]{1,0:T(8,128)(2,1)S(1)}, u32[]{:S(2)}, u32[]{:S(2)}) collective-permute-start(bf16[64,4096]{1,0:T(8,128)(2,1)S(1)} %convert_element_type.52), channel_id=1, source_target_pairs={{0,8},{8,16},{16,24},{24,0},{1,9},{9,17},{17,25},{25,1},{2,10},{10... | collective-permute-start | bytes 1572872 | tf_op jit(solution)/shard_map/ppermute | solution.py:26
  29.4 0.1 slice.71
  29.5 0.7 %fusion.48 = (s32[1]{0:T(128)}, s32[1]{0:T(128)}, s32[1]{0:T(128)}, s32[1]{0:T(128)}) fusion(s32[4]{0:T(128)S(1)} %bitcast.81, s32[]{:T(128)S(6)} %select_n.158, s32[]{:T(128)S(6)} %select_n.157, s32[]{:T(128)S(6)} %select_n.129, s32[]{:T(128)S(6)} %select_n.152), kind=kLoop, calls=%fused_computation.72 | loop fusion | bytes 48 | tf_op jit(solution)/shard_map/jit(dynamic_index_in_dim)/dynamic_slice | solution.py:209
  32.7 0.7 %fusion.47 = (s32[1]{0:T(128)}, s32[1]{0:T(128)}) fusion(s32[2]{0:T(128)S(1)} %slice.71, s32[]{:T(128)S(6)} %select_n.160, s32[]{:T(128)S(6)} %select_n.154), kind=kLoop, calls=%fused_computation.71 | loop fusion | bytes 24 | tf_op jit(solution)/shard_map/jit(dynamic_index_in_dim)/dynamic_slice | solution.py:214
  34.7 0.0 collective-permute-done.3
  34.7 0.1 collective-permute-start.5
  34.8 7.2 %collective-permute-done.4 = bf16[64,4096]{1,0:T(8,128)(2,1)S(1)} collective-permute-done((bf16[64,4096]{1,0:T(8,128)(2,1)S(1)}, bf16[64,4096]{1,0:T(8,128)(2,1)S(1)}, u32[]{:S(2)}, u32[]{:S(2)}) %collective-permute-start.4) | collective-permute-done | bytes 524320 | tf_op jit(solution)/shard_map/ppermute | solution.py:26
  41.9 0.0 collective-permute-start.6
  41.9 0.1 select_bitcast_fusion.2
  42.0 1.1 %pad_maximum_fusion = bf16[2,64,4096]{2,1,0:T(8,128)(2,1)} fusion(bf16[1,64,4096]{2,1,0:T(8,128)(2,1)S(1)} %select_bitcast_fusion.2), kind=kLoop, calls=%fused_computation.23 | loop fusion | flops 524288 | bytes 1572864 | tf_op jit(solution)/shard_map/stack | solution.py:221
  43.1 0.0 collective-permute-done.5
  43.1 0.8 %collective-permute-done.6 = bf16[64,4096]{1,0:T(8,128)(2,1)S(1)} collective-permute-done((bf16[64,4096]{1,0:T(8,128)(2,1)S(1)}, bf16[64,4096]{1,0:T(8,128)(2,1)S(1)}, u32[]{:S(2)}, u32[]{:S(2)}) %collective-permute-start.6) | collective-permute-done | bytes 524320 | tf_op jit(solution)/shard_map/ppermute | solution.py:20
  43.8 0.9 %bitcast_dynamic-update-slice_fusion = bf16[1,2,64,4096]{3,2,1,0:T(8,128)(2,1)} fusion(bf16[1,2,64,4096]{3,2,1,0:T(8,128)(2,1)} %bitcast.77, bf16[64,4096]{1,0:T(8,128)(2,1)S(1)} %collective-permute-done.5, bf16[64,4096]{1,0:T(8,128)(2,1)S(1)} %collective-permute-done.6, pred[]{:T(512)} %bitcast.22), kind=kLoop, calls=%fused_computation.31 | loop fusion | flops 262144 | bytes 1573376 | tf_op jit(solution)/shard_map/dynamic_update_slice | solution.py:222
  (22 shorter events, 0.2 us)
Async XLA Ops:
  0.0 7.2 %copy-start.4 = (s32[1,4]{1,0:T(1,128)S(1)}, s32[1,4]{1,0:T(1,128)}, u32[]{:S(2)}) copy-start(s32[1,4]{1,0:T(1,128)} %param.5) | copy-start | bytes 52
  0.0 7.2 %copy-start.5 = (s32[1,2]{1,0:T(1,128)S(1)}, s32[1,2]{1,0:T(1,128)}, u32[]{:S(2)}) copy-start(s32[1,2]{1,0:T(1,128)} %param.7) | copy-start | bytes 28
  2.6 9.3 %copy-start.3 = (s32[1,4,8]{2,1,0:T(4,128)S(1)}, s32[1,4,8]{2,1,0:T(4,128)}, u32[]{:S(2)}) copy-start(s32[1,4,8]{2,1,0:T(4,128)} %param.6) | copy-start | bytes 388
  4.1 13.4 %collective-permute-start = (bf16[64,2048]{1,0:T(8,128)(2,1)S(1)}, bf16[64,2048]{1,0:T(8,128)(2,1)S(1)}, u32[]{:S(2)}, u32[]{:S(2)}) collective-permute-start(bf16[64,2048]{1,0:T(8,128)(2,1)S(1)} %slice.72), channel_id=1, source_target_pairs={{0,2},{1,3},{2,0},{3,1},{4,6},{5,7},{6,4},{7,5},{8,10},{9,11},{10,... | collective-permute-start | bytes 786440 | tf_op jit(solution)/shard_map/ppermute | solution.py:60
  7.8 19.9 %collective-permute-start.2 = (s32[6]{0:T(128)}, s32[6]{0:T(128)S(1)}, u32[]{:S(2)}, u32[]{:S(2)}) collective-permute-start(s32[6]{0:T(128)} %pad_add_fusion.1), channel_id=1, source_target_pairs={{0,8},{8,16},{16,24},{24,0},{1,9},{9,17},{17,25},{25,1},{2,10},{10... | collective-permute-start | bytes 80 | tf_op jit(solution)/shard_map/ppermute | solution.py:26
  12.1 0.7 %copy-start = (s32[8]{0:T(128)}, s32[8]{0:T(128)S(1)}, u32[]{:S(2)}) copy-start(s32[8]{0:T(128)S(1)} %get-tuple-element.22) | copy-start | bytes 100
  14.9 4.1 %copy-start.1 = (s32[8]{0:T(128)S(1)}, s32[8]{0:T(128)}, u32[]{:S(2)}) copy-start(s32[8]{0:T(128)} %copy-done) | copy-start | bytes 100
  15.3 4.2 %copy-start.2 = (s32[64]{0:T(128)S(1)}, s32[64]{0:T(128)}, u32[]{:S(2)}) copy-start(s32[64]{0:T(128)} %get-tuple-element.13) | copy-start | bytes 772
  15.7 19.0 %collective-permute-start.3 = (bf16[64,4096]{1,0:T(8,128)(2,1)S(1)}, bf16[64,4096]{1,0:T(8,128)(2,1)S(1)}, u32[]{:S(2)}, u32[]{:S(2)}) collective-permute-start(bf16[64,4096]{1,0:T(8,128)(2,1)S(1)} %convert_element_type.48), channel_id=1, source_target_pairs={{0,8},{8,16},{16,24},{24,0},{1,9},{9,17},{17,25},{25,1},{2,10},{10... | collective-permute-start | bytes 1572872 | tf_op jit(solution)/shard_map/ppermute | solution.py:26
  17.5 7.3 %collective-permute-start.1 = (bf16[64,2048]{1,0:T(8,128)(2,1)S(1)}, bf16[64,2048]{1,0:T(8,128)(2,1)S(1)}, u32[]{:S(2)}, u32[]{:S(2)}) collective-permute-start(bf16[64,2048]{1,0:T(8,128)(2,1)S(1)} %broadcast_select_fusion), channel_id=1, source_target_pairs={{0,1},{1,0},{2,3},{3,2},{4,5},{5,4},{6,7},{7,6},{8,9},{9,8},{10,11... | collective-permute-start | bytes 786440 | tf_op jit(solution)/shard_map/ppermute | solution.py:65
  27.8 14.2 %collective-permute-start.4 = (bf16[64,4096]{1,0:T(8,128)(2,1)S(1)}, bf16[64,4096]{1,0:T(8,128)(2,1)S(1)}, u32[]{:S(2)}, u32[]{:S(2)}) collective-permute-start(bf16[64,4096]{1,0:T(8,128)(2,1)S(1)} %convert_element_type.52), channel_id=1, source_target_pairs={{0,8},{8,16},{16,24},{24,0},{1,9},{9,17},{17,25},{25,1},{2,10},{10... | collective-permute-start | bytes 1572872 | tf_op jit(solution)/shard_map/ppermute | solution.py:26
  34.7 8.4 %collective-permute-start.5 = (bf16[64,4096]{1,0:T(8,128)(2,1)S(1)}, bf16[64,4096]{1,0:T(8,128)(2,1)S(1)}, u32[]{:S(2)}, u32[]{:S(2)}) collective-permute-start(bf16[64,4096]{1,0:T(8,128)(2,1)S(1)} %collective-permute-done.3), channel_id=1, source_target_pairs={{0,4},{4,0},{1,5},{5,1},{2,6},{6,2},{3,7},{7,3},{8,12},{12,8},{9,1... | collective-permute-start | bytes 1572872 | tf_op jit(solution)/shard_map/ppermute | solution.py:20
  41.9 1.9 %collective-permute-start.6 = (bf16[64,4096]{1,0:T(8,128)(2,1)S(1)}, bf16[64,4096]{1,0:T(8,128)(2,1)S(1)}, u32[]{:S(2)}, u32[]{:S(2)}) collective-permute-start(bf16[64,4096]{1,0:T(8,128)(2,1)S(1)} %collective-permute-done.4), channel_id=1, source_target_pairs={{0,4},{4,0},{1,5},{5,1},{2,6},{6,2},{3,7},{7,3},{8,12},{12,8},{9,1... | collective-permute-start | bytes 1572872 | tf_op jit(solution)/shard_map/ppermute | solution.py:20

commit v26 on v25

--- a/solution.py
+++ b/solution.py
@@ -166,11 +166,13 @@
     def pick(first_if, a, b):
         return jnp.where(first_if, a, b)
 
-    short_rows = pick(swap_second, own_rows[0], own_rows[1])
+    def short_part(lo, hi):
+        return pick(swap_second, own_rows[0, :, lo:hi], own_rows[1, :, lo:hi])
+
     short_out = attend_row(
-        short_rows[:, :D],
-        short_rows[:, D:D + key_value_width],
-        short_rows[:, D + key_value_width:],
+        short_part(0, D),
+        short_part(D, D + key_value_width),
+        short_part(D + key_value_width, D + 2 * key_value_width),
         query_pos,
         query_pos,
         pick(swap_second, own_ends[0], own_ends[1]),

time: 45 us -> 51.2 us (1.14)
  other arithmetic: 6.71 us -> 9.67 us
  local copies, waits for them, and re-layouts: 5.48 us -> 7.72 us
  matrix products: 2.21 us -> 3.14 us
    unnamed x18 -> x23, local copies, waits for them, and re-layouts: 0.27 us -> 2.46 us
    concatenate x1, other arithmetic: 0.07 us -> 1.01 us  [shards(): kv_all = jnp.concatenate(pieces, axis=0)]
    dot_general x2, matrix products: 1.09 us -> 2.03 us  [attend_row(): jnp.einsum('qkgd,skd->kgqs', queries, keys, preferred_element_type=jnp.fl...]
    select_n x1, other arithmetic: 0.03 us -> 0.73 us  [gathered(): onward = jnp.where(odd, over_y, block)]
    unnamed x0 -> x1, other arithmetic: none -> 0.68 us
    convert_element_type x1, other arithmetic: 0.01 us -> 0.6 us  [attend_row(): valid = (query_pos < length).astype(jnp.float32)]
    select_n x1 -> x2, other arithmetic: 1.48 us -> 1.51 us  [pick(): return jnp.where(first_if, a, b)]
  transfers between devices with their start and end apart: 7 -> 7, of which waited for: 3 -> 3; matrix products, arithmetic and copies ran while one was open for 24% -> 33% of each run, Pallas kernels for 0% -> 0%
where the time goes in v26:
time: 51.2 us; the launch traced here: 50.9 us
  waiting for transfers between devices  13 us (25%)
  other arithmetic  9.67 us (19%)
  starting transfers between devices  9.46 us (18%)
  between operations  7.89 us (15%)
  local copies, waits for them, and re-layouts  7.72 us (15%)
  matrix products  3.14 us (6%)
    ppermute x3, waiting for transfers between devices, passed_along(): return lax.ppermute(value, axis, pairs)  6.8 us
    ppermute x1, waiting for transfers between devices, gathered(): over_x = lax.ppermute(onward, 'seq', [(j, j ^ 1) for j in range(4)])  5.43 us
    ppermute x3, starting transfers between devices, passed_along(): return lax.ppermute(value, axis, pairs)  4.83 us
    ppermute x1, starting transfers between devices, gathered(): over_y = lax.ppermute(block, 'seq', [(j, j ^ 2) for j in range(4)])  3.06 us
    unnamed x23, local copies, waits for them, and re-layouts  2.46 us
    dot_general x2, matrix products, attend_row(): jnp.einsum('qkgd,skd->kgqs', queries, keys, preferred_element_type=jnp.fl...  2.03 us
    convert_element_type x4, local copies, waits for them, and re-layouts, attend_row(): return result.reshape(seg_len, D).astype(jnp.bfloat16)  1.59 us
    select_n x2, other arithmetic, pick(): return jnp.where(first_if, a, b)  1.51 us
  transfers between devices with their start and end apart: 7, of which 3 were waited for; matrix products, arithmetic and copies ran while one was open for 33% of the time, Pallas kernels for 0%

profile of v26, /device:TPU:0, one launch (start us, length us, event | category | flops | bytes accessed | tf_op | source)
XLA Modules:
  0.0 50.9 jit_solution(12373943584173940687)
XLA Ops:
  0.0 0.9 %constant_dynamic-slice_fusion.1 = s32[1,2]{1,0:T(1,128)S(1)} fusion(s32[1,4]{1,0:T(1,128)} %param.5, s32[]{:T(128)S(6)} %select_n.152), kind=kLoop, calls=%fused_computation.63 | loop fusion | bytes 20 | tf_op jit(solution)/shard_map/dynamic_slice | solution.py:163
  0.9 0.6 %fusion.51 = (s32[1,1]{1,0:T(1,128)}, s32[1,1]{1,0:T(1,128)}) fusion(s32[1,2]{1,0:T(1,128)S(1)} %constant_dynamic-slice_fusion.1), kind=kLoop, calls=%fused_computation.75 | loop fusion | bytes 16 | tf_op jit(solution)/shard_map/slice | solution.py:164
  2.7 0.0 copy-start.5
  2.7 1.5 %select_bitcast_fusion = bf16[64,6144]{1,0:T(8,128)(2,1)S(1)} fusion(bf16[1,2,64,6144]{3,2,1,0:T(8,128)(2,1)} %param.4, pred[]{:T(512)S(6)} %ge.32), kind=kLoop, calls=%fused_computation.29 | loop fusion | flops 393216 | bytes 2359297 | tf_op jit(solution)/shard_map/jit(_where)/select_n | solution.py:167
  4.2 3.1 %collective-permute-start = (bf16[64,2048]{1,0:T(8,128)(2,1)S(1)}, bf16[64,2048]{1,0:T(8,128)(2,1)S(1)}, u32[]{:S(2)}, u32[]{:S(2)}) collective-permute-start(bf16[64,2048]{1,0:T(8,128)(2,1)S(1)} %slice.82), channel_id=1, source_target_pairs={{0,2},{1,3},{2,0},{3,1},{4,6},{5,7},{6,4},{7,5},{8,10},{9,11},{10,... | collective-permute-start | bytes 786440 | tf_op jit(solution)/shard_map/ppermute | solution.py:60
  7.3 0.6 %pad_add_fusion.1 = s32[6]{0:T(128)} fusion(s32[2]{0:T(128)S(1)} %bitcast.87, s32[4]{0:T(128)S(1)} %bitcast.86), kind=kLoop, calls=%fused_computation.66 | loop fusion | flops 6 | bytes 48 | tf_op jit(solution)/shard_map/concatenate | solution.py:186
  7.9 1.6 %collective-permute-start.2 = (s32[6]{0:T(128)}, s32[6]{0:T(128)S(1)}, u32[]{:S(2)}, u32[]{:S(2)}) collective-permute-start(s32[6]{0:T(128)} %pad_add_fusion.1), channel_id=1, source_target_pairs={{0,8},{8,16},{16,24},{24,0},{1,9},{9,17},{17,25},{25,1},{2,10},{10... | collective-permute-start | bytes 80 | tf_op jit(solution)/shard_map/ppermute | solution.py:26
  9.5 0.7 %fusion.34 = (bf16[8,8,8,128]{3,1,2,0:T(8,128)(2,1)S(1)}, bf16[8,8,8,128]{3,1,2,0:T(8,128)(2,1)}) fusion(bf16[2,64,6144]{2,1,0:T(8,128)(2,1)S(1)} %bitcast.77, pred[]{:T(512)S(6)} %ge.32), kind=kLoop, calls=%fused_computation.47 | loop fusion | flops 131072 | bytes 786433
  10.2 0.1 slice_select_fusion
  12.8 0.2 reduce_window_sum.11
  13.0 0.6 %convert_reduce_fusion.2 = (s32[64]{0:T(128)}, s32[64]{0:T(128)S(1)}) fusion(s32[64]{0:T(128)S(1)} %iota_add_fusion, s32[8]{0:T(128)S(1)} %get-tuple-element.20, s32[8]{0:T(128)S(1)} %get-tuple-element.19), kind=kLoop, calls=%fused_computation.54 | loop fusion | flops 2944 | bytes 832 | tf_op jit(solution)/shard_map/reduce_sum | solution.py:30
  13.6 0.1 compare_and_fusion.1
  13.7 1.6 %copy.44 = bf16[8,8,8,128]{3,2,1,0:T(8,128)(2,1)} copy(bf16[8,8,8,128]{3,1,2,0:T(8,128)(2,1)} %get-tuple-element.16) | data formatting | bytes 262144
  15.3 0.4 select_n.174
  15.6 0.7 %copy.43 = bf16[8,8,8,128]{3,2,1,0:T(8,128)(2,1)} copy(bf16[8,8,8,128]{3,1,2,0:T(8,128)(2,1)S(1)} %get-tuple-element.15) | data formatting | bytes 262144
  16.3 1.6 %fusion.16 = f32[8,4,64,64]{2,3,1,0:T(8,128)S(1)} fusion(bf16[64,8,4,128]{3,2,1,0:T(4,128)(2,1)S(1)} %select_n.174, bf16[64,8,128,1]{2,1,0,3:T(8,128)(2,1)} %bitcast.81), kind=kOutput, calls=%fused_computation.17 | convolution fusion | flops 33685504 | bytes 1179648 | tf_op jit(solution)/shard_map/qkgd,skd->kgqs/dot_general | solution.py:44
  17.9 0.3 fusion.52
  18.2 0.6 %compare_convert_fusion = (f32[64]{0:T(128)}, f32[64]{0:T(128)S(1)}) fusion(s32[]{:T(128)S(6)} %select_n.180, s32[]{:T(128)S(6)} %mul.54, s32[]{:T(128)S(6)} %select_n.177), kind=kLoop, calls=%fused_computation.55 | loop fusion | flops 320 | bytes 524 | tf_op jit(solution)/shard_map/convert_element_type | solution.py:53
  18.8 0.7 %fusion.19 = bf16[64,8,4,128]{3,0,2,1:T(8,128)(2,1)S(1)} fusion(f32[64]{0:T(128)S(1)} %get-tuple-element.32, f32[64,8,4]{0,2,1:T(4,128)S(1)} %bitcast.88, bf16[64,8,128,1]{2,1,0,3:T(8,128)(2,1)S(1)} %bitcast.83, f32[8,4,64,64]{2,3,1,0:T(8,128)S(1)} %fusion.16, pred[64,64]{0,1:T(8,128)(4,1)S(1)} %compare_and_fusion.1), kind=kOutput, calls=%fused_computation.21 | convolution fusion | flops 34867264 | bytes 1192192 | tf_op jit(solution)/shard_map/kgqs,skd->qkgd/dot_general | solution.py:51
  19.5 0.4 copy.23
  19.9 0.4 convert_element_type.48
  20.3 1.6 %collective-permute-start.3 = (bf16[64,4096]{1,0:T(8,128)(2,1)S(1)}, bf16[64,4096]{1,0:T(8,128)(2,1)S(1)}, u32[]{:S(2)}, u32[]{:S(2)}) collective-permute-start(bf16[64,4096]{1,0:T(8,128)(2,1)S(1)} %convert_element_type.48), channel_id=1, source_target_pairs={{0,8},{8,16},{16,24},{24,0},{1,9},{9,17},{17,25},{25,1},{2,10},{10... | collective-permute-start | bytes 1572872 | tf_op jit(solution)/shard_map/ppermute | solution.py:26
  22.0 0.1 pad_add_fusion
  22.0 0.7 %broadcast_select_fusion = bf16[64,2048]{1,0:T(8,128)(2,1)} fusion(bf16[64,2048]{1,0:T(8,128)(2,1)S(1)} %collective-permute-done, pred[]{:T(512)S(6)} %eq.43, bf16[64,6144]{1,0:T(8,128)(2,1)S(1)} %select_bitcast_fusion), kind=kLoop, calls=%fused_computation.43 | loop fusion | flops 131072 | bytes 786433 | tf_op jit(solution)/shard_map/jit(_where)/select_n | solution.py:62
  22.8 1.5 %collective-permute-start.1 = (bf16[64,2048]{1,0:T(8,128)(2,1)}, bf16[64,2048]{1,0:T(8,128)(2,1)}, u32[]{:S(2)}, u32[]{:S(2)}) collective-permute-start(bf16[64,2048]{1,0:T(8,128)(2,1)} %broadcast_select_fusion), channel_id=1, source_target_pairs={{0,1},{1,0},{2,3},{3,2},{4,5},{5,4},{6,7},{7,6},{8,9},{9,8},{10,11... | collective-permute-start | bytes 786440 | tf_op jit(solution)/shard_map/ppermute | solution.py:65
  24.3 0.1 convert_reduce_fusion
  24.4 0.4 reshape.89
  24.8 0.1 compare_and_fusion
  24.9 5.4 %collective-permute-done.1 = bf16[64,2048]{1,0:T(8,128)(2,1)} collective-permute-done((bf16[64,2048]{1,0:T(8,128)(2,1)}, bf16[64,2048]{1,0:T(8,128)(2,1)}, u32[]{:S(2)}, u32[]{:S(2)}) %collective-permute-start.1) | collective-permute-done | bytes 262176 | tf_op jit(solution)/shard_map/ppermute | solution.py:65
  30.3 1.0 %pad_maximum_fusion.1 = bf16[192,2048]{1,0:T(8,128)(2,1)S(1)} fusion(bf16[64,2048]{1,0:T(8,128)(2,1)} %collective-permute-done.1, bf16[64,2048]{1,0:T(8,128)(2,1)S(1)} %collective-permute-done, bf16[64,2048]{1,0:T(8,128)(2,1)S(1)} %slice.82), kind=kLoop, calls=%fused_computation.28 | loop fusion | flops 2359296 | bytes 1572864 | tf_op jit(solution)/shard_map/concatenate | solution.py:194
  31.3 0.1 slice_bitcast_fusion.1
  31.4 0.1 copy.42
  31.4 0.1 copy.41
  31.5 0.5 fusion.25
  32.0 1.0 %fusion.53 = (f32[8,4,64]{2,1,0:T(4,128)S(1)}, bf16[8,4,64,192]{3,2,1,0:T(8,128)(2,1)S(1)}) fusion(f32[8,192,64,4]{1,2,3,0:T(8,128)S(1)} %fusion.25, pred[64,192]{1,0:T(8,128)(4,1)S(1)} %compare_and_fusion), kind=kOutput, calls=%fused_computation.77 | output fusion | flops 2752703 | bytes 2379776 | tf_op jit(solution)/shard_map/sub | solution.py:48
  33.0 0.5 fusion.20
  33.4 0.4 copy.27
  33.8 0.4 convert_element_type.52
  34.2 1.6 %collective-permute-start.4 = (bf16[64,4096]{1,0:T(8,128)(2,1)S(1)}, bf16[64,4096]{1,0:T(8,128)(2,1)S(1)}, u32[]{:S(2)}, u32[]{:S(2)}) collective-permute-start(bf16[64,4096]{1,0:T(8,128)(2,1)S(1)} %convert_element_type.52), channel_id=1, source_target_pairs={{0,8},{8,16},{16,24},{24,0},{1,9},{9,17},{17,25},{25,1},{2,10},{10... | collective-permute-start | bytes 1572872 | tf_op jit(solution)/shard_map/ppermute | solution.py:26
  35.9 0.1 slice.81
  36.0 0.7 %fusion.50 = (s32[1]{0:T(128)}, s32[1]{0:T(128)}, s32[1]{0:T(128)}, s32[1]{0:T(128)}) fusion(s32[4]{0:T(128)S(1)} %bitcast.84, s32[]{:T(128)S(6)} %select_n.187, s32[]{:T(128)S(6)} %select_n.186, s32[]{:T(128)S(6)} %select_n.152, s32[]{:T(128)S(6)} %select_n.181), kind=kLoop, calls=%fused_computation.74 | loop fusion | bytes 48 | tf_op jit(solution)/shard_map/jit(dynamic_index_in_dim)/dynamic_slice | solution.py:211
  39.2 0.7 %fusion.49 = (s32[1]{0:T(128)}, s32[1]{0:T(128)}) fusion(s32[2]{0:T(128)S(1)} %slice.81, s32[]{:T(128)S(6)} %select_n.189, s32[]{:T(128)S(6)} %select_n.183), kind=kLoop, calls=%fused_computation.73 | loop fusion | bytes 24 | tf_op jit(solution)/shard_map/jit(dynamic_index_in_dim)/dynamic_slice | solution.py:216
  41.2 0.1 collective-permute-start.5
  41.3 6.8 %collective-permute-done.4 = bf16[64,4096]{1,0:T(8,128)(2,1)S(1)} collective-permute-done((bf16[64,4096]{1,0:T(8,128)(2,1)S(1)}, bf16[64,4096]{1,0:T(8,128)(2,1)S(1)}, u32[]{:S(2)}, u32[]{:S(2)}) %collective-permute-start.4) | collective-permute-done | bytes 524320 | tf_op jit(solution)/shard_map/ppermute | solution.py:26
  48.1 0.1 select_bitcast_fusion.1
  48.1 1.1 %pad_maximum_fusion = bf16[2,64,4096]{2,1,0:T(8,128)(2,1)} fusion(bf16[1,64,4096]{2,1,0:T(8,128)(2,1)S(1)} %select_bitcast_fusion.1), kind=kLoop, calls=%fused_computation.23 | loop fusion | flops 524288 | bytes 1572864 | tf_op jit(solution)/shard_map/stack | solution.py:223
  49.2 0.8 %collective-permute-done.6 = bf16[64,4096]{1,0:T(8,128)(2,1)S(1)} collective-permute-done((bf16[64,4096]{1,0:T(8,128)(2,1)S(1)}, bf16[64,4096]{1,0:T(8,128)(2,1)S(1)}, u32[]{:S(2)}, u32[]{:S(2)}) %collective-permute-start.6) | collective-permute-done | bytes 524320 | tf_op jit(solution)/shard_map/ppermute | solution.py:20
  50.0 0.9 %bitcast_dynamic-update-slice_fusion = bf16[1,2,64,4096]{3,2,1,0:T(8,128)(2,1)} fusion(bf16[1,2,64,4096]{3,2,1,0:T(8,128)(2,1)} %bitcast.80, bf16[64,4096]{1,0:T(8,128)(2,1)S(1)} %collective-permute-done.5, bf16[64,4096]{1,0:T(8,128)(2,1)S(1)} %collective-permute-done.6, pred[]{:T(512)} %bitcast.22), kind=kLoop, calls=%fused_computation.31 | loop fusion | flops 262144 | bytes 1573376 | tf_op jit(solution)/shard_map/dynamic_update_slice | solution.py:224
  (28 shorter events, 0.1 us)
Async XLA Ops:
  0.0 7.3 %copy-start.7 = (s32[1,4]{1,0:T(1,128)S(1)}, s32[1,4]{1,0:T(1,128)}, u32[]{:S(2)}) copy-start(s32[1,4]{1,0:T(1,128)} %param.5) | copy-start | bytes 52
  0.0 9.5 %copy-start = (bf16[1,2,64,6144]{3,2,1,0:T(8,128)(2,1)S(1)}, bf16[1,2,64,6144]{3,2,1,0:T(8,128)(2,1)}, u32[]{:S(2)}) copy-start(bf16[1,2,64,6144]{3,2,1,0:T(8,128)(2,1)} %param.4) | copy-start | bytes 4718596
  0.0 7.3 %copy-start.8 = (s32[1,2]{1,0:T(1,128)S(1)}, s32[1,2]{1,0:T(1,128)}, u32[]{:S(2)}) copy-start(s32[1,2]{1,0:T(1,128)} %param.7) | copy-start | bytes 28
  2.7 10.0 %copy-start.5 = (s32[1,4,8]{2,1,0:T(4,128)S(1)}, s32[1,4,8]{2,1,0:T(4,128)}, u32[]{:S(2)}) copy-start(s32[1,4,8]{2,1,0:T(4,128)} %param.6) | copy-start | bytes 388
  4.2 17.8 %collective-permute-start = (bf16[64,2048]{1,0:T(8,128)(2,1)S(1)}, bf16[64,2048]{1,0:T(8,128)(2,1)S(1)}, u32[]{:S(2)}, u32[]{:S(2)}) collective-permute-start(bf16[64,2048]{1,0:T(8,128)(2,1)S(1)} %slice.82), channel_id=1, source_target_pairs={{0,2},{1,3},{2,0},{3,1},{4,6},{5,7},{6,4},{7,5},{8,10},{9,11},{10,... | collective-permute-start | bytes 786440 | tf_op jit(solution)/shard_map/ppermute | solution.py:60
  7.9 26.3 %collective-permute-start.2 = (s32[6]{0:T(128)}, s32[6]{0:T(128)S(1)}, u32[]{:S(2)}, u32[]{:S(2)}) collective-permute-start(s32[6]{0:T(128)} %pad_add_fusion.1), channel_id=1, source_target_pairs={{0,8},{8,16},{16,24},{24,0},{1,9},{9,17},{17,25},{25,1},{2,10},{10... | collective-permute-start | bytes 80 | tf_op jit(solution)/shard_map/ppermute | solution.py:26
  13.0 0.7 %copy-start.2 = (s32[8]{0:T(128)}, s32[8]{0:T(128)S(1)}, u32[]{:S(2)}) copy-start(s32[8]{0:T(128)S(1)} %get-tuple-element.20) | copy-start | bytes 100
  16.3 2.5 %copy-start.1 = (bf16[8,8,8,128]{3,2,1,0:T(8,128)(2,1)S(1)}, bf16[8,8,8,128]{3,2,1,0:T(8,128)(2,1)}, u32[]{:S(2)}) copy-start(bf16[8,8,8,128]{3,2,1,0:T(8,128)(2,1)} %copy.43) | copy-start | bytes 393220
  19.5 4.8 %copy-start.3 = (s32[8]{0:T(128)S(1)}, s32[8]{0:T(128)}, u32[]{:S(2)}) copy-start(s32[8]{0:T(128)} %copy-done.2) | copy-start | bytes 100
  19.9 4.8 %copy-start.4 = (s32[64]{0:T(128)S(1)}, s32[64]{0:T(128)}, u32[]{:S(2)}) copy-start(s32[64]{0:T(128)} %get-tuple-element.13) | copy-start | bytes 772
  20.3 20.9 %collective-permute-start.3 = (bf16[64,4096]{1,0:T(8,128)(2,1)S(1)}, bf16[64,4096]{1,0:T(8,128)(2,1)S(1)}, u32[]{:S(2)}, u32[]{:S(2)}) collective-permute-start(bf16[64,4096]{1,0:T(8,128)(2,1)S(1)} %convert_element_type.48), channel_id=1, source_target_pairs={{0,8},{8,16},{16,24},{24,0},{1,9},{9,17},{17,25},{25,1},{2,10},{10... | collective-permute-start | bytes 1572872 | tf_op jit(solution)/shard_map/ppermute | solution.py:26
  22.8 7.5 %collective-permute-start.1 = (bf16[64,2048]{1,0:T(8,128)(2,1)}, bf16[64,2048]{1,0:T(8,128)(2,1)}, u32[]{:S(2)}, u32[]{:S(2)}) collective-permute-start(bf16[64,2048]{1,0:T(8,128)(2,1)} %broadcast_select_fusion), channel_id=1, source_target_pairs={{0,1},{1,0},{2,3},{3,2},{4,5},{5,4},{6,7},{7,6},{8,9},{9,8},{10,11... | collective-permute-start | bytes 786440 | tf_op jit(solution)/shard_map/ppermute | solution.py:65
  32.0 1.0 %copy-start.6 = (f32[64]{0:T(128)S(1)}, f32[64]{0:T(128)}, u32[]{:S(2)}) copy-start(f32[64]{0:T(128)} %get-tuple-element.31) | copy-start | bytes 772
  34.2 13.8 %collective-permute-start.4 = (bf16[64,4096]{1,0:T(8,128)(2,1)S(1)}, bf16[64,4096]{1,0:T(8,128)(2,1)S(1)}, u32[]{:S(2)}, u32[]{:S(2)}) collective-permute-start(bf16[64,4096]{1,0:T(8,128)(2,1)S(1)} %convert_element_type.52), channel_id=1, source_target_pairs={{0,8},{8,16},{16,24},{24,0},{1,9},{9,17},{17,25},{25,1},{2,10},{10... | collective-permute-start | bytes 1572872 | tf_op jit(solution)/shard_map/ppermute | solution.py:26
  41.2 8.0 %collective-permute-start.5 = (bf16[64,4096]{1,0:T(8,128)(2,1)S(1)}, bf16[64,4096]{1,0:T(8,128)(2,1)S(1)}, u32[]{:S(2)}, u32[]{:S(2)}) collective-permute-start(bf16[64,4096]{1,0:T(8,128)(2,1)S(1)} %collective-permute-done.3), channel_id=1, source_target_pairs={{0,4},{4,0},{1,5},{5,1},{2,6},{6,2},{3,7},{7,3},{8,12},{12,8},{9,1... | collective-permute-start | bytes 1572872 | tf_op jit(solution)/shard_map/ppermute | solution.py:20
  48.1 1.9 %collective-permute-start.6 = (bf16[64,4096]{1,0:T(8,128)(2,1)S(1)}, bf16[64,4096]{1,0:T(8,128)(2,1)S(1)}, u32[]{:S(2)}, u32[]{:S(2)}) collective-permute-start(bf16[64,4096]{1,0:T(8,128)(2,1)S(1)} %collective-permute-done.4), channel_id=1, source_target_pairs={{0,4},{4,0},{1,5},{5,1},{2,6},{6,2},{3,7},{7,3},{8,12},{12,8},{9,1... | collective-permute-start | bytes 1572872 | tf_op jit(solution)/shard_map/ppermute | solution.py:20
